TPU v7x, 256 devices: a whole 4x4x8 slice. The times are simulated.
256 devices in a mesh: seq: 32 (over x, z), head: 8 (over y, core).
Axes of the slice: x: 4, y: 4, z: 8, core: 2. Of those that a mesh axis runs over, the one named last changes fastest.
Arguments:
- queries: bfloat16 [16384, 8192], P('seq', 'head'), may hold values from -48 to 48
- keys: bfloat16 [16384, 1024], P('seq', 'head'), may hold values from -48 to 48
- values: bfloat16 [16384, 1024], P('seq', 'head'), may hold values from -6 to 6
- offsets: int32 [64], P('seq'), may hold values from 0 to 24064, as said below
- query_map: bfloat16 [64, 128, 64], P('head'), may hold values from -0.5 to 0.5
- key_map: bfloat16 [64, 128, 64], P('head'), may hold values from -0.5 to 0.5
- window_logit: float32 [64], P('head'), may hold values from -2 to 6
Outputs:
- attn_rows: bfloat16 [16384, 8192], P(('seq', 'head'))
Inputs may be any that keep to these rules, and one draw needn't show every extreme that they name: offsets[0] = 0, and each span's offset exceeds the one before by 256 or 512.
All inputs are finite; a program needn't handle non-finite values.
Results may differ from a plain program's by a relative error of at most 0.004.
The roundings to bfloat16 on the way count: a program that leaves them out, or rounds other values in their place, can miss the bound.
Values may be sent and summed in bfloat16 or wider, within the bound.
No kernel may reach another device: no remote copies, remote signals or barrier semaphores. Data moves between devices by JAX's collectives and lax.ppermute only.
A program may use at most 128 MiB of HBM per device.

v0:
```python
import math

import jax
import jax.numpy as jnp
from jax import lax
from jax.sharding import PartitionSpec as P

WINDOW = 64
BLOCK = 512
SPAN = 256


def passed_along(value, axis, steps):
    count = lax.axis_size(axis)
    first, last = (max(0, -steps), min(count, count - steps))
    return lax.ppermute(value, axis, [(source, source + steps) for source in range(first, last)])


def angle_tables(positions, half):
    frequency = [500000.0 ** (-float(order) / half) for order in range(half)]
    coarse = jnp.asarray([4096.0 * value % (2.0 * math.pi) for value in frequency], jnp.float32)
    medium = jnp.asarray([64.0 * value % (2.0 * math.pi) for value in frequency], jnp.float32)
    finest = jnp.asarray(frequency, jnp.float32)
    upper = (positions // 4096).astype(jnp.float32)[:, None] * coarse[None, :]
    middle = (positions // 64 % 64).astype(jnp.float32)[:, None] * medium[None, :]
    lower = (positions % 64).astype(jnp.float32)[:, None] * finest[None, :]
    cos_high = jnp.cos(upper) * jnp.cos(middle) - jnp.sin(upper) * jnp.sin(middle)
    sin_high = jnp.sin(upper) * jnp.cos(middle) + jnp.cos(upper) * jnp.sin(middle)
    cosine = cos_high * jnp.cos(lower) - sin_high * jnp.sin(lower)
    sine = sin_high * jnp.cos(lower) + cos_high * jnp.sin(lower)
    return (cosine, sine)


def rotate(rows, cosine, sine):
    half = rows.shape[-1] // 2
    first = rows[..., :half]
    second = rows[..., half:]
    cos_rows = cosine[:, None, :]
    sin_rows = sine[:, None, :]
    return jnp.concatenate(
        [first * cos_rows - second * sin_rows, second * cos_rows + first * sin_rows], axis=-1
    )


def two_softmax(logits):
    return jnp.concatenate(
        [jax.nn.softmax(logits, axis=-1), jax.nn.softmax(-logits, axis=-1)], axis=-1
    )


def split_parts(full_value):
    high_part = full_value.astype(jnp.bfloat16)
    rest_part = (full_value - high_part.astype(jnp.float32)).astype(jnp.bfloat16)
    return (high_part, rest_part)


def body(queries, keys, values, offsets, query_map, key_map, window_logit):
    tokens = queries.shape[0]
    heads = query_map.shape[0]
    head_dim = query_map.shape[1]
    feat = query_map.shape[2]
    kv_local = keys.shape[1] // head_dim
    group = heads // kv_local
    blocks = tokens // BLOCK
    extent = BLOCK + WINDOW
    positions = (offsets[:, None] + jnp.arange(SPAN, dtype=jnp.int32)[None, :]).reshape(tokens)
    cosine, sine = angle_tables(positions, head_dim // 2)
    rot_q = rotate(
        queries.reshape(tokens, heads, head_dim).astype(jnp.float32), cosine, sine
    ).astype(jnp.bfloat16)
    rot_k = rotate(
        keys.reshape(tokens, kv_local, head_dim).astype(jnp.float32), cosine, sine
    ).astype(jnp.bfloat16)
    value_rows = values.reshape(tokens, kv_local, head_dim)
    tail_keys, tail_values = passed_along(
        (rot_k[tokens - WINDOW :], value_rows[tokens - WINDOW :]), "seq", 1
    )
    ext_keys = jnp.concatenate([tail_keys, rot_k], axis=0)
    ext_values = jnp.concatenate([tail_values, value_rows], axis=0)
    valid = (jnp.arange(tokens + WINDOW) >= WINDOW) | (lax.axis_index("seq") > 0)
    query_logits = jnp.einsum("nhd,hdf->nhf", rot_q, query_map, preferred_element_type=jnp.float32)
    phi_query = (
        two_softmax(query_logits).astype(jnp.bfloat16).reshape(tokens, kv_local, group, 2 * feat)
    )
    grouped_map = key_map.reshape(kv_local, group, head_dim, feat)
    key_logits = jnp.einsum(
        "ngd,gkdf->ngkf", ext_keys, grouped_map, preferred_element_type=jnp.float32
    )
    phi_key = jnp.where(valid[:, None, None, None], two_softmax(key_logits), 0.0).astype(
        jnp.bfloat16
    )
    lag_phi = phi_key[:tokens].reshape(blocks, BLOCK, kv_local, group, 2 * feat)
    lag_values = ext_values[:tokens].reshape(blocks, BLOCK, kv_local, head_dim)
    block_states = jnp.einsum(
        "bjgkf,bjgd->bgkfd", lag_phi, lag_values, preferred_element_type=jnp.float32
    )
    block_norms = jnp.sum(lag_phi, axis=1, dtype=jnp.float32)
    total_state = jnp.sum(block_states, axis=0)
    total_norm = jnp.sum(block_norms, axis=0)
    before_state = jnp.concatenate(
        [jnp.zeros_like(block_states), jnp.cumsum(block_states, axis=0)[:-1]], axis=0
    )
    before_norm = jnp.concatenate(
        [jnp.zeros_like(block_norms), jnp.cumsum(block_norms, axis=0)[:-1]], axis=0
    )
    empty_state = jnp.zeros_like(total_state)
    empty_norm = jnp.zeros_like(total_norm)

    def forward_step(index, carry):
        moved = passed_along((carry[0] + total_state, carry[1] + total_norm), "seq", 1)
        return (moved[0], moved[1])

    prior_state, prior_norm = lax.fori_loop(
        0, lax.axis_size("seq") - 1, forward_step, (empty_state, empty_norm)
    )
    factor = jax.nn.sigmoid(window_logit).reshape(kv_local, group)
    rot_grouped = rot_q.reshape(tokens, kv_local, group, head_dim)
    row_index = jnp.arange(BLOCK)[:, None]
    col_index = jnp.arange(extent)[None, :]
    window_mask = (col_index > row_index) & (col_index <= row_index + WINDOW)
    linear_mask = col_index <= row_index
    live = valid[None, :]
    scores = jnp.einsum(
        "igkd,jgd->gkij", rot_grouped, ext_keys, preferred_element_type=jnp.float32
    ) / math.sqrt(head_dim)
    near_window = window_mask & live
    peak = jnp.max(jnp.where(near_window, scores, -jnp.inf), axis=-1, keepdims=True)
    weights = jnp.where(near_window, jnp.exp(scores - peak), 0.0)
    window_sum = jnp.sum(weights, axis=-1)
    affinity = jnp.einsum("igkf,jgkf->gkij", phi_query, phi_key, preferred_element_type=jnp.float32)
    affinity = jnp.where(linear_mask & live, affinity, 0.0)
    near_sum = jnp.sum(affinity, axis=-1)
    window_num = jnp.einsum(
        "gkij,jgd->igkd",
        weights.astype(jnp.bfloat16),
        ext_values,
        preferred_element_type=jnp.float32,
    )
    near_num = jnp.einsum(
        "gkij,jgd->igkd",
        affinity.astype(jnp.bfloat16),
        ext_values,
        preferred_element_type=jnp.float32,
    )
    state_now = prior_state + before_state[0]
    norm_now = prior_norm + before_norm[0]
    state_high, state_rest = split_parts(state_now)
    norm_high, norm_rest = split_parts(norm_now)
    far_num = jnp.einsum(
        "igkf,gkfd->igkd", phi_query, state_high, preferred_element_type=jnp.float32
    )
    far_num = far_num + jnp.einsum(
        "igkf,gkfd->igkd", phi_query, state_rest, preferred_element_type=jnp.float32
    )
    far_sum = jnp.einsum("igkf,gkf->igk", phi_query, norm_high, preferred_element_type=jnp.float32)
    far_sum = far_sum + jnp.einsum(
        "igkf,gkf->igk", phi_query, norm_rest, preferred_element_type=jnp.float32
    )
    head_factor = factor[None, :, :, None]
    numerator = head_factor * window_num + (1.0 - head_factor) * (near_num + far_num)
    denominator = factor[None] * jnp.transpose(window_sum, (2, 0, 1)) + (1.0 - factor[None]) * (
        jnp.transpose(near_sum, (2, 0, 1)) + far_sum
    )
    outputs = (numerator / denominator[..., None]).astype(jnp.bfloat16)
    result = outputs.reshape(tokens, heads * head_dim)
    return lax.all_to_all(result, "head", split_axis=0, concat_axis=1, tiled=True)


def solution(mesh):
    in_specs = (
        P("seq", "head"),
        P("seq", "head"),
        P("seq", "head"),
        P("seq"),
        P("head", None, None),
        P("head", None, None),
        P("head"),
    )
    out_specs = P(("seq", "head"), None)
    return jax.shard_map(body, mesh=mesh, in_specs=in_specs, out_specs=out_specs, check_vma=False)
```

profile of v0, /device:TPU:2, one launch (start us, length us, event | category | flops | bytes accessed | tf_op | source)
XLA Modules:
  0.0 574.2 jit_solution(12890598103782393555)
XLA Ops:
  1.9 2.4 subtract_convert_fusion.2
  4.4 3.8 collective-permute-start.3
  8.9 3.8 collective-permute-start.2
  12.7 2.2 fusion.67
  17.4 1.9 copy.69
  19.3 1.9 copy.70
  21.3 2.8 subtract_convert_fusion
  28.0 2.5 divide_convert_fusion
  32.5 2.3 copy.47
  36.2 3.6 fusion.25
  39.8 3.1 fusion.24
  42.9 4.0 convert_reduce_fusion
  48.2 486.7 %while.12 = (s32[]{:T(128)}, f32[1,8,128,128]{3,2,1,0:T(8,128)S(1)}, f32[1,8,128]{2,1,0:T(8,128)S(1)}, f32[1,8,128,128]{3,2,1,0:T(8,128)S(1)}, f32[1,8,128]{2,1,0:T(8,128)S(1)}, /*index=5*/s32[]{:T(128)}) while((s32[]{:T(128)}, f32[1,8,128,128]{3,2,1,0:T(8,128)S(1)}, f32[1,8,128]{2,1,0:T(8,128)S(1)}, f32[1,8,128,128]{3,2,1,0:T(8,128)S(1)}, ...), condition=%wide.region_11.12_spmd, body=%wide.region_10.11_spmd.sunk | while | flops 132098 | bytes 3698837 | solution.py:113
  48.3 4.0 collective-permute-start
  52.3 5.0 collective-permute-start.1
  57.3 8.3 %collective-permute-done.1 = f32[1,8,128]{2,1,0:T(8,128)S(1)} collective-permute-done((f32[1,8,128]{2,1,0:T(8,128)S(1)}, f32[1,8,128]{2,1,0:T(8,128)S(1)}, u32[]{:S(2)}, u32[]{:S(2)}) %collective-permute-start.1) | collective-permute-done | bytes 4128 | tf_op jit(solution)/shard_map/while/body/eval_jaxpr/ppermute | solution.py:16
  65.7 2.4 collective-permute-start
  68.1 4.4 collective-permute-start.1
  72.5 9.6 %collective-permute-done.1 = f32[1,8,128]{2,1,0:T(8,128)S(1)} collective-permute-done((f32[1,8,128]{2,1,0:T(8,128)S(1)}, f32[1,8,128]{2,1,0:T(8,128)S(1)}, u32[]{:S(2)}, u32[]{:S(2)}) %collective-permute-start.1) | collective-permute-done | bytes 4128 | tf_op jit(solution)/shard_map/while/body/eval_jaxpr/ppermute | solution.py:16
  84.0 2.7 collective-permute-start.1
  86.8 10.8 %collective-permute-done.1 = f32[1,8,128]{2,1,0:T(8,128)S(1)} collective-permute-done((f32[1,8,128]{2,1,0:T(8,128)S(1)}, f32[1,8,128]{2,1,0:T(8,128)S(1)}, u32[]{:S(2)}, u32[]{:S(2)}) %collective-permute-start.1) | collective-permute-done | bytes 4128 | tf_op jit(solution)/shard_map/while/body/eval_jaxpr/ppermute | solution.py:16
  97.7 1.9 collective-permute-start
  101.5 10.8 %collective-permute-done.1 = f32[1,8,128]{2,1,0:T(8,128)S(1)} collective-permute-done((f32[1,8,128]{2,1,0:T(8,128)S(1)}, f32[1,8,128]{2,1,0:T(8,128)S(1)}, u32[]{:S(2)}, u32[]{:S(2)}) %collective-permute-start.1) | collective-permute-done | bytes 4128 | tf_op jit(solution)/shard_map/while/body/eval_jaxpr/ppermute | solution.py:16
  112.4 1.9 collective-permute-start
  116.2 9.9 %collective-permute-done.1 = f32[1,8,128]{2,1,0:T(8,128)S(1)} collective-permute-done((f32[1,8,128]{2,1,0:T(8,128)S(1)}, f32[1,8,128]{2,1,0:T(8,128)S(1)}, u32[]{:S(2)}, u32[]{:S(2)}) %collective-permute-start.1) | collective-permute-done | bytes 4128 | tf_op jit(solution)/shard_map/while/body/eval_jaxpr/ppermute | solution.py:16
  128.1 1.9 collective-permute-start.1
  130.1 9.4 %collective-permute-done.1 = f32[1,8,128]{2,1,0:T(8,128)S(1)} collective-permute-done((f32[1,8,128]{2,1,0:T(8,128)S(1)}, f32[1,8,128]{2,1,0:T(8,128)S(1)}, u32[]{:S(2)}, u32[]{:S(2)}) %collective-permute-start.1) | collective-permute-done | bytes 4128 | tf_op jit(solution)/shard_map/while/body/eval_jaxpr/ppermute | solution.py:16
  141.4 1.9 collective-permute-start.1
  143.4 10.0 %collective-permute-done.1 = f32[1,8,128]{2,1,0:T(8,128)S(1)} collective-permute-done((f32[1,8,128]{2,1,0:T(8,128)S(1)}, f32[1,8,128]{2,1,0:T(8,128)S(1)}, u32[]{:S(2)}, u32[]{:S(2)}) %collective-permute-start.1) | collective-permute-done | bytes 4128 | tf_op jit(solution)/shard_map/while/body/eval_jaxpr/ppermute | solution.py:16
  155.4 1.9 collective-permute-start.1
  157.3 11.1 %collective-permute-done.1 = f32[1,8,128]{2,1,0:T(8,128)S(1)} collective-permute-done((f32[1,8,128]{2,1,0:T(8,128)S(1)}, f32[1,8,128]{2,1,0:T(8,128)S(1)}, u32[]{:S(2)}, u32[]{:S(2)}) %collective-permute-start.1) | collective-permute-done | bytes 4128 | tf_op jit(solution)/shard_map/while/body/eval_jaxpr/ppermute | solution.py:16
  168.5 1.9 collective-permute-start
  172.4 12.3 %collective-permute-done.1 = f32[1,8,128]{2,1,0:T(8,128)S(1)} collective-permute-done((f32[1,8,128]{2,1,0:T(8,128)S(1)}, f32[1,8,128]{2,1,0:T(8,128)S(1)}, u32[]{:S(2)}, u32[]{:S(2)}) %collective-permute-start.1) | collective-permute-done | bytes 4128 | tf_op jit(solution)/shard_map/while/body/eval_jaxpr/ppermute | solution.py:16
  188.6 13.4 %collective-permute-done.1 = f32[1,8,128]{2,1,0:T(8,128)S(1)} collective-permute-done((f32[1,8,128]{2,1,0:T(8,128)S(1)}, f32[1,8,128]{2,1,0:T(8,128)S(1)}, u32[]{:S(2)}, u32[]{:S(2)}) %collective-permute-start.1) | collective-permute-done | bytes 4128 | tf_op jit(solution)/shard_map/while/body/eval_jaxpr/ppermute | solution.py:16
  205.9 14.6 %collective-permute-done.1 = f32[1,8,128]{2,1,0:T(8,128)S(1)} collective-permute-done((f32[1,8,128]{2,1,0:T(8,128)S(1)}, f32[1,8,128]{2,1,0:T(8,128)S(1)}, u32[]{:S(2)}, u32[]{:S(2)}) %collective-permute-start.1) | collective-permute-done | bytes 4128 | tf_op jit(solution)/shard_map/while/body/eval_jaxpr/ppermute | solution.py:16
  224.4 14.3 %collective-permute-done.1 = f32[1,8,128]{2,1,0:T(8,128)S(1)} collective-permute-done((f32[1,8,128]{2,1,0:T(8,128)S(1)}, f32[1,8,128]{2,1,0:T(8,128)S(1)}, u32[]{:S(2)}, u32[]{:S(2)}) %collective-permute-start.1) | collective-permute-done | bytes 4128 | tf_op jit(solution)/shard_map/while/body/eval_jaxpr/ppermute | solution.py:16
  242.7 13.5 %collective-permute-done.1 = f32[1,8,128]{2,1,0:T(8,128)S(1)} collective-permute-done((f32[1,8,128]{2,1,0:T(8,128)S(1)}, f32[1,8,128]{2,1,0:T(8,128)S(1)}, u32[]{:S(2)}, u32[]{:S(2)}) %collective-permute-start.1) | collective-permute-done | bytes 4128 | tf_op jit(solution)/shard_map/while/body/eval_jaxpr/ppermute | solution.py:16
  258.2 1.9 collective-permute-start.1
  260.1 12.6 %collective-permute-done.1 = f32[1,8,128]{2,1,0:T(8,128)S(1)} collective-permute-done((f32[1,8,128]{2,1,0:T(8,128)S(1)}, f32[1,8,128]{2,1,0:T(8,128)S(1)}, u32[]{:S(2)}, u32[]{:S(2)}) %collective-permute-start.1) | collective-permute-done | bytes 4128 | tf_op jit(solution)/shard_map/while/body/eval_jaxpr/ppermute | solution.py:16
  276.6 11.7 %collective-permute-done.1 = f32[1,8,128]{2,1,0:T(8,128)S(1)} collective-permute-done((f32[1,8,128]{2,1,0:T(8,128)S(1)}, f32[1,8,128]{2,1,0:T(8,128)S(1)}, u32[]{:S(2)}, u32[]{:S(2)}) %collective-permute-start.1) | collective-permute-done | bytes 4128 | tf_op jit(solution)/shard_map/while/body/eval_jaxpr/ppermute | solution.py:16
  290.4 1.9 collective-permute-start.1
  292.3 10.9 %collective-permute-done.1 = f32[1,8,128]{2,1,0:T(8,128)S(1)} collective-permute-done((f32[1,8,128]{2,1,0:T(8,128)S(1)}, f32[1,8,128]{2,1,0:T(8,128)S(1)}, u32[]{:S(2)}, u32[]{:S(2)}) %collective-permute-start.1) | collective-permute-done | bytes 4128 | tf_op jit(solution)/shard_map/while/body/eval_jaxpr/ppermute | solution.py:16
  305.2 1.9 collective-permute-start.1
  307.1 10.0 %collective-permute-done.1 = f32[1,8,128]{2,1,0:T(8,128)S(1)} collective-permute-done((f32[1,8,128]{2,1,0:T(8,128)S(1)}, f32[1,8,128]{2,1,0:T(8,128)S(1)}, u32[]{:S(2)}, u32[]{:S(2)}) %collective-permute-start.1) | collective-permute-done | bytes 4128 | tf_op jit(solution)/shard_map/while/body/eval_jaxpr/ppermute | solution.py:16
  321.1 9.4 %collective-permute-done.1 = f32[1,8,128]{2,1,0:T(8,128)S(1)} collective-permute-done((f32[1,8,128]{2,1,0:T(8,128)S(1)}, f32[1,8,128]{2,1,0:T(8,128)S(1)}, u32[]{:S(2)}, u32[]{:S(2)}) %collective-permute-start.1) | collective-permute-done | bytes 4128 | tf_op jit(solution)/shard_map/while/body/eval_jaxpr/ppermute | solution.py:16
  334.4 9.9 %collective-permute-done.1 = f32[1,8,128]{2,1,0:T(8,128)S(1)} collective-permute-done((f32[1,8,128]{2,1,0:T(8,128)S(1)}, f32[1,8,128]{2,1,0:T(8,128)S(1)}, u32[]{:S(2)}, u32[]{:S(2)}) %collective-permute-start.1) | collective-permute-done | bytes 4128 | tf_op jit(solution)/shard_map/while/body/eval_jaxpr/ppermute | solution.py:16
  348.2 11.0 %collective-permute-done.1 = f32[1,8,128]{2,1,0:T(8,128)S(1)} collective-permute-done((f32[1,8,128]{2,1,0:T(8,128)S(1)}, f32[1,8,128]{2,1,0:T(8,128)S(1)}, u32[]{:S(2)}, u32[]{:S(2)}) %collective-permute-start.1) | collective-permute-done | bytes 4128 | tf_op jit(solution)/shard_map/while/body/eval_jaxpr/ppermute | solution.py:16
  363.1 12.2 %collective-permute-done.1 = f32[1,8,128]{2,1,0:T(8,128)S(1)} collective-permute-done((f32[1,8,128]{2,1,0:T(8,128)S(1)}, f32[1,8,128]{2,1,0:T(8,128)S(1)}, u32[]{:S(2)}, u32[]{:S(2)}) %collective-permute-start.1) | collective-permute-done | bytes 4128 | tf_op jit(solution)/shard_map/while/body/eval_jaxpr/ppermute | solution.py:16
  379.2 13.3 %collective-permute-done.1 = f32[1,8,128]{2,1,0:T(8,128)S(1)} collective-permute-done((f32[1,8,128]{2,1,0:T(8,128)S(1)}, f32[1,8,128]{2,1,0:T(8,128)S(1)}, u32[]{:S(2)}, u32[]{:S(2)}) %collective-permute-start.1) | collective-permute-done | bytes 4128 | tf_op jit(solution)/shard_map/while/body/eval_jaxpr/ppermute | solution.py:16
  396.5 14.4 %collective-permute-done.1 = f32[1,8,128]{2,1,0:T(8,128)S(1)} collective-permute-done((f32[1,8,128]{2,1,0:T(8,128)S(1)}, f32[1,8,128]{2,1,0:T(8,128)S(1)}, u32[]{:S(2)}, u32[]{:S(2)}) %collective-permute-start.1) | collective-permute-done | bytes 4128 | tf_op jit(solution)/shard_map/while/body/eval_jaxpr/ppermute | solution.py:16
  414.8 14.4 %collective-permute-done.1 = f32[1,8,128]{2,1,0:T(8,128)S(1)} collective-permute-done((f32[1,8,128]{2,1,0:T(8,128)S(1)}, f32[1,8,128]{2,1,0:T(8,128)S(1)}, u32[]{:S(2)}, u32[]{:S(2)}) %collective-permute-start.1) | collective-permute-done | bytes 4128 | tf_op jit(solution)/shard_map/while/body/eval_jaxpr/ppermute | solution.py:16
  433.2 13.6 %collective-permute-done.1 = f32[1,8,128]{2,1,0:T(8,128)S(1)} collective-permute-done((f32[1,8,128]{2,1,0:T(8,128)S(1)}, f32[1,8,128]{2,1,0:T(8,128)S(1)}, u32[]{:S(2)}, u32[]{:S(2)}) %collective-permute-start.1) | collective-permute-done | bytes 4128 | tf_op jit(solution)/shard_map/while/body/eval_jaxpr/ppermute | solution.py:16
  450.7 12.7 %collective-permute-done.1 = f32[1,8,128]{2,1,0:T(8,128)S(1)} collective-permute-done((f32[1,8,128]{2,1,0:T(8,128)S(1)}, f32[1,8,128]{2,1,0:T(8,128)S(1)}, u32[]{:S(2)}, u32[]{:S(2)}) %collective-permute-start.1) | collective-permute-done | bytes 4128 | tf_op jit(solution)/shard_map/while/body/eval_jaxpr/ppermute | solution.py:16
  467.4 11.9 %collective-permute-done.1 = f32[1,8,128]{2,1,0:T(8,128)S(1)} collective-permute-done((f32[1,8,128]{2,1,0:T(8,128)S(1)}, f32[1,8,128]{2,1,0:T(8,128)S(1)}, u32[]{:S(2)}, u32[]{:S(2)}) %collective-permute-start.1) | collective-permute-done | bytes 4128 | tf_op jit(solution)/shard_map/while/body/eval_jaxpr/ppermute | solution.py:16
  483.2 11.0 %collective-permute-done.1 = f32[1,8,128]{2,1,0:T(8,128)S(1)} collective-permute-done((f32[1,8,128]{2,1,0:T(8,128)S(1)}, f32[1,8,128]{2,1,0:T(8,128)S(1)}, u32[]{:S(2)}, u32[]{:S(2)}) %collective-permute-start.1) | collective-permute-done | bytes 4128 | tf_op jit(solution)/shard_map/while/body/eval_jaxpr/ppermute | solution.py:16
  498.2 10.2 %collective-permute-done.1 = f32[1,8,128]{2,1,0:T(8,128)S(1)} collective-permute-done((f32[1,8,128]{2,1,0:T(8,128)S(1)}, f32[1,8,128]{2,1,0:T(8,128)S(1)}, u32[]{:S(2)}, u32[]{:S(2)}) %collective-permute-start.1) | collective-permute-done | bytes 4128 | tf_op jit(solution)/shard_map/while/body/eval_jaxpr/ppermute | solution.py:16
  512.3 9.4 %collective-permute-done.1 = f32[1,8,128]{2,1,0:T(8,128)S(1)} collective-permute-done((f32[1,8,128]{2,1,0:T(8,128)S(1)}, f32[1,8,128]{2,1,0:T(8,128)S(1)}, u32[]{:S(2)}, u32[]{:S(2)}) %collective-permute-start.1) | collective-permute-done | bytes 4128 | tf_op jit(solution)/shard_map/while/body/eval_jaxpr/ppermute | solution.py:16
  525.5 9.4 %collective-permute-done.1 = f32[1,8,128]{2,1,0:T(8,128)S(1)} collective-permute-done((f32[1,8,128]{2,1,0:T(8,128)S(1)}, f32[1,8,128]{2,1,0:T(8,128)S(1)}, u32[]{:S(2)}, u32[]{:S(2)}) %collective-permute-start.1) | collective-permute-done | bytes 4128 | tf_op jit(solution)/shard_map/while/body/eval_jaxpr/ppermute | solution.py:16
  538.3 2.6 fusion.2
  540.9 1.9 fusion.5
  542.9 2.2 fusion.14
  546.7 2.9 fusion.10
  549.6 2.1 fusion.21
  552.9 20.2 %all_to_all.19 = bf16[8,64,1024]{2,1,0:T(8,128)(2,1)S(1)} all-to-all(bf16[8,64,1024]{2,1,0:T(8,128)(2,1)S(1)} %all_to_all.14), channel_id=1, replica_groups=mesh['seq'=32,'head'=8] {'head'}, dimensions={0} | all-to-all | bytes 2097152 | tf_op jit(solution)/shard_map/all_to_all | solution.py:166
  (231 shorter events, 115.0 us)
Async XLA Ops:
  4.4 26.7 %collective-permute-start.3 = (bf16[64,1,128]{0,2,1:T(8,128)(2,1)S(1)}, bf16[64,1,128]{0,2,1:T(8,128)(2,1)S(1)}, u32[]{:S(2)}, u32[]{:S(2)}) collective-permute-start(bf16[64,1,128]{0,2,1:T(8,128)(2,1)S(1)} %pad_maximum_fusion.12), channel_id=1, source_target_pairs={{0,8},{8,16},{16,24},{24,32},{32,40},{40,48},{48,56},{56,64},{64,7... | collective-permute-start | bytes 49160 | tf_op jit(solution)/shard_map/ppermute | solution.py:16
  8.9 38.0 %collective-permute-start.2 = (bf16[64,1,128]{2,0,1:T(8,128)(2,1)S(1)}, bf16[64,1,128]{2,0,1:T(8,128)(2,1)}, u32[]{:S(2)}, u32[]{:S(2)}) collective-permute-start(bf16[64,1,128]{2,0,1:T(8,128)(2,1)S(1)} %slice_bitcast_fusion), channel_id=1, source_target_pairs={{0,8},{8,16},{16,24},{24,32},{32,40},{40,48},{48,56},{56,64},{64,7... | collective-permute-start | bytes 49160 | tf_op jit(solution)/shard_map/ppermute | solution.py:16
  48.3 17.3 %collective-permute-start = (f32[1,8,128,128]{3,2,1,0:T(8,128)S(1)}, f32[1,8,128,128]{3,2,1,0:T(8,128)S(1)}, u32[]{:S(2)}, u32[]{:S(2)}) collective-permute-start(f32[1,8,128,128]{3,2,1,0:T(8,128)S(1)} %add.246), channel_id=1, source_target_pairs={{0,8},{8,16},{16,24},{24,32},{32,40},{40,48},{48,56},{56,64},{64,7... | collective-permute-start | bytes 1572872 | tf_op jit(solution)/shard_map/while/body/eval_jaxpr/ppermute | solution.py:16
  52.3 13.3 %collective-permute-start.1 = (f32[1,8,128]{2,1,0:T(8,128)S(1)}, f32[1,8,128]{2,1,0:T(8,128)S(1)}, u32[]{:S(2)}, u32[]{:S(2)}) collective-permute-start(f32[1,8,128]{2,1,0:T(8,128)S(1)} %add.247), channel_id=1, source_target_pairs={{0,8},{8,16},{16,24},{24,32},{32,40},{40,48},{48,56},{56,64},{64,7... | collective-permute-start | bytes 12296 | tf_op jit(solution)/shard_map/while/body/eval_jaxpr/ppermute | solution.py:16
  65.7 16.3 %collective-permute-start = (f32[1,8,128,128]{3,2,1,0:T(8,128)S(1)}, f32[1,8,128,128]{3,2,1,0:T(8,128)S(1)}, u32[]{:S(2)}, u32[]{:S(2)}) collective-permute-start(f32[1,8,128,128]{3,2,1,0:T(8,128)S(1)} %add.246), channel_id=1, source_target_pairs={{0,8},{8,16},{16,24},{24,32},{32,40},{40,48},{48,56},{56,64},{64,7... | collective-permute-start | bytes 1572872 | tf_op jit(solution)/shard_map/while/body/eval_jaxpr/ppermute | solution.py:16
  68.1 14.0 %collective-permute-start.1 = (f32[1,8,128]{2,1,0:T(8,128)S(1)}, f32[1,8,128]{2,1,0:T(8,128)S(1)}, u32[]{:S(2)}, u32[]{:S(2)}) collective-permute-start(f32[1,8,128]{2,1,0:T(8,128)S(1)} %add.247), channel_id=1, source_target_pairs={{0,8},{8,16},{16,24},{24,32},{32,40},{40,48},{48,56},{56,64},{64,7... | collective-permute-start | bytes 12296 | tf_op jit(solution)/shard_map/while/body/eval_jaxpr/ppermute | solution.py:16
  82.1 15.5 %collective-permute-start = (f32[1,8,128,128]{3,2,1,0:T(8,128)S(1)}, f32[1,8,128,128]{3,2,1,0:T(8,128)S(1)}, u32[]{:S(2)}, u32[]{:S(2)}) collective-permute-start(f32[1,8,128,128]{3,2,1,0:T(8,128)S(1)} %add.246), channel_id=1, source_target_pairs={{0,8},{8,16},{16,24},{24,32},{32,40},{40,48},{48,56},{56,64},{64,7... | collective-permute-start | bytes 1572872 | tf_op jit(solution)/shard_map/while/body/eval_jaxpr/ppermute | solution.py:16
  84.0 13.5 %collective-permute-start.1 = (f32[1,8,128]{2,1,0:T(8,128)S(1)}, f32[1,8,128]{2,1,0:T(8,128)S(1)}, u32[]{:S(2)}, u32[]{:S(2)}) collective-permute-start(f32[1,8,128]{2,1,0:T(8,128)S(1)} %add.247), channel_id=1, source_target_pairs={{0,8},{8,16},{16,24},{24,32},{32,40},{40,48},{48,56},{56,64},{64,7... | collective-permute-start | bytes 12296 | tf_op jit(solution)/shard_map/while/body/eval_jaxpr/ppermute | solution.py:16
  97.7 14.6 %collective-permute-start = (f32[1,8,128,128]{3,2,1,0:T(8,128)S(1)}, f32[1,8,128,128]{3,2,1,0:T(8,128)S(1)}, u32[]{:S(2)}, u32[]{:S(2)}) collective-permute-start(f32[1,8,128,128]{3,2,1,0:T(8,128)S(1)} %add.246), channel_id=1, source_target_pairs={{0,8},{8,16},{16,24},{24,32},{32,40},{40,48},{48,56},{56,64},{64,7... | collective-permute-start | bytes 1572872 | tf_op jit(solution)/shard_map/while/body/eval_jaxpr/ppermute | solution.py:16
  99.6 12.7 %collective-permute-start.1 = (f32[1,8,128]{2,1,0:T(8,128)S(1)}, f32[1,8,128]{2,1,0:T(8,128)S(1)}, u32[]{:S(2)}, u32[]{:S(2)}) collective-permute-start(f32[1,8,128]{2,1,0:T(8,128)S(1)} %add.247), channel_id=1, source_target_pairs={{0,8},{8,16},{16,24},{24,32},{32,40},{40,48},{48,56},{56,64},{64,7... | collective-permute-start | bytes 12296 | tf_op jit(solution)/shard_map/while/body/eval_jaxpr/ppermute | solution.py:16
  112.4 13.8 %collective-permute-start = (f32[1,8,128,128]{3,2,1,0:T(8,128)S(1)}, f32[1,8,128,128]{3,2,1,0:T(8,128)S(1)}, u32[]{:S(2)}, u32[]{:S(2)}) collective-permute-start(f32[1,8,128,128]{3,2,1,0:T(8,128)S(1)} %add.246), channel_id=1, source_target_pairs={{0,8},{8,16},{16,24},{24,32},{32,40},{40,48},{48,56},{56,64},{64,7... | collective-permute-start | bytes 1572872 | tf_op jit(solution)/shard_map/while/body/eval_jaxpr/ppermute | solution.py:16
  114.3 11.8 %collective-permute-start.1 = (f32[1,8,128]{2,1,0:T(8,128)S(1)}, f32[1,8,128]{2,1,0:T(8,128)S(1)}, u32[]{:S(2)}, u32[]{:S(2)}) collective-permute-start(f32[1,8,128]{2,1,0:T(8,128)S(1)} %add.247), channel_id=1, source_target_pairs={{0,8},{8,16},{16,24},{24,32},{32,40},{40,48},{48,56},{56,64},{64,7... | collective-permute-start | bytes 12296 | tf_op jit(solution)/shard_map/while/body/eval_jaxpr/ppermute | solution.py:16
  126.2 13.2 %collective-permute-start = (f32[1,8,128,128]{3,2,1,0:T(8,128)S(1)}, f32[1,8,128,128]{3,2,1,0:T(8,128)S(1)}, u32[]{:S(2)}, u32[]{:S(2)}) collective-permute-start(f32[1,8,128,128]{3,2,1,0:T(8,128)S(1)} %add.246), channel_id=1, source_target_pairs={{0,8},{8,16},{16,24},{24,32},{32,40},{40,48},{48,56},{56,64},{64,7... | collective-permute-start | bytes 1572872 | tf_op jit(solution)/shard_map/while/body/eval_jaxpr/ppermute | solution.py:16
  128.1 11.3 %collective-permute-start.1 = (f32[1,8,128]{2,1,0:T(8,128)S(1)}, f32[1,8,128]{2,1,0:T(8,128)S(1)}, u32[]{:S(2)}, u32[]{:S(2)}) collective-permute-start(f32[1,8,128]{2,1,0:T(8,128)S(1)} %add.247), channel_id=1, source_target_pairs={{0,8},{8,16},{16,24},{24,32},{32,40},{40,48},{48,56},{56,64},{64,7... | collective-permute-start | bytes 12296 | tf_op jit(solution)/shard_map/while/body/eval_jaxpr/ppermute | solution.py:16
  139.5 13.9 %collective-permute-start = (f32[1,8,128,128]{3,2,1,0:T(8,128)S(1)}, f32[1,8,128,128]{3,2,1,0:T(8,128)S(1)}, u32[]{:S(2)}, u32[]{:S(2)}) collective-permute-start(f32[1,8,128,128]{3,2,1,0:T(8,128)S(1)} %add.246), channel_id=1, source_target_pairs={{0,8},{8,16},{16,24},{24,32},{32,40},{40,48},{48,56},{56,64},{64,7... | collective-permute-start | bytes 1572872 | tf_op jit(solution)/shard_map/while/body/eval_jaxpr/ppermute | solution.py:16
  141.4 11.9 %collective-permute-start.1 = (f32[1,8,128]{2,1,0:T(8,128)S(1)}, f32[1,8,128]{2,1,0:T(8,128)S(1)}, u32[]{:S(2)}, u32[]{:S(2)}) collective-permute-start(f32[1,8,128]{2,1,0:T(8,128)S(1)} %add.247), channel_id=1, source_target_pairs={{0,8},{8,16},{16,24},{24,32},{32,40},{40,48},{48,56},{56,64},{64,7... | collective-permute-start | bytes 12296 | tf_op jit(solution)/shard_map/while/body/eval_jaxpr/ppermute | solution.py:16
  153.4 15.0 %collective-permute-start = (f32[1,8,128,128]{3,2,1,0:T(8,128)S(1)}, f32[1,8,128,128]{3,2,1,0:T(8,128)S(1)}, u32[]{:S(2)}, u32[]{:S(2)}) collective-permute-start(f32[1,8,128,128]{3,2,1,0:T(8,128)S(1)} %add.246), channel_id=1, source_target_pairs={{0,8},{8,16},{16,24},{24,32},{32,40},{40,48},{48,56},{56,64},{64,7... | collective-permute-start | bytes 1572872 | tf_op jit(solution)/shard_map/while/body/eval_jaxpr/ppermute | solution.py:16
  155.4 13.1 %collective-permute-start.1 = (f32[1,8,128]{2,1,0:T(8,128)S(1)}, f32[1,8,128]{2,1,0:T(8,128)S(1)}, u32[]{:S(2)}, u32[]{:S(2)}) collective-permute-start(f32[1,8,128]{2,1,0:T(8,128)S(1)} %add.247), channel_id=1, source_target_pairs={{0,8},{8,16},{16,24},{24,32},{32,40},{40,48},{48,56},{56,64},{64,7... | collective-permute-start | bytes 12296 | tf_op jit(solution)/shard_map/while/body/eval_jaxpr/ppermute | solution.py:16
  168.5 16.2 %collective-permute-start = (f32[1,8,128,128]{3,2,1,0:T(8,128)S(1)}, f32[1,8,128,128]{3,2,1,0:T(8,128)S(1)}, u32[]{:S(2)}, u32[]{:S(2)}) collective-permute-start(f32[1,8,128,128]{3,2,1,0:T(8,128)S(1)} %add.246), channel_id=1, source_target_pairs={{0,8},{8,16},{16,24},{24,32},{32,40},{40,48},{48,56},{56,64},{64,7... | collective-permute-start | bytes 1572872 | tf_op jit(solution)/shard_map/while/body/eval_jaxpr/ppermute | solution.py:16
  170.4 14.2 %collective-permute-start.1 = (f32[1,8,128]{2,1,0:T(8,128)S(1)}, f32[1,8,128]{2,1,0:T(8,128)S(1)}, u32[]{:S(2)}, u32[]{:S(2)}) collective-permute-start(f32[1,8,128]{2,1,0:T(8,128)S(1)} %add.247), channel_id=1, source_target_pairs={{0,8},{8,16},{16,24},{24,32},{32,40},{40,48},{48,56},{56,64},{64,7... | collective-permute-start | bytes 12296 | tf_op jit(solution)/shard_map/while/body/eval_jaxpr/ppermute | solution.py:16
  184.7 17.3 %collective-permute-start = (f32[1,8,128,128]{3,2,1,0:T(8,128)S(1)}, f32[1,8,128,128]{3,2,1,0:T(8,128)S(1)}, u32[]{:S(2)}, u32[]{:S(2)}) collective-permute-start(f32[1,8,128,128]{3,2,1,0:T(8,128)S(1)} %add.246), channel_id=1, source_target_pairs={{0,8},{8,16},{16,24},{24,32},{32,40},{40,48},{48,56},{56,64},{64,7... | collective-permute-start | bytes 1572872 | tf_op jit(solution)/shard_map/while/body/eval_jaxpr/ppermute | solution.py:16
  186.6 15.4 %collective-permute-start.1 = (f32[1,8,128]{2,1,0:T(8,128)S(1)}, f32[1,8,128]{2,1,0:T(8,128)S(1)}, u32[]{:S(2)}, u32[]{:S(2)}) collective-permute-start(f32[1,8,128]{2,1,0:T(8,128)S(1)} %add.247), channel_id=1, source_target_pairs={{0,8},{8,16},{16,24},{24,32},{32,40},{40,48},{48,56},{56,64},{64,7... | collective-permute-start | bytes 12296 | tf_op jit(solution)/shard_map/while/body/eval_jaxpr/ppermute | solution.py:16
  202.1 18.4 %collective-permute-start = (f32[1,8,128,128]{3,2,1,0:T(8,128)S(1)}, f32[1,8,128,128]{3,2,1,0:T(8,128)S(1)}, u32[]{:S(2)}, u32[]{:S(2)}) collective-permute-start(f32[1,8,128,128]{3,2,1,0:T(8,128)S(1)} %add.246), channel_id=1, source_target_pairs={{0,8},{8,16},{16,24},{24,32},{32,40},{40,48},{48,56},{56,64},{64,7... | collective-permute-start | bytes 1572872 | tf_op jit(solution)/shard_map/while/body/eval_jaxpr/ppermute | solution.py:16
  204.0 16.5 %collective-permute-start.1 = (f32[1,8,128]{2,1,0:T(8,128)S(1)}, f32[1,8,128]{2,1,0:T(8,128)S(1)}, u32[]{:S(2)}, u32[]{:S(2)}) collective-permute-start(f32[1,8,128]{2,1,0:T(8,128)S(1)} %add.247), channel_id=1, source_target_pairs={{0,8},{8,16},{16,24},{24,32},{32,40},{40,48},{48,56},{56,64},{64,7... | collective-permute-start | bytes 12296 | tf_op jit(solution)/shard_map/while/body/eval_jaxpr/ppermute | solution.py:16
  220.6 18.2 %collective-permute-start = (f32[1,8,128,128]{3,2,1,0:T(8,128)S(1)}, f32[1,8,128,128]{3,2,1,0:T(8,128)S(1)}, u32[]{:S(2)}, u32[]{:S(2)}) collective-permute-start(f32[1,8,128,128]{3,2,1,0:T(8,128)S(1)} %add.246), channel_id=1, source_target_pairs={{0,8},{8,16},{16,24},{24,32},{32,40},{40,48},{48,56},{56,64},{64,7... | collective-permute-start | bytes 1572872 | tf_op jit(solution)/shard_map/while/body/eval_jaxpr/ppermute | solution.py:16
  222.5 16.2 %collective-permute-start.1 = (f32[1,8,128]{2,1,0:T(8,128)S(1)}, f32[1,8,128]{2,1,0:T(8,128)S(1)}, u32[]{:S(2)}, u32[]{:S(2)}) collective-permute-start(f32[1,8,128]{2,1,0:T(8,128)S(1)} %add.247), channel_id=1, source_target_pairs={{0,8},{8,16},{16,24},{24,32},{32,40},{40,48},{48,56},{56,64},{64,7... | collective-permute-start | bytes 12296 | tf_op jit(solution)/shard_map/while/body/eval_jaxpr/ppermute | solution.py:16
  238.8 17.3 %collective-permute-start = (f32[1,8,128,128]{3,2,1,0:T(8,128)S(1)}, f32[1,8,128,128]{3,2,1,0:T(8,128)S(1)}, u32[]{:S(2)}, u32[]{:S(2)}) collective-permute-start(f32[1,8,128,128]{3,2,1,0:T(8,128)S(1)} %add.246), channel_id=1, source_target_pairs={{0,8},{8,16},{16,24},{24,32},{32,40},{40,48},{48,56},{56,64},{64,7... | collective-permute-start | bytes 1572872 | tf_op jit(solution)/shard_map/while/body/eval_jaxpr/ppermute | solution.py:16
  240.8 15.4 %collective-permute-start.1 = (f32[1,8,128]{2,1,0:T(8,128)S(1)}, f32[1,8,128]{2,1,0:T(8,128)S(1)}, u32[]{:S(2)}, u32[]{:S(2)}) collective-permute-start(f32[1,8,128]{2,1,0:T(8,128)S(1)} %add.247), channel_id=1, source_target_pairs={{0,8},{8,16},{16,24},{24,32},{32,40},{40,48},{48,56},{56,64},{64,7... | collective-permute-start | bytes 12296 | tf_op jit(solution)/shard_map/while/body/eval_jaxpr/ppermute | solution.py:16
  256.2 16.5 %collective-permute-start = (f32[1,8,128,128]{3,2,1,0:T(8,128)S(1)}, f32[1,8,128,128]{3,2,1,0:T(8,128)S(1)}, u32[]{:S(2)}, u32[]{:S(2)}) collective-permute-start(f32[1,8,128,128]{3,2,1,0:T(8,128)S(1)} %add.246), channel_id=1, source_target_pairs={{0,8},{8,16},{16,24},{24,32},{32,40},{40,48},{48,56},{56,64},{64,7... | collective-permute-start | bytes 1572872 | tf_op jit(solution)/shard_map/while/body/eval_jaxpr/ppermute | solution.py:16
  258.2 14.5 %collective-permute-start.1 = (f32[1,8,128]{2,1,0:T(8,128)S(1)}, f32[1,8,128]{2,1,0:T(8,128)S(1)}, u32[]{:S(2)}, u32[]{:S(2)}) collective-permute-start(f32[1,8,128]{2,1,0:T(8,128)S(1)} %add.247), channel_id=1, source_target_pairs={{0,8},{8,16},{16,24},{24,32},{32,40},{40,48},{48,56},{56,64},{64,7... | collective-permute-start | bytes 12296 | tf_op jit(solution)/shard_map/while/body/eval_jaxpr/ppermute | solution.py:16
  272.7 15.6 %collective-permute-start = (f32[1,8,128,128]{3,2,1,0:T(8,128)S(1)}, f32[1,8,128,128]{3,2,1,0:T(8,128)S(1)}, u32[]{:S(2)}, u32[]{:S(2)}) collective-permute-start(f32[1,8,128,128]{3,2,1,0:T(8,128)S(1)} %add.246), channel_id=1, source_target_pairs={{0,8},{8,16},{16,24},{24,32},{32,40},{40,48},{48,56},{56,64},{64,7... | collective-permute-start | bytes 1572872 | tf_op jit(solution)/shard_map/while/body/eval_jaxpr/ppermute | solution.py:16
  274.7 13.7 %collective-permute-start.1 = (f32[1,8,128]{2,1,0:T(8,128)S(1)}, f32[1,8,128]{2,1,0:T(8,128)S(1)}, u32[]{:S(2)}, u32[]{:S(2)}) collective-permute-start(f32[1,8,128]{2,1,0:T(8,128)S(1)} %add.247), channel_id=1, source_target_pairs={{0,8},{8,16},{16,24},{24,32},{32,40},{40,48},{48,56},{56,64},{64,7... | collective-permute-start | bytes 12296 | tf_op jit(solution)/shard_map/while/body/eval_jaxpr/ppermute | solution.py:16
  288.4 14.8 %collective-permute-start = (f32[1,8,128,128]{3,2,1,0:T(8,128)S(1)}, f32[1,8,128,128]{3,2,1,0:T(8,128)S(1)}, u32[]{:S(2)}, u32[]{:S(2)}) collective-permute-start(f32[1,8,128,128]{3,2,1,0:T(8,128)S(1)} %add.246), channel_id=1, source_target_pairs={{0,8},{8,16},{16,24},{24,32},{32,40},{40,48},{48,56},{56,64},{64,7... | collective-permute-start | bytes 1572872 | tf_op jit(solution)/shard_map/while/body/eval_jaxpr/ppermute | solution.py:16
  290.4 12.8 %collective-permute-start.1 = (f32[1,8,128]{2,1,0:T(8,128)S(1)}, f32[1,8,128]{2,1,0:T(8,128)S(1)}, u32[]{:S(2)}, u32[]{:S(2)}) collective-permute-start(f32[1,8,128]{2,1,0:T(8,128)S(1)} %add.247), channel_id=1, source_target_pairs={{0,8},{8,16},{16,24},{24,32},{32,40},{40,48},{48,56},{56,64},{64,7... | collective-permute-start | bytes 12296 | tf_op jit(solution)/shard_map/while/body/eval_jaxpr/ppermute | solution.py:16
  303.3 13.9 %collective-permute-start = (f32[1,8,128,128]{3,2,1,0:T(8,128)S(1)}, f32[1,8,128,128]{3,2,1,0:T(8,128)S(1)}, u32[]{:S(2)}, u32[]{:S(2)}) collective-permute-start(f32[1,8,128,128]{3,2,1,0:T(8,128)S(1)} %add.246), channel_id=1, source_target_pairs={{0,8},{8,16},{16,24},{24,32},{32,40},{40,48},{48,56},{56,64},{64,7... | collective-permute-start | bytes 1572872 | tf_op jit(solution)/shard_map/while/body/eval_jaxpr/ppermute | solution.py:16
  305.2 12.0 %collective-permute-start.1 = (f32[1,8,128]{2,1,0:T(8,128)S(1)}, f32[1,8,128]{2,1,0:T(8,128)S(1)}, u32[]{:S(2)}, u32[]{:S(2)}) collective-permute-start(f32[1,8,128]{2,1,0:T(8,128)S(1)} %add.247), channel_id=1, source_target_pairs={{0,8},{8,16},{16,24},{24,32},{32,40},{40,48},{48,56},{56,64},{64,7... | collective-permute-start | bytes 12296 | tf_op jit(solution)/shard_map/while/body/eval_jaxpr/ppermute | solution.py:16
  317.2 13.2 %collective-permute-start = (f32[1,8,128,128]{3,2,1,0:T(8,128)S(1)}, f32[1,8,128,128]{3,2,1,0:T(8,128)S(1)}, u32[]{:S(2)}, u32[]{:S(2)}) collective-permute-start(f32[1,8,128,128]{3,2,1,0:T(8,128)S(1)} %add.246), channel_id=1, source_target_pairs={{0,8},{8,16},{16,24},{24,32},{32,40},{40,48},{48,56},{56,64},{64,7... | collective-permute-start | bytes 1572872 | tf_op jit(solution)/shard_map/while/body/eval_jaxpr/ppermute | solution.py:16
  319.2 11.3 %collective-permute-start.1 = (f32[1,8,128]{2,1,0:T(8,128)S(1)}, f32[1,8,128]{2,1,0:T(8,128)S(1)}, u32[]{:S(2)}, u32[]{:S(2)}) collective-permute-start(f32[1,8,128]{2,1,0:T(8,128)S(1)} %add.247), channel_id=1, source_target_pairs={{0,8},{8,16},{16,24},{24,32},{32,40},{40,48},{48,56},{56,64},{64,7... | collective-permute-start | bytes 12296 | tf_op jit(solution)/shard_map/while/body/eval_jaxpr/ppermute | solution.py:16
  330.5 13.7 %collective-permute-start = (f32[1,8,128,128]{3,2,1,0:T(8,128)S(1)}, f32[1,8,128,128]{3,2,1,0:T(8,128)S(1)}, u32[]{:S(2)}, u32[]{:S(2)}) collective-permute-start(f32[1,8,128,128]{3,2,1,0:T(8,128)S(1)} %add.246), channel_id=1, source_target_pairs={{0,8},{8,16},{16,24},{24,32},{32,40},{40,48},{48,56},{56,64},{64,7... | collective-permute-start | bytes 1572872 | tf_op jit(solution)/shard_map/while/body/eval_jaxpr/ppermute | solution.py:16
  332.5 11.8 %collective-permute-start.1 = (f32[1,8,128]{2,1,0:T(8,128)S(1)}, f32[1,8,128]{2,1,0:T(8,128)S(1)}, u32[]{:S(2)}, u32[]{:S(2)}) collective-permute-start(f32[1,8,128]{2,1,0:T(8,128)S(1)} %add.247), channel_id=1, source_target_pairs={{0,8},{8,16},{16,24},{24,32},{32,40},{40,48},{48,56},{56,64},{64,7... | collective-permute-start | bytes 12296 | tf_op jit(solution)/shard_map/while/body/eval_jaxpr/ppermute | solution.py:16
  344.3 14.9 %collective-permute-start = (f32[1,8,128,128]{3,2,1,0:T(8,128)S(1)}, f32[1,8,128,128]{3,2,1,0:T(8,128)S(1)}, u32[]{:S(2)}, u32[]{:S(2)}) collective-permute-start(f32[1,8,128,128]{3,2,1,0:T(8,128)S(1)} %add.246), channel_id=1, source_target_pairs={{0,8},{8,16},{16,24},{24,32},{32,40},{40,48},{48,56},{56,64},{64,7... | collective-permute-start | bytes 1572872 | tf_op jit(solution)/shard_map/while/body/eval_jaxpr/ppermute | solution.py:16
  346.3 12.9 %collective-permute-start.1 = (f32[1,8,128]{2,1,0:T(8,128)S(1)}, f32[1,8,128]{2,1,0:T(8,128)S(1)}, u32[]{:S(2)}, u32[]{:S(2)}) collective-permute-start(f32[1,8,128]{2,1,0:T(8,128)S(1)} %add.247), channel_id=1, source_target_pairs={{0,8},{8,16},{16,24},{24,32},{32,40},{40,48},{48,56},{56,64},{64,7... | collective-permute-start | bytes 12296 | tf_op jit(solution)/shard_map/while/body/eval_jaxpr/ppermute | solution.py:16
  359.3 16.0 %collective-permute-start = (f32[1,8,128,128]{3,2,1,0:T(8,128)S(1)}, f32[1,8,128,128]{3,2,1,0:T(8,128)S(1)}, u32[]{:S(2)}, u32[]{:S(2)}) collective-permute-start(f32[1,8,128,128]{3,2,1,0:T(8,128)S(1)} %add.246), channel_id=1, source_target_pairs={{0,8},{8,16},{16,24},{24,32},{32,40},{40,48},{48,56},{56,64},{64,7... | collective-permute-start | bytes 1572872 | tf_op jit(solution)/shard_map/while/body/eval_jaxpr/ppermute | solution.py:16
  361.2 14.1 %collective-permute-start.1 = (f32[1,8,128]{2,1,0:T(8,128)S(1)}, f32[1,8,128]{2,1,0:T(8,128)S(1)}, u32[]{:S(2)}, u32[]{:S(2)}) collective-permute-start(f32[1,8,128]{2,1,0:T(8,128)S(1)} %add.247), channel_id=1, source_target_pairs={{0,8},{8,16},{16,24},{24,32},{32,40},{40,48},{48,56},{56,64},{64,7... | collective-permute-start | bytes 12296 | tf_op jit(solution)/shard_map/while/body/eval_jaxpr/ppermute | solution.py:16
  375.3 17.2 %collective-permute-start = (f32[1,8,128,128]{3,2,1,0:T(8,128)S(1)}, f32[1,8,128,128]{3,2,1,0:T(8,128)S(1)}, u32[]{:S(2)}, u32[]{:S(2)}) collective-permute-start(f32[1,8,128,128]{3,2,1,0:T(8,128)S(1)} %add.246), channel_id=1, source_target_pairs={{0,8},{8,16},{16,24},{24,32},{32,40},{40,48},{48,56},{56,64},{64,7... | collective-permute-start | bytes 1572872 | tf_op jit(solution)/shard_map/while/body/eval_jaxpr/ppermute | solution.py:16
  377.3 15.2 %collective-permute-start.1 = (f32[1,8,128]{2,1,0:T(8,128)S(1)}, f32[1,8,128]{2,1,0:T(8,128)S(1)}, u32[]{:S(2)}, u32[]{:S(2)}) collective-permute-start(f32[1,8,128]{2,1,0:T(8,128)S(1)} %add.247), channel_id=1, source_target_pairs={{0,8},{8,16},{16,24},{24,32},{32,40},{40,48},{48,56},{56,64},{64,7... | collective-permute-start | bytes 12296 | tf_op jit(solution)/shard_map/while/body/eval_jaxpr/ppermute | solution.py:16
  392.6 18.3 %collective-permute-start = (f32[1,8,128,128]{3,2,1,0:T(8,128)S(1)}, f32[1,8,128,128]{3,2,1,0:T(8,128)S(1)}, u32[]{:S(2)}, u32[]{:S(2)}) collective-permute-start(f32[1,8,128,128]{3,2,1,0:T(8,128)S(1)} %add.246), channel_id=1, source_target_pairs={{0,8},{8,16},{16,24},{24,32},{32,40},{40,48},{48,56},{56,64},{64,7... | collective-permute-start | bytes 1572872 | tf_op jit(solution)/shard_map/while/body/eval_jaxpr/ppermute | solution.py:16
  394.5 16.4 %collective-permute-start.1 = (f32[1,8,128]{2,1,0:T(8,128)S(1)}, f32[1,8,128]{2,1,0:T(8,128)S(1)}, u32[]{:S(2)}, u32[]{:S(2)}) collective-permute-start(f32[1,8,128]{2,1,0:T(8,128)S(1)} %add.247), channel_id=1, source_target_pairs={{0,8},{8,16},{16,24},{24,32},{32,40},{40,48},{48,56},{56,64},{64,7... | collective-permute-start | bytes 12296 | tf_op jit(solution)/shard_map/while/body/eval_jaxpr/ppermute | solution.py:16
  411.0 18.3 %collective-permute-start = (f32[1,8,128,128]{3,2,1,0:T(8,128)S(1)}, f32[1,8,128,128]{3,2,1,0:T(8,128)S(1)}, u32[]{:S(2)}, u32[]{:S(2)}) collective-permute-start(f32[1,8,128,128]{3,2,1,0:T(8,128)S(1)} %add.246), channel_id=1, source_target_pairs={{0,8},{8,16},{16,24},{24,32},{32,40},{40,48},{48,56},{56,64},{64,7... | collective-permute-start | bytes 1572872 | tf_op jit(solution)/shard_map/while/body/eval_jaxpr/ppermute | solution.py:16
  412.9 16.4 %collective-permute-start.1 = (f32[1,8,128]{2,1,0:T(8,128)S(1)}, f32[1,8,128]{2,1,0:T(8,128)S(1)}, u32[]{:S(2)}, u32[]{:S(2)}) collective-permute-start(f32[1,8,128]{2,1,0:T(8,128)S(1)} %add.247), channel_id=1, source_target_pairs={{0,8},{8,16},{16,24},{24,32},{32,40},{40,48},{48,56},{56,64},{64,7... | collective-permute-start | bytes 12296 | tf_op jit(solution)/shard_map/while/body/eval_jaxpr/ppermute | solution.py:16
  429.3 17.5 %collective-permute-start = (f32[1,8,128,128]{3,2,1,0:T(8,128)S(1)}, f32[1,8,128,128]{3,2,1,0:T(8,128)S(1)}, u32[]{:S(2)}, u32[]{:S(2)}) collective-permute-start(f32[1,8,128,128]{3,2,1,0:T(8,128)S(1)} %add.246), channel_id=1, source_target_pairs={{0,8},{8,16},{16,24},{24,32},{32,40},{40,48},{48,56},{56,64},{64,7... | collective-permute-start | bytes 1572872 | tf_op jit(solution)/shard_map/while/body/eval_jaxpr/ppermute | solution.py:16
  431.3 15.5 %collective-permute-start.1 = (f32[1,8,128]{2,1,0:T(8,128)S(1)}, f32[1,8,128]{2,1,0:T(8,128)S(1)}, u32[]{:S(2)}, u32[]{:S(2)}) collective-permute-start(f32[1,8,128]{2,1,0:T(8,128)S(1)} %add.247), channel_id=1, source_target_pairs={{0,8},{8,16},{16,24},{24,32},{32,40},{40,48},{48,56},{56,64},{64,7... | collective-permute-start | bytes 12296 | tf_op jit(solution)/shard_map/while/body/eval_jaxpr/ppermute | solution.py:16
  446.9 16.6 %collective-permute-start = (f32[1,8,128,128]{3,2,1,0:T(8,128)S(1)}, f32[1,8,128,128]{3,2,1,0:T(8,128)S(1)}, u32[]{:S(2)}, u32[]{:S(2)}) collective-permute-start(f32[1,8,128,128]{3,2,1,0:T(8,128)S(1)} %add.246), channel_id=1, source_target_pairs={{0,8},{8,16},{16,24},{24,32},{32,40},{40,48},{48,56},{56,64},{64,7... | collective-permute-start | bytes 1572872 | tf_op jit(solution)/shard_map/while/body/eval_jaxpr/ppermute | solution.py:16
  448.8 14.7 %collective-permute-start.1 = (f32[1,8,128]{2,1,0:T(8,128)S(1)}, f32[1,8,128]{2,1,0:T(8,128)S(1)}, u32[]{:S(2)}, u32[]{:S(2)}) collective-permute-start(f32[1,8,128]{2,1,0:T(8,128)S(1)} %add.247), channel_id=1, source_target_pairs={{0,8},{8,16},{16,24},{24,32},{32,40},{40,48},{48,56},{56,64},{64,7... | collective-permute-start | bytes 12296 | tf_op jit(solution)/shard_map/while/body/eval_jaxpr/ppermute | solution.py:16
  463.5 15.7 %collective-permute-start = (f32[1,8,128,128]{3,2,1,0:T(8,128)S(1)}, f32[1,8,128,128]{3,2,1,0:T(8,128)S(1)}, u32[]{:S(2)}, u32[]{:S(2)}) collective-permute-start(f32[1,8,128,128]{3,2,1,0:T(8,128)S(1)} %add.246), channel_id=1, source_target_pairs={{0,8},{8,16},{16,24},{24,32},{32,40},{40,48},{48,56},{56,64},{64,7... | collective-permute-start | bytes 1572872 | tf_op jit(solution)/shard_map/while/body/eval_jaxpr/ppermute | solution.py:16
  465.5 13.8 %collective-permute-start.1 = (f32[1,8,128]{2,1,0:T(8,128)S(1)}, f32[1,8,128]{2,1,0:T(8,128)S(1)}, u32[]{:S(2)}, u32[]{:S(2)}) collective-permute-start(f32[1,8,128]{2,1,0:T(8,128)S(1)} %add.247), channel_id=1, source_target_pairs={{0,8},{8,16},{16,24},{24,32},{32,40},{40,48},{48,56},{56,64},{64,7... | collective-permute-start | bytes 12296 | tf_op jit(solution)/shard_map/while/body/eval_jaxpr/ppermute | solution.py:16
  479.3 14.9 %collective-permute-start = (f32[1,8,128,128]{3,2,1,0:T(8,128)S(1)}, f32[1,8,128,128]{3,2,1,0:T(8,128)S(1)}, u32[]{:S(2)}, u32[]{:S(2)}) collective-permute-start(f32[1,8,128,128]{3,2,1,0:T(8,128)S(1)} %add.246), channel_id=1, source_target_pairs={{0,8},{8,16},{16,24},{24,32},{32,40},{40,48},{48,56},{56,64},{64,7... | collective-permute-start | bytes 1572872 | tf_op jit(solution)/shard_map/while/body/eval_jaxpr/ppermute | solution.py:16
  481.3 12.9 %collective-permute-start.1 = (f32[1,8,128]{2,1,0:T(8,128)S(1)}, f32[1,8,128]{2,1,0:T(8,128)S(1)}, u32[]{:S(2)}, u32[]{:S(2)}) collective-permute-start(f32[1,8,128]{2,1,0:T(8,128)S(1)} %add.247), channel_id=1, source_target_pairs={{0,8},{8,16},{16,24},{24,32},{32,40},{40,48},{48,56},{56,64},{64,7... | collective-permute-start | bytes 12296 | tf_op jit(solution)/shard_map/while/body/eval_jaxpr/ppermute | solution.py:16
  494.3 14.0 %collective-permute-start = (f32[1,8,128,128]{3,2,1,0:T(8,128)S(1)}, f32[1,8,128,128]{3,2,1,0:T(8,128)S(1)}, u32[]{:S(2)}, u32[]{:S(2)}) collective-permute-start(f32[1,8,128,128]{3,2,1,0:T(8,128)S(1)} %add.246), channel_id=1, source_target_pairs={{0,8},{8,16},{16,24},{24,32},{32,40},{40,48},{48,56},{56,64},{64,7... | collective-permute-start | bytes 1572872 | tf_op jit(solution)/shard_map/while/body/eval_jaxpr/ppermute | solution.py:16
  496.2 12.1 %collective-permute-start.1 = (f32[1,8,128]{2,1,0:T(8,128)S(1)}, f32[1,8,128]{2,1,0:T(8,128)S(1)}, u32[]{:S(2)}, u32[]{:S(2)}) collective-permute-start(f32[1,8,128]{2,1,0:T(8,128)S(1)} %add.247), channel_id=1, source_target_pairs={{0,8},{8,16},{16,24},{24,32},{32,40},{40,48},{48,56},{56,64},{64,7... | collective-permute-start | bytes 12296 | tf_op jit(solution)/shard_map/while/body/eval_jaxpr/ppermute | solution.py:16
  508.4 13.2 %collective-permute-start = (f32[1,8,128,128]{3,2,1,0:T(8,128)S(1)}, f32[1,8,128,128]{3,2,1,0:T(8,128)S(1)}, u32[]{:S(2)}, u32[]{:S(2)}) collective-permute-start(f32[1,8,128,128]{3,2,1,0:T(8,128)S(1)} %add.246), channel_id=1, source_target_pairs={{0,8},{8,16},{16,24},{24,32},{32,40},{40,48},{48,56},{56,64},{64,7... | collective-permute-start | bytes 1572872 | tf_op jit(solution)/shard_map/while/body/eval_jaxpr/ppermute | solution.py:16
  510.3 11.3 %collective-permute-start.1 = (f32[1,8,128]{2,1,0:T(8,128)S(1)}, f32[1,8,128]{2,1,0:T(8,128)S(1)}, u32[]{:S(2)}, u32[]{:S(2)}) collective-permute-start(f32[1,8,128]{2,1,0:T(8,128)S(1)} %add.247), channel_id=1, source_target_pairs={{0,8},{8,16},{16,24},{24,32},{32,40},{40,48},{48,56},{56,64},{64,7... | collective-permute-start | bytes 12296 | tf_op jit(solution)/shard_map/while/body/eval_jaxpr/ppermute | solution.py:16
  521.7 13.2 %collective-permute-start = (f32[1,8,128,128]{3,2,1,0:T(8,128)S(1)}, f32[1,8,128,128]{3,2,1,0:T(8,128)S(1)}, u32[]{:S(2)}, u32[]{:S(2)}) collective-permute-start(f32[1,8,128,128]{3,2,1,0:T(8,128)S(1)} %add.246), channel_id=1, source_target_pairs={{0,8},{8,16},{16,24},{24,32},{32,40},{40,48},{48,56},{56,64},{64,7... | collective-permute-start | bytes 1572872 | tf_op jit(solution)/shard_map/while/body/eval_jaxpr/ppermute | solution.py:16
  523.6 11.3 %collective-permute-start.1 = (f32[1,8,128]{2,1,0:T(8,128)S(1)}, f32[1,8,128]{2,1,0:T(8,128)S(1)}, u32[]{:S(2)}, u32[]{:S(2)}) collective-permute-start(f32[1,8,128]{2,1,0:T(8,128)S(1)} %add.247), channel_id=1, source_target_pairs={{0,8},{8,16},{16,24},{24,32},{32,40},{40,48},{48,56},{56,64},{64,7... | collective-permute-start | bytes 12296 | tf_op jit(solution)/shard_map/while/body/eval_jaxpr/ppermute | solution.py:16
  (28 other events, 639.5 us)
where the time goes:
time: 576 us; the launch traced here: 574 us
  waiting for transfers between devices  356 us (62%)
  starting transfers between devices  136 us (24%)
  other arithmetic  30.5 us (5%)
  blocking collectives  20.2 us (4%)
  matrix products  17 us (3%)
  local copies, waits for them, and re-layouts  13.6 us (2%)
    ppermute x64, waiting for transfers between devices, passed_along(): lax.ppermute(value, axis, [(source, source + steps) for source in range(f...  356 us
    ppermute x64, starting transfers between devices, passed_along(): lax.ppermute(value, axis, [(source, source + steps) for source in range(f...  136 us
    all_to_all x1, blocking collectives, body(): lax.all_to_all(result, 'head', split_axis=0, concat_axis=1, tiled=True)  20.2 us
  transfers between devices with their start and end apart: 64, of which 31 were waited for; matrix products, arithmetic and copies ran while one was open for 6% of the time, Pallas kernels for 0%

commit v1 on v0

--- a/solution.py
+++ b/solution.py
@@ -103,16 +103,21 @@
     before_norm = jnp.concatenate(
         [jnp.zeros_like(block_norms), jnp.cumsum(block_norms, axis=0)[:-1]], axis=0
     )
-    empty_state = jnp.zeros_like(total_state)
-    empty_norm = jnp.zeros_like(total_norm)
-
-    def forward_step(index, carry):
-        moved = passed_along((carry[0] + total_state, carry[1] + total_norm), "seq", 1)
-        return (moved[0], moved[1])
-
-    prior_state, prior_norm = lax.fori_loop(
-        0, lax.axis_size("seq") - 1, forward_step, (empty_state, empty_norm)
-    )
+    state_shape = total_state.shape
+    state_size = total_state.size
+    packed = jnp.concatenate([total_state.reshape(-1), total_norm.reshape(-1)])
+    inclusive = packed
+    exclusive = jnp.zeros_like(packed)
+    count = lax.axis_size("seq")
+    steps = 1
+    while steps < count:
+        received = passed_along(inclusive, "seq", steps)
+        exclusive = exclusive + received
+        if 2 * steps < count:
+            inclusive = inclusive + received
+        steps *= 2
+    prior_state = exclusive[:state_size].reshape(state_shape)
+    prior_norm = exclusive[state_size:].reshape(total_norm.shape)
     factor = jax.nn.sigmoid(window_logit).reshape(kv_local, group)
     rot_grouped = rot_q.reshape(tokens, kv_local, group, head_dim)
     row_index = jnp.arange(BLOCK)[:, None]

time: 576 us -> 183 us (0.32)
  waiting for transfers between devices: 356 us -> 66.6 us
  starting transfers between devices: 136 us -> 30.1 us
    ppermute x64 -> x7, waiting for transfers between devices: 356 us -> 66.6 us  [passed_along(): lax.ppermute(value, axis, [(source, source + steps) for source in range(f...]
    ppermute x64 -> x7, starting transfers between devices: 136 us -> 30.1 us  [passed_along(): lax.ppermute(value, axis, [(source, source + steps) for source in range(f...]
  transfers between devices with their start and end apart: 64 -> 7, of which waited for: 31 -> 5; matrix products, arithmetic and copies ran while one was open for 6% -> 27% of each run, Pallas kernels for 0% -> 0%
where the time goes in v1:
time: 183 us; the launch traced here: 180 us
  waiting for transfers between devices  66.6 us (36%)
  starting transfers between devices  30.1 us (16%)
  other arithmetic  26.1 us (14%)
  matrix products  21 us (11%)
  blocking collectives  20.3 us (11%)
  local copies, waits for them, and re-layouts  15.4 us (8%)
    ppermute x7, waiting for transfers between devices, passed_along(): lax.ppermute(value, axis, [(source, source + steps) for source in range(f...  66.6 us
    ppermute x7, starting transfers between devices, passed_along(): lax.ppermute(value, axis, [(source, source + steps) for source in range(f...  30.1 us
    all_to_all x1, blocking collectives, body(): lax.all_to_all(result, 'head', split_axis=0, concat_axis=1, tiled=True)  20.3 us
    unnamed x51, local copies, waits for them, and re-layouts  7.32 us
    another operation x3, other arithmetic  5.46 us
    dot_general x1, matrix products, body(): jnp.einsum('gkij,jgd->igkd', weights.astype(jnp.bfloat16), ext_values, pr...  4.25 us
    reduce_sum x1, other arithmetic, body(): block_norms = jnp.sum(lag_phi, axis=1, dtype=jnp.float32)  3.97 us
  transfers between devices with their start and end apart: 7, of which 5 were waited for; matrix products, arithmetic and copies ran while one was open for 27% of the time, Pallas kernels for 0%

profile of v1, /device:TPU:2, one launch (start us, length us, event | category | flops | bytes accessed | tf_op | source)
XLA Modules:
  0.0 180.1 jit_solution(2676932125891021271)
XLA Ops:
  0.0 0.8 add_bitcast_fusion
  0.9 1.0 copy.37
  1.9 2.4 %subtract_convert_fusion.3 = (bf16[512,1,64]{0,2,1:T(8,128)(2,1)S(1)}, bf16[512,1,64]{0,2,1:T(8,128)(2,1)S(1)}) fusion(f32[512,1,128]{0,2,1:T(8,128)S(1)} %bitcast_convert_fusion, f32[64]{0:T(128)} %constant.76.clone, f32[512]{0:T(512)S(1)} %get-tuple-element.25, f32[64]{0:T(128)} %constant.75.clone, f32[512]{0:T(512)S(1)} %get-tuple-element.24, ...), kind=kLoop, calls=%fused_computation.118 | loop fusion | flops 753664 | bytes 400128 | tf_op jit(solution)/shard_map/convert.6
  4.3 0.1 pad_maximum_fusion.13
  4.4 3.8 %collective-permute-start.1 = (bf16[64,1,128]{0,2,1:T(8,128)(2,1)S(1)}, bf16[64,1,128]{0,2,1:T(8,128)(2,1)S(1)}, u32[]{:S(2)}, u32[]{:S(2)}) collective-permute-start(bf16[64,1,128]{0,2,1:T(8,128)(2,1)S(1)} %pad_maximum_fusion.13), channel_id=1, source_target_pairs={{0,8},{8,16},{16,24},{24,32},{32,40},{40,48},{48,56},{56,64},{64,7... | collective-permute-start | bytes 49160 | tf_op jit(solution)/shard_map/ppermute | solution.py:16
  8.2 1.3 slice_bitcast_fusion
  9.5 3.8 %collective-permute-start = (bf16[64,1,128]{2,0,1:T(8,128)(2,1)}, bf16[64,1,128]{2,0,1:T(8,128)(2,1)}, u32[]{:S(2)}, u32[]{:S(2)}) collective-permute-start(bf16[64,1,128]{2,0,1:T(8,128)(2,1)} %slice_bitcast_fusion), channel_id=1, source_target_pairs={{0,8},{8,16},{16,24},{24,32},{32,40},{40,48},{48,56},{56,64},{64,7... | collective-permute-start | bytes 49160 | tf_op jit(solution)/shard_map/ppermute | solution.py:16
  13.3 2.2 %fusion.64 = (f32[512,64]{0,1:T(8,128)S(1)}, f32[512,64]{0,1:T(8,128)S(1)}) fusion(f32[64]{0:T(128)} %constant.76.clone, f32[512]{0:T(512)S(1)} %get-tuple-element.25, f32[64]{0:T(128)} %constant.75.clone, f32[512]{0:T(512)S(1)} %get-tuple-element.24, f32[64]{0:T(128)} %constant.74.clone, f32[512]{0:T(512)S(1)} %get-tuple-element.23), kind=kLoop, calls=%fused_computation.105 | loop fusion | flops 491520 | bytes 269056 | tf_op jit(solution)/shard_map/sub | solution.py:29
  15.5 0.8 copy.40
  16.3 0.8 copy.42
  17.2 0.5 copy.38
  17.7 0.3 fusion.108
  18.0 1.9 %copy.65 = f32[512,8,64]{2,0,1:T(8,128)} copy(f32[512,8,64]{0,2,1:T(8,128)S(1)} %get-tuple-element.18) | data formatting | bytes 2097152
  19.9 1.9 %copy.66 = f32[512,8,64]{2,0,1:T(8,128)} copy(f32[512,8,64]{0,2,1:T(8,128)S(1)} %get-tuple-element.17) | data formatting | bytes 2097152
  21.9 2.8 %subtract_convert_fusion = (bf16[512,8,64]{2,0,1:T(8,128)(2,1)S(1)}, bf16[512,8,64]{2,0,1:T(8,128)(2,1)S(1)}) fusion(f32[512,8,64]{2,0,1:T(8,128)} %copy.66, f32[512,8,64]{2,0,1:T(8,128)} %copy.65, f32[512,64]{1,0:T(8,128)S(1)} %copy-done.11, f32[512,64]{1,0:T(8,128)S(1)} %copy-done.10), kind=kLoop, calls=%fused_computation.34 | loop fusion | flops 2097152 | bytes 3407872 | tf_op jit(solution)/shard_map/convert.4
  24.7 1.8 %fusion.110 = (f32[512,8]{0,1:T(8,128)S(1)}, f32[512,8,64]{0,2,1:T(8,128)}) fusion(bf16[8,128,64]{1,2,0:T(8,128)(2,1)S(1)} %copy-done, bf16[512,8,64]{2,0,1:T(8,128)(2,1)S(1)} %get-tuple-element.14, bf16[512,8,64]{2,0,1:T(8,128)(2,1)S(1)} %get-tuple-element.13), kind=kOutput, calls=%fused_computation.174 | convolution fusion | flops 69730368 | bytes 2244608 | tf_op jit(solution)/shard_map/sub | solution.py:47
  26.5 2.5 %fusion.109 = (f32[512,8]{0,1:T(8,128)}, f32[512,8,64]{0,2,1:T(8,128)}) fusion(bf16[8,128,64]{1,2,0:T(8,128)(2,1)S(1)} %copy-done, bf16[512,8,64]{2,0,1:T(8,128)(2,1)S(1)} %get-tuple-element.14, bf16[512,8,64]{2,0,1:T(8,128)(2,1)S(1)} %get-tuple-element.13), kind=kOutput, calls=%fused_computation.173 | convolution fusion | flops 69992512 | bytes 2244608 | tf_op jit(solution)/shard_map/sub | solution.py:47
  29.0 0.6 iota_add_fusion
  29.6 0.0 collective-permute-done.1
  29.6 1.5 fusion.58
  31.1 2.3 %copy.45 = f32[576,8,64]{2,1,0:T(8,128)S(1)} copy(f32[576,8,64]{0,2,1:T(8,128)} %bitcast.171) | data formatting | bytes 2359296 | tf_op jit(solution)/shard_map/ngd,gkdf->ngkf/dot_general | solution.py:86
  33.4 1.3 bitcast_reduce_fusion
  34.7 3.6 %fusion.25 = (f32[576,8]{1,0:T(8,128)S(1)}, f32[576,8]{1,0:T(8,128)S(1)}) fusion(f32[576,8,64]{2,1,0:T(8,128)S(1)} %copy.45, f32[576,8]{1,0:T(8,128)S(1)} %get-tuple-element.7, f32[576,8]{1,0:T(8,128)S(1)} %get-tuple-element.8), kind=kLoop, calls=%fused_computation.39 | loop fusion | flops 1465344 | bytes 1253376 | tf_op jit(solution)/shard_map/reduce_sum | solution.py:47
  38.3 3.1 %fusion.24 = (bf16[576,1,8,64]{3,2,0,1:T(8,128)(2,1)S(1)}, bf16[576,1,8,64]{3,2,0,1:T(8,128)(2,1)S(1)}) fusion(f32[576,8,64]{2,1,0:T(8,128)S(1)} %copy.45, f32[576,8]{1,0:T(8,128)S(1)} %get-tuple-element.5, f32[576,8]{1,0:T(8,128)S(1)} %get-tuple-element.7, f32[576,8]{1,0:T(8,128)S(1)} %get-tuple-element.6, f32[576,8]{1,0:T(8,128)S(1)} %get-tuple-element.8), kind=kLoop, calls=%fused_computation.38 | loop fusion | flops 2064384 | bytes 2433024 | tf_op jit(solution)/shard_map/div | solution.py:47
  41.5 0.0 copy-start.19
  41.5 4.0 %convert_reduce_fusion = (f32[8,128]{1,0:T(8,128)S(1)}, bf16[512,1,8,128]{3,2,0,1:T(8,128)(2,1)S(1)}) fusion(bf16[576,1,8,64]{3,2,0,1:T(8,128)(2,1)S(1)} %get-tuple-element.16, bf16[576,1,8,64]{3,2,0,1:T(8,128)(2,1)S(1)} %get-tuple-element.15, pred[512]{0:T(512)(128)(4,1)S(1)} %slice-done), kind=kLoop, calls=%fused_computation.32 | loop fusion | flops 3668992 | bytes 2232832 | tf_op jit(solution)/shard_map/reduce_sum | solution.py:97
  45.5 0.0 copy-start.8
  45.5 1.3 fusion.36
  46.9 4.0 %collective-permute-start.2 = (f32[132096]{0:T(1024)S(1)}, f32[132096]{0:T(1024)S(1)}, u32[]{:S(2)}, u32[]{:S(2)}) collective-permute-start(f32[132096]{0:T(1024)S(1)} %pad_maximum_fusion.3), channel_id=1, source_target_pairs={{0,8},{8,16},{16,24},{24,32},{32,40},{40,48},{48,56},{56,64},{64,7... | collective-permute-start | bytes 1585160 | tf_op jit(solution)/shard_map/ppermute | solution.py:16
  50.9 0.3 fusion.33
  51.3 0.0 copy-start.20
  51.4 0.3 divide_convert_fusion
  51.7 12.4 %collective-permute-done.2 = f32[132096]{0:T(1024)S(1)} collective-permute-done((f32[132096]{0:T(1024)S(1)}, f32[132096]{0:T(1024)S(1)}, u32[]{:S(2)}, u32[]{:S(2)}) %collective-permute-start.2) | collective-permute-done | bytes 528416 | tf_op jit(solution)/shard_map/ppermute | solution.py:16
  64.1 0.1 fusion.106
  64.2 4.3 %collective-permute-start.3 = (f32[132096]{0:T(1024)S(1)}, f32[132096]{0:T(1024)S(1)}, u32[]{:S(2)}, u32[]{:S(2)}) collective-permute-start(f32[132096]{0:T(1024)S(1)} %fusion.106), channel_id=1, source_target_pairs={{0,16},{8,24},{16,32},{24,40},{32,48},{40,56},{48,64},{56,72},{64,... | collective-permute-start | bytes 1585160 | tf_op jit(solution)/shard_map/ppermute | solution.py:16
  68.5 2.6 %fusion.2 = (f32[8,512]{1,0:T(8,128)S(1)}, f32[576,512,8]{1,0,2:T(8,128)S(1)}) fusion(pred[512,576]{0,1:T(8,128)(4,1)S(1)} %get-tuple-element.27, bf16[512,8,64]{2,0,1:T(8,128)(2,1)S(1)} %copy-done.2, bf16[512,8,64]{2,0,1:T(8,128)(2,1)S(1)} %get-tuple-element.13, bf16[512,1,64]{0,2,1:T(8,128)(2,1)S(1)} %copy-done.7, bf16[512,1,64]{0,2,1:T(8,128)(2,1)S(1)} %copy-done.5, ...), kind=kOutput, calls=%fused_computation.4 | convolution fusion | flops 613593088 | bytes 10944512 | tf_op jit(solution)/shard_map/igkd,jgd->gkij/dot_general | solution.py:128
  71.1 20.2 %collective-permute-done.3 = f32[132096]{0:T(1024)S(1)} collective-permute-done((f32[132096]{0:T(1024)S(1)}, f32[132096]{0:T(1024)S(1)}, u32[]{:S(2)}, u32[]{:S(2)}) %collective-permute-start.3) | collective-permute-done | bytes 528416 | tf_op jit(solution)/shard_map/ppermute | solution.py:16
  91.4 0.1 add.180
  91.4 6.5 %collective-permute-start.4 = (f32[132096]{0:T(1024)S(1)}, f32[132096]{0:T(1024)S(1)}, u32[]{:S(2)}, u32[]{:S(2)}) collective-permute-start(f32[132096]{0:T(1024)S(1)} %add.180), channel_id=1, source_target_pairs={{0,32},{8,40},{16,48},{24,56},{32,64},{40,72},{48,80},{56,88},{64,... | collective-permute-start | bytes 1585160 | tf_op jit(solution)/shard_map/ppermute | solution.py:16
  97.9 1.9 %fusion.5 = f32[8,512]{1,0:T(8,128)S(1)} fusion(f32[576,512,8]{1,0,2:T(8,128)S(1)} %get-tuple-element.33, f32[8,512]{1,0:T(8,128)S(1)} %get-tuple-element.32, pred[512,576]{0,1:T(8,128)(4,1)S(1)} %get-tuple-element.27), kind=kLoop, calls=%fused_computation.9 | loop fusion | flops 9433088 | bytes 9764864 | tf_op jit(solution)/shard_map/reduce_sum | solution.py:134
  99.9 21.4 %collective-permute-done.4 = f32[132096]{0:T(1024)S(1)} collective-permute-done((f32[132096]{0:T(1024)S(1)}, f32[132096]{0:T(1024)S(1)}, u32[]{:S(2)}, u32[]{:S(2)}) %collective-permute-start.4) | collective-permute-done | bytes 528416 | tf_op jit(solution)/shard_map/ppermute | solution.py:16
  121.2 0.1 add.182
  121.3 3.5 %collective-permute-start.5 = (f32[132096]{0:T(1024)S(1)}, f32[132096]{0:T(1024)S(1)}, u32[]{:S(2)}, u32[]{:S(2)}) collective-permute-start(f32[132096]{0:T(1024)S(1)} %add.182), channel_id=1, source_target_pairs={{0,64},{8,72},{16,80},{24,88},{32,96},{40,104},{48,112},{56,120},{... | collective-permute-start | bytes 1585160 | tf_op jit(solution)/shard_map/ppermute | solution.py:16
  124.9 4.3 %fusion.10 = f32[128,8,512]{2,0,1:T(8,128)} fusion(f32[576,512,8]{1,0,2:T(8,128)S(1)} %get-tuple-element.33, f32[8,512]{1,0:T(8,128)S(1)} %get-tuple-element.32, pred[512,576]{0,1:T(8,128)(4,1)S(1)} %get-tuple-element.27, bf16[64,1,128]{2,0,1:T(8,128)(2,1)} %collective-permute-done, bf16[512,1,128]{2,0,1:T(8,128)(2,1)S(1)} %bitcast.182), kind=kOutput, calls=%fused_computation.14 | convolution fusion | flops 613711872 | bytes 11993088 | tf_op jit(solution)/shard_map/gkij,jgd->igkd/dot_general | solution.py:138
  129.1 8.0 %collective-permute-done.5 = f32[132096]{0:T(1024)S(1)} collective-permute-done((f32[132096]{0:T(1024)S(1)}, f32[132096]{0:T(1024)S(1)}, u32[]{:S(2)}, u32[]{:S(2)}) %collective-permute-start.5) | collective-permute-done | bytes 528416 | tf_op jit(solution)/shard_map/ppermute | solution.py:16
  137.1 0.1 add.184
  137.2 4.2 %collective-permute-start.6 = (f32[132096]{0:T(1024)S(1)}, f32[132096]{0:T(1024)S(1)}, u32[]{:S(2)}, u32[]{:S(2)}) collective-permute-start(f32[132096]{0:T(1024)S(1)} %add.184), channel_id=1, source_target_pairs={{0,128},{8,136},{16,144},{24,152},{32,160},{40,168},{48,176},{56,1... | collective-permute-start | bytes 1585160 | tf_op jit(solution)/shard_map/ppermute | solution.py:16
  141.3 2.2 %fusion.14 = bf16[576,8,128]{2,1,0:T(8,128)(2,1)S(1)} fusion(bf16[576,8,64]{2,1,0:T(8,128)(2,1)S(1)} %bitcast.169, bf16[576,8,64]{2,1,0:T(8,128)(2,1)S(1)} %bitcast.168, pred[576]{0:T(1024)(128)(4,1)S(1)} %copy-done.18), kind=kLoop, calls=%fused_computation.18 | loop fusion | flops 2949120 | bytes 2359872 | tf_op jit(solution)/shard_map/convert_element_type | solution.py:89
  143.5 3.6 %select_reduce_fusion = (f32[8,512]{1,0:T(8,128)S(1)}, bf16[8,512,576]{1,2,0:T(8,128)(2,1)}) fusion(pred[512,576]{0,1:T(8,128)(4,1)S(1)} %get-tuple-element.26, bf16[512,8,64]{0,2,1:T(8,128)(2,1)S(1)} %get-tuple-element.36, bf16[512,8,64]{0,2,1:T(8,128)(2,1)S(1)} %get-tuple-element.37, bf16[576,8,128]{2,1,0:T(8,128)(2,1)S(1)} %fusion.14), kind=kOutput, calls=%fused_computation.7 | convolution fusion | flops 613150720 | bytes 7258112 | tf_op jit(solution)/shard_map/igkf,jgkf->gkij/dot_general | solution.py:135
  147.1 4.5 %collective-permute-done.6 = f32[132096]{0:T(1024)S(1)} collective-permute-done((f32[132096]{0:T(1024)S(1)}, f32[132096]{0:T(1024)S(1)}, u32[]{:S(2)}, u32[]{:S(2)}) %collective-permute-start.6) | collective-permute-done | bytes 528416 | tf_op jit(solution)/shard_map/ppermute | solution.py:16
  151.6 0.2 add_add_fusion
  151.9 0.2 copy.49
  152.1 0.4 fusion.39
  152.5 0.4 fusion.73
  153.0 0.2 fusion.82
  153.2 0.2 fusion.80
  153.5 0.1 fusion.78
  153.5 0.9 copy-done.22
  154.4 0.9 copy-done.21
  155.3 2.1 %fusion.21 = bf16[512,1,8,128]{0,3,2,1:T(8,128)(2,1)S(1)} fusion(f32[8,128,512]{2,1,0:T(8,128)S(1)} %fusion.73, f32[8,128,512]{2,1,0:T(8,128)S(1)} %fusion.39, f32[128,8,512]{2,0,1:T(8,128)S(1)} %copy-done.21, bf16[8,512,576]{1,2,0:T(8,128)(2,1)S(1)} %copy-done.22, pred[512,576]{0,1:T(8,128)(4,1)S(1)} %get-tuple-element.26, f32[512,8]{0,1:T(8,128)S(1)} %fusion.78, ...), kind=kOutput, calls=%fused_computation.35 | convolution fusion | flops 610304000 | bytes 12517440 | tf_op jit(solution)/shard_map/gkij,jgd->igkd/dot_general | solution.py:144
  157.5 0.8 copy.53
  158.2 0.5 all_to_all.14
  158.8 20.3 %all_to_all.19 = bf16[8,64,1024]{2,1,0:T(8,128)(2,1)S(1)} all-to-all(bf16[8,64,1024]{2,1,0:T(8,128)(2,1)S(1)} %all_to_all.14), channel_id=1, replica_groups=mesh['seq'=32,'head'=8] {'head'}, dimensions={0} | all-to-all | bytes 2097152 | tf_op jit(solution)/shard_map/all_to_all | solution.py:171
  179.1 1.1 copy.67
  (53 shorter events, 0.2 us)
Async XLA Ops:
  0.0 24.7 %copy-start = (bf16[8,128,64]{1,2,0:T(8,128)(2,1)S(1)}, bf16[8,128,64]{1,2,0:T(8,128)(2,1)}, u32[]{:S(2)}) copy-start(bf16[8,128,64]{1,2,0:T(8,128)(2,1)} %param.14) | copy-start | bytes 393220
  0.0 17.2 %copy-start.9 = (bf16[512,1024]{1,0:T(8,128)(2,1)S(1)}, bf16[512,1024]{1,0:T(8,128)(2,1)}, u32[]{:S(2)}) copy-start(bf16[512,1024]{1,0:T(8,128)(2,1)} %param.10) | copy-start | bytes 3145732
  4.3 25.4 %copy-start.4 = (bf16[512,1,64]{0,2,1:T(8,128)(2,1)}, bf16[512,1,64]{0,2,1:T(8,128)(2,1)S(1)}, u32[]{:S(2)}) copy-start(bf16[512,1,64]{0,2,1:T(8,128)(2,1)S(1)} %get-tuple-element.19) | copy-start | bytes 196612
  4.3 25.4 %copy-start.6 = (bf16[512,1,64]{0,2,1:T(8,128)(2,1)}, bf16[512,1,64]{0,2,1:T(8,128)(2,1)S(1)}, u32[]{:S(2)}) copy-start(bf16[512,1,64]{0,2,1:T(8,128)(2,1)S(1)} %get-tuple-element.20) | copy-start | bytes 196612
  4.4 25.2 %collective-permute-start.1 = (bf16[64,1,128]{0,2,1:T(8,128)(2,1)S(1)}, bf16[64,1,128]{0,2,1:T(8,128)(2,1)S(1)}, u32[]{:S(2)}, u32[]{:S(2)}) collective-permute-start(bf16[64,1,128]{0,2,1:T(8,128)(2,1)S(1)} %pad_maximum_fusion.13), channel_id=1, source_target_pairs={{0,8},{8,16},{16,24},{24,32},{32,40},{40,48},{48,56},{56,64},{64,7... | collective-permute-start | bytes 49160 | tf_op jit(solution)/shard_map/ppermute | solution.py:16
  9.5 36.0 %collective-permute-start = (bf16[64,1,128]{2,0,1:T(8,128)(2,1)}, bf16[64,1,128]{2,0,1:T(8,128)(2,1)}, u32[]{:S(2)}, u32[]{:S(2)}) collective-permute-start(bf16[64,1,128]{2,0,1:T(8,128)(2,1)} %slice_bitcast_fusion), channel_id=1, source_target_pairs={{0,8},{8,16},{16,24},{24,32},{32,40},{40,48},{48,56},{56,64},{64,7... | collective-permute-start | bytes 49160 | tf_op jit(solution)/shard_map/ppermute | solution.py:16
  19.9 1.9 %copy-start.10 = (f32[512,64]{1,0:T(8,128)S(1)}, f32[512,64]{1,0:T(8,128)}, u32[]{:S(2)}) copy-start(f32[512,64]{1,0:T(8,128)} %copy.40) | copy-start | bytes 393220
  19.9 1.9 %copy-start.11 = (f32[512,64]{1,0:T(8,128)S(1)}, f32[512,64]{1,0:T(8,128)}, u32[]{:S(2)}) copy-start(f32[512,64]{1,0:T(8,128)} %copy.42) | copy-start | bytes 393220
  24.7 4.3 %copy-start.1 = (bf16[512,8,64]{2,0,1:T(8,128)(2,1)}, bf16[512,8,64]{2,0,1:T(8,128)(2,1)S(1)}, u32[]{:S(2)}) copy-start(bf16[512,8,64]{2,0,1:T(8,128)(2,1)S(1)} %get-tuple-element.14) | copy-start | bytes 1572868
  26.5 3.1 %copy-start.14 = (bf16[8,128,64]{1,2,0:T(8,128)(2,1)S(1)}, bf16[8,128,64]{1,2,0:T(8,128)(2,1)}, u32[]{:S(2)}) copy-start(bf16[8,128,64]{1,2,0:T(8,128)(2,1)} %param.15) | copy-start | bytes 393220
  29.6 1.5 copy-start.17
  29.6 1.5 copy-start.12
  38.3 3.1 %slice-start = ((pred[576]{0:T(1024)(128)(4,1)}), pred[512]{0:T(512)(128)(4,1)S(1)}, s32[]{:S(2)}) async-start(pred[576]{0:T(1024)(128)(4,1)} %copy-done.17), calls=%async_computation.1 | async-start | bytes 1024 | tf_op jit(solution)/shard_map/slice | solution.py:92
  41.5 4.1 %copy-start.19 = (bf16[512,128]{1,0:T(8,128)(2,1)S(1)}, bf16[512,128]{1,0:T(8,128)(2,1)}, u32[]{:S(2)}) copy-start(bf16[512,128]{1,0:T(8,128)(2,1)} %param.12) | copy-start | bytes 393220
  45.5 5.5 %copy-start.16 = (s32[512]{0:T(512)S(1)}, s32[512]{0:T(512)}, u32[]{:S(2)}) copy-start(s32[512]{0:T(512)} %iota_add_fusion) | copy-start | bytes 6148
  45.5 5.5 %copy-start.18 = (pred[576]{0:T(1024)(128)(4,1)S(1)}, pred[576]{0:T(1024)(128)(4,1)}, u32[]{:S(2)}) copy-start(pred[576]{0:T(1024)(128)(4,1)} %copy-done.17) | copy-start | bytes 1732
  45.5 5.8 %copy-start.3 = (f32[512,8,64]{0,2,1:T(8,128)S(1)}, f32[512,8,64]{0,2,1:T(8,128)}, u32[]{:S(2)}) copy-start(f32[512,8,64]{0,2,1:T(8,128)} %get-tuple-element.31) | copy-start | bytes 3145732
  45.5 5.8 %copy-start.8 = (f32[512,8,64]{0,2,1:T(8,128)S(1)}, f32[512,8,64]{0,2,1:T(8,128)}, u32[]{:S(2)}) copy-start(f32[512,8,64]{0,2,1:T(8,128)} %get-tuple-element.29) | copy-start | bytes 3145732
  45.5 5.8 %copy-start.15 = (f32[512,8]{0,1:T(8,128)S(1)}, f32[512,8]{0,1:T(8,128)}, u32[]{:S(2)}) copy-start(f32[512,8]{0,1:T(8,128)} %get-tuple-element.28) | copy-start | bytes 49156
  46.9 17.2 %collective-permute-start.2 = (f32[132096]{0:T(1024)S(1)}, f32[132096]{0:T(1024)S(1)}, u32[]{:S(2)}, u32[]{:S(2)}) collective-permute-start(f32[132096]{0:T(1024)S(1)} %pad_maximum_fusion.3), channel_id=1, source_target_pairs={{0,8},{8,16},{16,24},{24,32},{32,40},{40,48},{48,56},{56,64},{64,7... | collective-permute-start | bytes 1585160 | tf_op jit(solution)/shard_map/ppermute | solution.py:16
  51.3 17.2 %copy-start.20 = (f32[8]{0:T(128)S(1)}, f32[8]{0:T(128)}, u32[]{:S(2)}) copy-start(f32[8]{0:T(128)} %param.16) | copy-start | bytes 100
  51.3 17.2 %copy-start.2 = (bf16[512,8,64]{2,0,1:T(8,128)(2,1)S(1)}, bf16[512,8,64]{2,0,1:T(8,128)(2,1)}, u32[]{:S(2)}) copy-start(bf16[512,8,64]{2,0,1:T(8,128)(2,1)} %copy-done.1) | copy-start | bytes 1572868
  51.3 17.2 %copy-start.5 = (bf16[512,1,64]{0,2,1:T(8,128)(2,1)S(1)}, bf16[512,1,64]{0,2,1:T(8,128)(2,1)}, u32[]{:S(2)}) copy-start(bf16[512,1,64]{0,2,1:T(8,128)(2,1)} %copy-done.4) | copy-start | bytes 196612
  51.3 17.2 %copy-start.7 = (bf16[512,1,64]{0,2,1:T(8,128)(2,1)S(1)}, bf16[512,1,64]{0,2,1:T(8,128)(2,1)}, u32[]{:S(2)}) copy-start(bf16[512,1,64]{0,2,1:T(8,128)(2,1)} %copy-done.6) | copy-start | bytes 196612
  51.4 17.2 %copy-start.13 = (bf16[64,1,128]{0,2,1:T(8,128)(2,1)S(1)}, bf16[64,1,128]{0,2,1:T(8,128)(2,1)}, u32[]{:S(2)}) copy-start(bf16[64,1,128]{0,2,1:T(8,128)(2,1)} %copy-done.12) | copy-start | bytes 49156
  64.2 27.2 %collective-permute-start.3 = (f32[132096]{0:T(1024)S(1)}, f32[132096]{0:T(1024)S(1)}, u32[]{:S(2)}, u32[]{:S(2)}) collective-permute-start(f32[132096]{0:T(1024)S(1)} %fusion.106), channel_id=1, source_target_pairs={{0,16},{8,24},{16,32},{24,40},{32,48},{40,56},{48,64},{56,72},{64,... | collective-permute-start | bytes 1585160 | tf_op jit(solution)/shard_map/ppermute | solution.py:16
  91.4 29.8 %collective-permute-start.4 = (f32[132096]{0:T(1024)S(1)}, f32[132096]{0:T(1024)S(1)}, u32[]{:S(2)}, u32[]{:S(2)}) collective-permute-start(f32[132096]{0:T(1024)S(1)} %add.180), channel_id=1, source_target_pairs={{0,32},{8,40},{16,48},{24,56},{32,64},{40,72},{48,80},{56,88},{64,... | collective-permute-start | bytes 1585160 | tf_op jit(solution)/shard_map/ppermute | solution.py:16
  121.3 15.8 %collective-permute-start.5 = (f32[132096]{0:T(1024)S(1)}, f32[132096]{0:T(1024)S(1)}, u32[]{:S(2)}, u32[]{:S(2)}) collective-permute-start(f32[132096]{0:T(1024)S(1)} %add.182), channel_id=1, source_target_pairs={{0,64},{8,72},{16,80},{24,88},{32,96},{40,104},{48,112},{56,120},{... | collective-permute-start | bytes 1585160 | tf_op jit(solution)/shard_map/ppermute | solution.py:16
  137.2 14.5 %collective-permute-start.6 = (f32[132096]{0:T(1024)S(1)}, f32[132096]{0:T(1024)S(1)}, u32[]{:S(2)}, u32[]{:S(2)}) collective-permute-start(f32[132096]{0:T(1024)S(1)} %add.184), channel_id=1, source_target_pairs={{0,128},{8,136},{16,144},{24,152},{32,160},{40,168},{48,176},{56,1... | collective-permute-start | bytes 1585160 | tf_op jit(solution)/shard_map/ppermute | solution.py:16
  152.1 2.3 %copy-start.22 = (bf16[8,512,576]{1,2,0:T(8,128)(2,1)S(1)}, bf16[8,512,576]{1,2,0:T(8,128)(2,1)}, u32[]{:S(2)}) copy-start(bf16[8,512,576]{1,2,0:T(8,128)(2,1)} %get-tuple-element.35) | copy-start | bytes 14155780
  153.0 2.4 %copy-start.21 = (f32[128,8,512]{2,0,1:T(8,128)S(1)}, f32[128,8,512]{2,0,1:T(8,128)}, u32[]{:S(2)}) copy-start(f32[128,8,512]{2,0,1:T(8,128)} %fusion.10) | copy-start | bytes 6291460

commit v2 on v1

--- a/solution.py
+++ b/solution.py
@@ -106,16 +106,26 @@
     state_shape = total_state.shape
     state_size = total_state.size
     packed = jnp.concatenate([total_state.reshape(-1), total_norm.reshape(-1)])
-    inclusive = packed
-    exclusive = jnp.zeros_like(packed)
     count = lax.axis_size("seq")
+    shifts = []
     steps = 1
     while steps < count:
-        received = passed_along(inclusive, "seq", steps)
-        exclusive = exclusive + received
-        if 2 * steps < count:
-            inclusive = inclusive + received
+        shifts.append(steps)
         steps *= 2
+    half = len(shifts) // 2 + 1
+    orders = (shifts, shifts[half:] + shifts[:half])
+    middle = packed.size // 2
+    pieces = []
+    for order, piece in zip(orders, (packed[:middle], packed[middle:])):
+        inclusive = piece
+        exclusive = jnp.zeros_like(piece)
+        for place, shift in enumerate(order):
+            received = passed_along(inclusive, "seq", shift)
+            exclusive = exclusive + received
+            if place + 1 < len(order):
+                inclusive = inclusive + received
+        pieces.append(exclusive)
+    exclusive = jnp.concatenate(pieces)
     prior_state = exclusive[:state_size].reshape(state_shape)
     prior_norm = exclusive[state_size:].reshape(total_norm.shape)
     factor = jax.nn.sigmoid(window_logit).reshape(kv_local, group)

time: 183 us -> 175 us (0.956)
  the two profiles are of different devices: /device:TPU:2 before, /device:TPU:6 now
where the time goes in v2:
time: 175 us; the launch traced here: 174 us
  waiting for transfers between devices  53.3 us (30%)
  starting transfers between devices  32.1 us (18%)
  other arithmetic  29.7 us (17%)
  matrix products  23 us (13%)
  blocking collectives  20.3 us (12%)
  local copies, waits for them, and re-layouts  15.4 us (9%)
    ppermute x12, waiting for transfers between devices, passed_along(): lax.ppermute(value, axis, [(source, source + steps) for source in range(f...  53.3 us
    ppermute x12, starting transfers between devices, passed_along(): lax.ppermute(value, axis, [(source, source + steps) for source in range(f...  32.1 us
    all_to_all x1, blocking collectives, body(): lax.all_to_all(result, 'head', split_axis=0, concat_axis=1, tiled=True)  20.3 us
    another operation x3, other arithmetic  7.66 us
    unnamed x51, local copies, waits for them, and re-layouts  7.31 us
    dot_general x1, matrix products, body(): jnp.einsum('gkij,jgd->igkd', weights.astype(jnp.bfloat16), ext_values, pr...  4.22 us
    reduce_sum x1, other arithmetic, body(): block_norms = jnp.sum(lag_phi, axis=1, dtype=jnp.float32)  3.97 us
    dot_general x1, matrix products, body(): jnp.einsum('gkij,jgd->igkd', affinity.astype(jnp.bfloat16), ext_values, p...  3.81 us
  transfers between devices with their start and end apart: 12, of which 7 were waited for; matrix products, arithmetic and copies ran while one was open for 30% of the time, Pallas kernels for 0%

profile of v2, /device:TPU:6, one launch (start us, length us, event | category | flops | bytes accessed | tf_op | source)
XLA Modules:
  0.0 174.5 jit_solution(6062518055198125291)
XLA Ops:
  0.0 0.8 add_bitcast_fusion
  0.9 1.0 copy.37
  1.9 2.4 %subtract_convert_fusion.3 = (bf16[512,1,64]{0,2,1:T(8,128)(2,1)S(1)}, bf16[512,1,64]{0,2,1:T(8,128)(2,1)S(1)}) fusion(f32[512,1,128]{0,2,1:T(8,128)S(1)} %bitcast_convert_fusion, f32[64]{0:T(128)} %constant.76.clone, f32[512]{0:T(512)S(1)} %get-tuple-element.27, f32[64]{0:T(128)} %constant.75.clone, f32[512]{0:T(512)S(1)} %get-tuple-element.26, ...), kind=kLoop, calls=%fused_computation.120 | loop fusion | flops 753664 | bytes 400128 | tf_op jit(solution)/shard_map/convert.6
  4.3 0.6 copy-done.5
  4.9 0.7 pad_maximum_fusion.14
  5.6 3.8 %collective-permute-start.1 = (bf16[64,1,128]{0,2,1:T(8,128)(2,1)}, bf16[64,1,128]{0,2,1:T(8,128)(2,1)}, u32[]{:S(2)}, u32[]{:S(2)}) collective-permute-start(bf16[64,1,128]{0,2,1:T(8,128)(2,1)} %pad_maximum_fusion.14), channel_id=1, source_target_pairs={{0,8},{8,16},{16,24},{24,32},{32,40},{40,48},{48,56},{56,64},{64,7... | collective-permute-start | bytes 49160 | tf_op jit(solution)/shard_map/ppermute | solution.py:16
  9.4 1.3 slice_bitcast_fusion
  10.7 3.8 %collective-permute-start = (bf16[64,1,128]{2,0,1:T(8,128)(2,1)}, bf16[64,1,128]{2,0,1:T(8,128)(2,1)}, u32[]{:S(2)}, u32[]{:S(2)}) collective-permute-start(bf16[64,1,128]{2,0,1:T(8,128)(2,1)} %slice_bitcast_fusion), channel_id=1, source_target_pairs={{0,8},{8,16},{16,24},{24,32},{32,40},{40,48},{48,56},{56,64},{64,7... | collective-permute-start | bytes 49160 | tf_op jit(solution)/shard_map/ppermute | solution.py:16
  14.6 2.2 %fusion.64 = (f32[512,64]{0,1:T(8,128)S(1)}, f32[512,64]{0,1:T(8,128)S(1)}) fusion(f32[64]{0:T(128)} %constant.76.clone, f32[512]{0:T(512)S(1)} %get-tuple-element.27, f32[64]{0:T(128)} %constant.75.clone, f32[512]{0:T(512)S(1)} %get-tuple-element.26, f32[64]{0:T(128)} %constant.74.clone, f32[512]{0:T(512)S(1)} %get-tuple-element.25), kind=kLoop, calls=%fused_computation.107 | loop fusion | flops 491520 | bytes 269056 | tf_op jit(solution)/shard_map/sub | solution.py:29
  16.7 0.8 copy.40
  17.6 0.8 copy.42
  18.4 0.5 copy.38
  19.0 0.3 fusion.107
  19.2 1.9 %copy.65 = f32[512,8,64]{2,0,1:T(8,128)} copy(f32[512,8,64]{0,2,1:T(8,128)S(1)} %get-tuple-element.18) | data formatting | bytes 2097152
  21.2 1.9 %copy.66 = f32[512,8,64]{2,0,1:T(8,128)} copy(f32[512,8,64]{0,2,1:T(8,128)S(1)} %get-tuple-element.17) | data formatting | bytes 2097152
  23.1 2.8 %subtract_convert_fusion = (bf16[512,8,64]{2,0,1:T(8,128)(2,1)S(1)}, bf16[512,8,64]{2,0,1:T(8,128)(2,1)S(1)}) fusion(f32[512,8,64]{2,0,1:T(8,128)} %copy.66, f32[512,8,64]{2,0,1:T(8,128)} %copy.65, f32[512,64]{1,0:T(8,128)} %copy.42, f32[512,64]{1,0:T(8,128)S(1)} %copy-done.12), kind=kLoop, calls=%fused_computation.34 | loop fusion | flops 2097152 | bytes 3407872 | tf_op jit(solution)/shard_map/convert.4
  26.0 0.9 fusion.109
  26.8 2.5 %fusion.108 = (f32[512,8]{0,1:T(8,128)}, f32[512,8,64]{0,2,1:T(8,128)}) fusion(bf16[8,128,64]{1,2,0:T(8,128)(2,1)S(1)} %copy-done, bf16[512,8,64]{2,0,1:T(8,128)(2,1)S(1)} %get-tuple-element.14, bf16[512,8,64]{2,0,1:T(8,128)(2,1)S(1)} %get-tuple-element.13), kind=kOutput, calls=%fused_computation.175 | convolution fusion | flops 69992512 | bytes 2244608 | tf_op jit(solution)/shard_map/sub | solution.py:47
  29.3 1.3 broadcast_subtract_fusion
  30.6 2.5 %divide_convert_fusion = (bf16[512,8,64]{0,2,1:T(8,128)(2,1)}, bf16[512,8,64]{0,2,1:T(8,128)(2,1)}) fusion(f32[512,8,64]{0,2,1:T(8,128)} %get-tuple-element.31, f32[512,8]{0,1:T(8,128)} %get-tuple-element.30, f32[512,8,64]{0,2,1:T(8,128)S(1)} %get-tuple-element.33, f32[512,8]{0,1:T(8,128)S(1)} %get-tuple-element.32), kind=kLoop, calls=%fused_computation.58 | loop fusion | flops 1048576 | bytes 3178496 | tf_op jit(solution)/shard_map/convert.3
  33.2 2.2 %fusion.58 = f32[576,512]{0,1} fusion(bf16[128,512]{0,1:T(8,128)(2,1)S(1)} %bitcast.177, bf16[512,1,64]{0,2,1:T(8,128)(2,1)S(1)} %copy-done.9, bf16[512,1,64]{0,2,1:T(8,128)(2,1)S(1)} %copy-done.6, bf16[64,1,128]{0,2,1:T(8,128)(2,1)} %collective-permute-done.1), kind=kOutput, calls=%fused_computation.101 | convolution fusion | flops 75939840 | bytes 1458176
  35.4 2.3 %copy.45 = f32[576,8,64]{2,1,0:T(8,128)S(1)} copy(f32[576,8,64]{0,2,1:T(8,128)} %bitcast.171) | data formatting | bytes 2359296 | tf_op jit(solution)/shard_map/ngd,gkdf->ngkf/dot_general | solution.py:86
  37.7 1.3 bitcast_reduce_fusion
  39.0 3.6 %fusion.25 = (f32[576,8]{1,0:T(8,128)S(1)}, f32[576,8]{1,0:T(8,128)S(1)}) fusion(f32[576,8,64]{2,1,0:T(8,128)S(1)} %copy.45, f32[576,8]{1,0:T(8,128)S(1)} %get-tuple-element.7, f32[576,8]{1,0:T(8,128)S(1)} %get-tuple-element.8), kind=kLoop, calls=%fused_computation.39 | loop fusion | flops 1465344 | bytes 1253376 | tf_op jit(solution)/shard_map/reduce_sum | solution.py:47
  42.6 3.1 %fusion.24 = (bf16[576,1,8,64]{3,2,0,1:T(8,128)(2,1)S(1)}, bf16[576,1,8,64]{3,2,0,1:T(8,128)(2,1)S(1)}) fusion(f32[576,8,64]{2,1,0:T(8,128)S(1)} %copy.45, f32[576,8]{1,0:T(8,128)S(1)} %get-tuple-element.5, f32[576,8]{1,0:T(8,128)S(1)} %get-tuple-element.7, f32[576,8]{1,0:T(8,128)S(1)} %get-tuple-element.6, f32[576,8]{1,0:T(8,128)S(1)} %get-tuple-element.8), kind=kLoop, calls=%fused_computation.38 | loop fusion | flops 2064384 | bytes 2433024 | tf_op jit(solution)/shard_map/div | solution.py:47
  45.8 4.0 %convert_reduce_fusion = (f32[8,128]{1,0:T(8,128)S(1)}, bf16[512,1,8,128]{3,2,0,1:T(8,128)(2,1)S(1)}) fusion(bf16[576,1,8,64]{3,2,0,1:T(8,128)(2,1)S(1)} %get-tuple-element.16, bf16[576,1,8,64]{3,2,0,1:T(8,128)(2,1)S(1)} %get-tuple-element.15, pred[512]{0:T(512)(128)(4,1)S(1)} %slice-done), kind=kLoop, calls=%fused_computation.32 | loop fusion | flops 3668992 | bytes 2232832 | tf_op jit(solution)/shard_map/reduce_sum | solution.py:97
  49.8 1.3 fusion.36
  51.1 4.0 %collective-permute-start.2 = (f32[66048]{0:T(1024)S(1)}, f32[66048]{0:T(1024)S(1)}, u32[]{:S(2)}, u32[]{:S(2)}) collective-permute-start(f32[66048]{0:T(1024)S(1)} %slice.72), channel_id=1, source_target_pairs={{0,8},{8,16},{16,24},{24,32},{32,40},{40,48},{48,56},{56,64},{64,7... | collective-permute-start | bytes 792584 | tf_op jit(solution)/shard_map/ppermute | solution.py:16
  55.2 0.3 fusion.33
  55.5 7.2 %collective-permute-done.2 = f32[66048]{0:T(1024)S(1)} collective-permute-done((f32[66048]{0:T(1024)S(1)}, f32[66048]{0:T(1024)S(1)}, u32[]{:S(2)}, u32[]{:S(2)}) %collective-permute-start.2) | collective-permute-done | bytes 264224 | tf_op jit(solution)/shard_map/ppermute | solution.py:16
  62.8 1.3 collective-permute-start.7
  64.1 4.3 %collective-permute-start.3 = (f32[66048]{0:T(1024)S(1)}, f32[66048]{0:T(1024)S(1)}, u32[]{:S(2)}, u32[]{:S(2)}) collective-permute-start(f32[66048]{0:T(1024)S(1)} %get-tuple-element.19), channel_id=1, source_target_pairs={{0,16},{8,24},{16,32},{24,40},{32,48},{40,56},{48,64},{56,72},{64,... | collective-permute-start | bytes 792584 | tf_op jit(solution)/shard_map/ppermute | solution.py:16
  68.4 3.2 %fusion.2 = (f32[8,512]{1,0:T(8,128)S(1)}, f32[576,512,8]{1,0,2:T(8,128)S(1)}) fusion(pred[512,576]{0,1:T(8,128)(4,1)S(1)} %get-tuple-element.29, bf16[512,8,64]{2,0,1:T(8,128)(2,1)S(1)} %copy-done.2, bf16[512,8,64]{2,0,1:T(8,128)(2,1)S(1)} %get-tuple-element.13, bf16[512,1,64]{0,2,1:T(8,128)(2,1)S(1)} %copy-done.10, bf16[512,1,64]{0,2,1:T(8,128)(2,1)S(1)} %copy-done.7, ...), kind=kOutput, calls=%fused_computation.4 | convolution fusion | flops 613593088 | bytes 10944512 | tf_op jit(solution)/shard_map/igkd,jgd->gkij/dot_general | solution.py:138
  71.7 1.3 collective-permute-start.8
  73.0 8.4 %collective-permute-done.3 = f32[66048]{0:T(1024)S(1)} collective-permute-done((f32[66048]{0:T(1024)S(1)}, f32[66048]{0:T(1024)S(1)}, u32[]{:S(2)}, u32[]{:S(2)}) %collective-permute-start.3) | collective-permute-done | bytes 264224 | tf_op jit(solution)/shard_map/ppermute | solution.py:16
  81.5 5.0 %collective-permute-start.4 = (f32[66048]{0:T(1024)S(1)}, f32[66048]{0:T(1024)S(1)}, u32[]{:S(2)}, u32[]{:S(2)}) collective-permute-start(f32[66048]{0:T(1024)S(1)} %add.204), channel_id=1, source_target_pairs={{0,32},{8,40},{16,48},{24,56},{32,64},{40,72},{48,80},{56,88},{64,... | collective-permute-start | bytes 792584 | tf_op jit(solution)/shard_map/ppermute | solution.py:16
  86.4 1.9 %fusion.5 = f32[8,512]{1,0:T(8,128)S(1)} fusion(f32[576,512,8]{1,0,2:T(8,128)S(1)} %get-tuple-element.35, f32[8,512]{1,0:T(8,128)S(1)} %get-tuple-element.34, pred[512,576]{0,1:T(8,128)(4,1)S(1)} %get-tuple-element.29), kind=kLoop, calls=%fused_computation.9 | loop fusion | flops 9433088 | bytes 9764864 | tf_op jit(solution)/shard_map/reduce_sum | solution.py:144
  88.4 2.0 %collective-permute-start.9 = (f32[66048]{0:T(1024)S(1)}, f32[66048]{0:T(1024)S(1)}, u32[]{:S(2)}, u32[]{:S(2)}) collective-permute-start(f32[66048]{0:T(1024)S(1)} %add.212), channel_id=1, source_target_pairs={{0,8},{8,16},{16,24},{24,32},{32,40},{40,48},{48,56},{56,64},{64,7... | collective-permute-start | bytes 792584 | tf_op jit(solution)/shard_map/ppermute | solution.py:16
  90.5 9.9 %collective-permute-done.4 = f32[66048]{0:T(1024)S(1)} collective-permute-done((f32[66048]{0:T(1024)S(1)}, f32[66048]{0:T(1024)S(1)}, u32[]{:S(2)}, u32[]{:S(2)}) %collective-permute-start.4) | collective-permute-done | bytes 264224 | tf_op jit(solution)/shard_map/ppermute | solution.py:16
  100.5 1.3 collective-permute-start.5
  101.8 4.2 %fusion.10 = f32[128,8,512]{2,0,1:T(8,128)} fusion(f32[576,512,8]{1,0,2:T(8,128)S(1)} %get-tuple-element.35, f32[8,512]{1,0:T(8,128)S(1)} %get-tuple-element.34, pred[512,576]{0,1:T(8,128)(4,1)S(1)} %get-tuple-element.29, bf16[64,1,128]{2,0,1:T(8,128)(2,1)} %collective-permute-done, bf16[512,1,128]{2,0,1:T(8,128)(2,1)S(1)} %bitcast.181), kind=kOutput, calls=%fused_computation.14 | convolution fusion | flops 613711872 | bytes 11993088 | tf_op jit(solution)/shard_map/gkij,jgd->igkd/dot_general | solution.py:148
  106.0 2.1 %fusion.14 = bf16[576,8,128]{2,1,0:T(8,128)(2,1)S(1)} fusion(bf16[576,8,64]{2,1,0:T(8,128)(2,1)S(1)} %bitcast.169, bf16[576,8,64]{2,1,0:T(8,128)(2,1)S(1)} %bitcast.168, pred[576]{0:T(1024)(128)(4,1)S(1)} %copy-done.17), kind=kLoop, calls=%fused_computation.18 | loop fusion | flops 2949120 | bytes 2359872 | tf_op jit(solution)/shard_map/convert_element_type | solution.py:89
  108.2 1.9 %collective-permute-start.10 = (f32[66048]{0:T(1024)S(1)}, f32[66048]{0:T(1024)S(1)}, u32[]{:S(2)}, u32[]{:S(2)}) collective-permute-start(f32[66048]{0:T(1024)S(1)} %add.214), channel_id=1, source_target_pairs={{0,16},{8,24},{16,32},{24,40},{32,48},{40,56},{48,64},{56,72},{64,... | collective-permute-start | bytes 792584 | tf_op jit(solution)/shard_map/ppermute | solution.py:16
  110.1 0.2 collective-permute-done.5
  110.4 1.3 collective-permute-start.6
  111.7 3.6 %select_reduce_fusion = (f32[8,512]{1,0:T(8,128)S(1)}, bf16[8,512,576]{1,2,0:T(8,128)(2,1)}) fusion(pred[512,576]{0,1:T(8,128)(4,1)S(1)} %get-tuple-element.28, bf16[512,8,64]{0,2,1:T(8,128)(2,1)S(1)} %copy-done.3, bf16[512,8,64]{0,2,1:T(8,128)(2,1)S(1)} %copy-done.4, bf16[576,8,128]{2,1,0:T(8,128)(2,1)S(1)} %fusion.14), kind=kOutput, calls=%fused_computation.7 | convolution fusion | flops 613150720 | bytes 7258112 | tf_op jit(solution)/shard_map/igkf,jgkf->gkij/dot_general | solution.py:145
  115.3 11.4 %collective-permute-done.10 = f32[66048]{0:T(1024)S(1)} collective-permute-done((f32[66048]{0:T(1024)S(1)}, f32[66048]{0:T(1024)S(1)}, u32[]{:S(2)}, u32[]{:S(2)}) %collective-permute-start.10) | collective-permute-done | bytes 264224 | tf_op jit(solution)/shard_map/ppermute | solution.py:16
  126.7 2.1 %collective-permute-start.11 = (f32[66048]{0:T(1024)S(1)}, f32[66048]{0:T(1024)S(1)}, u32[]{:S(2)}, u32[]{:S(2)}) collective-permute-start(f32[66048]{0:T(1024)S(1)} %add.216), channel_id=1, source_target_pairs={{0,32},{8,40},{16,48},{24,56},{32,64},{40,72},{48,80},{56,88},{64,... | collective-permute-start | bytes 792584 | tf_op jit(solution)/shard_map/ppermute | solution.py:16
  128.9 0.1 add_add_fusion.1
  129.0 16.0 %collective-permute-done.11 = f32[66048]{0:T(1024)S(1)} collective-permute-done((f32[66048]{0:T(1024)S(1)}, f32[66048]{0:T(1024)S(1)}, u32[]{:S(2)}, u32[]{:S(2)}) %collective-permute-start.11) | collective-permute-done | bytes 264224 | tf_op jit(solution)/shard_map/ppermute | solution.py:16
  145.0 0.1 add_add_fusion
  145.1 0.2 copy.49
  145.3 0.4 fusion.39
  145.8 0.4 fusion.73
  146.2 0.2 fusion.82
  146.5 0.2 fusion.80
  146.7 0.1 copy-done.20
  147.0 0.2 copy-done.14
  147.2 0.8 copy-done.22
  148.0 3.8 %fusion.21 = bf16[512,1,8,128]{0,3,2,1:T(8,128)(2,1)S(1)} fusion(f32[8,128,512]{2,1,0:T(8,128)S(1)} %fusion.73, f32[8,128,512]{2,1,0:T(8,128)S(1)} %fusion.39, f32[128,8,512]{2,0,1:T(8,128)S(1)} %copy-done.22, bf16[8,512,576]{1,2,0:T(8,128)(2,1)} %get-tuple-element.37, pred[512,576]{0,1:T(8,128)(4,1)S(1)} %copy-done.14, f32[512,8]{0,1:T(8,128)S(1)} %fusion.78, ...), kind=kOutput, calls=%fused_computation.35 | convolution fusion | flops 610304000 | bytes 12517440 | tf_op jit(solution)/shard_map/gkij,jgd->igkd/dot_general | solution.py:154
  151.8 0.8 copy.53
  152.6 0.5 all_to_all.14
  153.1 20.3 %all_to_all.19 = bf16[8,64,1024]{2,1,0:T(8,128)(2,1)S(1)} all-to-all(bf16[8,64,1024]{2,1,0:T(8,128)(2,1)S(1)} %all_to_all.14), channel_id=1, replica_groups=mesh['seq'=32,'head'=8] {'head'}, dimensions={0} | all-to-all | bytes 2097152 | tf_op jit(solution)/shard_map/all_to_all | solution.py:181
  173.4 1.1 copy.67
  (68 shorter events, 0.7 us)
Async XLA Ops:
  0.0 26.0 %copy-start = (bf16[8,128,64]{1,2,0:T(8,128)(2,1)S(1)}, bf16[8,128,64]{1,2,0:T(8,128)(2,1)}, u32[]{:S(2)}) copy-start(bf16[8,128,64]{1,2,0:T(8,128)(2,1)} %param.14) | copy-start | bytes 393220
  0.0 18.4 %copy-start.11 = (bf16[512,1024]{1,0:T(8,128)(2,1)S(1)}, bf16[512,1024]{1,0:T(8,128)(2,1)}, u32[]{:S(2)}) copy-start(bf16[512,1024]{1,0:T(8,128)(2,1)} %param.10) | copy-start | bytes 3145732
  4.3 0.6 copy-start.5
  4.3 1.3 copy-start.8
  5.6 27.5 %collective-permute-start.1 = (bf16[64,1,128]{0,2,1:T(8,128)(2,1)}, bf16[64,1,128]{0,2,1:T(8,128)(2,1)}, u32[]{:S(2)}, u32[]{:S(2)}) collective-permute-start(bf16[64,1,128]{0,2,1:T(8,128)(2,1)} %pad_maximum_fusion.14), channel_id=1, source_target_pairs={{0,8},{8,16},{16,24},{24,32},{32,40},{40,48},{48,56},{56,64},{64,7... | collective-permute-start | bytes 49160 | tf_op jit(solution)/shard_map/ppermute | solution.py:16
  10.7 39.0 %collective-permute-start = (bf16[64,1,128]{2,0,1:T(8,128)(2,1)}, bf16[64,1,128]{2,0,1:T(8,128)(2,1)}, u32[]{:S(2)}, u32[]{:S(2)}) collective-permute-start(bf16[64,1,128]{2,0,1:T(8,128)(2,1)} %slice_bitcast_fusion), channel_id=1, source_target_pairs={{0,8},{8,16},{16,24},{24,32},{32,40},{40,48},{48,56},{56,64},{64,7... | collective-permute-start | bytes 49160 | tf_op jit(solution)/shard_map/ppermute | solution.py:16
  21.2 2.0 %copy-start.12 = (f32[512,64]{1,0:T(8,128)S(1)}, f32[512,64]{1,0:T(8,128)}, u32[]{:S(2)}) copy-start(f32[512,64]{1,0:T(8,128)} %copy.40) | copy-start | bytes 393220
  25.9 3.3 %copy-start.1 = (bf16[512,8,64]{2,0,1:T(8,128)(2,1)}, bf16[512,8,64]{2,0,1:T(8,128)(2,1)S(1)}, u32[]{:S(2)}) copy-start(bf16[512,8,64]{2,0,1:T(8,128)(2,1)S(1)} %get-tuple-element.14) | copy-start | bytes 1572868
  29.3 3.9 %copy-start.6 = (bf16[512,1,64]{0,2,1:T(8,128)(2,1)S(1)}, bf16[512,1,64]{0,2,1:T(8,128)(2,1)}, u32[]{:S(2)}) copy-start(bf16[512,1,64]{0,2,1:T(8,128)(2,1)} %copy-done.5) | copy-start | bytes 196612
  29.3 3.9 %copy-start.9 = (bf16[512,1,64]{0,2,1:T(8,128)(2,1)S(1)}, bf16[512,1,64]{0,2,1:T(8,128)(2,1)}, u32[]{:S(2)}) copy-start(bf16[512,1,64]{0,2,1:T(8,128)(2,1)} %copy-done.8) | copy-start | bytes 196612
  29.3 3.9 %copy-start.15 = (bf16[8,128,64]{1,2,0:T(8,128)(2,1)S(1)}, bf16[8,128,64]{1,2,0:T(8,128)(2,1)}, u32[]{:S(2)}) copy-start(bf16[8,128,64]{1,2,0:T(8,128)(2,1)} %param.15) | copy-start | bytes 393220
  33.1 4.6 %copy-start.16 = (pred[576]{0:T(1024)(128)(4,1)}, pred[576]{0:T(1024)(128)(4,1)S(1)}, u32[]{:S(2)}) copy-start(pred[576]{0:T(1024)(128)(4,1)S(1)} %fusion.84) | copy-start | bytes 1732
  42.6 3.1 %slice-start = ((pred[576]{0:T(1024)(128)(4,1)}), pred[512]{0:T(512)(128)(4,1)S(1)}, s32[]{:S(2)}) async-start(pred[576]{0:T(1024)(128)(4,1)} %copy-done.16), calls=%async_computation.1 | async-start | bytes 1024 | tf_op jit(solution)/shard_map/slice | solution.py:92
  45.8 4.0 %copy-start.18 = (bf16[512,128]{1,0:T(8,128)(2,1)S(1)}, bf16[512,128]{1,0:T(8,128)(2,1)}, u32[]{:S(2)}) copy-start(bf16[512,128]{1,0:T(8,128)(2,1)} %param.12) | copy-start | bytes 393220
  45.8 9.4 %copy-start.17 = (pred[576]{0:T(1024)(128)(4,1)S(1)}, pred[576]{0:T(1024)(128)(4,1)}, u32[]{:S(2)}) copy-start(pred[576]{0:T(1024)(128)(4,1)} %copy-done.16) | copy-start | bytes 1732
  49.8 18.6 %copy-start.2 = (bf16[512,8,64]{2,0,1:T(8,128)(2,1)S(1)}, bf16[512,8,64]{2,0,1:T(8,128)(2,1)}, u32[]{:S(2)}) copy-start(bf16[512,8,64]{2,0,1:T(8,128)(2,1)} %copy-done.1) | copy-start | bytes 1572868
  49.8 18.6 %copy-start.7 = (bf16[512,1,64]{0,2,1:T(8,128)(2,1)S(1)}, bf16[512,1,64]{0,2,1:T(8,128)(2,1)}, u32[]{:S(2)}) copy-start(bf16[512,1,64]{0,2,1:T(8,128)(2,1)} %copy-done.5) | copy-start | bytes 196612
  49.8 18.6 %copy-start.10 = (bf16[512,1,64]{0,2,1:T(8,128)(2,1)S(1)}, bf16[512,1,64]{0,2,1:T(8,128)(2,1)}, u32[]{:S(2)}) copy-start(bf16[512,1,64]{0,2,1:T(8,128)(2,1)} %copy-done.8) | copy-start | bytes 196612
  51.1 11.6 %collective-permute-start.2 = (f32[66048]{0:T(1024)S(1)}, f32[66048]{0:T(1024)S(1)}, u32[]{:S(2)}, u32[]{:S(2)}) collective-permute-start(f32[66048]{0:T(1024)S(1)} %slice.72), channel_id=1, source_target_pairs={{0,8},{8,16},{16,24},{24,32},{32,40},{40,48},{48,56},{56,64},{64,7... | collective-permute-start | bytes 792584 | tf_op jit(solution)/shard_map/ppermute | solution.py:16
  55.5 56.2 %copy-start.13 = (pred[512,576]{0,1:T(8,128)(4,1)}, pred[512,576]{0,1:T(8,128)(4,1)S(1)}, u32[]{:S(2)}) copy-start(pred[512,576]{0,1:T(8,128)(4,1)S(1)} %get-tuple-element.28) | copy-start | bytes 884740
  62.8 8.9 %collective-permute-start.7 = (f32[66048]{0:T(1024)S(1)}, f32[66048]{0:T(1024)S(1)}, u32[]{:S(2)}, u32[]{:S(2)}) collective-permute-start(f32[66048]{0:T(1024)S(1)} %get-tuple-element.20), channel_id=1, source_target_pairs={{0,64},{8,72},{16,80},{24,88},{32,96},{40,104},{48,112},{56,120},{... | collective-permute-start | bytes 792584 | tf_op jit(solution)/shard_map/ppermute | solution.py:16
  64.1 17.4 %collective-permute-start.3 = (f32[66048]{0:T(1024)S(1)}, f32[66048]{0:T(1024)S(1)}, u32[]{:S(2)}, u32[]{:S(2)}) collective-permute-start(f32[66048]{0:T(1024)S(1)} %get-tuple-element.19), channel_id=1, source_target_pairs={{0,16},{8,24},{16,32},{24,40},{32,48},{40,56},{48,64},{56,72},{64,... | collective-permute-start | bytes 792584 | tf_op jit(solution)/shard_map/ppermute | solution.py:16
  71.7 16.7 %collective-permute-start.8 = (f32[66048]{0:T(1024)S(1)}, f32[66048]{0:T(1024)S(1)}, u32[]{:S(2)}, u32[]{:S(2)}) collective-permute-start(f32[66048]{0:T(1024)S(1)} %add.210), channel_id=1, source_target_pairs={{0,128},{8,136},{16,144},{24,152},{32,160},{40,168},{48,176},{56,1... | collective-permute-start | bytes 792584 | tf_op jit(solution)/shard_map/ppermute | solution.py:16
  81.5 18.9 %collective-permute-start.4 = (f32[66048]{0:T(1024)S(1)}, f32[66048]{0:T(1024)S(1)}, u32[]{:S(2)}, u32[]{:S(2)}) collective-permute-start(f32[66048]{0:T(1024)S(1)} %add.204), channel_id=1, source_target_pairs={{0,32},{8,40},{16,48},{24,56},{32,64},{40,72},{48,80},{56,88},{64,... | collective-permute-start | bytes 792584 | tf_op jit(solution)/shard_map/ppermute | solution.py:16
  88.4 19.7 %collective-permute-start.9 = (f32[66048]{0:T(1024)S(1)}, f32[66048]{0:T(1024)S(1)}, u32[]{:S(2)}, u32[]{:S(2)}) collective-permute-start(f32[66048]{0:T(1024)S(1)} %add.212), channel_id=1, source_target_pairs={{0,8},{8,16},{16,24},{24,32},{32,40},{40,48},{48,56},{56,64},{64,7... | collective-permute-start | bytes 792584 | tf_op jit(solution)/shard_map/ppermute | solution.py:16
  100.5 9.9 %collective-permute-start.5 = (f32[66048]{0:T(1024)S(1)}, f32[66048]{0:T(1024)S(1)}, u32[]{:S(2)}, u32[]{:S(2)}) collective-permute-start(f32[66048]{0:T(1024)S(1)} %add.206), channel_id=1, source_target_pairs={{0,64},{8,72},{16,80},{24,88},{32,96},{40,104},{48,112},{56,120},{... | collective-permute-start | bytes 792584 | tf_op jit(solution)/shard_map/ppermute | solution.py:16
  106.0 5.7 %copy-start.3 = (bf16[512,8,64]{0,2,1:T(8,128)(2,1)S(1)}, bf16[512,8,64]{0,2,1:T(8,128)(2,1)}, u32[]{:S(2)}) copy-start(bf16[512,8,64]{0,2,1:T(8,128)(2,1)} %get-tuple-element.38) | copy-start | bytes 1572868
  106.0 5.7 %copy-start.4 = (bf16[512,8,64]{0,2,1:T(8,128)(2,1)S(1)}, bf16[512,8,64]{0,2,1:T(8,128)(2,1)}, u32[]{:S(2)}) copy-start(bf16[512,8,64]{0,2,1:T(8,128)(2,1)} %get-tuple-element.39) | copy-start | bytes 1572868
  108.2 18.5 %collective-permute-start.10 = (f32[66048]{0:T(1024)S(1)}, f32[66048]{0:T(1024)S(1)}, u32[]{:S(2)}, u32[]{:S(2)}) collective-permute-start(f32[66048]{0:T(1024)S(1)} %add.214), channel_id=1, source_target_pairs={{0,16},{8,24},{16,32},{24,40},{32,48},{40,56},{48,64},{56,72},{64,... | collective-permute-start | bytes 792584 | tf_op jit(solution)/shard_map/ppermute | solution.py:16
  110.4 18.5 %collective-permute-start.6 = (f32[66048]{0:T(1024)S(1)}, f32[66048]{0:T(1024)S(1)}, u32[]{:S(2)}, u32[]{:S(2)}) collective-permute-start(f32[66048]{0:T(1024)S(1)} %add.208), channel_id=1, source_target_pairs={{0,128},{8,136},{16,144},{24,152},{32,160},{40,168},{48,176},{56,1... | collective-permute-start | bytes 792584 | tf_op jit(solution)/shard_map/ppermute | solution.py:16
  126.7 18.2 %collective-permute-start.11 = (f32[66048]{0:T(1024)S(1)}, f32[66048]{0:T(1024)S(1)}, u32[]{:S(2)}, u32[]{:S(2)}) collective-permute-start(f32[66048]{0:T(1024)S(1)} %add.216), channel_id=1, source_target_pairs={{0,32},{8,40},{16,48},{24,56},{32,64},{40,72},{48,80},{56,88},{64,... | collective-permute-start | bytes 792584 | tf_op jit(solution)/shard_map/ppermute | solution.py:16
  146.2 0.7 copy-start.20
  146.2 0.7 copy-start.21
  146.2 1.0 copy-start.14
  146.2 1.0 copy-start.19
  146.2 1.8 %copy-start.22 = (f32[128,8,512]{2,0,1:T(8,128)S(1)}, f32[128,8,512]{2,0,1:T(8,128)}, u32[]{:S(2)}) copy-start(f32[128,8,512]{2,0,1:T(8,128)} %fusion.10) | copy-start | bytes 6291460

commit v3 on v2

--- a/solution.py
+++ b/solution.py
@@ -65,9 +65,6 @@
     extent = BLOCK + WINDOW
     positions = (offsets[:, None] + jnp.arange(SPAN, dtype=jnp.int32)[None, :]).reshape(tokens)
     cosine, sine = angle_tables(positions, head_dim // 2)
-    rot_q = rotate(
-        queries.reshape(tokens, heads, head_dim).astype(jnp.float32), cosine, sine
-    ).astype(jnp.bfloat16)
     rot_k = rotate(
         keys.reshape(tokens, kv_local, head_dim).astype(jnp.float32), cosine, sine
     ).astype(jnp.bfloat16)
@@ -78,10 +75,6 @@
     ext_keys = jnp.concatenate([tail_keys, rot_k], axis=0)
     ext_values = jnp.concatenate([tail_values, value_rows], axis=0)
     valid = (jnp.arange(tokens + WINDOW) >= WINDOW) | (lax.axis_index("seq") > 0)
-    query_logits = jnp.einsum("nhd,hdf->nhf", rot_q, query_map, preferred_element_type=jnp.float32)
-    phi_query = (
-        two_softmax(query_logits).astype(jnp.bfloat16).reshape(tokens, kv_local, group, 2 * feat)
-    )
     grouped_map = key_map.reshape(kv_local, group, head_dim, feat)
     key_logits = jnp.einsum(
         "ngd,gkdf->ngkf", ext_keys, grouped_map, preferred_element_type=jnp.float32
@@ -121,11 +114,21 @@
         exclusive = jnp.zeros_like(piece)
         for place, shift in enumerate(order):
             received = passed_along(inclusive, "seq", shift)
+            if not pieces and place == 0:
+                first_received = received
             exclusive = exclusive + received
             if place + 1 < len(order):
                 inclusive = inclusive + received
         pieces.append(exclusive)
     exclusive = jnp.concatenate(pieces)
+    queries, first_received = lax.optimization_barrier((queries, first_received))
+    rot_q = rotate(
+        queries.reshape(tokens, heads, head_dim).astype(jnp.float32), cosine, sine
+    ).astype(jnp.bfloat16)
+    query_logits = jnp.einsum("nhd,hdf->nhf", rot_q, query_map, preferred_element_type=jnp.float32)
+    phi_query = (
+        two_softmax(query_logits).astype(jnp.bfloat16).reshape(tokens, kv_local, group, 2 * feat)
+    )
     prior_state = exclusive[:state_size].reshape(state_shape)
     prior_norm = exclusive[state_size:].reshape(total_norm.shape)
     factor = jax.nn.sigmoid(window_logit).reshape(kv_local, group)

time: 175 us -> 165 us (0.943)
  the two profiles are of different devices: /device:TPU:6 before, /device:TPU:2 now
where the time goes in v3:
time: 165 us; the launch traced here: 164 us
  starting transfers between devices  39.7 us (24%)
  other arithmetic  35.6 us (22%)
  waiting for transfers between devices  32.2 us (20%)
  matrix products  20.6 us (12%)
  blocking collectives  20.3 us (12%)
  local copies, waits for them, and re-layouts  15.1 us (9%)
    ppermute x12, starting transfers between devices, passed_along(): lax.ppermute(value, axis, [(source, source + steps) for source in range(f...  39.7 us
    ppermute x12, waiting for transfers between devices, passed_along(): lax.ppermute(value, axis, [(source, source + steps) for source in range(f...  32.2 us
    all_to_all x1, blocking collectives, body(): lax.all_to_all(result, 'head', split_axis=0, concat_axis=1, tiled=True)  20.3 us
    unnamed x72, local copies, waits for them, and re-layouts  7.08 us
    another operation x3, other arithmetic  6.37 us
    convert_element_type x1, other arithmetic, body(): jnp.where(valid[:, None, None, None], two_softmax(key_logits), 0.0)  4.3 us
    reduce_sum x1, other arithmetic, body(): block_norms = jnp.sum(lag_phi, axis=1, dtype=jnp.float32)  3.97 us
    add x8, other arithmetic, body(): inclusive = inclusive + received  3.93 us
  transfers between devices with their start and end apart: 12, of which 6 were waited for; matrix products, arithmetic and copies ran while one was open for 31% of the time, Pallas kernels for 0%

profile of v3, /device:TPU:2, one launch (start us, length us, event | category | flops | bytes accessed | tf_op | source)
XLA Modules:
  0.0 164.3 jit_solution(4703808684866071236)
XLA Ops:
  0.0 0.8 add_bitcast_fusion
  0.8 1.0 copy.37
  1.8 2.4 %subtract_convert_fusion.3 = (bf16[512,1,64]{0,2,1:T(8,128)(2,1)S(1)}, bf16[512,1,64]{0,2,1:T(8,128)(2,1)S(1)}) fusion(f32[512,1,128]{0,2,1:T(8,128)S(1)} %bitcast_convert_fusion, f32[64]{0:T(128)} %constant.76.clone, f32[512]{0:T(512)S(1)} %get-tuple-element.29, f32[64]{0:T(128)} %constant.75.clone, f32[512]{0:T(512)S(1)} %get-tuple-element.28, ...), kind=kLoop, calls=%fused_computation.120 | loop fusion | flops 753664 | bytes 400128 | tf_op jit(solution)/shard_map/convert.6
  4.3 3.8 %collective-permute-start.1 = (bf16[64,1,128]{0,2,1:T(8,128)(2,1)S(1)}, bf16[64,1,128]{0,2,1:T(8,128)(2,1)S(1)}, u32[]{:S(2)}, u32[]{:S(2)}) collective-permute-start(bf16[64,1,128]{0,2,1:T(8,128)(2,1)S(1)} %pad_maximum_fusion.14), channel_id=1, source_target_pairs={{0,8},{8,16},{16,24},{24,32},{32,40},{40,48},{48,56},{56,64},{64,7... | collective-permute-start | bytes 49160 | tf_op jit(solution)/shard_map/ppermute | solution.py:16
  8.1 0.7 slice_bitcast_fusion
  8.8 3.8 %collective-permute-start = (bf16[64,1,128]{2,0,1:T(8,128)(2,1)S(1)}, bf16[64,1,128]{2,0,1:T(8,128)(2,1)S(1)}, u32[]{:S(2)}, u32[]{:S(2)}) collective-permute-start(bf16[64,1,128]{2,0,1:T(8,128)(2,1)S(1)} %slice_bitcast_fusion), channel_id=1, source_target_pairs={{0,8},{8,16},{16,24},{24,32},{32,40},{40,48},{48,56},{56,64},{64,7... | collective-permute-start | bytes 49160 | tf_op jit(solution)/shard_map/ppermute | solution.py:16
  12.7 1.2 fusion.33
  13.9 2.2 %fusion.64 = (f32[512,64]{0,1:T(8,128)S(1)}, f32[512,64]{0,1:T(8,128)S(1)}) fusion(f32[64]{0:T(128)} %constant.76.clone, f32[512]{0:T(512)S(1)} %get-tuple-element.29, f32[64]{0:T(128)} %constant.75.clone, f32[512]{0:T(512)S(1)} %get-tuple-element.28, f32[64]{0:T(128)} %constant.74.clone, f32[512]{0:T(512)S(1)} %get-tuple-element.27), kind=kLoop, calls=%fused_computation.107 | loop fusion | flops 491520 | bytes 269056 | tf_op jit(solution)/shard_map/sub | solution.py:29
  16.1 1.5 fusion.58
  17.6 2.3 %copy.39 = f32[576,8,64]{2,1,0:T(8,128)S(1)} copy(f32[576,8,64]{0,2,1:T(8,128)} %bitcast.171) | data formatting | bytes 2359296 | tf_op jit(solution)/shard_map/ngd,gkdf->ngkf/dot_general | solution.py:79
  19.9 1.3 bitcast_reduce_fusion
  21.2 3.6 %fusion.25 = (f32[576,8]{1,0:T(8,128)S(1)}, f32[576,8]{1,0:T(8,128)S(1)}) fusion(f32[576,8,64]{2,1,0:T(8,128)S(1)} %copy.39, f32[576,8]{1,0:T(8,128)S(1)} %get-tuple-element.9, f32[576,8]{1,0:T(8,128)S(1)} %get-tuple-element.10), kind=kLoop, calls=%fused_computation.39 | loop fusion | flops 1465344 | bytes 1253376 | tf_op jit(solution)/shard_map/reduce_sum | solution.py:47
  24.8 3.1 %fusion.24 = (bf16[576,1,8,64]{3,2,0,1:T(8,128)(2,1)S(1)}, bf16[576,1,8,64]{3,2,0,1:T(8,128)(2,1)S(1)}) fusion(f32[576,8,64]{2,1,0:T(8,128)S(1)} %copy.39, f32[576,8]{1,0:T(8,128)S(1)} %get-tuple-element.7, f32[576,8]{1,0:T(8,128)S(1)} %get-tuple-element.9, f32[576,8]{1,0:T(8,128)S(1)} %get-tuple-element.8, f32[576,8]{1,0:T(8,128)S(1)} %get-tuple-element.10), kind=kLoop, calls=%fused_computation.38 | loop fusion | flops 2064384 | bytes 2433024 | tf_op jit(solution)/shard_map/div | solution.py:47
  28.0 4.0 %convert_reduce_fusion = (f32[8,128]{1,0:T(8,128)S(1)}, bf16[512,1,8,128]{3,2,0,1:T(8,128)(2,1)S(1)}) fusion(bf16[576,1,8,64]{3,2,0,1:T(8,128)(2,1)S(1)} %get-tuple-element.18, bf16[576,1,8,64]{3,2,0,1:T(8,128)(2,1)S(1)} %get-tuple-element.17, pred[512]{0:T(512)(128)(4,1)S(1)} %slice-done), kind=kLoop, calls=%fused_computation.32 | loop fusion | flops 3668992 | bytes 2232832 | tf_op jit(solution)/shard_map/reduce_sum | solution.py:90
  32.0 0.5 fusion.36
  32.6 0.8 copy-done.5
  33.4 4.0 %collective-permute-start.2 = (f32[66048]{0:T(1024)S(1)}, f32[66048]{0:T(1024)S(1)}, u32[]{:S(2)}, u32[]{:S(2)}) collective-permute-start(f32[66048]{0:T(1024)S(1)} %slice.70), channel_id=1, source_target_pairs={{0,8},{8,16},{16,24},{24,32},{32,40},{40,48},{48,56},{56,64},{64,7... | collective-permute-start | bytes 792584 | tf_op jit(solution)/shard_map/ppermute | solution.py:16
  37.4 0.8 copy.43
  38.2 0.9 copy.45
  39.1 4.3 %fusion.14 = bf16[576,8,128]{2,1,0:T(8,128)(2,1)} fusion(bf16[576,8,64]{2,1,0:T(8,128)(2,1)} %bitcast.169, bf16[576,8,64]{2,1,0:T(8,128)(2,1)S(1)} %bitcast.168, pred[576]{0:T(1024)(128)(4,1)S(1)} %copy-done.25), kind=kLoop, calls=%fused_computation.18 | loop fusion | flops 2949120 | bytes 2359872 | tf_op jit(solution)/shard_map/convert_element_type | solution.py:82
  43.4 1.7 %collective-permute-done.2 = f32[66048]{0:T(1024)S(1)} collective-permute-done((f32[66048]{0:T(1024)S(1)}, f32[66048]{0:T(1024)S(1)}, u32[]{:S(2)}, u32[]{:S(2)}) %collective-permute-start.2) | collective-permute-done | bytes 264224 | tf_op jit(solution)/shard_map/ppermute | solution.py:16
  45.1 0.5 copy.41
  45.6 0.3 fusion.107
  45.9 1.9 %copy.65 = f32[512,8,64]{2,0,1:T(8,128)} copy(f32[512,8,64]{0,2,1:T(8,128)S(1)} %get-tuple-element.20) | data formatting | bytes 2097152
  47.9 1.9 %copy.66 = f32[512,8,64]{2,0,1:T(8,128)} copy(f32[512,8,64]{0,2,1:T(8,128)S(1)} %get-tuple-element.19) | data formatting | bytes 2097152
  49.9 3.4 %collective-permute-start.7 = (f32[66048]{0:T(1024)S(1)}, f32[66048]{0:T(1024)S(1)}, u32[]{:S(2)}, u32[]{:S(2)}) collective-permute-start(f32[66048]{0:T(1024)S(1)} %get-tuple-element.22), channel_id=1, source_target_pairs={{0,64},{8,72},{16,80},{24,88},{32,96},{40,104},{48,112},{56,120},{... | collective-permute-start | bytes 792584 | tf_op jit(solution)/shard_map/ppermute | solution.py:16
  53.3 4.6 %collective-permute-start.3 = (f32[66048]{0:T(1024)S(1)}, f32[66048]{0:T(1024)S(1)}, u32[]{:S(2)}, u32[]{:S(2)}) collective-permute-start(f32[66048]{0:T(1024)S(1)} %get-tuple-element.21), channel_id=1, source_target_pairs={{0,16},{8,24},{16,32},{24,40},{32,48},{40,56},{48,64},{56,72},{64,... | collective-permute-start | bytes 792584 | tf_op jit(solution)/shard_map/ppermute | solution.py:16
  57.9 2.9 %subtract_convert_fusion = (bf16[512,8,64]{2,0,1:T(8,128)(2,1)S(1)}, bf16[512,8,64]{2,0,1:T(8,128)(2,1)S(1)}) fusion(f32[512,8,64]{2,0,1:T(8,128)} %copy.66, f32[512,8,64]{2,0,1:T(8,128)} %copy.65, f32[512,64]{1,0:T(8,128)} %copy.45, f32[512,64]{1,0:T(8,128)} %copy.43), kind=kLoop, calls=%fused_computation.34 | loop fusion | flops 2097152 | bytes 3407872 | tf_op jit(solution)/shard_map/convert.4
  60.8 2.6 %fusion.2 = (f32[8,512]{1,0:T(8,128)S(1)}, f32[576,512,8]{1,0,2:T(8,128)S(1)}) fusion(pred[512,576]{0,1:T(8,128)(4,1)S(1)} %copy-done.4, bf16[512,8,64]{2,0,1:T(8,128)(2,1)S(1)} %get-tuple-element.16, bf16[512,8,64]{2,0,1:T(8,128)(2,1)S(1)} %get-tuple-element.15, bf16[512,1,64]{0,2,1:T(8,128)(2,1)S(1)} %copy-done.15, bf16[512,1,64]{0,2,1:T(8,128)(2,1)S(1)} %copy-done.13, ...), kind=kOutput, calls=%fused_computation.4 | convolution fusion | flops 613593088 | bytes 10944512 | tf_op jit(solution)/shard_map/igkd,jgd->gkij/dot_general | solution.py:141
  63.4 2.5 %fusion.5 = f32[8,512]{1,0:T(8,128)} fusion(f32[576,512,8]{1,0,2:T(8,128)S(1)} %get-tuple-element.37, f32[8,512]{1,0:T(8,128)S(1)} %get-tuple-element.36, pred[512,576]{0,1:T(8,128)(4,1)S(1)} %copy-done.4), kind=kLoop, calls=%fused_computation.9 | loop fusion | flops 9433088 | bytes 9764864 | tf_op jit(solution)/shard_map/reduce_sum | solution.py:147
  66.0 3.5 %fusion.10 = f32[128,8,512]{2,0,1:T(8,128)} fusion(f32[576,512,8]{1,0,2:T(8,128)S(1)} %get-tuple-element.37, f32[8,512]{1,0:T(8,128)S(1)} %get-tuple-element.36, pred[512,576]{0,1:T(8,128)(4,1)S(1)} %copy-done.4, bf16[64,1,128]{2,0,1:T(8,128)(2,1)S(1)} %copy-done.30, bf16[512,1,128]{2,0,1:T(8,128)(2,1)S(1)} %bitcast.181), kind=kOutput, calls=%fused_computation.14 | convolution fusion | flops 613711872 | bytes 11993088 | tf_op jit(solution)/shard_map/gkij,jgd->igkd/dot_general | solution.py:151
  69.5 0.8 add.210
  70.3 2.7 %collective-permute-start.8 = (f32[66048]{0:T(1024)}, f32[66048]{0:T(1024)}, u32[]{:S(2)}, u32[]{:S(2)}) collective-permute-start(f32[66048]{0:T(1024)} %add.210), channel_id=1, source_target_pairs={{0,128},{8,136},{16,144},{24,152},{32,160},{40,168},{48,176},{56,1... | collective-permute-start | bytes 792584 | tf_op jit(solution)/shard_map/ppermute | solution.py:16
  72.9 0.8 add.204
  73.7 4.0 %collective-permute-start.4 = (f32[66048]{0:T(1024)}, f32[66048]{0:T(1024)}, u32[]{:S(2)}, u32[]{:S(2)}) collective-permute-start(f32[66048]{0:T(1024)} %add.204), channel_id=1, source_target_pairs={{0,32},{8,40},{16,48},{24,56},{32,64},{40,72},{48,80},{56,88},{64,... | collective-permute-start | bytes 792584 | tf_op jit(solution)/shard_map/ppermute | solution.py:16
  77.8 1.5 fusion.109
  79.2 2.5 %fusion.108 = (f32[512,8]{0,1:T(8,128)}, f32[512,8,64]{0,2,1:T(8,128)}) fusion(bf16[8,128,64]{1,2,0:T(8,128)(2,1)S(1)} %copy-done, bf16[512,8,64]{2,0,1:T(8,128)(2,1)S(1)} %get-tuple-element.16, bf16[512,8,64]{2,0,1:T(8,128)(2,1)S(1)} %get-tuple-element.15), kind=kOutput, calls=%fused_computation.175 | convolution fusion | flops 69992512 | bytes 2244608 | tf_op jit(solution)/shard_map/sub | solution.py:47
  81.7 1.1 add.212
  82.8 1.9 %collective-permute-start.9 = (f32[66048]{0:T(1024)S(1)}, f32[66048]{0:T(1024)S(1)}, u32[]{:S(2)}, u32[]{:S(2)}) collective-permute-start(f32[66048]{0:T(1024)S(1)} %add.212), channel_id=1, source_target_pairs={{0,8},{8,16},{16,24},{24,32},{32,40},{40,48},{48,56},{56,64},{64,7... | collective-permute-start | bytes 792584 | tf_op jit(solution)/shard_map/ppermute | solution.py:16
  84.7 6.5 %collective-permute-done.4 = f32[66048]{0:T(1024)} collective-permute-done((f32[66048]{0:T(1024)}, f32[66048]{0:T(1024)}, u32[]{:S(2)}, u32[]{:S(2)}) %collective-permute-start.4) | collective-permute-done | bytes 264224 | tf_op jit(solution)/shard_map/ppermute | solution.py:16
  91.3 1.1 add.206
  92.3 1.9 %collective-permute-start.5 = (f32[66048]{0:T(1024)S(1)}, f32[66048]{0:T(1024)S(1)}, u32[]{:S(2)}, u32[]{:S(2)}) collective-permute-start(f32[66048]{0:T(1024)S(1)} %add.206), channel_id=1, source_target_pairs={{0,64},{8,72},{16,80},{24,88},{32,96},{40,104},{48,112},{56,120},{... | collective-permute-start | bytes 792584 | tf_op jit(solution)/shard_map/ppermute | solution.py:16
  94.3 1.1 divide_convert_fusion
  95.4 2.9 %collective-permute-done.9 = f32[66048]{0:T(1024)S(1)} collective-permute-done((f32[66048]{0:T(1024)S(1)}, f32[66048]{0:T(1024)S(1)}, u32[]{:S(2)}, u32[]{:S(2)}) %collective-permute-start.9) | collective-permute-done | bytes 264224 | tf_op jit(solution)/shard_map/ppermute | solution.py:16
  98.4 4.3 %collective-permute-start.10 = (f32[66048]{0:T(1024)S(1)}, f32[66048]{0:T(1024)S(1)}, u32[]{:S(2)}, u32[]{:S(2)}) collective-permute-start(f32[66048]{0:T(1024)S(1)} %add.214), channel_id=1, source_target_pairs={{0,16},{8,24},{16,32},{24,40},{32,48},{40,56},{48,64},{56,72},{64,... | collective-permute-start | bytes 792584 | tf_op jit(solution)/shard_map/ppermute | solution.py:16
  102.7 0.4 collective-permute-done.5
  103.2 1.7 %collective-permute-start.6 = (f32[66048]{0:T(1024)S(1)}, f32[66048]{0:T(1024)S(1)}, u32[]{:S(2)}, u32[]{:S(2)}) collective-permute-start(f32[66048]{0:T(1024)S(1)} %add.208), channel_id=1, source_target_pairs={{0,128},{8,136},{16,144},{24,152},{32,160},{40,168},{48,176},{56,1... | collective-permute-start | bytes 792584 | tf_op jit(solution)/shard_map/ppermute | solution.py:16
  105.0 3.6 %select_reduce_fusion = (f32[8,512]{1,0:T(8,128)S(1)}, bf16[8,512,576]{1,2,0:T(8,128)(2,1)}) fusion(pred[512,576]{0,1:T(8,128)(4,1)S(1)} %copy-done.18, bf16[512,8,64]{0,2,1:T(8,128)(2,1)S(1)} %get-tuple-element.40, bf16[512,8,64]{0,2,1:T(8,128)(2,1)S(1)} %get-tuple-element.41, bf16[576,8,128]{2,1,0:T(8,128)(2,1)S(1)} %copy-done.7), kind=kOutput, calls=%fused_computation.7 | convolution fusion | flops 613150720 | bytes 7258112 | tf_op jit(solution)/shard_map/igkf,jgkf->gkij/dot_general | solution.py:148
  108.6 6.1 %collective-permute-done.10 = f32[66048]{0:T(1024)S(1)} collective-permute-done((f32[66048]{0:T(1024)S(1)}, f32[66048]{0:T(1024)S(1)}, u32[]{:S(2)}, u32[]{:S(2)}) %collective-permute-start.10) | collective-permute-done | bytes 264224 | tf_op jit(solution)/shard_map/ppermute | solution.py:16
  114.8 3.6 %collective-permute-start.11 = (f32[66048]{0:T(1024)S(1)}, f32[66048]{0:T(1024)S(1)}, u32[]{:S(2)}, u32[]{:S(2)}) collective-permute-start(f32[66048]{0:T(1024)S(1)} %add.216), channel_id=1, source_target_pairs={{0,32},{8,40},{16,48},{24,56},{32,64},{40,72},{48,80},{56,88},{64,... | collective-permute-start | bytes 792584 | tf_op jit(solution)/shard_map/ppermute | solution.py:16
  118.4 1.0 add_add_fusion.1
  119.4 14.5 %collective-permute-done.11 = f32[66048]{0:T(1024)S(1)} collective-permute-done((f32[66048]{0:T(1024)S(1)}, f32[66048]{0:T(1024)S(1)}, u32[]{:S(2)}, u32[]{:S(2)}) %collective-permute-start.11) | collective-permute-done | bytes 264224 | tf_op jit(solution)/shard_map/ppermute | solution.py:16
  133.9 1.1 add_add_fusion
  135.1 0.2 copy.49
  135.3 0.4 fusion.39
  135.7 0.4 fusion.73
  136.2 0.2 fusion.82
  136.4 0.2 fusion.80
  137.2 0.8 copy-done.33
  138.0 3.7 %fusion.21 = bf16[512,1,8,128]{0,3,2,1:T(8,128)(2,1)S(1)} fusion(f32[8,128,512]{2,1,0:T(8,128)S(1)} %fusion.73, f32[8,128,512]{2,1,0:T(8,128)S(1)} %fusion.39, f32[128,8,512]{2,0,1:T(8,128)S(1)} %copy-done.33, bf16[8,512,576]{1,2,0:T(8,128)(2,1)} %get-tuple-element.39, pred[512,576]{0,1:T(8,128)(4,1)S(1)} %copy-done.19, f32[512,8]{0,1:T(8,128)S(1)} %fusion.78, ...), kind=kOutput, calls=%fused_computation.35 | convolution fusion | flops 610304000 | bytes 12517440 | tf_op jit(solution)/shard_map/gkij,jgd->igkd/dot_general | solution.py:157
  141.7 0.8 copy.53
  142.4 0.5 all_to_all.14
  142.9 20.3 %all_to_all.19 = bf16[8,64,1024]{2,1,0:T(8,128)(2,1)S(1)} all-to-all(bf16[8,64,1024]{2,1,0:T(8,128)(2,1)S(1)} %all_to_all.14), channel_id=1, replica_groups=mesh['seq'=32,'head'=8] {'head'}, dimensions={0} | all-to-all | bytes 2097152 | tf_op jit(solution)/shard_map/all_to_all | solution.py:184
  163.2 1.1 copy.67
  (90 shorter events, 1.1 us)
Async XLA Ops:
  0.0 77.7 %copy-start = (bf16[8,128,64]{1,2,0:T(8,128)(2,1)S(1)}, bf16[8,128,64]{1,2,0:T(8,128)(2,1)}, u32[]{:S(2)}) copy-start(bf16[8,128,64]{1,2,0:T(8,128)(2,1)} %param.14) | copy-start | bytes 393220
  0.0 16.1 %copy-start.22 = (bf16[8,128,64]{1,2,0:T(8,128)(2,1)S(1)}, bf16[8,128,64]{1,2,0:T(8,128)(2,1)}, u32[]{:S(2)}) copy-start(bf16[8,128,64]{1,2,0:T(8,128)(2,1)} %param.15) | copy-start | bytes 393220
  4.2 13.4 %copy-start.12 = (bf16[512,1,64]{0,2,1:T(8,128)(2,1)}, bf16[512,1,64]{0,2,1:T(8,128)(2,1)S(1)}, u32[]{:S(2)}) copy-start(bf16[512,1,64]{0,2,1:T(8,128)(2,1)S(1)} %get-tuple-element.23) | copy-start | bytes 196612
  4.2 13.4 %copy-start.14 = (bf16[512,1,64]{0,2,1:T(8,128)(2,1)}, bf16[512,1,64]{0,2,1:T(8,128)(2,1)S(1)}, u32[]{:S(2)}) copy-start(bf16[512,1,64]{0,2,1:T(8,128)(2,1)S(1)} %get-tuple-element.24) | copy-start | bytes 196612
  4.3 11.8 %collective-permute-start.1 = (bf16[64,1,128]{0,2,1:T(8,128)(2,1)S(1)}, bf16[64,1,128]{0,2,1:T(8,128)(2,1)S(1)}, u32[]{:S(2)}, u32[]{:S(2)}) collective-permute-start(bf16[64,1,128]{0,2,1:T(8,128)(2,1)S(1)} %pad_maximum_fusion.14), channel_id=1, source_target_pairs={{0,8},{8,16},{16,24},{24,32},{32,40},{40,48},{48,56},{56,64},{64,7... | collective-permute-start | bytes 49160 | tf_op jit(solution)/shard_map/ppermute | solution.py:16
  8.8 23.1 %collective-permute-start = (bf16[64,1,128]{2,0,1:T(8,128)(2,1)S(1)}, bf16[64,1,128]{2,0,1:T(8,128)(2,1)S(1)}, u32[]{:S(2)}, u32[]{:S(2)}) collective-permute-start(bf16[64,1,128]{2,0,1:T(8,128)(2,1)S(1)} %slice_bitcast_fusion), channel_id=1, source_target_pairs={{0,8},{8,16},{16,24},{24,32},{32,40},{40,48},{48,56},{56,64},{64,7... | collective-permute-start | bytes 49160 | tf_op jit(solution)/shard_map/ppermute | solution.py:16
  12.7 7.2 %copy-start.24 = (pred[576]{0:T(1024)(128)(4,1)}, pred[576]{0:T(1024)(128)(4,1)S(1)}, u32[]{:S(2)}) copy-start(pred[576]{0:T(1024)(128)(4,1)S(1)} %fusion.84) | copy-start | bytes 1732
  16.1 1.5 copy-start.20
  24.8 3.2 %slice-start = ((pred[576]{0:T(1024)(128)(4,1)}), pred[512]{0:T(512)(128)(4,1)S(1)}, s32[]{:S(2)}) async-start(pred[576]{0:T(1024)(128)(4,1)} %copy-done.24), calls=%async_computation.1 | async-start | bytes 1024 | tf_op jit(solution)/shard_map/slice | solution.py:85
  27.9 4.6 %copy-start.1 = (bf16[576,1,8,64]{3,2,0,1:T(8,128)(2,1)}, bf16[576,1,8,64]{3,2,0,1:T(8,128)(2,1)S(1)}, u32[]{:S(2)}) copy-start(bf16[576,1,8,64]{3,2,0,1:T(8,128)(2,1)S(1)} %get-tuple-element.17) | copy-start | bytes 1769476
  27.9 4.6 %copy-start.3 = (bf16[576,1,8,64]{3,2,0,1:T(8,128)(2,1)}, bf16[576,1,8,64]{3,2,0,1:T(8,128)(2,1)S(1)}, u32[]{:S(2)}) copy-start(bf16[576,1,8,64]{3,2,0,1:T(8,128)(2,1)S(1)} %get-tuple-element.18) | copy-start | bytes 1769476
  27.9 4.0 %copy-start.26 = (bf16[512,128]{1,0:T(8,128)(2,1)S(1)}, bf16[512,128]{1,0:T(8,128)(2,1)}, u32[]{:S(2)}) copy-start(bf16[512,128]{1,0:T(8,128)(2,1)} %param.12) | copy-start | bytes 393220
  28.0 9.4 %copy-start.32 = (f32[8]{0:T(128)S(1)}, f32[8]{0:T(128)}, u32[]{:S(2)}) copy-start(f32[8]{0:T(128)} %param.16) | copy-start | bytes 100
  32.0 7.1 %copy-start.25 = (pred[576]{0:T(1024)(128)(4,1)S(1)}, pred[576]{0:T(1024)(128)(4,1)}, u32[]{:S(2)}) copy-start(pred[576]{0:T(1024)(128)(4,1)} %copy-done.24) | copy-start | bytes 1732
  32.0 0.6 copy-start.29
  32.6 0.8 copy-start.5
  33.4 5.7 %copy-start.2 = (bf16[576,1,8,64]{3,2,0,1:T(8,128)(2,1)S(1)}, bf16[576,1,8,64]{3,2,0,1:T(8,128)(2,1)}, u32[]{:S(2)}) copy-start(bf16[576,1,8,64]{3,2,0,1:T(8,128)(2,1)} %copy-done.1) | copy-start | bytes 1769476
  33.4 11.7 %collective-permute-start.2 = (f32[66048]{0:T(1024)S(1)}, f32[66048]{0:T(1024)S(1)}, u32[]{:S(2)}, u32[]{:S(2)}) collective-permute-start(f32[66048]{0:T(1024)S(1)} %slice.70), channel_id=1, source_target_pairs={{0,8},{8,16},{16,24},{24,32},{32,40},{40,48},{48,56},{56,64},{64,7... | collective-permute-start | bytes 792584 | tf_op jit(solution)/shard_map/ppermute | solution.py:16
  37.4 7.7 %copy-start.17 = (bf16[512,1024]{1,0:T(8,128)(2,1)S(1)}, bf16[512,1024]{1,0:T(8,128)(2,1)}, u32[]{:S(2)}) copy-start(bf16[512,1024]{1,0:T(8,128)(2,1)} %param.10) | copy-start | bytes 3145732
  47.8 2.0 %copy-start.6 = (f32[8,128,128]{2,1,0:T(8,128)S(1)}, f32[8,128,128]{2,1,0:T(8,128)}, u32[]{:S(2)}) copy-start(f32[8,128,128]{2,1,0:T(8,128)} %copy-done.5) | copy-start | bytes 1572868
  49.9 19.6 %collective-permute-start.7 = (f32[66048]{0:T(1024)S(1)}, f32[66048]{0:T(1024)S(1)}, u32[]{:S(2)}, u32[]{:S(2)}) collective-permute-start(f32[66048]{0:T(1024)S(1)} %get-tuple-element.22), channel_id=1, source_target_pairs={{0,64},{8,72},{16,80},{24,88},{32,96},{40,104},{48,112},{56,120},{... | collective-permute-start | bytes 792584 | tf_op jit(solution)/shard_map/ppermute | solution.py:16
  53.3 7.5 %copy-start.4 = (pred[512,576]{0,1:T(8,128)(4,1)S(1)}, pred[512,576]{0,1:T(8,128)(4,1)}, u32[]{:S(2)}) copy-start(pred[512,576]{0,1:T(8,128)(4,1)} %get-tuple-element.31) | copy-start | bytes 884740
  53.3 7.5 %copy-start.13 = (bf16[512,1,64]{0,2,1:T(8,128)(2,1)S(1)}, bf16[512,1,64]{0,2,1:T(8,128)(2,1)}, u32[]{:S(2)}) copy-start(bf16[512,1,64]{0,2,1:T(8,128)(2,1)} %copy-done.12) | copy-start | bytes 196612
  53.3 7.5 %copy-start.15 = (bf16[512,1,64]{0,2,1:T(8,128)(2,1)S(1)}, bf16[512,1,64]{0,2,1:T(8,128)(2,1)}, u32[]{:S(2)}) copy-start(bf16[512,1,64]{0,2,1:T(8,128)(2,1)} %copy-done.14) | copy-start | bytes 196612
  53.3 7.5 %copy-start.21 = (bf16[64,1,128]{0,2,1:T(8,128)(2,1)S(1)}, bf16[64,1,128]{0,2,1:T(8,128)(2,1)}, u32[]{:S(2)}) copy-start(bf16[64,1,128]{0,2,1:T(8,128)(2,1)} %copy-done.20) | copy-start | bytes 49156
  53.3 19.6 %collective-permute-start.3 = (f32[66048]{0:T(1024)S(1)}, f32[66048]{0:T(1024)S(1)}, u32[]{:S(2)}, u32[]{:S(2)}) collective-permute-start(f32[66048]{0:T(1024)S(1)} %get-tuple-element.21), channel_id=1, source_target_pairs={{0,16},{8,24},{16,32},{24,40},{32,48},{40,56},{48,64},{56,72},{64,... | collective-permute-start | bytes 792584 | tf_op jit(solution)/shard_map/ppermute | solution.py:16
  63.4 2.6 %copy-start.27 = (bf16[512,128]{1,0:T(8,128)(2,1)S(1)}, bf16[512,128]{1,0:T(8,128)(2,1)}, u32[]{:S(2)}) copy-start(bf16[512,128]{1,0:T(8,128)(2,1)} %param.12) | copy-start | bytes 393220
  63.4 2.5 %copy-start.30 = (bf16[64,1,128]{2,0,1:T(8,128)(2,1)S(1)}, bf16[64,1,128]{2,0,1:T(8,128)(2,1)}, u32[]{:S(2)}) copy-start(bf16[64,1,128]{2,0,1:T(8,128)(2,1)} %copy-done.29) | copy-start | bytes 49156
  69.5 4.2 %copy-start.8 = (f32[66048]{0:T(1024)}, f32[66048]{0:T(1024)S(1)}, u32[]{:S(2)}) copy-start(f32[66048]{0:T(1024)S(1)} %collective-permute-done.7) | copy-start | bytes 792580
  70.3 11.4 %collective-permute-start.8 = (f32[66048]{0:T(1024)}, f32[66048]{0:T(1024)}, u32[]{:S(2)}, u32[]{:S(2)}) collective-permute-start(f32[66048]{0:T(1024)} %add.210), channel_id=1, source_target_pairs={{0,128},{8,136},{16,144},{24,152},{32,160},{40,168},{48,176},{56,1... | collective-permute-start | bytes 792584 | tf_op jit(solution)/shard_map/ppermute | solution.py:16
  72.9 0.8 copy-start.10
  73.7 17.5 %collective-permute-start.4 = (f32[66048]{0:T(1024)}, f32[66048]{0:T(1024)}, u32[]{:S(2)}, u32[]{:S(2)}) collective-permute-start(f32[66048]{0:T(1024)} %add.204), channel_id=1, source_target_pairs={{0,32},{8,40},{16,48},{24,56},{32,64},{40,72},{48,80},{56,88},{64,... | collective-permute-start | bytes 792584 | tf_op jit(solution)/shard_map/ppermute | solution.py:16
  81.7 12.6 %copy-start.16 = (f32[512,8,64]{0,2,1:T(8,128)S(1)}, f32[512,8,64]{0,2,1:T(8,128)}, u32[]{:S(2)}) copy-start(f32[512,8,64]{0,2,1:T(8,128)} %get-tuple-element.33) | copy-start | bytes 3145732
  82.8 15.6 %collective-permute-start.9 = (f32[66048]{0:T(1024)S(1)}, f32[66048]{0:T(1024)S(1)}, u32[]{:S(2)}, u32[]{:S(2)}) collective-permute-start(f32[66048]{0:T(1024)S(1)} %add.212), channel_id=1, source_target_pairs={{0,8},{8,16},{16,24},{24,32},{32,40},{40,48},{48,56},{56,64},{64,7... | collective-permute-start | bytes 792584 | tf_op jit(solution)/shard_map/ppermute | solution.py:16
  92.3 10.8 %collective-permute-start.5 = (f32[66048]{0:T(1024)S(1)}, f32[66048]{0:T(1024)S(1)}, u32[]{:S(2)}, u32[]{:S(2)}) collective-permute-start(f32[66048]{0:T(1024)S(1)} %add.206), channel_id=1, source_target_pairs={{0,64},{8,72},{16,80},{24,88},{32,96},{40,104},{48,112},{56,120},{... | collective-permute-start | bytes 792584 | tf_op jit(solution)/shard_map/ppermute | solution.py:16
  94.3 10.7 %copy-start.7 = (bf16[576,8,128]{2,1,0:T(8,128)(2,1)S(1)}, bf16[576,8,128]{2,1,0:T(8,128)(2,1)}, u32[]{:S(2)}) copy-start(bf16[576,8,128]{2,1,0:T(8,128)(2,1)} %fusion.14) | copy-start | bytes 3538948
  94.3 10.7 %copy-start.18 = (pred[512,576]{0,1:T(8,128)(4,1)S(1)}, pred[512,576]{0,1:T(8,128)(4,1)}, u32[]{:S(2)}) copy-start(pred[512,576]{0,1:T(8,128)(4,1)} %get-tuple-element.30) | copy-start | bytes 884740
  98.4 16.3 %collective-permute-start.10 = (f32[66048]{0:T(1024)S(1)}, f32[66048]{0:T(1024)S(1)}, u32[]{:S(2)}, u32[]{:S(2)}) collective-permute-start(f32[66048]{0:T(1024)S(1)} %add.214), channel_id=1, source_target_pairs={{0,16},{8,24},{16,32},{24,40},{32,48},{40,56},{48,64},{56,72},{64,... | collective-permute-start | bytes 792584 | tf_op jit(solution)/shard_map/ppermute | solution.py:16
  103.2 15.2 %collective-permute-start.6 = (f32[66048]{0:T(1024)S(1)}, f32[66048]{0:T(1024)S(1)}, u32[]{:S(2)}, u32[]{:S(2)}) collective-permute-start(f32[66048]{0:T(1024)S(1)} %add.208), channel_id=1, source_target_pairs={{0,128},{8,136},{16,144},{24,152},{32,160},{40,168},{48,176},{56,1... | collective-permute-start | bytes 792584 | tf_op jit(solution)/shard_map/ppermute | solution.py:16
  105.0 13.4 %copy-start.11 = (f32[66048]{0:T(1024)S(1)}, f32[66048]{0:T(1024)}, u32[]{:S(2)}) copy-start(f32[66048]{0:T(1024)} %copy-done.10) | copy-start | bytes 792580
  108.6 25.3 %copy-start.9 = (f32[66048]{0:T(1024)S(1)}, f32[66048]{0:T(1024)}, u32[]{:S(2)}) copy-start(f32[66048]{0:T(1024)} %copy-done.8) | copy-start | bytes 792580
  114.8 19.2 %collective-permute-start.11 = (f32[66048]{0:T(1024)S(1)}, f32[66048]{0:T(1024)S(1)}, u32[]{:S(2)}, u32[]{:S(2)}) collective-permute-start(f32[66048]{0:T(1024)S(1)} %add.216), channel_id=1, source_target_pairs={{0,32},{8,40},{16,48},{24,56},{32,64},{40,72},{48,80},{56,88},{64,... | collective-permute-start | bytes 792584 | tf_op jit(solution)/shard_map/ppermute | solution.py:16
  136.1 0.7 copy-start.23
  136.1 1.0 copy-start.19
  136.2 1.0 copy-start.28
  136.2 1.0 copy-start.31
  136.2 1.8 %copy-start.33 = (f32[128,8,512]{2,0,1:T(8,128)S(1)}, f32[128,8,512]{2,0,1:T(8,128)}, u32[]{:S(2)}) copy-start(f32[128,8,512]{2,0,1:T(8,128)} %fusion.10) | copy-start | bytes 6291460

commit v4 on v3

--- a/solution.py
+++ b/solution.py
@@ -69,25 +69,33 @@
         keys.reshape(tokens, kv_local, head_dim).astype(jnp.float32), cosine, sine
     ).astype(jnp.bfloat16)
     value_rows = values.reshape(tokens, kv_local, head_dim)
-    tail_keys, tail_values = passed_along(
-        (rot_k[tokens - WINDOW :], value_rows[tokens - WINDOW :]), "seq", 1
-    )
+    tail_both = passed_along(
+        jnp.concatenate([rot_k[tokens - WINDOW :], value_rows[tokens - WINDOW :]], axis=-1),
+        "seq",
+        1,
+    )
+    tail_keys = tail_both[..., :head_dim]
+    tail_values = tail_both[..., head_dim:]
     ext_keys = jnp.concatenate([tail_keys, rot_k], axis=0)
     ext_values = jnp.concatenate([tail_values, value_rows], axis=0)
     valid = (jnp.arange(tokens + WINDOW) >= WINDOW) | (lax.axis_index("seq") > 0)
     grouped_map = key_map.reshape(kv_local, group, head_dim, feat)
     key_logits = jnp.einsum(
-        "ngd,gkdf->ngkf", ext_keys, grouped_map, preferred_element_type=jnp.float32
-    )
-    phi_key = jnp.where(valid[:, None, None, None], two_softmax(key_logits), 0.0).astype(
-        jnp.bfloat16
-    )
-    lag_phi = phi_key[:tokens].reshape(blocks, BLOCK, kv_local, group, 2 * feat)
-    lag_values = ext_values[:tokens].reshape(blocks, BLOCK, kv_local, head_dim)
+        "ngd,gkdf->gkfn", ext_keys, grouped_map, preferred_element_type=jnp.float32
+    )
+    phi_key = jnp.where(
+        valid[None, None, None, :],
+        jnp.concatenate(
+            [jax.nn.softmax(key_logits, axis=-2), jax.nn.softmax(-key_logits, axis=-2)], axis=-2
+        ),
+        0.0,
+    ).astype(jnp.bfloat16)
+    lag_phi = phi_key[..., :tokens]
+    lag_values = ext_values[:tokens]
     block_states = jnp.einsum(
-        "bjgkf,bjgd->bgkfd", lag_phi, lag_values, preferred_element_type=jnp.float32
-    )
-    block_norms = jnp.sum(lag_phi, axis=1, dtype=jnp.float32)
+        "gkfj,jgd->gkfd", lag_phi, lag_values, preferred_element_type=jnp.float32
+    )[None]
+    block_norms = jnp.sum(lag_phi, axis=-1, dtype=jnp.float32)[None]
     total_state = jnp.sum(block_states, axis=0)
     total_norm = jnp.sum(block_norms, axis=0)
     before_state = jnp.concatenate(
@@ -145,7 +153,7 @@
     peak = jnp.max(jnp.where(near_window, scores, -jnp.inf), axis=-1, keepdims=True)
     weights = jnp.where(near_window, jnp.exp(scores - peak), 0.0)
     window_sum = jnp.sum(weights, axis=-1)
-    affinity = jnp.einsum("igkf,jgkf->gkij", phi_query, phi_key, preferred_element_type=jnp.float32)
+    affinity = jnp.einsum("igkf,gkfj->gkij", phi_query, phi_key, preferred_element_type=jnp.float32)
     affinity = jnp.where(linear_mask & live, affinity, 0.0)
     near_sum = jnp.sum(affinity, axis=-1)
     window_num = jnp.einsum(

time: 165 us -> 176 us (1.067)
  waiting for transfers between devices: 32.2 us -> 41.8 us
  local copies, waits for them, and re-layouts: 15.1 us -> 19.9 us
  other arithmetic: 35.6 us -> 31.1 us
  starting transfers between devices: 39.7 us -> 41.6 us
    ppermute x12 -> x11, waiting for transfers between devices: 32.2 us -> 41.8 us  [passed_along(): lax.ppermute(value, axis, [(source, source + steps) for source in range(f...]
    reduce_sum x2 -> x1, other arithmetic: 7.57 us -> 0.73 us  [body(): block_norms = jnp.sum(lag_phi, axis=-1, dtype=jnp.float32)[None]]
    sub x0 -> x2, other arithmetic: none -> 6.14 us  [the longest x1 3.91 us: body(): jax.nn.softmax(-key_logits, axis=-2)]
    convert_element_type x1 -> x0, other arithmetic: 4.3 us -> none  [body(): jnp.where(valid[:, None, None, None], two_softmax(key_logits), 0.0)]
    unnamed x72 -> x65, local copies, waits for them, and re-layouts: 7.08 us -> 11.1 us
    dot_general x1, matrix products: 3.51 us -> 6.16 us  [body(): jnp.einsum('gkij,jgd->igkd', weights.astype(jnp.bfloat16), ext_values, pr...]
    concatenate x1 -> x3, other arithmetic: 0.08 us -> 2.5 us  [the longest x2 2.41 us: body(): jnp.concatenate([jax.nn.softmax(key_logits, axis=-2), jax.nn.softmax(-key...]
    ppermute x12 -> x11, starting transfers between devices: 39.7 us -> 41.6 us  [passed_along(): lax.ppermute(value, axis, [(source, source + steps) for source in range(f...]
  transfers between devices with their start and end apart: 12 -> 11, of which waited for: 6 -> 6; matrix products, arithmetic and copies ran while one was open for 31% -> 19% of each run, Pallas kernels for 0% -> 0%
where the time goes in v4:
time: 176 us; the launch traced here: 175 us
  waiting for transfers between devices  41.8 us (24%)
  starting transfers between devices  41.6 us (24%)
  other arithmetic  31.1 us (18%)
  blocking collectives  20.3 us (12%)
  local copies, waits for them, and re-layouts  19.9 us (11%)
  matrix products  19.6 us (11%)
    ppermute x11, waiting for transfers between devices, passed_along(): lax.ppermute(value, axis, [(source, source + steps) for source in range(f...  41.8 us
    ppermute x11, starting transfers between devices, passed_along(): lax.ppermute(value, axis, [(source, source + steps) for source in range(f...  41.6 us
    all_to_all x1, blocking collectives, body(): lax.all_to_all(result, 'head', split_axis=0, concat_axis=1, tiled=True)  20.3 us
    unnamed x65, local copies, waits for them, and re-layouts  11.1 us
    another operation x3, other arithmetic  6.37 us
    dot_general x1, matrix products, body(): jnp.einsum('gkij,jgd->igkd', weights.astype(jnp.bfloat16), ext_values, pr...  6.16 us
    sub x1, other arithmetic, body(): jax.nn.softmax(-key_logits, axis=-2)  3.91 us
  transfers between devices with their start and end apart: 11, of which 6 were waited for; matrix products, arithmetic and copies ran while one was open for 19% of the time, Pallas kernels for 0%

profile of v4, /device:TPU:2, one launch (start us, length us, event | category | flops | bytes accessed | tf_op | source)
XLA Modules:
  0.0 174.9 jit_solution(15201395500300317668)
XLA Ops:
  0.0 0.8 add_bitcast_fusion
  0.8 0.7 slice.60
  1.6 1.0 copy.37
  2.7 2.4 %subtract_convert_fusion.3 = (bf16[512,1,64]{0,2,1:T(8,128)(2,1)S(1)}, bf16[512,1,64]{0,2,1:T(8,128)(2,1)S(1)}) fusion(f32[512,1,128]{0,2,1:T(8,128)S(1)} %bitcast_convert_fusion, f32[64]{0:T(128)} %constant.76.clone, f32[512]{0:T(512)S(1)} %get-tuple-element.25, f32[64]{0:T(128)} %constant.75.clone, f32[512]{0:T(512)S(1)} %get-tuple-element.24, ...), kind=kLoop, calls=%fused_computation.122 | loop fusion | flops 753664 | bytes 400128 | tf_op jit(solution)/shard_map/convert.6
  5.2 3.8 %collective-permute-start = (bf16[64,1,256]{0,2,1:T(8,128)(2,1)S(1)}, bf16[64,1,256]{0,2,1:T(8,128)(2,1)S(1)}, u32[]{:S(2)}, u32[]{:S(2)}) collective-permute-start(bf16[64,1,256]{0,2,1:T(8,128)(2,1)S(1)} %fusion.82), channel_id=1, source_target_pairs={{0,8},{8,16},{16,24},{24,32},{32,40},{40,48},{48,56},{56,64},{64,7... | collective-permute-start | bytes 98312 | tf_op jit(solution)/shard_map/ppermute | solution.py:16
  9.0 2.2 %fusion.69 = (f32[512,64]{0,1:T(8,128)S(1)}, f32[512,64]{0,1:T(8,128)S(1)}) fusion(f32[64]{0:T(128)} %constant.76.clone, f32[512]{0:T(512)S(1)} %get-tuple-element.25, f32[64]{0:T(128)} %constant.75.clone, f32[512]{0:T(512)S(1)} %get-tuple-element.24, f32[64]{0:T(128)} %constant.74.clone, f32[512]{0:T(512)S(1)} %get-tuple-element.23), kind=kLoop, calls=%fused_computation.109 | loop fusion | flops 491520 | bytes 269056 | tf_op jit(solution)/shard_map/sub | solution.py:29
  11.2 1.1 fusion.40
  12.3 0.9 copy.45
  13.2 0.8 copy.47
  14.0 1.1 collective-permute-done
  15.1 0.6 copy-done.15
  15.7 0.4 fusion.63
  16.2 1.9 %copy.41 = f32[576,8,64]{2,0,1:T(8,128)} copy(f32[576,8,64]{0,2,1:T(8,128)S(1)} %bitcast.177) | data formatting | bytes 2359296 | tf_op jit(solution)/shard_map/ngd,gkdf->gkfn/dot_general | solution.py:83
  18.1 3.9 %fusion.117 = (f32[8,576]{1,0:T(8,128)S(1)}, f32[8,64,576]{1,2,0:T(8,128)S(1)}) fusion(f32[576,8,64]{2,0,1:T(8,128)} %copy.41), kind=kOutput, calls=%fused_computation.180 | output fusion | flops 1179711 | bytes 2377728 | tf_op jit(solution)/shard_map/sub | solution.py:89
  22.0 2.2 %fusion.118 = (f32[8,576]{1,0:T(8,128)S(1)}, f32[8,64,576]{1,2,0:T(8,128)S(1)}) fusion(f32[576,8,64]{2,0,1:T(8,128)S(1)} %copy-done.2), kind=kOutput, calls=%fused_computation.181 | output fusion | flops 589887 | bytes 2377728 | tf_op jit(solution)/shard_map/sub | solution.py:89
  24.2 1.6 fusion.124
  25.9 1.6 broadcast_divide_fusion.1
  27.6 0.8 fusion.125
  28.4 0.5 copy-done.3
  28.8 0.7 convert_reduce_fusion
  29.7 0.5 fusion.41
  30.3 2.8 %collective-permute-start.1 = (f32[66048]{0:T(1024)S(1)}, f32[66048]{0:T(1024)S(1)}, u32[]{:S(2)}, u32[]{:S(2)}) collective-permute-start(f32[66048]{0:T(1024)S(1)} %slice.80), channel_id=1, source_target_pairs={{0,8},{8,16},{16,24},{24,32},{32,40},{40,48},{48,56},{56,64},{64,7... | collective-permute-start | bytes 792584 | tf_op jit(solution)/shard_map/ppermute | solution.py:16
  33.0 1.6 broadcast_divide_fusion
  34.6 6.9 %collective-permute-done.1 = f32[66048]{0:T(1024)S(1)} collective-permute-done((f32[66048]{0:T(1024)S(1)}, f32[66048]{0:T(1024)S(1)}, u32[]{:S(2)}, u32[]{:S(2)}) %collective-permute-start.1) | collective-permute-done | bytes 264224 | tf_op jit(solution)/shard_map/ppermute | solution.py:16
  41.5 0.9 slice_add_fusion
  42.4 3.2 %collective-permute-start.2 = (f32[66048]{0:T(1024)}, f32[66048]{0:T(1024)}, u32[]{:S(2)}, u32[]{:S(2)}) collective-permute-start(f32[66048]{0:T(1024)} %get-tuple-element.15), channel_id=1, source_target_pairs={{0,16},{8,24},{16,32},{24,40},{32,48},{40,56},{48,64},{56,72},{64,... | collective-permute-start | bytes 792584 | tf_op jit(solution)/shard_map/ppermute | solution.py:16
  45.6 3.6 %collective-permute-start.6 = (f32[66048]{0:T(1024)}, f32[66048]{0:T(1024)}, u32[]{:S(2)}, u32[]{:S(2)}) collective-permute-start(f32[66048]{0:T(1024)} %get-tuple-element.16), channel_id=1, source_target_pairs={{0,64},{8,72},{16,80},{24,88},{32,96},{40,104},{48,112},{56,120},{... | collective-permute-start | bytes 792584 | tf_op jit(solution)/shard_map/ppermute | solution.py:16
  49.2 1.5 copy.43
  50.7 0.3 fusion.115
  51.0 2.0 %copy.69 = f32[512,8,64]{2,0,1:T(8,128)} copy(f32[512,8,64]{0,2,1:T(8,128)S(1)} %get-tuple-element.13) | data formatting | bytes 2097152
  52.9 1.9 %copy.68 = f32[512,8,64]{2,0,1:T(8,128)} copy(f32[512,8,64]{0,2,1:T(8,128)S(1)} %get-tuple-element.14) | data formatting | bytes 2097152
  54.9 2.8 %subtract_convert_fusion = (bf16[512,8,64]{2,0,1:T(8,128)(2,1)S(1)}, bf16[512,8,64]{2,0,1:T(8,128)(2,1)S(1)}) fusion(f32[512,8,64]{2,0,1:T(8,128)} %copy.69, f32[512,8,64]{2,0,1:T(8,128)} %copy.68, f32[512,64]{1,0:T(8,128)S(1)} %copy-done.14, f32[512,64]{1,0:T(8,128)S(1)} %copy-done.13), kind=kLoop, calls=%fused_computation.37 | loop fusion | flops 2097152 | bytes 3407872 | tf_op jit(solution)/shard_map/convert.4
  57.8 2.6 %fusion.4 = (f32[8,512]{1,0:T(8,128)S(1)}, f32[576,512,8]{1,0,2:T(8,128)S(1)}) fusion(pred[512,576]{0,1:T(8,128)(4,1)S(1)} %copy-done.4, bf16[512,8,64]{2,0,1:T(8,128)(2,1)S(1)} %get-tuple-element.12, bf16[512,8,64]{2,0,1:T(8,128)(2,1)S(1)} %get-tuple-element.11, bf16[512,1,64]{0,2,1:T(8,128)(2,1)S(1)} %copy-done.11, bf16[512,1,64]{0,2,1:T(8,128)(2,1)S(1)} %copy-done.9, ...), kind=kOutput, calls=%fused_computation.6 | convolution fusion | flops 613593088 | bytes 10944512 | tf_op jit(solution)/shard_map/igkd,jgd->gkij/dot_general | solution.py:149
  60.4 3.7 %copy-done.1 = f32[576,512,8]{1,0,2:T(8,128)} copy-done((f32[576,512,8]{1,0,2:T(8,128)}, f32[576,512,8]{1,0,2:T(8,128)S(1)}, u32[]{:S(2)}) %copy-start.1) | copy-done | bytes 9437208
  64.0 2.5 %fusion.7 = f32[8,512]{1,0:T(8,128)} fusion(f32[576,512,8]{1,0,2:T(8,128)S(1)} %get-tuple-element.37, f32[8,512]{1,0:T(8,128)S(1)} %get-tuple-element.36, pred[512,576]{0,1:T(8,128)(4,1)S(1)} %copy-done.4), kind=kLoop, calls=%fused_computation.11 | loop fusion | flops 9433088 | bytes 9764864 | tf_op jit(solution)/shard_map/reduce_sum | solution.py:155
  66.6 2.4 %fusion.119 = (f32[512,8]{0,1:T(8,128)}, f32[512,8,64]{0,2,1:T(8,128)}) fusion(bf16[8,128,64]{1,2,0:T(8,128)(2,1)S(1)} %copy-done, bf16[512,8,64]{2,0,1:T(8,128)(2,1)S(1)} %get-tuple-element.12, bf16[512,8,64]{2,0,1:T(8,128)(2,1)S(1)} %get-tuple-element.11), kind=kOutput, calls=%fused_computation.182 | convolution fusion | flops 69992512 | bytes 2244608 | tf_op jit(solution)/shard_map/sub | solution.py:47
  69.0 1.5 fusion.120
  70.5 1.1 add.201
  71.6 5.8 %collective-permute-start.3 = (f32[66048]{0:T(1024)S(1)}, f32[66048]{0:T(1024)S(1)}, u32[]{:S(2)}, u32[]{:S(2)}) collective-permute-start(f32[66048]{0:T(1024)S(1)} %add.201), channel_id=1, source_target_pairs={{0,32},{8,40},{16,48},{24,56},{32,64},{40,72},{48,80},{56,88},{64,... | collective-permute-start | bytes 792584 | tf_op jit(solution)/shard_map/ppermute | solution.py:16
  77.4 1.1 add.207
  78.5 1.9 %collective-permute-start.7 = (f32[66048]{0:T(1024)S(1)}, f32[66048]{0:T(1024)S(1)}, u32[]{:S(2)}, u32[]{:S(2)}) collective-permute-start(f32[66048]{0:T(1024)S(1)} %add.207), channel_id=1, source_target_pairs={{0,128},{8,136},{16,144},{24,152},{32,160},{40,168},{48,176},{56,1... | collective-permute-start | bytes 792584 | tf_op jit(solution)/shard_map/ppermute | solution.py:16
  80.5 1.2 divide_convert_fusion
  81.7 4.0 %collective-permute-done.3 = f32[66048]{0:T(1024)S(1)} collective-permute-done((f32[66048]{0:T(1024)S(1)}, f32[66048]{0:T(1024)S(1)}, u32[]{:S(2)}, u32[]{:S(2)}) %collective-permute-start.3) | collective-permute-done | bytes 264224 | tf_op jit(solution)/shard_map/ppermute | solution.py:16
  85.8 3.3 %collective-permute-start.4 = (f32[66048]{0:T(1024)S(1)}, f32[66048]{0:T(1024)S(1)}, u32[]{:S(2)}, u32[]{:S(2)}) collective-permute-start(f32[66048]{0:T(1024)S(1)} %add.203), channel_id=1, source_target_pairs={{0,64},{8,72},{16,80},{24,88},{32,96},{40,104},{48,112},{56,120},{... | collective-permute-start | bytes 792584 | tf_op jit(solution)/shard_map/ppermute | solution.py:16
  89.2 10.2 %collective-permute-start.8 = (f32[66048]{0:T(1024)S(1)}, f32[66048]{0:T(1024)S(1)}, u32[]{:S(2)}, u32[]{:S(2)}) collective-permute-start(f32[66048]{0:T(1024)S(1)} %add.209), channel_id=1, source_target_pairs={{0,8},{8,16},{16,24},{24,32},{32,40},{40,48},{48,56},{56,64},{64,7... | collective-permute-start | bytes 792584 | tf_op jit(solution)/shard_map/ppermute | solution.py:16
  99.4 2.3 %select_reduce_fusion = (f32[8,512]{1,0:T(8,128)S(1)}, bf16[8,512,576]{1,2,0:T(8,128)(2,1)S(1)}) fusion(pred[512,576]{0,1:T(8,128)(4,1)S(1)} %copy-done.17, bf16[512,8,64]{0,2,1:T(8,128)(2,1)S(1)} %get-tuple-element.40, bf16[512,8,64]{0,2,1:T(8,128)(2,1)S(1)} %get-tuple-element.41, bf16[8,64,576]{1,2,0:T(8,128)(2,1)S(1)} %copy-done.7, ...), kind=kOutput, calls=%fused_computation.9 | convolution fusion | flops 616099840 | bytes 7258688 | tf_op jit(solution)/shard_map/igkf,gkfj->gkij/dot_general | solution.py:156
  101.8 0.9 collective-permute-done.4
  102.7 1.3 collective-permute-start.5
  104.1 3.5 %collective-permute-start.9 = (f32[66048]{0:T(1024)S(1)}, f32[66048]{0:T(1024)S(1)}, u32[]{:S(2)}, u32[]{:S(2)}) collective-permute-start(f32[66048]{0:T(1024)S(1)} %add.211), channel_id=1, source_target_pairs={{0,16},{8,24},{16,32},{24,40},{32,48},{40,56},{48,64},{56,72},{64,... | collective-permute-start | bytes 792584 | tf_op jit(solution)/shard_map/ppermute | solution.py:16
  107.6 2.5 %fusion.10 = f32[128,8,512]{2,0,1:T(8,128)} fusion(bf16[8,512,576]{1,2,0:T(8,128)(2,1)S(1)} %get-tuple-element.39, pred[512,576]{0,1:T(8,128)(4,1)S(1)} %copy-done.17, bf16[64,1,128]{2,0,1:T(8,128)(2,1)S(1)} %copy-done.24, bf16[512,1,128]{2,0,1:T(8,128)(2,1)S(1)} %bitcast.183), kind=kOutput, calls=%fused_computation.14 | convolution fusion | flops 606633984 | bytes 7258112 | tf_op jit(solution)/shard_map/gkij,jgd->igkd/dot_general | solution.py:165
  110.0 12.2 %collective-permute-done.9 = f32[66048]{0:T(1024)S(1)} collective-permute-done((f32[66048]{0:T(1024)S(1)}, f32[66048]{0:T(1024)S(1)}, u32[]{:S(2)}, u32[]{:S(2)}) %collective-permute-start.9) | collective-permute-done | bytes 264224 | tf_op jit(solution)/shard_map/ppermute | solution.py:16
  122.2 2.1 %collective-permute-start.10 = (f32[66048]{0:T(1024)S(1)}, f32[66048]{0:T(1024)S(1)}, u32[]{:S(2)}, u32[]{:S(2)}) collective-permute-start(f32[66048]{0:T(1024)S(1)} %add.213), channel_id=1, source_target_pairs={{0,32},{8,40},{16,48},{24,56},{32,64},{40,72},{48,80},{56,88},{64,... | collective-permute-start | bytes 792584 | tf_op jit(solution)/shard_map/ppermute | solution.py:16
  124.4 1.1 add_add_fusion.1
  125.4 16.7 %collective-permute-done.10 = f32[66048]{0:T(1024)S(1)} collective-permute-done((f32[66048]{0:T(1024)S(1)}, f32[66048]{0:T(1024)S(1)}, u32[]{:S(2)}, u32[]{:S(2)}) %collective-permute-start.10) | collective-permute-done | bytes 264224 | tf_op jit(solution)/shard_map/ppermute | solution.py:16
  142.2 1.0 add_add_fusion
  143.5 0.4 fusion.78
  143.9 0.4 fusion.44
  144.6 0.2 fusion.86
  145.3 0.8 copy-done.29
  146.1 6.2 %fusion.24 = bf16[512,1,8,128]{0,3,2,1:T(8,128)(2,1)S(1)} fusion(f32[8,128,512]{2,1,0:T(8,128)S(1)} %fusion.78, f32[8,128,512]{2,1,0:T(8,128)S(1)} %fusion.44, f32[128,8,512]{2,0,1:T(8,128)S(1)} %copy-done.29, f32[576,512,8]{1,0,2:T(8,128)} %copy-done.1, f32[8,512]{1,0:T(8,128)S(1)} %copy-done.22, pred[512,576]{0,1:T(8,128)(4,1)S(1)} %copy-done.5, ...), kind=kOutput, calls=%fused_computation.38 | convolution fusion | flops 617381888 | bytes 17252416 | tf_op jit(solution)/shard_map/gkij,jgd->igkd/dot_general | solution.py:159
  152.2 0.8 copy.54
  153.0 0.5 all_to_all.14
  153.5 20.3 %all_to_all.19 = bf16[8,64,1024]{2,1,0:T(8,128)(2,1)S(1)} all-to-all(bf16[8,64,1024]{2,1,0:T(8,128)(2,1)S(1)} %all_to_all.14), channel_id=1, replica_groups=mesh['seq'=32,'head'=8] {'head'}, dimensions={0} | all-to-all | bytes 2097152 | tf_op jit(solution)/shard_map/all_to_all | solution.py:192
  173.8 1.1 copy.70
  (85 shorter events, 1.8 us)
Async XLA Ops:
  0.0 66.6 %copy-start = (bf16[8,128,64]{1,2,0:T(8,128)(2,1)S(1)}, bf16[8,128,64]{1,2,0:T(8,128)(2,1)}, u32[]{:S(2)}) copy-start(bf16[8,128,64]{1,2,0:T(8,128)(2,1)} %param.14) | copy-start | bytes 393220
  0.0 12.3 %copy-start.28 = (f32[8]{0:T(128)S(1)}, f32[8]{0:T(128)}, u32[]{:S(2)}) copy-start(f32[8]{0:T(128)} %param.16) | copy-start | bytes 100
  0.0 15.7 %copy-start.20 = (bf16[8,128,64]{1,2,0:T(8,128)(2,1)S(1)}, bf16[8,128,64]{1,2,0:T(8,128)(2,1)}, u32[]{:S(2)}) copy-start(bf16[8,128,64]{1,2,0:T(8,128)(2,1)} %param.15) | copy-start | bytes 393220
  5.1 11.1 %copy-start.8 = (bf16[512,1,64]{0,2,1:T(8,128)(2,1)}, bf16[512,1,64]{0,2,1:T(8,128)(2,1)S(1)}, u32[]{:S(2)}) copy-start(bf16[512,1,64]{0,2,1:T(8,128)(2,1)S(1)} %get-tuple-element.17) | copy-start | bytes 196612
  5.1 11.1 %copy-start.10 = (bf16[512,1,64]{0,2,1:T(8,128)(2,1)}, bf16[512,1,64]{0,2,1:T(8,128)(2,1)S(1)}, u32[]{:S(2)}) copy-start(bf16[512,1,64]{0,2,1:T(8,128)(2,1)S(1)} %get-tuple-element.18) | copy-start | bytes 196612
  5.2 10.0 %collective-permute-start = (bf16[64,1,256]{0,2,1:T(8,128)(2,1)S(1)}, bf16[64,1,256]{0,2,1:T(8,128)(2,1)S(1)}, u32[]{:S(2)}, u32[]{:S(2)}) collective-permute-start(bf16[64,1,256]{0,2,1:T(8,128)(2,1)S(1)} %fusion.82), channel_id=1, source_target_pairs={{0,8},{8,16},{16,24},{24,32},{32,40},{40,48},{48,56},{56,64},{64,7... | collective-permute-start | bytes 98312 | tf_op jit(solution)/shard_map/ppermute | solution.py:16
  11.2 6.9 %copy-start.26 = (pred[576]{0:T(1024)(128)(4,1)}, pred[576]{0:T(1024)(128)(4,1)S(1)}, u32[]{:S(2)}) copy-start(pred[576]{0:T(1024)(128)(4,1)S(1)} %fusion.90) | copy-start | bytes 1732
  15.1 0.6 copy-start.15
  18.1 3.9 %copy-start.2 = (f32[576,8,64]{2,0,1:T(8,128)S(1)}, f32[576,8,64]{2,0,1:T(8,128)}, u32[]{:S(2)}) copy-start(f32[576,8,64]{2,0,1:T(8,128)} %copy.41) | copy-start | bytes 3538948
  27.5 0.9 slice-start
  27.6 2.0 %copy-start.23 = (bf16[64,1,128]{2,0,1:T(8,128)(2,1)}, bf16[64,1,128]{2,0,1:T(8,128)(2,1)S(1)}, u32[]{:S(2)}) copy-start(bf16[64,1,128]{2,0,1:T(8,128)(2,1)S(1)} %copy.39) | copy-start | bytes 49156
  27.6 1.3 copy-start.3
  28.8 0.9 copy-start.18
  30.3 11.3 %collective-permute-start.1 = (f32[66048]{0:T(1024)S(1)}, f32[66048]{0:T(1024)S(1)}, u32[]{:S(2)}, u32[]{:S(2)}) collective-permute-start(f32[66048]{0:T(1024)S(1)} %slice.80), channel_id=1, source_target_pairs={{0,8},{8,16},{16,24},{24,32},{32,40},{40,48},{48,56},{56,64},{64,7... | collective-permute-start | bytes 792584 | tf_op jit(solution)/shard_map/ppermute | solution.py:16
  42.4 28.1 %collective-permute-start.2 = (f32[66048]{0:T(1024)}, f32[66048]{0:T(1024)}, u32[]{:S(2)}, u32[]{:S(2)}) collective-permute-start(f32[66048]{0:T(1024)} %get-tuple-element.15), channel_id=1, source_target_pairs={{0,16},{8,24},{16,32},{24,40},{32,48},{40,56},{48,64},{56,72},{64,... | collective-permute-start | bytes 792584 | tf_op jit(solution)/shard_map/ppermute | solution.py:16
  45.6 31.8 %collective-permute-start.6 = (f32[66048]{0:T(1024)}, f32[66048]{0:T(1024)}, u32[]{:S(2)}, u32[]{:S(2)}) collective-permute-start(f32[66048]{0:T(1024)} %get-tuple-element.16), channel_id=1, source_target_pairs={{0,64},{8,72},{16,80},{24,88},{32,96},{40,104},{48,112},{56,120},{... | collective-permute-start | bytes 792584 | tf_op jit(solution)/shard_map/ppermute | solution.py:16
  52.9 1.9 %copy-start.13 = (f32[512,64]{1,0:T(8,128)S(1)}, f32[512,64]{1,0:T(8,128)}, u32[]{:S(2)}) copy-start(f32[512,64]{1,0:T(8,128)} %copy.45) | copy-start | bytes 393220
  52.9 1.9 %copy-start.14 = (f32[512,64]{1,0:T(8,128)S(1)}, f32[512,64]{1,0:T(8,128)}, u32[]{:S(2)}) copy-start(f32[512,64]{1,0:T(8,128)} %copy.47) | copy-start | bytes 393220
  54.9 2.9 %copy-start.4 = (pred[512,576]{0,1:T(8,128)(4,1)S(1)}, pred[512,576]{0,1:T(8,128)(4,1)}, u32[]{:S(2)}) copy-start(pred[512,576]{0,1:T(8,128)(4,1)} %get-tuple-element.26) | copy-start | bytes 884740
  54.9 2.9 %copy-start.9 = (bf16[512,1,64]{0,2,1:T(8,128)(2,1)S(1)}, bf16[512,1,64]{0,2,1:T(8,128)(2,1)}, u32[]{:S(2)}) copy-start(bf16[512,1,64]{0,2,1:T(8,128)(2,1)} %copy-done.8) | copy-start | bytes 196612
  54.9 2.9 %copy-start.11 = (bf16[512,1,64]{0,2,1:T(8,128)(2,1)S(1)}, bf16[512,1,64]{0,2,1:T(8,128)(2,1)}, u32[]{:S(2)}) copy-start(bf16[512,1,64]{0,2,1:T(8,128)(2,1)} %copy-done.10) | copy-start | bytes 196612
  54.9 2.9 %copy-start.16 = (bf16[64,1,128]{0,2,1:T(8,128)(2,1)S(1)}, bf16[64,1,128]{0,2,1:T(8,128)(2,1)}, u32[]{:S(2)}) copy-start(bf16[64,1,128]{0,2,1:T(8,128)(2,1)} %copy-done.15) | copy-start | bytes 49156
  60.4 3.7 %copy-start.1 = (f32[576,512,8]{1,0,2:T(8,128)}, f32[576,512,8]{1,0,2:T(8,128)S(1)}, u32[]{:S(2)}) copy-start(f32[576,512,8]{1,0,2:T(8,128)S(1)} %get-tuple-element.37) | copy-start | bytes 28311556
  60.4 6.2 %copy-start.21 = (f32[8,512]{1,0:T(8,128)}, f32[8,512]{1,0:T(8,128)S(1)}, u32[]{:S(2)}) copy-start(f32[8,512]{1,0:T(8,128)S(1)} %get-tuple-element.36) | copy-start | bytes 49156
  70.5 10.0 %copy-start.12 = (f32[512,8,64]{0,2,1:T(8,128)S(1)}, f32[512,8,64]{0,2,1:T(8,128)}, u32[]{:S(2)}) copy-start(f32[512,8,64]{0,2,1:T(8,128)} %get-tuple-element.33) | copy-start | bytes 3145732
  71.6 14.1 %collective-permute-start.3 = (f32[66048]{0:T(1024)S(1)}, f32[66048]{0:T(1024)S(1)}, u32[]{:S(2)}, u32[]{:S(2)}) collective-permute-start(f32[66048]{0:T(1024)S(1)} %add.201), channel_id=1, source_target_pairs={{0,32},{8,40},{16,48},{24,56},{32,64},{40,72},{48,80},{56,88},{64,... | collective-permute-start | bytes 792584 | tf_op jit(solution)/shard_map/ppermute | solution.py:16
  78.5 10.6 %collective-permute-start.7 = (f32[66048]{0:T(1024)S(1)}, f32[66048]{0:T(1024)S(1)}, u32[]{:S(2)}, u32[]{:S(2)}) collective-permute-start(f32[66048]{0:T(1024)S(1)} %add.207), channel_id=1, source_target_pairs={{0,128},{8,136},{16,144},{24,152},{32,160},{40,168},{48,176},{56,1... | collective-permute-start | bytes 792584 | tf_op jit(solution)/shard_map/ppermute | solution.py:16
  80.4 18.9 %copy-start.6 = (bf16[8,64,576]{1,2,0:T(8,128)(2,1)S(1)}, bf16[8,64,576]{1,2,0:T(8,128)(2,1)}, u32[]{:S(2)}) copy-start(bf16[8,64,576]{1,2,0:T(8,128)(2,1)} %broadcast_divide_fusion.1) | copy-start | bytes 1769476
  80.5 18.9 %copy-start.7 = (bf16[8,64,576]{1,2,0:T(8,128)(2,1)S(1)}, bf16[8,64,576]{1,2,0:T(8,128)(2,1)}, u32[]{:S(2)}) copy-start(bf16[8,64,576]{1,2,0:T(8,128)(2,1)} %broadcast_divide_fusion) | copy-start | bytes 1769476
  80.5 18.9 %copy-start.17 = (pred[512,576]{0,1:T(8,128)(4,1)S(1)}, pred[512,576]{0,1:T(8,128)(4,1)}, u32[]{:S(2)}) copy-start(pred[512,576]{0,1:T(8,128)(4,1)} %get-tuple-element.27) | copy-start | bytes 884740
  80.5 18.9 %copy-start.27 = (pred[576]{0:T(1024)(128)(4,1)S(1)}, pred[576]{0:T(1024)(128)(4,1)}, u32[]{:S(2)}) copy-start(pred[576]{0:T(1024)(128)(4,1)} %copy-done.26) | copy-start | bytes 1732
  85.8 16.9 %collective-permute-start.4 = (f32[66048]{0:T(1024)S(1)}, f32[66048]{0:T(1024)S(1)}, u32[]{:S(2)}, u32[]{:S(2)}) collective-permute-start(f32[66048]{0:T(1024)S(1)} %add.203), channel_id=1, source_target_pairs={{0,64},{8,72},{16,80},{24,88},{32,96},{40,104},{48,112},{56,120},{... | collective-permute-start | bytes 792584 | tf_op jit(solution)/shard_map/ppermute | solution.py:16
  89.2 14.9 %collective-permute-start.8 = (f32[66048]{0:T(1024)S(1)}, f32[66048]{0:T(1024)S(1)}, u32[]{:S(2)}, u32[]{:S(2)}) collective-permute-start(f32[66048]{0:T(1024)S(1)} %add.209), channel_id=1, source_target_pairs={{0,8},{8,16},{16,24},{24,32},{32,40},{40,48},{48,56},{56,64},{64,7... | collective-permute-start | bytes 792584 | tf_op jit(solution)/shard_map/ppermute | solution.py:16
  99.4 8.2 %copy-start.19 = (bf16[512,128]{1,0:T(8,128)(2,1)S(1)}, bf16[512,128]{1,0:T(8,128)(2,1)}, u32[]{:S(2)}) copy-start(bf16[512,128]{1,0:T(8,128)(2,1)} %param.12) | copy-start | bytes 393220
  99.4 8.1 %copy-start.24 = (bf16[64,1,128]{2,0,1:T(8,128)(2,1)S(1)}, bf16[64,1,128]{2,0,1:T(8,128)(2,1)}, u32[]{:S(2)}) copy-start(bf16[64,1,128]{2,0,1:T(8,128)(2,1)} %copy-done.23) | copy-start | bytes 49156
  102.7 21.7 %collective-permute-start.5 = (f32[66048]{0:T(1024)S(1)}, f32[66048]{0:T(1024)S(1)}, u32[]{:S(2)}, u32[]{:S(2)}) collective-permute-start(f32[66048]{0:T(1024)S(1)} %add.205), channel_id=1, source_target_pairs={{0,128},{8,136},{16,144},{24,152},{32,160},{40,168},{48,176},{56,1... | collective-permute-start | bytes 792584 | tf_op jit(solution)/shard_map/ppermute | solution.py:16
  104.1 18.1 %collective-permute-start.9 = (f32[66048]{0:T(1024)S(1)}, f32[66048]{0:T(1024)S(1)}, u32[]{:S(2)}, u32[]{:S(2)}) collective-permute-start(f32[66048]{0:T(1024)S(1)} %add.211), channel_id=1, source_target_pairs={{0,16},{8,24},{16,32},{24,40},{32,48},{40,56},{48,64},{56,72},{64,... | collective-permute-start | bytes 792584 | tf_op jit(solution)/shard_map/ppermute | solution.py:16
  122.2 19.9 %collective-permute-start.10 = (f32[66048]{0:T(1024)S(1)}, f32[66048]{0:T(1024)S(1)}, u32[]{:S(2)}, u32[]{:S(2)}) collective-permute-start(f32[66048]{0:T(1024)S(1)} %add.213), channel_id=1, source_target_pairs={{0,32},{8,40},{16,48},{24,56},{32,64},{40,72},{48,80},{56,88},{64,... | collective-permute-start | bytes 792584 | tf_op jit(solution)/shard_map/ppermute | solution.py:16
  144.3 0.7 copy-start.25
  144.3 1.0 copy-start.5
  144.3 1.0 copy-start.22
  144.4 1.7 copy-start.29

commit v5 on v3

--- a/solution.py
+++ b/solution.py
@@ -11,7 +11,8 @@
 
 
 def passed_along(value, axis, steps):
-    count = lax.axis_size(axis)
+    names = axis if isinstance(axis, tuple) else (axis,)
+    count = math.prod(lax.axis_size(name) for name in names)
     first, last = (max(0, -steps), min(count, count - steps))
     return lax.ppermute(value, axis, [(source, source + steps) for source in range(first, last)])
 
@@ -70,11 +71,11 @@
     ).astype(jnp.bfloat16)
     value_rows = values.reshape(tokens, kv_local, head_dim)
     tail_keys, tail_values = passed_along(
-        (rot_k[tokens - WINDOW :], value_rows[tokens - WINDOW :]), "seq", 1
+        (rot_k[tokens - WINDOW :], value_rows[tokens - WINDOW :]), ("sx", "sz"), 1
     )
     ext_keys = jnp.concatenate([tail_keys, rot_k], axis=0)
     ext_values = jnp.concatenate([tail_values, value_rows], axis=0)
-    valid = (jnp.arange(tokens + WINDOW) >= WINDOW) | (lax.axis_index("seq") > 0)
+    valid = (jnp.arange(tokens + WINDOW) >= WINDOW) | (lax.axis_index("sx") > 0) | (lax.axis_index("sz") > 0)
     grouped_map = key_map.reshape(kv_local, group, head_dim, feat)
     key_logits = jnp.einsum(
         "ngd,gkdf->ngkf", ext_keys, grouped_map, preferred_element_type=jnp.float32
@@ -99,28 +100,25 @@
     state_shape = total_state.shape
     state_size = total_state.size
     packed = jnp.concatenate([total_state.reshape(-1), total_norm.reshape(-1)])
-    count = lax.axis_size("seq")
-    shifts = []
-    steps = 1
-    while steps < count:
-        shifts.append(steps)
-        steps *= 2
-    half = len(shifts) // 2 + 1
-    orders = (shifts, shifts[half:] + shifts[:half])
-    middle = packed.size // 2
-    pieces = []
-    for order, piece in zip(orders, (packed[:middle], packed[middle:])):
-        inclusive = piece
-        exclusive = jnp.zeros_like(piece)
-        for place, shift in enumerate(order):
-            received = passed_along(inclusive, "seq", shift)
-            if not pieces and place == 0:
-                first_received = received
+    def exclusive_scan(value, axis):
+        count = lax.axis_size(axis)
+        inclusive = value
+        exclusive = jnp.zeros_like(value)
+        first = None
+        steps = 1
+        while steps < count:
+            received = passed_along(inclusive, axis, steps)
+            first = received if first is None else first
             exclusive = exclusive + received
-            if place + 1 < len(order):
+            if 2 * steps < count:
                 inclusive = inclusive + received
-        pieces.append(exclusive)
-    exclusive = jnp.concatenate(pieces)
+            steps *= 2
+        return exclusive, first
+
+    row_total = lax.psum(packed, "sz")
+    inner, first_received = exclusive_scan(packed, "sz")
+    outer, _ = exclusive_scan(row_total, "sx")
+    exclusive = inner + outer
     queries, first_received = lax.optimization_barrier((queries, first_received))
     rot_q = rotate(
         queries.reshape(tokens, heads, head_dim).astype(jnp.float32), cosine, sine
@@ -185,14 +183,22 @@
 
 
 def solution(mesh):
+    seq_count = mesh.shape["seq"]
+    inner = math.gcd(seq_count, 8)
+    split_mesh = jax.sharding.Mesh(
+        mesh.devices.reshape(seq_count // inner, inner, mesh.shape["head"]), ("sx", "sz", "head")
+    )
+    rows = ("sx", "sz")
     in_specs = (
-        P("seq", "head"),
-        P("seq", "head"),
-        P("seq", "head"),
-        P("seq"),
+        P(rows, "head"),
+        P(rows, "head"),
+        P(rows, "head"),
+        P(rows),
         P("head", None, None),
         P("head", None, None),
         P("head"),
     )
-    out_specs = P(("seq", "head"), None)
-    return jax.shard_map(body, mesh=mesh, in_specs=in_specs, out_specs=out_specs, check_vma=False)
+    out_specs = P(("sx", "sz", "head"), None)
+    return jax.shard_map(
+        body, mesh=split_mesh, in_specs=in_specs, out_specs=out_specs, check_vma=False
+    )

time: 165 us -> 222 us (1.35)
  the two profiles are of different devices: /device:TPU:2 before, /device:TPU:160 now
where the time goes in v5:
time: 222 us; the launch traced here: 221 us
  waiting for transfers between devices  88.4 us (40%)
  other arithmetic  34.5 us (16%)
  matrix products  22.5 us (10%)
  local copies, waits for them, and re-layouts  22.3 us (10%)
  blocking collectives  20.1 us (9%)
  starting transfers between devices  19.6 us (9%)
  between operations  14 us (6%)
    psum x1, waiting for transfers between devices, body(): row_total = lax.psum(packed, 'sz')  68.3 us
    all_to_all x1, blocking collectives, body(): lax.all_to_all(result, 'head', split_axis=0, concat_axis=1, tiled=True)  20.1 us
    ppermute x7, waiting for transfers between devices, passed_along(): lax.ppermute(value, axis, [(source, source + steps) for source in range(f...  20 us
    ppermute x7, starting transfers between devices, passed_along(): lax.ppermute(value, axis, [(source, source + steps) for source in range(f...  19.6 us
    unnamed x74, local copies, waits for them, and re-layouts  11.3 us
    dot_general x1, matrix products, body(): jnp.einsum('gkij,jgd->igkd', weights.astype(jnp.bfloat16), ext_values, pr...  7.13 us
    another operation x3, other arithmetic  5.46 us
  transfers between devices with their start and end apart: 8, of which 3 were waited for; matrix products, arithmetic and copies ran while one was open for 23% of the time, Pallas kernels for 0%

profile of v5, /device:TPU:160, one launch (start us, length us, event | category | flops | bytes accessed | tf_op | source)
XLA Modules:
  0.0 221.4 jit_solution(13633600873984047340)
XLA Ops:
  6.5 0.8 add_bitcast_fusion
  7.3 1.0 copy.37
  8.4 2.4 %subtract_convert_fusion.3 = (bf16[512,1,64]{0,2,1:T(8,128)(2,1)S(1)}, bf16[512,1,64]{0,2,1:T(8,128)(2,1)S(1)}) fusion(f32[512,1,128]{0,2,1:T(8,128)S(1)} %bitcast_convert_fusion, f32[64]{0:T(128)} %constant.80.clone, f32[512]{0:T(512)S(1)} %get-tuple-element.27, f32[64]{0:T(128)} %constant.79.clone, f32[512]{0:T(512)S(1)} %get-tuple-element.26, ...), kind=kLoop, calls=%fused_computation.118 | loop fusion | flops 753664 | bytes 400128 | tf_op jit(solution)/shard_map/convert.6
  10.7 0.1 pad_maximum_fusion.13
  10.8 2.9 %collective-permute-start.1 = (bf16[64,1,128]{0,2,1:T(8,128)(2,1)S(1)}, bf16[64,1,128]{0,2,1:T(8,128)(2,1)S(1)}, u32[]{:S(2)}, u32[]{:S(2)}) collective-permute-start(bf16[64,1,128]{0,2,1:T(8,128)(2,1)S(1)} %pad_maximum_fusion.13), channel_id=1, source_target_pairs={{0,8},{8,16},{16,24},{24,32},{32,40},{40,48},{48,56},{56,64},{64,7... | collective-permute-start | bytes 49160 | tf_op jit(solution)/shard_map/ppermute | solution.py:17
  13.8 0.7 slice_bitcast_fusion
  14.5 2.9 %collective-permute-start = (bf16[64,1,128]{2,0,1:T(8,128)(2,1)S(1)}, bf16[64,1,128]{2,0,1:T(8,128)(2,1)S(1)}, u32[]{:S(2)}, u32[]{:S(2)}) collective-permute-start(bf16[64,1,128]{2,0,1:T(8,128)(2,1)S(1)} %slice_bitcast_fusion), channel_id=1, source_target_pairs={{0,8},{8,16},{16,24},{24,32},{32,40},{40,48},{48,56},{56,64},{64,7... | collective-permute-start | bytes 49160 | tf_op jit(solution)/shard_map/ppermute | solution.py:17
  17.4 2.9 %fusion.64 = (f32[512,64]{0,1:T(8,128)}, f32[512,64]{0,1:T(8,128)}) fusion(f32[64]{0:T(128)} %constant.80.clone, f32[512]{0:T(512)S(1)} %get-tuple-element.27, f32[64]{0:T(128)} %constant.79.clone, f32[512]{0:T(512)S(1)} %get-tuple-element.26, f32[64]{0:T(128)} %constant.78.clone, f32[512]{0:T(512)S(1)} %get-tuple-element.25), kind=kLoop, calls=%fused_computation.105 | loop fusion | flops 491520 | bytes 269056 | tf_op jit(solution)/shard_map/sub | solution.py:30
  20.3 1.2 broadcast_subtract_fusion
  21.6 2.4 %fusion.58 = f32[576,512]{0,1} fusion(bf16[128,512]{0,1:T(8,128)(2,1)} %bitcast.177, bf16[512,1,64]{0,2,1:T(8,128)(2,1)S(1)} %get-tuple-element.22, bf16[512,1,64]{0,2,1:T(8,128)(2,1)S(1)} %get-tuple-element.21, bf16[64,1,128]{0,2,1:T(8,128)(2,1)S(1)} %collective-permute-done.1), kind=kOutput, calls=%fused_computation.99 | convolution fusion | flops 75939840 | bytes 1458176
  24.0 2.3 %copy.39 = f32[576,8,64]{2,1,0:T(8,128)S(1)} copy(f32[576,8,64]{0,2,1:T(8,128)} %bitcast.171) | data formatting | bytes 2359296 | tf_op jit(solution)/shard_map/ngd,gkdf->ngkf/dot_general | solution.py:80
  26.3 1.3 bitcast_reduce_fusion
  27.6 3.6 %fusion.25 = (f32[576,8]{1,0:T(8,128)S(1)}, f32[576,8]{1,0:T(8,128)S(1)}) fusion(f32[576,8,64]{2,1,0:T(8,128)S(1)} %copy.39, f32[576,8]{1,0:T(8,128)S(1)} %get-tuple-element.9, f32[576,8]{1,0:T(8,128)S(1)} %get-tuple-element.10), kind=kLoop, calls=%fused_computation.39 | loop fusion | flops 1465344 | bytes 1253376 | tf_op jit(solution)/shard_map/reduce_sum | solution.py:48
  31.2 3.1 %fusion.24 = (bf16[576,1,8,64]{3,2,0,1:T(8,128)(2,1)S(1)}, bf16[576,1,8,64]{3,2,0,1:T(8,128)(2,1)S(1)}) fusion(f32[576,8,64]{2,1,0:T(8,128)S(1)} %copy.39, f32[576,8]{1,0:T(8,128)S(1)} %get-tuple-element.7, f32[576,8]{1,0:T(8,128)S(1)} %get-tuple-element.9, f32[576,8]{1,0:T(8,128)S(1)} %get-tuple-element.8, f32[576,8]{1,0:T(8,128)S(1)} %get-tuple-element.10), kind=kLoop, calls=%fused_computation.38 | loop fusion | flops 2064384 | bytes 2433024 | tf_op jit(solution)/shard_map/div | solution.py:48
  34.3 4.0 %convert_reduce_fusion = (f32[8,128]{1,0:T(8,128)S(1)}, bf16[512,1,8,128]{3,2,0,1:T(8,128)(2,1)S(1)}) fusion(bf16[576,1,8,64]{3,2,0,1:T(8,128)(2,1)S(1)} %get-tuple-element.18, bf16[576,1,8,64]{3,2,0,1:T(8,128)(2,1)S(1)} %get-tuple-element.17, pred[512]{0:T(512)(128)(4,1)S(1)} %slice-done), kind=kLoop, calls=%fused_computation.34 | loop fusion | flops 3668992 | bytes 2232832 | tf_op jit(solution)/shard_map/reduce_sum | solution.py:91
  38.4 0.5 fusion.36
  38.9 0.0 copy-done.31
  39.0 0.7 copy-done.11
  39.7 2.1 collective-permute-start.2
  41.8 0.6 iota_add_fusion
  42.3 1.7 copy.43
  44.1 1.7 copy.45
  45.8 1.8 fusion.33
  47.6 2.9 %fusion.14 = bf16[576,8,128]{2,1,0:T(8,128)(2,1)} fusion(bf16[576,8,64]{2,1,0:T(8,128)(2,1)S(1)} %bitcast.169, bf16[576,8,64]{2,1,0:T(8,128)(2,1)S(1)} %bitcast.168, pred[576]{0:T(1024)(128)(4,1)S(1)} %copy-done.26), kind=kLoop, calls=%fused_computation.18 | loop fusion | flops 2949120 | bytes 2359872 | tf_op jit(solution)/shard_map/convert_element_type | solution.py:83
  50.5 4.4 %collective-permute-done.2 = f32[132096]{0:T(1024)S(1)} collective-permute-done((f32[132096]{0:T(1024)S(1)}, f32[132096]{0:T(1024)S(1)}, u32[]{:S(2)}, u32[]{:S(2)}) %collective-permute-start.2) | collective-permute-done | bytes 528416 | tf_op jit(solution)/shard_map/ppermute | solution.py:17
  54.9 1.7 copy.41
  56.6 0.3 fusion.109
  56.9 1.9 copy.65
  58.8 1.9 copy.66
  60.8 2.8 %subtract_convert_fusion = (bf16[512,8,64]{2,0,1:T(8,128)(2,1)S(1)}, bf16[512,8,64]{2,0,1:T(8,128)(2,1)S(1)}) fusion(f32[512,8,64]{2,0,1:T(8,128)} %copy.66, f32[512,8,64]{2,0,1:T(8,128)} %copy.65, f32[512,64]{1,0:T(8,128)S(1)} %copy-done.19, f32[512,64]{1,0:T(8,128)S(1)} %copy-done.18), kind=kLoop, calls=%fused_computation.33 | loop fusion | flops 2097152 | bytes 3407872 | tf_op jit(solution)/shard_map/convert.4
  63.6 0.9 fusion.111
  64.5 1.9 fusion.110
  66.4 0.0 all-reduce.2.cloned.1.call-update
  66.4 2.1 fusion.107
  68.4 1.9 collective-permute-start.3
  70.4 3.5 %fusion.2 = (f32[8,512]{1,0:T(8,128)S(1)}, f32[576,512,8]{1,0,2:T(8,128)S(1)}) fusion(pred[512,576]{0,1:T(8,128)(4,1)} %get-tuple-element.29, bf16[512,8,64]{2,0,1:T(8,128)(2,1)S(1)} %get-tuple-element.16, bf16[512,8,64]{2,0,1:T(8,128)(2,1)S(1)} %get-tuple-element.15, bf16[512,1,64]{0,2,1:T(8,128)(2,1)S(1)} %copy-done.16, ...), kind=kOutput, calls=%fused_computation.4 | convolution fusion | flops 613593088 | bytes 10944512 | tf_op jit(solution)/shard_map/igkd,jgd->gkij/dot_general | solution.py:139
  73.9 3.7 %copy-done.1 = f32[576,512,8]{1,0,2:T(8,128)} copy-done((f32[576,512,8]{1,0,2:T(8,128)}, f32[576,512,8]{1,0,2:T(8,128)S(1)}, u32[]{:S(2)}) %copy-start.1) | copy-done | bytes 9437208
  77.6 1.9 fusion.5
  79.5 68.3 %all-reduce.2.cloned.1.call-done = f32[132096]{0:T(1024)} async-done(((f32[132096]{0:T(1024)}), f32[132096]{0:T(1024)}) %all-reduce.2.cloned.1.call-update) | async-done | bytes 528400 | tf_op jit(solution)/shard_map/psum | solution.py:118
  147.9 3.5 %collective-permute-start.5 = (f32[132096]{0:T(1024)}, f32[132096]{0:T(1024)S(1)}, u32[]{:S(2)}, u32[]{:S(2)}) collective-permute-start(f32[132096]{0:T(1024)} %all-reduce.2.cloned.1.call-done), channel_id=1, source_target_pairs={{0,64},{64,128},{128,192},{1,65},{65,129},{129,193},{2,66},{66,130... | collective-permute-start | bytes 1585160 | tf_op jit(solution)/shard_map/ppermute | solution.py:17
  151.4 7.1 %fusion.10 = f32[128,8,512]{2,0,1:T(8,128)} fusion(f32[576,512,8]{1,0,2:T(8,128)} %copy-done.1, f32[8,512]{1,0:T(8,128)S(1)} %get-tuple-element.34, pred[512,576]{0,1:T(8,128)(4,1)S(1)} %copy-done.7, bf16[64,1,128]{2,0,1:T(8,128)(2,1)S(1)} %copy-done.32, bf16[512,1,128]{2,0,1:T(8,128)(2,1)S(1)} %bitcast.182), kind=kOutput, calls=%fused_computation.14 | convolution fusion | flops 613711872 | bytes 11993088 | tf_op jit(solution)/shard_map/gkij,jgd->igkd/dot_general | solution.py:149
  158.6 1.3 add.179
  159.9 1.4 collective-permute-start.4
  161.4 0.1 add.181
  161.4 4.8 %collective-permute-start.6 = (f32[132096]{0:T(1024)S(1)}, f32[132096]{0:T(1024)S(1)}, u32[]{:S(2)}, u32[]{:S(2)}) collective-permute-start(f32[132096]{0:T(1024)S(1)} %add.181), channel_id=1, source_target_pairs={{0,128},{64,192},{1,129},{65,193},{2,130},{66,194},{3,131},{67,195... | collective-permute-start | bytes 1585160 | tf_op jit(solution)/shard_map/ppermute | solution.py:17
  166.3 0.3 divide_convert_fusion
  166.6 3.6 %select_reduce_fusion = (f32[8,512]{1,0:T(8,128)S(1)}, bf16[8,512,576]{1,2,0:T(8,128)(2,1)}) fusion(pred[512,576]{0,1:T(8,128)(4,1)S(1)} %copy-done.21, bf16[512,8,64]{0,2,1:T(8,128)(2,1)S(1)} %get-tuple-element.38, bf16[512,8,64]{0,2,1:T(8,128)(2,1)S(1)} %get-tuple-element.39, bf16[576,8,128]{2,1,0:T(8,128)(2,1)S(1)} %copy-done.12), kind=kOutput, calls=%fused_computation.7 | convolution fusion | flops 613150720 | bytes 7258112 | tf_op jit(solution)/shard_map/igkf,jgkf->gkij/dot_general | solution.py:146
  170.3 15.6 %collective-permute-done.4 = f32[132096]{0:T(1024)S(1)} collective-permute-done((f32[132096]{0:T(1024)S(1)}, f32[132096]{0:T(1024)S(1)}, u32[]{:S(2)}, u32[]{:S(2)}) %collective-permute-start.4) | collective-permute-done | bytes 528416 | tf_op jit(solution)/shard_map/ppermute | solution.py:17
  185.9 1.2 add_add_fusion
  187.2 0.2 copy.49
  187.4 0.4 fusion.39
  187.8 0.4 fusion.73
  188.3 0.2 fusion.82
  188.5 0.2 fusion.80
  188.8 0.5 copy-done.29
  189.3 0.1 fusion.78
  189.3 0.4 copy-done.34
  189.7 0.2 copy-done.22
  190.0 0.7 copy-done.33
  190.7 1.4 fusion.21
  192.2 0.8 copy.53
  192.9 0.5 all_to_all.14
  193.4 20.1 %all_to_all.19 = bf16[8,64,1024]{2,1,0:T(8,128)(2,1)S(1)} all-to-all(bf16[8,64,1024]{2,1,0:T(8,128)(2,1)S(1)} %all_to_all.14), channel_id=1, replica_groups=mesh['sx'=4,'sz'=8,'head'=8] {'head'}, dimensions={0} | all-to-all | bytes 2097152 | tf_op jit(solution)/shard_map/all_to_all | solution.py:182
  213.5 1.1 copy.67
  (79 shorter events, 0.3 us)
Async XLA Ops:
  6.5 57.1 %copy-start = (bf16[8,128,64]{1,2,0:T(8,128)(2,1)S(1)}, bf16[8,128,64]{1,2,0:T(8,128)(2,1)}, u32[]{:S(2)}) copy-start(bf16[8,128,64]{1,2,0:T(8,128)(2,1)} %param.14) | copy-start | bytes 393220
  10.7 13.2 %copy-start.13 = (bf16[512,1,64]{0,2,1:T(8,128)(2,1)}, bf16[512,1,64]{0,2,1:T(8,128)(2,1)S(1)}, u32[]{:S(2)}) copy-start(bf16[512,1,64]{0,2,1:T(8,128)(2,1)S(1)} %get-tuple-element.21) | copy-start | bytes 196612
  10.7 13.2 %copy-start.15 = (bf16[512,1,64]{0,2,1:T(8,128)(2,1)}, bf16[512,1,64]{0,2,1:T(8,128)(2,1)S(1)}, u32[]{:S(2)}) copy-start(bf16[512,1,64]{0,2,1:T(8,128)(2,1)S(1)} %get-tuple-element.22) | copy-start | bytes 196612
  10.8 10.7 %collective-permute-start.1 = (bf16[64,1,128]{0,2,1:T(8,128)(2,1)S(1)}, bf16[64,1,128]{0,2,1:T(8,128)(2,1)S(1)}, u32[]{:S(2)}, u32[]{:S(2)}) collective-permute-start(bf16[64,1,128]{0,2,1:T(8,128)(2,1)S(1)} %pad_maximum_fusion.13), channel_id=1, source_target_pairs={{0,8},{8,16},{16,24},{24,32},{32,40},{40,48},{48,56},{56,64},{64,7... | collective-permute-start | bytes 49160 | tf_op jit(solution)/shard_map/ppermute | solution.py:17
  14.5 23.9 %collective-permute-start = (bf16[64,1,128]{2,0,1:T(8,128)(2,1)S(1)}, bf16[64,1,128]{2,0,1:T(8,128)(2,1)S(1)}, u32[]{:S(2)}, u32[]{:S(2)}) collective-permute-start(bf16[64,1,128]{2,0,1:T(8,128)(2,1)S(1)} %slice_bitcast_fusion), channel_id=1, source_target_pairs={{0,8},{8,16},{16,24},{24,32},{32,40},{40,48},{48,56},{56,64},{64,7... | collective-permute-start | bytes 49160 | tf_op jit(solution)/shard_map/ppermute | solution.py:17
  21.6 4.7 %copy-start.25 = (pred[576]{0:T(1024)(128)(4,1)}, pred[576]{0:T(1024)(128)(4,1)S(1)}, u32[]{:S(2)}) copy-start(pred[576]{0:T(1024)(128)(4,1)S(1)} %fusion.85) | copy-start | bytes 1732
  21.6 2.4 %copy-start.23 = (bf16[64,1,128]{0,2,1:T(8,128)(2,1)}, bf16[64,1,128]{0,2,1:T(8,128)(2,1)S(1)}, u32[]{:S(2)}) copy-start(bf16[64,1,128]{0,2,1:T(8,128)(2,1)S(1)} %collective-permute-done.1) | copy-start | bytes 49156
  31.2 3.2 %slice-start = ((pred[576]{0:T(1024)(128)(4,1)}), pred[512]{0:T(512)(128)(4,1)S(1)}, s32[]{:S(2)}) async-start(pred[576]{0:T(1024)(128)(4,1)} %copy-done.25), calls=%async_computation.2 | async-start | bytes 1024 | tf_op jit(solution)/shard_map/slice | solution.py:86
  34.3 4.5 %copy-start.2 = (bf16[576,1,8,64]{3,2,0,1:T(8,128)(2,1)}, bf16[576,1,8,64]{3,2,0,1:T(8,128)(2,1)S(1)}, u32[]{:S(2)}) copy-start(bf16[576,1,8,64]{3,2,0,1:T(8,128)(2,1)S(1)} %get-tuple-element.17) | copy-start | bytes 1769476
  34.3 4.5 %copy-start.4 = (bf16[576,1,8,64]{3,2,0,1:T(8,128)(2,1)}, bf16[576,1,8,64]{3,2,0,1:T(8,128)(2,1)S(1)}, u32[]{:S(2)}) copy-start(bf16[576,1,8,64]{3,2,0,1:T(8,128)(2,1)S(1)} %get-tuple-element.18) | copy-start | bytes 1769476
  34.3 4.0 %copy-start.27 = (bf16[512,128]{1,0:T(8,128)(2,1)S(1)}, bf16[512,128]{1,0:T(8,128)(2,1)}, u32[]{:S(2)}) copy-start(bf16[512,128]{1,0:T(8,128)(2,1)} %param.12) | copy-start | bytes 393220
  38.3 7.5 %copy-start.26 = (pred[576]{0:T(1024)(128)(4,1)S(1)}, pred[576]{0:T(1024)(128)(4,1)}, u32[]{:S(2)}) copy-start(pred[576]{0:T(1024)(128)(4,1)} %copy-done.25) | copy-start | bytes 1732
  38.3 0.6 copy-start.31
  38.9 0.8 copy-start.11
  38.9 8.8 %copy-start.3 = (bf16[576,1,8,64]{3,2,0,1:T(8,128)(2,1)S(1)}, bf16[576,1,8,64]{3,2,0,1:T(8,128)(2,1)}, u32[]{:S(2)}) copy-start(bf16[576,1,8,64]{3,2,0,1:T(8,128)(2,1)} %copy-done.2) | copy-start | bytes 1769476
  38.9 8.8 %copy-start.5 = (bf16[576,1,8,64]{3,2,0,1:T(8,128)(2,1)S(1)}, bf16[576,1,8,64]{3,2,0,1:T(8,128)(2,1)}, u32[]{:S(2)}) copy-start(bf16[576,1,8,64]{3,2,0,1:T(8,128)(2,1)} %copy-done.4) | copy-start | bytes 1769476
  39.7 10.9 %copy-start.8 = (f32[132096]{0:T(1024)}, f32[132096]{0:T(1024)S(1)}, u32[]{:S(2)}) copy-start(f32[132096]{0:T(1024)S(1)} %pad_maximum_fusion.3) | copy-start | bytes 1585156
  39.7 15.2 %collective-permute-start.2 = (f32[132096]{0:T(1024)S(1)}, f32[132096]{0:T(1024)S(1)}, u32[]{:S(2)}, u32[]{:S(2)}) collective-permute-start(f32[132096]{0:T(1024)S(1)} %pad_maximum_fusion.3), channel_id=1, source_target_pairs={{0,8},{8,16},{16,24},{24,32},{32,40},{40,48},{48,56},{1,9},{9,17},... | collective-permute-start | bytes 1585160 | tf_op jit(solution)/shard_map/ppermute | solution.py:17
  54.9 1.7 copy-start.9
  54.9 92.9 %all-reduce.2.cloned.1.call-start = ((), (), s32[]{:S(2)}) async-start(), calls=%async_computation.1 | async-start | bytes 1056768 | tf_op jit(solution)/shard_map/psum | solution.py:118
  58.8 2.0 copy-start.18
  58.8 2.0 copy-start.19
  64.5 5.9 %copy-start.14 = (bf16[512,1,64]{0,2,1:T(8,128)(2,1)S(1)}, bf16[512,1,64]{0,2,1:T(8,128)(2,1)}, u32[]{:S(2)}) copy-start(bf16[512,1,64]{0,2,1:T(8,128)(2,1)} %copy-done.13) | copy-start | bytes 196612
  64.5 5.9 %copy-start.16 = (bf16[512,1,64]{0,2,1:T(8,128)(2,1)S(1)}, bf16[512,1,64]{0,2,1:T(8,128)(2,1)}, u32[]{:S(2)}) copy-start(bf16[512,1,64]{0,2,1:T(8,128)(2,1)} %copy-done.15) | copy-start | bytes 196612
  64.5 5.9 %copy-start.24 = (bf16[64,1,128]{0,2,1:T(8,128)(2,1)S(1)}, bf16[64,1,128]{0,2,1:T(8,128)(2,1)}, u32[]{:S(2)}) copy-start(bf16[64,1,128]{0,2,1:T(8,128)(2,1)} %copy-done.23) | copy-start | bytes 49156
  68.4 90.1 %collective-permute-start.3 = (f32[132096]{0:T(1024)}, f32[132096]{0:T(1024)}, u32[]{:S(2)}, u32[]{:S(2)}) collective-permute-start(f32[132096]{0:T(1024)} %fusion.107), channel_id=1, source_target_pairs={{0,16},{8,24},{16,32},{24,40},{32,48},{40,56},{1,17},{9,25},{17,33... | collective-permute-start | bytes 1585160 | tf_op jit(solution)/shard_map/ppermute | solution.py:17
  70.4 7.2 %copy-start.6 = (pred[512,576]{0,1:T(8,128)(4,1)S(1)}, pred[512,576]{0,1:T(8,128)(4,1)}, u32[]{:S(2)}) copy-start(pred[512,576]{0,1:T(8,128)(4,1)} %get-tuple-element.29) | copy-start | bytes 884740
  73.9 3.7 %copy-start.1 = (f32[576,512,8]{1,0,2:T(8,128)}, f32[576,512,8]{1,0,2:T(8,128)S(1)}, u32[]{:S(2)}) copy-start(f32[576,512,8]{1,0,2:T(8,128)S(1)} %get-tuple-element.35) | copy-start | bytes 28311556
  77.6 73.8 %copy-start.7 = (pred[512,576]{0,1:T(8,128)(4,1)S(1)}, pred[512,576]{0,1:T(8,128)(4,1)}, u32[]{:S(2)}) copy-start(pred[512,576]{0,1:T(8,128)(4,1)} %get-tuple-element.29) | copy-start | bytes 884740
  77.6 73.8 %copy-start.28 = (bf16[512,128]{1,0:T(8,128)(2,1)S(1)}, bf16[512,128]{1,0:T(8,128)(2,1)}, u32[]{:S(2)}) copy-start(bf16[512,128]{1,0:T(8,128)(2,1)} %param.12) | copy-start | bytes 393220
  77.6 73.9 %copy-start.32 = (bf16[64,1,128]{2,0,1:T(8,128)(2,1)S(1)}, bf16[64,1,128]{2,0,1:T(8,128)(2,1)}, u32[]{:S(2)}) copy-start(bf16[64,1,128]{2,0,1:T(8,128)(2,1)} %copy-done.31) | copy-start | bytes 49156
  147.9 13.5 %copy-start.20 = (f32[132096]{0:T(1024)S(1)}, f32[132096]{0:T(1024)}, u32[]{:S(2)}) copy-start(f32[132096]{0:T(1024)} %all-reduce.2.cloned.1.call-done) | copy-start | bytes 1585156
  147.9 13.5 %collective-permute-start.5 = (f32[132096]{0:T(1024)}, f32[132096]{0:T(1024)S(1)}, u32[]{:S(2)}, u32[]{:S(2)}) collective-permute-start(f32[132096]{0:T(1024)} %all-reduce.2.cloned.1.call-done), channel_id=1, source_target_pairs={{0,64},{64,128},{128,192},{1,65},{65,129},{129,193},{2,66},{66,130... | collective-permute-start | bytes 1585160 | tf_op jit(solution)/shard_map/ppermute | solution.py:17
  158.6 7.7 %copy-start.17 = (f32[512,8,64]{0,2,1:T(8,128)S(1)}, f32[512,8,64]{0,2,1:T(8,128)}, u32[]{:S(2)}) copy-start(f32[512,8,64]{0,2,1:T(8,128)} %get-tuple-element.31) | copy-start | bytes 3145732
  159.9 6.7 %copy-start.12 = (bf16[576,8,128]{2,1,0:T(8,128)(2,1)S(1)}, bf16[576,8,128]{2,1,0:T(8,128)(2,1)}, u32[]{:S(2)}) copy-start(bf16[576,8,128]{2,1,0:T(8,128)(2,1)} %fusion.14) | copy-start | bytes 3538948
  159.9 6.7 %copy-start.21 = (pred[512,576]{0,1:T(8,128)(4,1)S(1)}, pred[512,576]{0,1:T(8,128)(4,1)}, u32[]{:S(2)}) copy-start(pred[512,576]{0,1:T(8,128)(4,1)} %get-tuple-element.28) | copy-start | bytes 884740
  159.9 26.0 %collective-permute-start.4 = (f32[132096]{0:T(1024)S(1)}, f32[132096]{0:T(1024)S(1)}, u32[]{:S(2)}, u32[]{:S(2)}) collective-permute-start(f32[132096]{0:T(1024)S(1)} %add.179), channel_id=1, source_target_pairs={{0,32},{8,40},{16,48},{24,56},{1,33},{9,41},{17,49},{25,57},{2,34}... | collective-permute-start | bytes 1585160 | tf_op jit(solution)/shard_map/ppermute | solution.py:17
  161.4 24.5 %collective-permute-start.6 = (f32[132096]{0:T(1024)S(1)}, f32[132096]{0:T(1024)S(1)}, u32[]{:S(2)}, u32[]{:S(2)}) collective-permute-start(f32[132096]{0:T(1024)S(1)} %add.181), channel_id=1, source_target_pairs={{0,128},{64,192},{1,129},{65,193},{2,130},{66,194},{3,131},{67,195... | collective-permute-start | bytes 1585160 | tf_op jit(solution)/shard_map/ppermute | solution.py:17
  166.6 19.3 %copy-start.10 = (f32[132096]{0:T(1024)S(1)}, f32[132096]{0:T(1024)}, u32[]{:S(2)}) copy-start(f32[132096]{0:T(1024)} %copy-done.9) | copy-start | bytes 1585156
  187.4 2.3 %copy-start.34 = (bf16[8,512,576]{1,2,0:T(8,128)(2,1)S(1)}, bf16[8,512,576]{1,2,0:T(8,128)(2,1)}, u32[]{:S(2)}) copy-start(bf16[8,512,576]{1,2,0:T(8,128)(2,1)} %get-tuple-element.37) | copy-start | bytes 14155780
  188.2 1.0 copy-start.29
  188.2 1.0 copy-start.30
  188.3 1.7 copy-start.22
  188.3 2.5 %copy-start.33 = (f32[128,8,512]{2,0,1:T(8,128)S(1)}, f32[128,8,512]{2,0,1:T(8,128)}, u32[]{:S(2)}) copy-start(f32[128,8,512]{2,0,1:T(8,128)} %fusion.10) | copy-start | bytes 6291460
Sparse Core Ops, SparseCore 0:
  66.5 81.3 all-reduce.1

commit v6 on v3

--- a/solution.py
+++ b/solution.py
@@ -69,9 +69,13 @@
         keys.reshape(tokens, kv_local, head_dim).astype(jnp.float32), cosine, sine
     ).astype(jnp.bfloat16)
     value_rows = values.reshape(tokens, kv_local, head_dim)
-    tail_keys, tail_values = passed_along(
-        (rot_k[tokens - WINDOW :], value_rows[tokens - WINDOW :]), "seq", 1
-    )
+    tail_both = passed_along(
+        jnp.concatenate([rot_k[tokens - WINDOW :], value_rows[tokens - WINDOW :]], axis=-1),
+        "seq",
+        1,
+    )
+    tail_keys = tail_both[..., :head_dim]
+    tail_values = tail_both[..., head_dim:]
     ext_keys = jnp.concatenate([tail_keys, rot_k], axis=0)
     ext_values = jnp.concatenate([tail_values, value_rows], axis=0)
     valid = (jnp.arange(tokens + WINDOW) >= WINDOW) | (lax.axis_index("seq") > 0)

time: 165 us -> 174 us (1.055)
  waiting for transfers between devices: 32.2 us -> 38.1 us
  local copies, waits for them, and re-layouts: 15.1 us -> 18.1 us
    ppermute x12 -> x11, waiting for transfers between devices: 32.2 us -> 38.1 us  [passed_along(): lax.ppermute(value, axis, [(source, source + steps) for source in range(f...]
    unnamed x72 -> x67, local copies, waits for them, and re-layouts: 7.08 us -> 9.9 us
    dot_general x1, matrix products: 3.51 us -> 6.17 us  [body(): jnp.einsum('gkij,jgd->igkd', weights.astype(jnp.bfloat16), ext_values, pr...]
    dot_general x1, matrix products: 3.64 us -> 1.52 us  [body(): jnp.einsum('igkf,jgkf->gkij', phi_query, phi_key, preferred_element_type=...]
    ppermute x12 -> x11, starting transfers between devices: 39.7 us -> 41.2 us  [passed_along(): lax.ppermute(value, axis, [(source, source + steps) for source in range(f...]
  transfers between devices with their start and end apart: 12 -> 11, of which waited for: 6 -> 6; matrix products, arithmetic and copies ran while one was open for 31% -> 20% of each run, Pallas kernels for 0% -> 0%
where the time goes in v6:
time: 174 us; the launch traced here: 173 us
  starting transfers between devices  41.2 us (24%)
  waiting for transfers between devices  38.1 us (22%)
  other arithmetic  34.9 us (20%)
  blocking collectives  20.3 us (12%)
  matrix products  19.9 us (11%)
  local copies, waits for them, and re-layouts  18.1 us (10%)
    ppermute x11, starting transfers between devices, passed_along(): lax.ppermute(value, axis, [(source, source + steps) for source in range(f...  41.2 us
    ppermute x11, waiting for transfers between devices, passed_along(): lax.ppermute(value, axis, [(source, source + steps) for source in range(f...  38.1 us
    all_to_all x1, blocking collectives, body(): lax.all_to_all(result, 'head', split_axis=0, concat_axis=1, tiled=True)  20.3 us
    unnamed x67, local copies, waits for them, and re-layouts  9.9 us
    another operation x3, other arithmetic  6.32 us
    dot_general x1, matrix products, body(): jnp.einsum('gkij,jgd->igkd', weights.astype(jnp.bfloat16), ext_values, pr...  6.17 us
    convert_element_type x1, other arithmetic, body(): jnp.where(valid[:, None, None, None], two_softmax(key_logits), 0.0)  4.38 us
    reduce_sum x1, other arithmetic, body(): block_norms = jnp.sum(lag_phi, axis=1, dtype=jnp.float32)  3.97 us
  transfers between devices with their start and end apart: 11, of which 6 were waited for; matrix products, arithmetic and copies ran while one was open for 20% of the time, Pallas kernels for 0%

profile of v6, /device:TPU:2, one launch (start us, length us, event | category | flops | bytes accessed | tf_op | source)
XLA Modules:
  0.0 173.2 jit_solution(2997060235024623168)
XLA Ops:
  0.0 0.8 add_bitcast_fusion
  0.8 0.7 slice.60
  1.6 1.0 copy.37
  2.7 2.4 %subtract_convert_fusion.3 = (bf16[512,1,64]{0,2,1:T(8,128)(2,1)S(1)}, bf16[512,1,64]{0,2,1:T(8,128)(2,1)S(1)}) fusion(f32[512,1,128]{0,2,1:T(8,128)S(1)} %bitcast_convert_fusion, f32[64]{0:T(128)} %constant.76.clone, f32[512]{0:T(512)S(1)} %get-tuple-element.31, f32[64]{0:T(128)} %constant.75.clone, f32[512]{0:T(512)S(1)} %get-tuple-element.30, ...), kind=kLoop, calls=%fused_computation.120 | loop fusion | flops 753664 | bytes 400128 | tf_op jit(solution)/shard_map/convert.6
  5.2 3.8 %collective-permute-start = (bf16[64,1,256]{0,2,1:T(8,128)(2,1)S(1)}, bf16[64,1,256]{0,2,1:T(8,128)(2,1)S(1)}, u32[]{:S(2)}, u32[]{:S(2)}) collective-permute-start(bf16[64,1,256]{0,2,1:T(8,128)(2,1)S(1)} %fusion.79), channel_id=1, source_target_pairs={{0,8},{8,16},{16,24},{24,32},{32,40},{40,48},{48,56},{56,64},{64,7... | collective-permute-start | bytes 98312 | tf_op jit(solution)/shard_map/ppermute | solution.py:16
  9.0 1.1 fusion.37
  10.2 2.2 %fusion.66 = (f32[512,64]{0,1:T(8,128)S(1)}, f32[512,64]{0,1:T(8,128)S(1)}) fusion(f32[64]{0:T(128)} %constant.76.clone, f32[512]{0:T(512)S(1)} %get-tuple-element.31, f32[64]{0:T(128)} %constant.75.clone, f32[512]{0:T(512)S(1)} %get-tuple-element.30, f32[64]{0:T(128)} %constant.74.clone, f32[512]{0:T(512)S(1)} %get-tuple-element.29), kind=kLoop, calls=%fused_computation.107 | loop fusion | flops 491520 | bytes 269056 | tf_op jit(solution)/shard_map/sub | solution.py:29
  12.3 2.8 %collective-permute-done = bf16[64,1,256]{0,2,1:T(8,128)(2,1)S(1)} collective-permute-done((bf16[64,1,256]{0,2,1:T(8,128)(2,1)S(1)}, bf16[64,1,256]{0,2,1:T(8,128)(2,1)S(1)}, u32[]{:S(2)}, u32[]{:S(2)}) %collective-permute-start) | collective-permute-done | bytes 32800 | tf_op jit(solution)/shard_map/ppermute | solution.py:16
  15.2 1.5 fusion.60
  16.7 2.3 %copy.41 = f32[576,8,64]{2,1,0:T(8,128)S(1)} copy(f32[576,8,64]{0,2,1:T(8,128)} %bitcast.174) | data formatting | bytes 2359296 | tf_op jit(solution)/shard_map/ngd,gkdf->ngkf/dot_general | solution.py:83
  19.0 1.3 bitcast_reduce_fusion
  20.3 3.6 %fusion.25 = (f32[576,8]{1,0:T(8,128)S(1)}, f32[576,8]{1,0:T(8,128)S(1)}) fusion(f32[576,8,64]{2,1,0:T(8,128)S(1)} %copy.41, f32[576,8]{1,0:T(8,128)S(1)} %get-tuple-element.9, f32[576,8]{1,0:T(8,128)S(1)} %get-tuple-element.10), kind=kLoop, calls=%fused_computation.39 | loop fusion | flops 1465344 | bytes 1253376 | tf_op jit(solution)/shard_map/reduce_sum | solution.py:47
  24.0 3.1 %fusion.24 = (bf16[576,1,8,64]{3,2,0,1:T(8,128)(2,1)S(1)}, bf16[576,1,8,64]{3,2,0,1:T(8,128)(2,1)S(1)}) fusion(f32[576,8,64]{2,1,0:T(8,128)S(1)} %copy.41, f32[576,8]{1,0:T(8,128)S(1)} %get-tuple-element.7, f32[576,8]{1,0:T(8,128)S(1)} %get-tuple-element.9, f32[576,8]{1,0:T(8,128)S(1)} %get-tuple-element.8, f32[576,8]{1,0:T(8,128)S(1)} %get-tuple-element.10), kind=kLoop, calls=%fused_computation.38 | loop fusion | flops 2064384 | bytes 2433024 | tf_op jit(solution)/shard_map/div | solution.py:47
  27.1 4.0 %convert_reduce_fusion = (f32[8,128]{1,0:T(8,128)S(1)}, bf16[512,1,8,128]{3,2,0,1:T(8,128)(2,1)S(1)}) fusion(bf16[576,1,8,64]{3,2,0,1:T(8,128)(2,1)S(1)} %get-tuple-element.18, bf16[576,1,8,64]{3,2,0,1:T(8,128)(2,1)S(1)} %get-tuple-element.17, pred[512]{0:T(512)(128)(4,1)S(1)} %slice-done), kind=kLoop, calls=%fused_computation.32 | loop fusion | flops 3668992 | bytes 2232832 | tf_op jit(solution)/shard_map/reduce_sum | solution.py:94
  31.1 0.5 fusion.38
  31.7 2.1 %collective-permute-start.1 = (f32[66048]{0:T(1024)S(1)}, f32[66048]{0:T(1024)S(1)}, u32[]{:S(2)}, u32[]{:S(2)}) collective-permute-start(f32[66048]{0:T(1024)S(1)} %slice.80), channel_id=1, source_target_pairs={{0,8},{8,16},{16,24},{24,32},{32,40},{40,48},{48,56},{56,64},{64,7... | collective-permute-start | bytes 792584 | tf_op jit(solution)/shard_map/ppermute | solution.py:16
  33.8 0.9 copy.45
  34.6 0.8 copy.47
  35.4 4.4 %fusion.14 = bf16[576,8,128]{2,1,0:T(8,128)(2,1)} fusion(bf16[576,8,64]{2,1,0:T(8,128)(2,1)} %bitcast.172, bf16[576,8,64]{2,1,0:T(8,128)(2,1)S(1)} %bitcast.171, pred[576]{0:T(1024)(128)(4,1)S(1)} %copy-done.26), kind=kLoop, calls=%fused_computation.18 | loop fusion | flops 2949120 | bytes 2359872 | tf_op jit(solution)/shard_map/convert_element_type | solution.py:86
  39.8 3.2 %collective-permute-done.1 = f32[66048]{0:T(1024)S(1)} collective-permute-done((f32[66048]{0:T(1024)S(1)}, f32[66048]{0:T(1024)S(1)}, u32[]{:S(2)}, u32[]{:S(2)}) %collective-permute-start.1) | collective-permute-done | bytes 264224 | tf_op jit(solution)/shard_map/ppermute | solution.py:16
  43.1 0.8 slice_add_fusion
  43.9 2.3 %collective-permute-start.2 = (f32[66048]{0:T(1024)}, f32[66048]{0:T(1024)}, u32[]{:S(2)}, u32[]{:S(2)}) collective-permute-start(f32[66048]{0:T(1024)} %get-tuple-element.21), channel_id=1, source_target_pairs={{0,16},{8,24},{16,32},{24,40},{32,48},{40,56},{48,64},{56,72},{64,... | collective-permute-start | bytes 792584 | tf_op jit(solution)/shard_map/ppermute | solution.py:16
  46.2 3.6 %collective-permute-start.6 = (f32[66048]{0:T(1024)}, f32[66048]{0:T(1024)}, u32[]{:S(2)}, u32[]{:S(2)}) collective-permute-start(f32[66048]{0:T(1024)} %get-tuple-element.22), channel_id=1, source_target_pairs={{0,64},{8,72},{16,80},{24,88},{32,96},{40,104},{48,112},{56,120},{... | collective-permute-start | bytes 792584 | tf_op jit(solution)/shard_map/ppermute | solution.py:16
  49.8 0.5 copy.43
  50.4 0.3 fusion.110
  50.6 1.9 %copy.69 = f32[512,8,64]{2,0,1:T(8,128)} copy(f32[512,8,64]{0,2,1:T(8,128)S(1)} %get-tuple-element.19) | data formatting | bytes 2097152
  52.6 1.9 %copy.68 = f32[512,8,64]{2,0,1:T(8,128)} copy(f32[512,8,64]{0,2,1:T(8,128)S(1)} %get-tuple-element.20) | data formatting | bytes 2097152
  54.5 2.8 %subtract_convert_fusion = (bf16[512,8,64]{2,0,1:T(8,128)(2,1)S(1)}, bf16[512,8,64]{2,0,1:T(8,128)(2,1)S(1)}) fusion(f32[512,8,64]{2,0,1:T(8,128)} %copy.69, f32[512,8,64]{2,0,1:T(8,128)} %copy.68, f32[512,64]{1,0:T(8,128)S(1)} %copy-done.15, f32[512,64]{1,0:T(8,128)S(1)} %copy-done.14), kind=kLoop, calls=%fused_computation.34 | loop fusion | flops 2097152 | bytes 3407872 | tf_op jit(solution)/shard_map/convert.4
  57.4 2.6 %fusion.2 = (f32[8,512]{1,0:T(8,128)S(1)}, f32[576,512,8]{1,0,2:T(8,128)S(1)}) fusion(pred[512,576]{0,1:T(8,128)(4,1)S(1)} %copy-done.5, bf16[512,8,64]{2,0,1:T(8,128)(2,1)S(1)} %get-tuple-element.16, bf16[512,8,64]{2,0,1:T(8,128)(2,1)S(1)} %get-tuple-element.15, bf16[512,1,64]{0,2,1:T(8,128)(2,1)S(1)} %copy-done.11, bf16[512,1,64]{0,2,1:T(8,128)(2,1)S(1)} %copy-done.9, ...), kind=kOutput, calls=%fused_computation.4 | convolution fusion | flops 613593088 | bytes 10944512 | tf_op jit(solution)/shard_map/igkd,jgd->gkij/dot_general | solution.py:145
  60.0 3.7 %copy-done.1 = f32[576,512,8]{1,0,2:T(8,128)} copy-done((f32[576,512,8]{1,0,2:T(8,128)}, f32[576,512,8]{1,0,2:T(8,128)S(1)}, u32[]{:S(2)}) %copy-start.1) | copy-done | bytes 9437208
  63.7 2.5 %fusion.5 = f32[8,512]{1,0:T(8,128)} fusion(f32[576,512,8]{1,0,2:T(8,128)S(1)} %get-tuple-element.39, f32[8,512]{1,0:T(8,128)S(1)} %get-tuple-element.38, pred[512,576]{0,1:T(8,128)(4,1)S(1)} %copy-done.5), kind=kLoop, calls=%fused_computation.9 | loop fusion | flops 9433088 | bytes 9764864 | tf_op jit(solution)/shard_map/reduce_sum | solution.py:151
  66.2 2.5 %fusion.112 = (f32[512,8]{0,1:T(8,128)}, f32[512,8,64]{0,2,1:T(8,128)}) fusion(bf16[8,128,64]{1,2,0:T(8,128)(2,1)S(1)} %copy-done, bf16[512,8,64]{2,0,1:T(8,128)(2,1)S(1)} %get-tuple-element.16, bf16[512,8,64]{2,0,1:T(8,128)(2,1)S(1)} %get-tuple-element.15), kind=kOutput, calls=%fused_computation.176 | convolution fusion | flops 69992512 | bytes 2244608 | tf_op jit(solution)/shard_map/sub | solution.py:47
  68.7 1.5 fusion.113
  70.1 1.1 add.201
  71.3 5.0 %collective-permute-start.3 = (f32[66048]{0:T(1024)S(1)}, f32[66048]{0:T(1024)S(1)}, u32[]{:S(2)}, u32[]{:S(2)}) collective-permute-start(f32[66048]{0:T(1024)S(1)} %add.201), channel_id=1, source_target_pairs={{0,32},{8,40},{16,48},{24,56},{32,64},{40,72},{48,80},{56,88},{64,... | collective-permute-start | bytes 792584 | tf_op jit(solution)/shard_map/ppermute | solution.py:16
  76.3 1.1 add.207
  77.4 1.9 %collective-permute-start.7 = (f32[66048]{0:T(1024)S(1)}, f32[66048]{0:T(1024)S(1)}, u32[]{:S(2)}, u32[]{:S(2)}) collective-permute-start(f32[66048]{0:T(1024)S(1)} %add.207), channel_id=1, source_target_pairs={{0,128},{8,136},{16,144},{24,152},{32,160},{40,168},{48,176},{56,1... | collective-permute-start | bytes 792584 | tf_op jit(solution)/shard_map/ppermute | solution.py:16
  79.3 1.1 divide_convert_fusion
  80.5 4.9 %collective-permute-done.3 = f32[66048]{0:T(1024)S(1)} collective-permute-done((f32[66048]{0:T(1024)S(1)}, f32[66048]{0:T(1024)S(1)}, u32[]{:S(2)}, u32[]{:S(2)}) %collective-permute-start.3) | collective-permute-done | bytes 264224 | tf_op jit(solution)/shard_map/ppermute | solution.py:16
  85.5 3.3 %collective-permute-start.4 = (f32[66048]{0:T(1024)S(1)}, f32[66048]{0:T(1024)S(1)}, u32[]{:S(2)}, u32[]{:S(2)}) collective-permute-start(f32[66048]{0:T(1024)S(1)} %add.203), channel_id=1, source_target_pairs={{0,64},{8,72},{16,80},{24,88},{32,96},{40,104},{48,112},{56,120},{... | collective-permute-start | bytes 792584 | tf_op jit(solution)/shard_map/ppermute | solution.py:16
  88.8 9.3 %collective-permute-start.8 = (f32[66048]{0:T(1024)S(1)}, f32[66048]{0:T(1024)S(1)}, u32[]{:S(2)}, u32[]{:S(2)}) collective-permute-start(f32[66048]{0:T(1024)S(1)} %add.209), channel_id=1, source_target_pairs={{0,8},{8,16},{16,24},{24,32},{32,40},{40,48},{48,56},{56,64},{64,7... | collective-permute-start | bytes 792584 | tf_op jit(solution)/shard_map/ppermute | solution.py:16
  98.2 1.5 select_reduce_fusion
  99.7 2.6 %collective-permute-done.4 = f32[66048]{0:T(1024)S(1)} collective-permute-done((f32[66048]{0:T(1024)S(1)}, f32[66048]{0:T(1024)S(1)}, u32[]{:S(2)}, u32[]{:S(2)}) %collective-permute-start.4) | collective-permute-done | bytes 264224 | tf_op jit(solution)/shard_map/ppermute | solution.py:16
  102.3 1.3 collective-permute-start.5
  103.7 4.1 %collective-permute-start.9 = (f32[66048]{0:T(1024)S(1)}, f32[66048]{0:T(1024)S(1)}, u32[]{:S(2)}, u32[]{:S(2)}) collective-permute-start(f32[66048]{0:T(1024)S(1)} %add.211), channel_id=1, source_target_pairs={{0,16},{8,24},{16,32},{24,40},{32,48},{40,56},{48,64},{56,72},{64,... | collective-permute-start | bytes 792584 | tf_op jit(solution)/shard_map/ppermute | solution.py:16
  107.7 2.4 %fusion.8 = f32[128,8,512]{2,0,1:T(8,128)} fusion(bf16[8,512,576]{1,2,0:T(8,128)(2,1)S(1)} %get-tuple-element.41, pred[512,576]{0,1:T(8,128)(4,1)S(1)} %copy-done.18, bf16[64,1,128]{2,0,1:T(8,128)(2,1)S(1)} %copy-done.24, bf16[512,1,128]{2,0,1:T(8,128)(2,1)S(1)} %bitcast.185), kind=kOutput, calls=%fused_computation.12 | convolution fusion | flops 606633984 | bytes 7258112 | tf_op jit(solution)/shard_map/gkij,jgd->igkd/dot_general | solution.py:161
  110.2 9.5 %collective-permute-done.9 = f32[66048]{0:T(1024)S(1)} collective-permute-done((f32[66048]{0:T(1024)S(1)}, f32[66048]{0:T(1024)S(1)}, u32[]{:S(2)}, u32[]{:S(2)}) %collective-permute-start.9) | collective-permute-done | bytes 264224 | tf_op jit(solution)/shard_map/ppermute | solution.py:16
  119.7 4.6 %collective-permute-start.10 = (f32[66048]{0:T(1024)S(1)}, f32[66048]{0:T(1024)S(1)}, u32[]{:S(2)}, u32[]{:S(2)}) collective-permute-start(f32[66048]{0:T(1024)S(1)} %add.213), channel_id=1, source_target_pairs={{0,32},{8,40},{16,48},{24,56},{32,64},{40,72},{48,80},{56,88},{64,... | collective-permute-start | bytes 792584 | tf_op jit(solution)/shard_map/ppermute | solution.py:16
  124.3 1.1 add_add_fusion.1
  125.4 15.1 %collective-permute-done.10 = f32[66048]{0:T(1024)S(1)} collective-permute-done((f32[66048]{0:T(1024)S(1)}, f32[66048]{0:T(1024)S(1)}, u32[]{:S(2)}, u32[]{:S(2)}) %collective-permute-start.10) | collective-permute-done | bytes 264224 | tf_op jit(solution)/shard_map/ppermute | solution.py:16
  140.5 1.0 add_add_fusion
  141.6 0.2 copy.51
  141.8 0.4 fusion.75
  142.2 0.4 fusion.41
  142.7 0.2 fusion.85
  142.9 0.2 fusion.83
  143.2 0.2 copy-done.22
  143.4 0.2 copy-done.6
  143.6 0.8 copy-done.30
  144.4 6.2 %fusion.21 = bf16[512,1,8,128]{0,3,2,1:T(8,128)(2,1)S(1)} fusion(f32[8,128,512]{2,1,0:T(8,128)S(1)} %fusion.75, f32[8,128,512]{2,1,0:T(8,128)S(1)} %fusion.41, f32[128,8,512]{2,0,1:T(8,128)S(1)} %copy-done.30, f32[576,512,8]{1,0,2:T(8,128)} %copy-done.1, f32[8,512]{1,0:T(8,128)S(1)} %copy-done.21, pred[512,576]{0,1:T(8,128)(4,1)S(1)} %copy-done.6, ...), kind=kOutput, calls=%fused_computation.35 | convolution fusion | flops 617381888 | bytes 17252416 | tf_op jit(solution)/shard_map/gkij,jgd->igkd/dot_general | solution.py:155
  150.6 0.8 copy.55
  151.3 0.5 all_to_all.14
  151.8 20.3 %all_to_all.19 = bf16[8,64,1024]{2,1,0:T(8,128)(2,1)S(1)} all-to-all(bf16[8,64,1024]{2,1,0:T(8,128)(2,1)S(1)} %all_to_all.14), channel_id=1, replica_groups=mesh['seq'=32,'head'=8] {'head'}, dimensions={0} | all-to-all | bytes 2097152 | tf_op jit(solution)/shard_map/all_to_all | solution.py:188
  172.1 1.1 copy.70
  (85 shorter events, 0.8 us)
Async XLA Ops:
  0.0 66.2 %copy-start = (bf16[8,128,64]{1,2,0:T(8,128)(2,1)S(1)}, bf16[8,128,64]{1,2,0:T(8,128)(2,1)}, u32[]{:S(2)}) copy-start(bf16[8,128,64]{1,2,0:T(8,128)(2,1)} %param.14) | copy-start | bytes 393220
  0.0 15.2 %copy-start.19 = (bf16[8,128,64]{1,2,0:T(8,128)(2,1)S(1)}, bf16[8,128,64]{1,2,0:T(8,128)(2,1)}, u32[]{:S(2)}) copy-start(bf16[8,128,64]{1,2,0:T(8,128)(2,1)} %param.15) | copy-start | bytes 393220
  5.0 11.7 %copy-start.8 = (bf16[512,1,64]{0,2,1:T(8,128)(2,1)}, bf16[512,1,64]{0,2,1:T(8,128)(2,1)S(1)}, u32[]{:S(2)}) copy-start(bf16[512,1,64]{0,2,1:T(8,128)(2,1)S(1)} %get-tuple-element.23) | copy-start | bytes 196612
  5.1 11.7 %copy-start.10 = (bf16[512,1,64]{0,2,1:T(8,128)(2,1)}, bf16[512,1,64]{0,2,1:T(8,128)(2,1)S(1)}, u32[]{:S(2)}) copy-start(bf16[512,1,64]{0,2,1:T(8,128)(2,1)S(1)} %get-tuple-element.24) | copy-start | bytes 196612
  5.2 10.0 %collective-permute-start = (bf16[64,1,256]{0,2,1:T(8,128)(2,1)S(1)}, bf16[64,1,256]{0,2,1:T(8,128)(2,1)S(1)}, u32[]{:S(2)}, u32[]{:S(2)}) collective-permute-start(bf16[64,1,256]{0,2,1:T(8,128)(2,1)S(1)} %fusion.79), channel_id=1, source_target_pairs={{0,8},{8,16},{16,24},{24,32},{32,40},{40,48},{48,56},{56,64},{64,7... | collective-permute-start | bytes 98312 | tf_op jit(solution)/shard_map/ppermute | solution.py:16
  9.0 10.0 %copy-start.25 = (pred[576]{0:T(1024)(128)(4,1)}, pred[576]{0:T(1024)(128)(4,1)S(1)}, u32[]{:S(2)}) copy-start(pred[576]{0:T(1024)(128)(4,1)S(1)} %fusion.87) | copy-start | bytes 1732
  15.1 1.6 copy-start.16
  15.2 15.9 %copy-start.23 = (bf16[64,1,128]{2,0,1:T(8,128)(2,1)}, bf16[64,1,128]{2,0,1:T(8,128)(2,1)S(1)}, u32[]{:S(2)}) copy-start(bf16[64,1,128]{2,0,1:T(8,128)(2,1)S(1)} %copy.39) | copy-start | bytes 49156
  23.9 3.2 %slice-start = ((pred[576]{0:T(1024)(128)(4,1)}), pred[512]{0:T(512)(128)(4,1)S(1)}, s32[]{:S(2)}) async-start(pred[576]{0:T(1024)(128)(4,1)} %copy-done.25), calls=%async_computation.1 | async-start | bytes 1024 | tf_op jit(solution)/shard_map/slice | solution.py:89
  27.1 4.5 %copy-start.2 = (bf16[576,1,8,64]{3,2,0,1:T(8,128)(2,1)}, bf16[576,1,8,64]{3,2,0,1:T(8,128)(2,1)S(1)}, u32[]{:S(2)}) copy-start(bf16[576,1,8,64]{3,2,0,1:T(8,128)(2,1)S(1)} %get-tuple-element.17) | copy-start | bytes 1769476
  27.1 4.5 %copy-start.4 = (bf16[576,1,8,64]{3,2,0,1:T(8,128)(2,1)}, bf16[576,1,8,64]{3,2,0,1:T(8,128)(2,1)S(1)}, u32[]{:S(2)}) copy-start(bf16[576,1,8,64]{3,2,0,1:T(8,128)(2,1)S(1)} %get-tuple-element.18) | copy-start | bytes 1769476
  27.1 4.0 %copy-start.27 = (bf16[512,128]{1,0:T(8,128)(2,1)S(1)}, bf16[512,128]{1,0:T(8,128)(2,1)}, u32[]{:S(2)}) copy-start(bf16[512,128]{1,0:T(8,128)(2,1)} %param.12) | copy-start | bytes 393220
  27.1 6.6 %copy-start.29 = (f32[8]{0:T(128)S(1)}, f32[8]{0:T(128)}, u32[]{:S(2)}) copy-start(f32[8]{0:T(128)} %param.16) | copy-start | bytes 100
  31.1 4.3 %copy-start.26 = (pred[576]{0:T(1024)(128)(4,1)S(1)}, pred[576]{0:T(1024)(128)(4,1)}, u32[]{:S(2)}) copy-start(pred[576]{0:T(1024)(128)(4,1)} %copy-done.25) | copy-start | bytes 1732
  31.6 3.8 %copy-start.3 = (bf16[576,1,8,64]{3,2,0,1:T(8,128)(2,1)S(1)}, bf16[576,1,8,64]{3,2,0,1:T(8,128)(2,1)}, u32[]{:S(2)}) copy-start(bf16[576,1,8,64]{3,2,0,1:T(8,128)(2,1)} %copy-done.2) | copy-start | bytes 1769476
  31.7 11.4 %collective-permute-start.1 = (f32[66048]{0:T(1024)S(1)}, f32[66048]{0:T(1024)S(1)}, u32[]{:S(2)}, u32[]{:S(2)}) collective-permute-start(f32[66048]{0:T(1024)S(1)} %slice.80), channel_id=1, source_target_pairs={{0,8},{8,16},{16,24},{24,32},{32,40},{40,48},{48,56},{56,64},{64,7... | collective-permute-start | bytes 792584 | tf_op jit(solution)/shard_map/ppermute | solution.py:16
  35.4 14.4 %copy-start.13 = (bf16[512,1024]{1,0:T(8,128)(2,1)S(1)}, bf16[512,1024]{1,0:T(8,128)(2,1)}, u32[]{:S(2)}) copy-start(bf16[512,1024]{1,0:T(8,128)(2,1)} %param.10) | copy-start | bytes 3145732
  43.9 26.2 %collective-permute-start.2 = (f32[66048]{0:T(1024)}, f32[66048]{0:T(1024)}, u32[]{:S(2)}, u32[]{:S(2)}) collective-permute-start(f32[66048]{0:T(1024)} %get-tuple-element.21), channel_id=1, source_target_pairs={{0,16},{8,24},{16,32},{24,40},{32,48},{40,56},{48,64},{56,72},{64,... | collective-permute-start | bytes 792584 | tf_op jit(solution)/shard_map/ppermute | solution.py:16
  46.2 30.1 %collective-permute-start.6 = (f32[66048]{0:T(1024)}, f32[66048]{0:T(1024)}, u32[]{:S(2)}, u32[]{:S(2)}) collective-permute-start(f32[66048]{0:T(1024)} %get-tuple-element.22), channel_id=1, source_target_pairs={{0,64},{8,72},{16,80},{24,88},{32,96},{40,104},{48,112},{56,120},{... | collective-permute-start | bytes 792584 | tf_op jit(solution)/shard_map/ppermute | solution.py:16
  52.6 1.9 %copy-start.14 = (f32[512,64]{1,0:T(8,128)S(1)}, f32[512,64]{1,0:T(8,128)}, u32[]{:S(2)}) copy-start(f32[512,64]{1,0:T(8,128)} %copy.45) | copy-start | bytes 393220
  52.6 1.9 %copy-start.15 = (f32[512,64]{1,0:T(8,128)S(1)}, f32[512,64]{1,0:T(8,128)}, u32[]{:S(2)}) copy-start(f32[512,64]{1,0:T(8,128)} %copy.47) | copy-start | bytes 393220
  54.5 2.9 %copy-start.5 = (pred[512,576]{0,1:T(8,128)(4,1)S(1)}, pred[512,576]{0,1:T(8,128)(4,1)}, u32[]{:S(2)}) copy-start(pred[512,576]{0,1:T(8,128)(4,1)} %get-tuple-element.32) | copy-start | bytes 884740
  54.5 2.9 %copy-start.9 = (bf16[512,1,64]{0,2,1:T(8,128)(2,1)S(1)}, bf16[512,1,64]{0,2,1:T(8,128)(2,1)}, u32[]{:S(2)}) copy-start(bf16[512,1,64]{0,2,1:T(8,128)(2,1)} %copy-done.8) | copy-start | bytes 196612
  54.5 2.9 %copy-start.11 = (bf16[512,1,64]{0,2,1:T(8,128)(2,1)S(1)}, bf16[512,1,64]{0,2,1:T(8,128)(2,1)}, u32[]{:S(2)}) copy-start(bf16[512,1,64]{0,2,1:T(8,128)(2,1)} %copy-done.10) | copy-start | bytes 196612
  54.5 2.9 %copy-start.17 = (bf16[64,1,128]{0,2,1:T(8,128)(2,1)S(1)}, bf16[64,1,128]{0,2,1:T(8,128)(2,1)}, u32[]{:S(2)}) copy-start(bf16[64,1,128]{0,2,1:T(8,128)(2,1)} %copy-done.16) | copy-start | bytes 49156
  60.0 3.7 %copy-start.1 = (f32[576,512,8]{1,0,2:T(8,128)}, f32[576,512,8]{1,0,2:T(8,128)S(1)}, u32[]{:S(2)}) copy-start(f32[576,512,8]{1,0,2:T(8,128)S(1)} %get-tuple-element.39) | copy-start | bytes 28311556
  60.0 6.2 %copy-start.20 = (f32[8,512]{1,0:T(8,128)}, f32[8,512]{1,0:T(8,128)S(1)}, u32[]{:S(2)}) copy-start(f32[8,512]{1,0:T(8,128)S(1)} %get-tuple-element.38) | copy-start | bytes 49156
  70.1 9.2 %copy-start.12 = (f32[512,8,64]{0,2,1:T(8,128)S(1)}, f32[512,8,64]{0,2,1:T(8,128)}, u32[]{:S(2)}) copy-start(f32[512,8,64]{0,2,1:T(8,128)} %get-tuple-element.35) | copy-start | bytes 3145732
  71.3 14.1 %collective-permute-start.3 = (f32[66048]{0:T(1024)S(1)}, f32[66048]{0:T(1024)S(1)}, u32[]{:S(2)}, u32[]{:S(2)}) collective-permute-start(f32[66048]{0:T(1024)S(1)} %add.201), channel_id=1, source_target_pairs={{0,32},{8,40},{16,48},{24,56},{32,64},{40,72},{48,80},{56,88},{64,... | collective-permute-start | bytes 792584 | tf_op jit(solution)/shard_map/ppermute | solution.py:16
  77.4 11.4 %collective-permute-start.7 = (f32[66048]{0:T(1024)S(1)}, f32[66048]{0:T(1024)S(1)}, u32[]{:S(2)}, u32[]{:S(2)}) collective-permute-start(f32[66048]{0:T(1024)S(1)} %add.207), channel_id=1, source_target_pairs={{0,128},{8,136},{16,144},{24,152},{32,160},{40,168},{48,176},{56,1... | collective-permute-start | bytes 792584 | tf_op jit(solution)/shard_map/ppermute | solution.py:16
  79.3 18.8 %copy-start.7 = (bf16[576,8,128]{2,1,0:T(8,128)(2,1)S(1)}, bf16[576,8,128]{2,1,0:T(8,128)(2,1)}, u32[]{:S(2)}) copy-start(bf16[576,8,128]{2,1,0:T(8,128)(2,1)} %fusion.14) | copy-start | bytes 3538948
  79.3 18.8 %copy-start.18 = (pred[512,576]{0,1:T(8,128)(4,1)S(1)}, pred[512,576]{0,1:T(8,128)(4,1)}, u32[]{:S(2)}) copy-start(pred[512,576]{0,1:T(8,128)(4,1)} %get-tuple-element.33) | copy-start | bytes 884740
  85.5 16.8 %collective-permute-start.4 = (f32[66048]{0:T(1024)S(1)}, f32[66048]{0:T(1024)S(1)}, u32[]{:S(2)}, u32[]{:S(2)}) collective-permute-start(f32[66048]{0:T(1024)S(1)} %add.203), channel_id=1, source_target_pairs={{0,64},{8,72},{16,80},{24,88},{32,96},{40,104},{48,112},{56,120},{... | collective-permute-start | bytes 792584 | tf_op jit(solution)/shard_map/ppermute | solution.py:16
  88.8 14.8 %collective-permute-start.8 = (f32[66048]{0:T(1024)S(1)}, f32[66048]{0:T(1024)S(1)}, u32[]{:S(2)}, u32[]{:S(2)}) collective-permute-start(f32[66048]{0:T(1024)S(1)} %add.209), channel_id=1, source_target_pairs={{0,8},{8,16},{16,24},{24,32},{32,40},{40,48},{48,56},{56,64},{64,7... | collective-permute-start | bytes 792584 | tf_op jit(solution)/shard_map/ppermute | solution.py:16
  98.1 9.6 %copy-start.24 = (bf16[64,1,128]{2,0,1:T(8,128)(2,1)S(1)}, bf16[64,1,128]{2,0,1:T(8,128)(2,1)}, u32[]{:S(2)}) copy-start(bf16[64,1,128]{2,0,1:T(8,128)(2,1)} %copy-done.23) | copy-start | bytes 49156
  98.1 9.6 %copy-start.28 = (bf16[512,128]{1,0:T(8,128)(2,1)S(1)}, bf16[512,128]{1,0:T(8,128)(2,1)}, u32[]{:S(2)}) copy-start(bf16[512,128]{1,0:T(8,128)(2,1)} %param.12) | copy-start | bytes 393220
  102.3 22.0 %collective-permute-start.5 = (f32[66048]{0:T(1024)S(1)}, f32[66048]{0:T(1024)S(1)}, u32[]{:S(2)}, u32[]{:S(2)}) collective-permute-start(f32[66048]{0:T(1024)S(1)} %add.205), channel_id=1, source_target_pairs={{0,128},{8,136},{16,144},{24,152},{32,160},{40,168},{48,176},{56,1... | collective-permute-start | bytes 792584 | tf_op jit(solution)/shard_map/ppermute | solution.py:16
  103.7 16.0 %collective-permute-start.9 = (f32[66048]{0:T(1024)S(1)}, f32[66048]{0:T(1024)S(1)}, u32[]{:S(2)}, u32[]{:S(2)}) collective-permute-start(f32[66048]{0:T(1024)S(1)} %add.211), channel_id=1, source_target_pairs={{0,16},{8,24},{16,32},{24,40},{32,48},{40,56},{48,64},{56,72},{64,... | collective-permute-start | bytes 792584 | tf_op jit(solution)/shard_map/ppermute | solution.py:16
  119.7 20.8 %collective-permute-start.10 = (f32[66048]{0:T(1024)S(1)}, f32[66048]{0:T(1024)S(1)}, u32[]{:S(2)}, u32[]{:S(2)}) collective-permute-start(f32[66048]{0:T(1024)S(1)} %add.213), channel_id=1, source_target_pairs={{0,32},{8,40},{16,48},{24,56},{32,64},{40,72},{48,80},{56,88},{64,... | collective-permute-start | bytes 792584 | tf_op jit(solution)/shard_map/ppermute | solution.py:16
  142.6 0.7 copy-start.22
  142.7 1.0 copy-start.6
  142.7 1.0 copy-start.21
  142.7 1.7 copy-start.30

commit v7 on v3

--- a/solution.py
+++ b/solution.py
@@ -96,9 +96,15 @@
     before_norm = jnp.concatenate(
         [jnp.zeros_like(block_norms), jnp.cumsum(block_norms, axis=0)[:-1]], axis=0
     )
-    state_shape = total_state.shape
-    state_size = total_state.size
-    packed = jnp.concatenate([total_state.reshape(-1), total_norm.reshape(-1)])
+    half_heads = group // 2
+    head_parts = (slice(0, half_heads), slice(half_heads, group))
+    state_part_size = total_state[:, head_parts[0]].size
+    halves = [
+        jnp.concatenate(
+            [total_state[:, part].reshape(-1), total_norm[:, part].reshape(-1)]
+        )
+        for part in head_parts
+    ]
     count = lax.axis_size("seq")
     shifts = []
     steps = 1
@@ -107,20 +113,21 @@
         steps *= 2
     half = len(shifts) // 2 + 1
     orders = (shifts, shifts[half:] + shifts[:half])
-    middle = packed.size // 2
     pieces = []
-    for order, piece in zip(orders, (packed[:middle], packed[middle:])):
+    for order, piece in zip(orders, halves):
         inclusive = piece
         exclusive = jnp.zeros_like(piece)
         for place, shift in enumerate(order):
             received = passed_along(inclusive, "seq", shift)
             if not pieces and place == 0:
                 first_received = received
-            exclusive = exclusive + received
+            if pieces and place + 1 == len(order):
+                held = received
+            else:
+                exclusive = exclusive + received
             if place + 1 < len(order):
                 inclusive = inclusive + received
         pieces.append(exclusive)
-    exclusive = jnp.concatenate(pieces)
     queries, first_received = lax.optimization_barrier((queries, first_received))
     rot_q = rotate(
         queries.reshape(tokens, heads, head_dim).astype(jnp.float32), cosine, sine
@@ -129,8 +136,6 @@
     phi_query = (
         two_softmax(query_logits).astype(jnp.bfloat16).reshape(tokens, kv_local, group, 2 * feat)
     )
-    prior_state = exclusive[:state_size].reshape(state_shape)
-    prior_norm = exclusive[state_size:].reshape(total_norm.shape)
     factor = jax.nn.sigmoid(window_logit).reshape(kv_local, group)
     rot_grouped = rot_q.reshape(tokens, kv_local, group, head_dim)
     row_index = jnp.arange(BLOCK)[:, None]
@@ -160,28 +165,44 @@
         ext_values,
         preferred_element_type=jnp.float32,
     )
-    state_now = prior_state + before_state[0]
-    norm_now = prior_norm + before_norm[0]
-    state_high, state_rest = split_parts(state_now)
-    norm_high, norm_rest = split_parts(norm_now)
-    far_num = jnp.einsum(
-        "igkf,gkfd->igkd", phi_query, state_high, preferred_element_type=jnp.float32
-    )
-    far_num = far_num + jnp.einsum(
-        "igkf,gkfd->igkd", phi_query, state_rest, preferred_element_type=jnp.float32
-    )
-    far_sum = jnp.einsum("igkf,gkf->igk", phi_query, norm_high, preferred_element_type=jnp.float32)
-    far_sum = far_sum + jnp.einsum(
-        "igkf,gkf->igk", phi_query, norm_rest, preferred_element_type=jnp.float32
-    )
     head_factor = factor[None, :, :, None]
-    numerator = head_factor * window_num + (1.0 - head_factor) * (near_num + far_num)
-    denominator = factor[None] * jnp.transpose(window_sum, (2, 0, 1)) + (1.0 - factor[None]) * (
-        jnp.transpose(near_sum, (2, 0, 1)) + far_sum
-    )
-    outputs = (numerator / denominator[..., None]).astype(jnp.bfloat16)
-    result = outputs.reshape(tokens, heads * head_dim)
-    return lax.all_to_all(result, "head", split_axis=0, concat_axis=1, tiled=True)
+    window_sum_rows = jnp.transpose(window_sum, (2, 0, 1))
+    near_sum_rows = jnp.transpose(near_sum, (2, 0, 1))
+    sent = []
+    for part, exclusive in zip(head_parts, pieces):
+        if sent:
+            sent[0], held = lax.optimization_barrier((sent[0], held))
+            exclusive = exclusive + held
+        prior_state = exclusive[:state_part_size].reshape(total_state[:, part].shape)
+        prior_norm = exclusive[state_part_size:].reshape(total_norm[:, part].shape)
+        state_now = prior_state + before_state[0][:, part]
+        norm_now = prior_norm + before_norm[0][:, part]
+        state_high, state_rest = split_parts(state_now)
+        norm_high, norm_rest = split_parts(norm_now)
+        phi_part = phi_query[:, :, part]
+        far_num = jnp.einsum(
+            "igkf,gkfd->igkd", phi_part, state_high, preferred_element_type=jnp.float32
+        )
+        far_num = far_num + jnp.einsum(
+            "igkf,gkfd->igkd", phi_part, state_rest, preferred_element_type=jnp.float32
+        )
+        far_sum = jnp.einsum("igkf,gkf->igk", phi_part, norm_high, preferred_element_type=jnp.float32)
+        far_sum = far_sum + jnp.einsum(
+            "igkf,gkf->igk", phi_part, norm_rest, preferred_element_type=jnp.float32
+        )
+        part_factor = head_factor[:, :, part]
+        numerator = part_factor * window_num[:, :, part] + (1.0 - part_factor) * (
+            near_num[:, :, part] + far_num
+        )
+        denominator = factor[None][:, :, part] * window_sum_rows[:, :, part] + (
+            1.0 - factor[None][:, :, part]
+        ) * (near_sum_rows[:, :, part] + far_sum)
+        outputs = (numerator / denominator[..., None]).astype(jnp.bfloat16)
+        result = outputs.reshape(tokens, -1)
+        moved = lax.all_to_all(result, "head", split_axis=0, concat_axis=1, tiled=True)
+        sent.append(moved.reshape(moved.shape[0], lax.axis_size("head"), -1))
+    joined = jnp.concatenate(sent, axis=-1)
+    return joined.reshape(joined.shape[0], -1)
 
 
 def solution(mesh):

time: 165 us -> 172 us (1.042)
  the two profiles are of different devices: /device:TPU:2 before, /device:TPU:6 now
where the time goes in v7:
time: 172 us; the launch traced here: 171 us
  waiting for transfers between devices  43.3 us (25%)
  other arithmetic  38.8 us (23%)
  starting transfers between devices  38.7 us (23%)
  matrix products  21 us (12%)
  blocking collectives  14.6 us (8%)
  local copies, waits for them, and re-layouts  13.9 us (8%)
    ppermute x12, waiting for transfers between devices, passed_along(): lax.ppermute(value, axis, [(source, source + steps) for source in range(f...  43.3 us
    ppermute x12, starting transfers between devices, passed_along(): lax.ppermute(value, axis, [(source, source + steps) for source in range(f...  34.2 us
    all_to_all x1, blocking collectives, body(): lax.all_to_all(result, 'head', split_axis=0, concat_axis=1, tiled=True)  14.6 us
    another operation x4, other arithmetic  6.76 us
    unnamed x66, local copies, waits for them, and re-layouts  5.16 us
    add x8, other arithmetic, body(): inclusive = inclusive + received  4.69 us
    all_to_all x1, starting transfers between devices, body(): lax.all_to_all(result, 'head', split_axis=0, concat_axis=1, tiled=True)  4.51 us
    reduce_sum x1, other arithmetic, body(): block_norms = jnp.sum(lag_phi, axis=1, dtype=jnp.float32)  3.97 us
  transfers between devices with their start and end apart: 13, of which 5 were waited for; matrix products, arithmetic and copies ran while one was open for 36% of the time, Pallas kernels for 0%

profile of v7, /device:TPU:6, one launch (start us, length us, event | category | flops | bytes accessed | tf_op | source)
XLA Modules:
  0.0 171.1 jit_solution(2972385659276251988)
XLA Ops:
  0.0 1.0 copy.49
  1.1 0.7 add_bitcast_fusion
  1.8 2.4 %subtract_convert_fusion.9 = (bf16[512,1,64]{0,2,1:T(8,128)(2,1)S(1)}, bf16[512,1,64]{0,2,1:T(8,128)(2,1)S(1)}) fusion(f32[512,1,128]{0,2,1:T(8,128)S(1)} %bitcast_convert_fusion, f32[64]{0:T(128)} %constant.76.clone, f32[512]{0:T(512)S(1)} %get-tuple-element.35, f32[64]{0:T(128)} %constant.75.clone, f32[512]{0:T(512)S(1)} %get-tuple-element.34, ...), kind=kLoop, calls=%fused_computation.138 | loop fusion | flops 753664 | bytes 400128 | tf_op jit(solution)/shard_map/convert.10
  4.3 3.8 %collective-permute-start.1 = (bf16[64,1,128]{0,2,1:T(8,128)(2,1)S(1)}, bf16[64,1,128]{0,2,1:T(8,128)(2,1)S(1)}, u32[]{:S(2)}, u32[]{:S(2)}) collective-permute-start(bf16[64,1,128]{0,2,1:T(8,128)(2,1)S(1)} %pad_maximum_fusion.14), channel_id=1, source_target_pairs={{0,8},{8,16},{16,24},{24,32},{32,40},{40,48},{48,56},{56,64},{64,7... | collective-permute-start | bytes 49160 | tf_op jit(solution)/shard_map/ppermute | solution.py:16
  8.1 0.7 slice_bitcast_fusion
  8.9 3.8 %collective-permute-start = (bf16[64,1,128]{2,0,1:T(8,128)(2,1)S(1)}, bf16[64,1,128]{2,0,1:T(8,128)(2,1)S(1)}, u32[]{:S(2)}, u32[]{:S(2)}) collective-permute-start(bf16[64,1,128]{2,0,1:T(8,128)(2,1)S(1)} %slice_bitcast_fusion), channel_id=1, source_target_pairs={{0,8},{8,16},{16,24},{24,32},{32,40},{40,48},{48,56},{56,64},{64,7... | collective-permute-start | bytes 49160 | tf_op jit(solution)/shard_map/ppermute | solution.py:16
  12.7 2.2 %fusion.78 = (f32[512,64]{0,1:T(8,128)S(1)}, f32[512,64]{0,1:T(8,128)S(1)}) fusion(f32[64]{0:T(128)} %constant.76.clone, f32[512]{0:T(512)S(1)} %get-tuple-element.35, f32[64]{0:T(128)} %constant.75.clone, f32[512]{0:T(512)S(1)} %get-tuple-element.34, f32[64]{0:T(128)} %constant.74.clone, f32[512]{0:T(512)S(1)} %get-tuple-element.33), kind=kLoop, calls=%fused_computation.128 | loop fusion | flops 491520 | bytes 269056 | tf_op jit(solution)/shard_map/sub | solution.py:29
  14.9 0.7 fusion.153
  15.5 0.7 fusion.152
  16.2 0.6 slice_bitcast_fusion.5
  16.8 1.1 fusion.37
  17.9 0.6 slice_bitcast_fusion.6
  18.6 0.8 copy.57
  19.4 0.9 copy.55
  20.3 1.5 fusion.72
  21.8 2.3 %copy.51 = f32[576,8,64]{2,1,0:T(8,128)S(1)} copy(f32[576,8,64]{0,2,1:T(8,128)} %bitcast.235) | data formatting | bytes 2359296 | tf_op jit(solution)/shard_map/ngd,gkdf->ngkf/dot_general | solution.py:79
  24.1 1.3 bitcast_reduce_fusion
  25.4 3.6 %fusion.21 = (f32[576,8]{1,0:T(8,128)S(1)}, f32[576,8]{1,0:T(8,128)S(1)}) fusion(f32[576,8,64]{2,1,0:T(8,128)S(1)} %copy.51, f32[576,8]{1,0:T(8,128)S(1)} %get-tuple-element.13, f32[576,8]{1,0:T(8,128)S(1)} %get-tuple-element.14), kind=kLoop, calls=%fused_computation.33 | loop fusion | flops 1465344 | bytes 1253376 | tf_op jit(solution)/shard_map/reduce_sum | solution.py:47
  29.0 3.1 %fusion.20 = (bf16[576,1,8,64]{3,2,0,1:T(8,128)(2,1)S(1)}, bf16[576,1,8,64]{3,2,0,1:T(8,128)(2,1)S(1)}) fusion(f32[576,8,64]{2,1,0:T(8,128)S(1)} %copy.51, f32[576,8]{1,0:T(8,128)S(1)} %get-tuple-element.11, f32[576,8]{1,0:T(8,128)S(1)} %get-tuple-element.13, f32[576,8]{1,0:T(8,128)S(1)} %get-tuple-element.12, f32[576,8]{1,0:T(8,128)S(1)} %get-tuple-element.14), kind=kLoop, calls=%fused_computation.32 | loop fusion | flops 2064384 | bytes 2433024 | tf_op jit(solution)/shard_map/div | solution.py:47
  32.2 4.0 %convert_reduce_fusion = (f32[8,128]{1,0:T(8,128)S(1)}, bf16[512,1,8,128]{3,2,0,1:T(8,128)(2,1)S(1)}) fusion(bf16[576,1,8,64]{3,2,0,1:T(8,128)(2,1)S(1)} %get-tuple-element.20, bf16[576,1,8,64]{3,2,0,1:T(8,128)(2,1)S(1)} %get-tuple-element.19, pred[512]{0:T(512)(128)(4,1)S(1)} %slice-done), kind=kLoop, calls=%fused_computation.29 | loop fusion | flops 3668992 | bytes 2232832 | tf_op jit(solution)/shard_map/reduce_sum | solution.py:90
  36.2 0.5 convolution_bitcast_fusion.1
  36.8 4.0 %collective-permute-start.2 = (f32[66048]{0:T(1024)S(1)}, f32[66048]{0:T(1024)S(1)}, u32[]{:S(2)}, u32[]{:S(2)}) collective-permute-start(f32[66048]{0:T(1024)S(1)} %pad_maximum_fusion.3), channel_id=1, source_target_pairs={{0,8},{8,16},{16,24},{24,32},{32,40},{40,48},{48,56},{56,64},{64,7... | collective-permute-start | bytes 792584 | tf_op jit(solution)/shard_map/ppermute | solution.py:16
  40.8 0.7 pad_maximum_fusion.4
  41.5 1.3 collective-permute-start.7
  42.8 2.9 %fusion.14 = bf16[576,8,128]{2,1,0:T(8,128)(2,1)} fusion(bf16[576,8,64]{2,1,0:T(8,128)(2,1)S(1)} %bitcast.233, bf16[576,8,64]{2,1,0:T(8,128)(2,1)S(1)} %bitcast.232, pred[576]{0:T(1024)(128)(4,1)S(1)} %copy-done.18), kind=kLoop, calls=%fused_computation.18 | loop fusion | flops 2949120 | bytes 2359872 | tf_op jit(solution)/shard_map/convert_element_type | solution.py:82
  45.7 2.9 %collective-permute-done.2 = f32[66048]{0:T(1024)S(1)} collective-permute-done((f32[66048]{0:T(1024)S(1)}, f32[66048]{0:T(1024)S(1)}, u32[]{:S(2)}, u32[]{:S(2)}) %collective-permute-start.2) | collective-permute-done | bytes 264224 | tf_op jit(solution)/shard_map/ppermute | solution.py:16
  48.7 0.5 copy.53
  49.2 0.7 fusion.135
  50.2 2.0 %copy.89 = f32[512,8,64]{2,0,1:T(8,128)} copy(f32[512,8,64]{0,2,1:T(8,128)S(1)} %get-tuple-element.23) | data formatting | bytes 2097152
  52.2 1.9 %copy.88 = f32[512,8,64]{2,0,1:T(8,128)} copy(f32[512,8,64]{0,2,1:T(8,128)S(1)} %get-tuple-element.24) | data formatting | bytes 2097152
  54.1 4.2 %collective-permute-start.3 = (f32[66048]{0:T(1024)}, f32[66048]{0:T(1024)}, u32[]{:S(2)}, u32[]{:S(2)}) collective-permute-start(f32[66048]{0:T(1024)} %fusion.135), channel_id=1, source_target_pairs={{0,16},{8,24},{16,32},{24,40},{32,48},{40,56},{48,64},{56,72},{64,... | collective-permute-start | bytes 792584 | tf_op jit(solution)/shard_map/ppermute | solution.py:16
  58.3 1.7 fusion.134
  60.0 1.5 collective-permute-start.8
  61.5 2.8 %subtract_convert_fusion = (bf16[512,8,64]{2,0,1:T(8,128)(2,1)S(1)}, bf16[512,8,64]{2,0,1:T(8,128)(2,1)S(1)}) fusion(f32[512,8,64]{2,0,1:T(8,128)} %copy.89, f32[512,8,64]{2,0,1:T(8,128)} %copy.88, f32[512,64]{1,0:T(8,128)S(1)} %copy-done.10, f32[512,64]{1,0:T(8,128)S(1)} %copy-done.11), kind=kLoop, calls=%fused_computation.28 | loop fusion | flops 2097152 | bytes 3407872 | tf_op jit(solution)/shard_map/convert.8
  64.3 2.5 %fusion.139 = (f32[512,8]{0,1:T(8,128)}, f32[512,8,64]{0,2,1:T(8,128)}) fusion(bf16[8,128,64]{1,2,0:T(8,128)(2,1)S(1)} %copy-done, bf16[512,8,64]{2,0,1:T(8,128)(2,1)S(1)} %get-tuple-element.18, bf16[512,8,64]{2,0,1:T(8,128)(2,1)S(1)} %get-tuple-element.17), kind=kOutput, calls=%fused_computation.226 | convolution fusion | flops 69992512 | bytes 2244608 | tf_op jit(solution)/shard_map/sub | solution.py:47
  66.8 2.6 %fusion.2 = (f32[8,512]{1,0:T(8,128)S(1)}, f32[576,512,8]{1,0,2:T(8,128)S(1)}) fusion(pred[512,576]{0,1:T(8,128)(4,1)S(1)} %copy-done.1, bf16[512,8,64]{2,0,1:T(8,128)(2,1)S(1)} %get-tuple-element.18, bf16[512,8,64]{2,0,1:T(8,128)(2,1)S(1)} %get-tuple-element.17, bf16[512,1,64]{0,2,1:T(8,128)(2,1)S(1)} %copy-done.8, bf16[512,1,64]{0,2,1:T(8,128)(2,1)S(1)} %copy-done.6, ...), kind=kOutput, calls=%fused_computation.4 | convolution fusion | flops 613593088 | bytes 10944512 | tf_op jit(solution)/shard_map/igkd,jgd->gkij/dot_general | solution.py:146
  69.4 2.5 %fusion.5 = f32[8,512]{1,0:T(8,128)} fusion(f32[576,512,8]{1,0,2:T(8,128)S(1)} %get-tuple-element.51, f32[8,512]{1,0:T(8,128)S(1)} %get-tuple-element.50, pred[512,576]{0,1:T(8,128)(4,1)S(1)} %copy-done.1), kind=kLoop, calls=%fused_computation.9 | loop fusion | flops 9433088 | bytes 9764864 | tf_op jit(solution)/shard_map/reduce_sum | solution.py:152
  72.0 3.5 %fusion.23 = f32[512,1,8,128]{0,3,2,1:T(8,128)} fusion(f32[576,512,8]{1,0,2:T(8,128)S(1)} %get-tuple-element.51, f32[8,512]{1,0:T(8,128)S(1)} %get-tuple-element.50, pred[512,576]{0,1:T(8,128)(4,1)S(1)} %copy-done.1, bf16[64,1,128]{2,0,1:T(8,128)(2,1)S(1)} %copy-done.29, bf16[512,1,128]{2,0,1:T(8,128)(2,1)S(1)} %bitcast.255), kind=kOutput, calls=%fused_computation.37 | convolution fusion | flops 613711872 | bytes 11993088 | tf_op jit(solution)/shard_map/gkij,jgd->igkd/dot_general | solution.py:156
  75.5 1.5 fusion.140
  76.9 1.2 add.231
  78.1 4.0 %collective-permute-start.4 = (f32[66048]{0:T(1024)S(1)}, f32[66048]{0:T(1024)S(1)}, u32[]{:S(2)}, u32[]{:S(2)}) collective-permute-start(f32[66048]{0:T(1024)S(1)} %add.231), channel_id=1, source_target_pairs={{0,32},{8,40},{16,48},{24,56},{32,64},{40,72},{48,80},{56,88},{64,... | collective-permute-start | bytes 792584 | tf_op jit(solution)/shard_map/ppermute | solution.py:16
  82.2 1.5 divide_convert_fusion
  83.7 7.7 %collective-permute-done.4 = f32[66048]{0:T(1024)S(1)} collective-permute-done((f32[66048]{0:T(1024)S(1)}, f32[66048]{0:T(1024)S(1)}, u32[]{:S(2)}, u32[]{:S(2)}) %collective-permute-start.4) | collective-permute-done | bytes 264224 | tf_op jit(solution)/shard_map/ppermute | solution.py:16
  91.4 1.3 collective-permute-start.5
  92.8 1.5 select_reduce_fusion
  94.3 1.0 add.248
  95.3 5.0 %collective-permute-start.9 = (f32[66048]{0:T(1024)S(1)}, f32[66048]{0:T(1024)S(1)}, u32[]{:S(2)}, u32[]{:S(2)}) collective-permute-start(f32[66048]{0:T(1024)S(1)} %add.248), channel_id=1, source_target_pairs={{0,8},{8,16},{16,24},{24,32},{32,40},{40,48},{48,56},{56,64},{64,7... | collective-permute-start | bytes 792584 | tf_op jit(solution)/shard_map/ppermute | solution.py:16
  100.3 9.7 %collective-permute-done.5 = f32[66048]{0:T(1024)S(1)} collective-permute-done((f32[66048]{0:T(1024)S(1)}, f32[66048]{0:T(1024)S(1)}, u32[]{:S(2)}, u32[]{:S(2)}) %collective-permute-start.5) | collective-permute-done | bytes 264224 | tf_op jit(solution)/shard_map/ppermute | solution.py:16
  110.0 1.5 collective-permute-start.6
  111.6 2.5 %fusion.26 = f32[512,1,8,128]{0,3,2,1:T(8,128)} fusion(bf16[8,512,576]{1,2,0:T(8,128)(2,1)S(1)} %get-tuple-element.53, pred[512,576]{0,1:T(8,128)(4,1)S(1)} %copy-done.12, bf16[64,1,128]{2,0,1:T(8,128)(2,1)S(1)} %copy-done.30, bf16[512,1,128]{2,0,1:T(8,128)(2,1)S(1)} %bitcast.256), kind=kOutput, calls=%fused_computation.38 | convolution fusion | flops 606633984 | bytes 7258112 | tf_op jit(solution)/shard_map/gkij,jgd->igkd/dot_general | solution.py:162
  114.1 1.9 %collective-permute-start.10 = (f32[66048]{0:T(1024)S(1)}, f32[66048]{0:T(1024)S(1)}, u32[]{:S(2)}, u32[]{:S(2)}) collective-permute-start(f32[66048]{0:T(1024)S(1)} %add.249), channel_id=1, source_target_pairs={{0,16},{8,24},{16,32},{24,40},{32,48},{40,56},{48,64},{56,72},{64,... | collective-permute-start | bytes 792584 | tf_op jit(solution)/shard_map/ppermute | solution.py:16
  116.1 3.8 %collective-permute-done.6 = f32[66048]{0:T(1024)S(1)} collective-permute-done((f32[66048]{0:T(1024)S(1)}, f32[66048]{0:T(1024)S(1)}, u32[]{:S(2)}, u32[]{:S(2)}) %collective-permute-start.6) | collective-permute-done | bytes 264224 | tf_op jit(solution)/shard_map/ppermute | solution.py:16
  119.8 1.1 add_add_fusion.1
  121.9 1.9 %fusion.48 = bf16[512,1,4,128]{0,3,2,1:T(8,128)(2,1)S(1)} fusion(f32[512,1,8,128]{0,3,2,1:T(8,128)} %fusion.26, f32[512,1,8,128]{0,3,2,1:T(8,128)} %fusion.23, f32[512,4]{0,1:T(4,128)S(1)} %fusion.99, f32[4]{0:T(128)S(1)} %copy-done.26, f32[4]{0:T(128)S(1)} %copy-done.27, f32[4,128,512]{2,1,0:T(8,128)S(1)} %fusion.92, ...), kind=kOutput, calls=%fused_computation.75 | convolution fusion | flops 69206016 | bytes 4464672 | tf_op jit(solution)/shard_map/igkf,gkfd->igkd/dot_general | solution.py:186
  123.8 0.3 copy.65
  124.1 1.0 all_to_all.24
  125.1 4.5 %all-to-all-start = ((bf16[8,64,512]{2,1,0:T(8,128)(2,1)}), bf16[8,64,512]{2,1,0:T(8,128)(2,1)S(1)}, u32[]{:S(2)}, u32[]{:S(2)}) async-start(bf16[8,64,512]{2,1,0:T(8,128)(2,1)} %all_to_all.24), calls=%async_computation | async-start | bytes 1048576 | tf_op jit(solution)/shard_map/all_to_all | solution.py:202
  129.7 1.9 %collective-permute-start.11 = (f32[66048]{0:T(1024)S(1)}, f32[66048]{0:T(1024)S(1)}, u32[]{:S(2)}, u32[]{:S(2)}) collective-permute-start(f32[66048]{0:T(1024)S(1)} %add.250), channel_id=1, source_target_pairs={{0,32},{8,40},{16,48},{24,56},{32,64},{40,72},{48,80},{56,88},{64,... | collective-permute-start | bytes 792584 | tf_op jit(solution)/shard_map/ppermute | solution.py:16
  131.6 19.3 %collective-permute-done.11 = f32[66048]{0:T(1024)S(1)} collective-permute-done((f32[66048]{0:T(1024)S(1)}, f32[66048]{0:T(1024)S(1)}, u32[]{:S(2)}, u32[]{:S(2)}) %collective-permute-start.11) | collective-permute-done | bytes 264224 | tf_op jit(solution)/shard_map/ppermute | solution.py:16
  150.9 1.1 add_add_fusion
  152.9 1.9 %fusion.49 = bf16[512,1,4,128]{0,3,2,1:T(8,128)(2,1)S(1)} fusion(f32[512,1,8,128]{0,3,2,1:T(8,128)} %fusion.26, f32[512,1,8,128]{0,3,2,1:T(8,128)} %fusion.23, f32[512,4]{0,1:T(4,128)S(1)} %fusion.96, f32[4]{0:T(128)S(1)} %copy-done.25, f32[4]{0:T(128)S(1)} %copy-done.24, f32[4,128,512]{2,1,0:T(8,128)S(1)} %fusion.89, ...), kind=kOutput, calls=%fused_computation.76 | convolution fusion | flops 69206016 | bytes 4464672 | tf_op jit(solution)/shard_map/igkf,gkfd->igkd/dot_general | solution.py:186
  154.8 0.3 copy.70
  155.3 14.6 %all_to_all.32 = bf16[8,64,512]{2,1,0:T(8,128)(2,1)S(1)} all-to-all(bf16[8,64,512]{2,1,0:T(8,128)(2,1)S(1)} %all_to_all.27), channel_id=1, replica_groups=mesh['seq'=32,'head'=8] {'head'}, dimensions={0} | all-to-all | bytes 1048576 | tf_op jit(solution)/shard_map/all_to_all | solution.py:202
  170.0 1.1 copy.90
  (105 shorter events, 3.0 us)
Async XLA Ops:
  0.0 64.3 %copy-start = (bf16[8,128,64]{1,2,0:T(8,128)(2,1)S(1)}, bf16[8,128,64]{1,2,0:T(8,128)(2,1)}, u32[]{:S(2)}) copy-start(bf16[8,128,64]{1,2,0:T(8,128)(2,1)} %param.14) | copy-start | bytes 393220
  0.0 20.3 %copy-start.15 = (bf16[8,128,64]{1,2,0:T(8,128)(2,1)S(1)}, bf16[8,128,64]{1,2,0:T(8,128)(2,1)}, u32[]{:S(2)}) copy-start(bf16[8,128,64]{1,2,0:T(8,128)(2,1)} %param.15) | copy-start | bytes 393220
  4.2 17.6 %copy-start.5 = (bf16[512,1,64]{0,2,1:T(8,128)(2,1)}, bf16[512,1,64]{0,2,1:T(8,128)(2,1)S(1)}, u32[]{:S(2)}) copy-start(bf16[512,1,64]{0,2,1:T(8,128)(2,1)S(1)} %get-tuple-element.27) | copy-start | bytes 196612
  4.2 17.6 %copy-start.7 = (bf16[512,1,64]{0,2,1:T(8,128)(2,1)}, bf16[512,1,64]{0,2,1:T(8,128)(2,1)S(1)}, u32[]{:S(2)}) copy-start(bf16[512,1,64]{0,2,1:T(8,128)(2,1)S(1)} %get-tuple-element.28) | copy-start | bytes 196612
  4.3 16.0 %collective-permute-start.1 = (bf16[64,1,128]{0,2,1:T(8,128)(2,1)S(1)}, bf16[64,1,128]{0,2,1:T(8,128)(2,1)S(1)}, u32[]{:S(2)}, u32[]{:S(2)}) collective-permute-start(bf16[64,1,128]{0,2,1:T(8,128)(2,1)S(1)} %pad_maximum_fusion.14), channel_id=1, source_target_pairs={{0,8},{8,16},{16,24},{24,32},{32,40},{40,48},{48,56},{56,64},{64,7... | collective-permute-start | bytes 49160 | tf_op jit(solution)/shard_map/ppermute | solution.py:16
  8.9 27.3 %collective-permute-start = (bf16[64,1,128]{2,0,1:T(8,128)(2,1)S(1)}, bf16[64,1,128]{2,0,1:T(8,128)(2,1)S(1)}, u32[]{:S(2)}, u32[]{:S(2)}) collective-permute-start(bf16[64,1,128]{2,0,1:T(8,128)(2,1)S(1)} %slice_bitcast_fusion), channel_id=1, source_target_pairs={{0,8},{8,16},{16,24},{24,32},{32,40},{40,48},{48,56},{56,64},{64,7... | collective-permute-start | bytes 49160 | tf_op jit(solution)/shard_map/ppermute | solution.py:16
  16.2 7.9 %copy-start.17 = (pred[576]{0:T(1024)(128)(4,1)}, pred[576]{0:T(1024)(128)(4,1)S(1)}, u32[]{:S(2)}) copy-start(pred[576]{0:T(1024)(128)(4,1)S(1)} %fusion.100) | copy-start | bytes 1732
  20.3 1.5 copy-start.13
  29.0 3.1 %slice-start = ((pred[576]{0:T(1024)(128)(4,1)}), pred[512]{0:T(512)(128)(4,1)S(1)}, s32[]{:S(2)}) async-start(pred[576]{0:T(1024)(128)(4,1)} %copy-done.17), calls=%async_computation.2 | async-start | bytes 1024 | tf_op jit(solution)/shard_map/slice | solution.py:85
  32.1 4.0 %copy-start.21 = (bf16[512,128]{1,0:T(8,128)(2,1)S(1)}, bf16[512,128]{1,0:T(8,128)(2,1)}, u32[]{:S(2)}) copy-start(bf16[512,128]{1,0:T(8,128)(2,1)} %param.12) | copy-start | bytes 393220
  36.1 6.7 %copy-start.18 = (pred[576]{0:T(1024)(128)(4,1)S(1)}, pred[576]{0:T(1024)(128)(4,1)}, u32[]{:S(2)}) copy-start(pred[576]{0:T(1024)(128)(4,1)} %copy-done.17) | copy-start | bytes 1732
  36.2 0.6 copy-start.28
  36.8 11.8 %copy-start.9 = (bf16[512,1024]{1,0:T(8,128)(2,1)S(1)}, bf16[512,1024]{1,0:T(8,128)(2,1)}, u32[]{:S(2)}) copy-start(bf16[512,1024]{1,0:T(8,128)(2,1)} %param.10) | copy-start | bytes 3145732
  36.8 11.8 %collective-permute-start.2 = (f32[66048]{0:T(1024)S(1)}, f32[66048]{0:T(1024)S(1)}, u32[]{:S(2)}, u32[]{:S(2)}) collective-permute-start(f32[66048]{0:T(1024)S(1)} %pad_maximum_fusion.3), channel_id=1, source_target_pairs={{0,8},{8,16},{16,24},{24,32},{32,40},{40,48},{48,56},{56,64},{64,7... | collective-permute-start | bytes 792584 | tf_op jit(solution)/shard_map/ppermute | solution.py:16
  41.5 16.7 %collective-permute-start.7 = (f32[66048]{0:T(1024)}, f32[66048]{0:T(1024)}, u32[]{:S(2)}, u32[]{:S(2)}) collective-permute-start(f32[66048]{0:T(1024)} %pad_maximum_fusion.4), channel_id=1, source_target_pairs={{0,64},{8,72},{16,80},{24,88},{32,96},{40,104},{48,112},{56,120},{... | collective-permute-start | bytes 792584 | tf_op jit(solution)/shard_map/ppermute | solution.py:16
  48.6 1.3 copy-start.3
  52.2 9.3 %copy-start.10 = (f32[512,64]{1,0:T(8,128)S(1)}, f32[512,64]{1,0:T(8,128)}, u32[]{:S(2)}) copy-start(f32[512,64]{1,0:T(8,128)} %copy.57) | copy-start | bytes 393220
  52.2 9.3 %copy-start.11 = (f32[512,64]{1,0:T(8,128)S(1)}, f32[512,64]{1,0:T(8,128)}, u32[]{:S(2)}) copy-start(f32[512,64]{1,0:T(8,128)} %copy.55) | copy-start | bytes 393220
  54.1 22.9 %collective-permute-start.3 = (f32[66048]{0:T(1024)}, f32[66048]{0:T(1024)}, u32[]{:S(2)}, u32[]{:S(2)}) collective-permute-start(f32[66048]{0:T(1024)} %fusion.135), channel_id=1, source_target_pairs={{0,16},{8,24},{16,32},{24,40},{32,48},{40,56},{48,64},{56,72},{64,... | collective-permute-start | bytes 792584 | tf_op jit(solution)/shard_map/ppermute | solution.py:16
  60.0 34.3 %collective-permute-start.8 = (f32[66048]{0:T(1024)}, f32[66048]{0:T(1024)S(1)}, u32[]{:S(2)}, u32[]{:S(2)}) collective-permute-start(f32[66048]{0:T(1024)} %fusion.134), channel_id=1, source_target_pairs={{0,128},{8,136},{16,144},{24,152},{32,160},{40,168},{48,176},{56,1... | collective-permute-start | bytes 792584 | tf_op jit(solution)/shard_map/ppermute | solution.py:16
  64.3 2.5 %copy-start.1 = (pred[512,576]{0,1:T(8,128)(4,1)S(1)}, pred[512,576]{0,1:T(8,128)(4,1)}, u32[]{:S(2)}) copy-start(pred[512,576]{0,1:T(8,128)(4,1)} %get-tuple-element.36) | copy-start | bytes 884740
  64.3 2.5 %copy-start.6 = (bf16[512,1,64]{0,2,1:T(8,128)(2,1)S(1)}, bf16[512,1,64]{0,2,1:T(8,128)(2,1)}, u32[]{:S(2)}) copy-start(bf16[512,1,64]{0,2,1:T(8,128)(2,1)} %copy-done.5) | copy-start | bytes 196612
  64.3 2.5 %copy-start.8 = (bf16[512,1,64]{0,2,1:T(8,128)(2,1)S(1)}, bf16[512,1,64]{0,2,1:T(8,128)(2,1)}, u32[]{:S(2)}) copy-start(bf16[512,1,64]{0,2,1:T(8,128)(2,1)} %copy-done.7) | copy-start | bytes 196612
  64.3 2.5 %copy-start.14 = (bf16[64,1,128]{0,2,1:T(8,128)(2,1)S(1)}, bf16[64,1,128]{0,2,1:T(8,128)(2,1)}, u32[]{:S(2)}) copy-start(bf16[64,1,128]{0,2,1:T(8,128)(2,1)} %copy-done.13) | copy-start | bytes 49156
  69.4 2.6 %copy-start.22 = (bf16[512,128]{1,0:T(8,128)(2,1)S(1)}, bf16[512,128]{1,0:T(8,128)(2,1)}, u32[]{:S(2)}) copy-start(bf16[512,128]{1,0:T(8,128)(2,1)} %param.12) | copy-start | bytes 393220
  69.4 2.6 %copy-start.29 = (bf16[64,1,128]{2,0,1:T(8,128)(2,1)S(1)}, bf16[64,1,128]{2,0,1:T(8,128)(2,1)}, u32[]{:S(2)}) copy-start(bf16[64,1,128]{2,0,1:T(8,128)(2,1)} %copy-done.28) | copy-start | bytes 49156
  76.9 15.8 %copy-start.2 = (bf16[576,8,128]{2,1,0:T(8,128)(2,1)S(1)}, bf16[576,8,128]{2,1,0:T(8,128)(2,1)}, u32[]{:S(2)}) copy-start(bf16[576,8,128]{2,1,0:T(8,128)(2,1)} %fusion.14) | copy-start | bytes 3538948
  76.9 15.8 %copy-start.12 = (pred[512,576]{0,1:T(8,128)(4,1)S(1)}, pred[512,576]{0,1:T(8,128)(4,1)}, u32[]{:S(2)}) copy-start(pred[512,576]{0,1:T(8,128)(4,1)} %get-tuple-element.37) | copy-start | bytes 884740
  78.1 13.3 %collective-permute-start.4 = (f32[66048]{0:T(1024)S(1)}, f32[66048]{0:T(1024)S(1)}, u32[]{:S(2)}, u32[]{:S(2)}) collective-permute-start(f32[66048]{0:T(1024)S(1)} %add.231), channel_id=1, source_target_pairs={{0,32},{8,40},{16,48},{24,56},{32,64},{40,72},{48,80},{56,88},{64,... | collective-permute-start | bytes 792584 | tf_op jit(solution)/shard_map/ppermute | solution.py:16
  91.4 18.6 %collective-permute-start.5 = (f32[66048]{0:T(1024)S(1)}, f32[66048]{0:T(1024)S(1)}, u32[]{:S(2)}, u32[]{:S(2)}) collective-permute-start(f32[66048]{0:T(1024)S(1)} %add.233), channel_id=1, source_target_pairs={{0,64},{8,72},{16,80},{24,88},{32,96},{40,104},{48,112},{56,120},{... | collective-permute-start | bytes 792584 | tf_op jit(solution)/shard_map/ppermute | solution.py:16
  92.7 18.8 %copy-start.23 = (bf16[512,128]{1,0:T(8,128)(2,1)S(1)}, bf16[512,128]{1,0:T(8,128)(2,1)}, u32[]{:S(2)}) copy-start(bf16[512,128]{1,0:T(8,128)(2,1)} %param.12) | copy-start | bytes 393220
  92.8 18.8 %copy-start.30 = (bf16[64,1,128]{2,0,1:T(8,128)(2,1)S(1)}, bf16[64,1,128]{2,0,1:T(8,128)(2,1)}, u32[]{:S(2)}) copy-start(bf16[64,1,128]{2,0,1:T(8,128)(2,1)} %copy-done.28) | copy-start | bytes 49156
  95.3 18.8 %collective-permute-start.9 = (f32[66048]{0:T(1024)S(1)}, f32[66048]{0:T(1024)S(1)}, u32[]{:S(2)}, u32[]{:S(2)}) collective-permute-start(f32[66048]{0:T(1024)S(1)} %add.248), channel_id=1, source_target_pairs={{0,8},{8,16},{16,24},{24,32},{32,40},{40,48},{48,56},{56,64},{64,7... | collective-permute-start | bytes 792584 | tf_op jit(solution)/shard_map/ppermute | solution.py:16
  110.0 9.8 %collective-permute-start.6 = (f32[66048]{0:T(1024)S(1)}, f32[66048]{0:T(1024)S(1)}, u32[]{:S(2)}, u32[]{:S(2)}) collective-permute-start(f32[66048]{0:T(1024)S(1)} %add.235), channel_id=1, source_target_pairs={{0,128},{8,136},{16,144},{24,152},{32,160},{40,168},{48,176},{56,1... | collective-permute-start | bytes 792584 | tf_op jit(solution)/shard_map/ppermute | solution.py:16
  114.0 5.8 %copy-start.4 = (f32[66048]{0:T(1024)S(1)}, f32[66048]{0:T(1024)}, u32[]{:S(2)}) copy-start(f32[66048]{0:T(1024)} %copy-done.3) | copy-start | bytes 792580
  114.1 15.5 %collective-permute-start.10 = (f32[66048]{0:T(1024)S(1)}, f32[66048]{0:T(1024)S(1)}, u32[]{:S(2)}, u32[]{:S(2)}) collective-permute-start(f32[66048]{0:T(1024)S(1)} %add.249), channel_id=1, source_target_pairs={{0,16},{8,24},{16,32},{24,40},{32,48},{40,56},{48,64},{56,72},{64,... | collective-permute-start | bytes 792584 | tf_op jit(solution)/shard_map/ppermute | solution.py:16
  120.9 0.9 copy-start.16
  120.9 0.9 copy-start.19
  120.9 0.9 copy-start.20
  120.9 1.0 copy-start.26
  121.0 1.0 copy-start.27
  125.1 25.7 %all-to-all-start = ((bf16[8,64,512]{2,1,0:T(8,128)(2,1)}), bf16[8,64,512]{2,1,0:T(8,128)(2,1)S(1)}, u32[]{:S(2)}, u32[]{:S(2)}) async-start(bf16[8,64,512]{2,1,0:T(8,128)(2,1)} %all_to_all.24), calls=%async_computation | async-start | bytes 1048576 | tf_op jit(solution)/shard_map/all_to_all | solution.py:202
  129.7 21.2 %collective-permute-start.11 = (f32[66048]{0:T(1024)S(1)}, f32[66048]{0:T(1024)S(1)}, u32[]{:S(2)}, u32[]{:S(2)}) collective-permute-start(f32[66048]{0:T(1024)S(1)} %add.250), channel_id=1, source_target_pairs={{0,32},{8,40},{16,48},{24,56},{32,64},{40,72},{48,80},{56,88},{64,... | collective-permute-start | bytes 792584 | tf_op jit(solution)/shard_map/ppermute | solution.py:16
  151.9 0.9 copy-start.24
  152.0 0.9 copy-start.25

commit v8 on v3

--- a/solution.py
+++ b/solution.py
@@ -3,6 +3,7 @@
 import jax
 import jax.numpy as jnp
 from jax import lax
+from jax.experimental import pallas as pl
 from jax.sharding import PartitionSpec as P
 
 WINDOW = 64
@@ -52,6 +53,49 @@
     high_part = full_value.astype(jnp.bfloat16)
     rest_part = (full_value - high_part.astype(jnp.float32)).astype(jnp.bfloat16)
     return (high_part, rest_part)
+
+
+def key_features(ext_keys2, key_map, ext_values2, mask, lag):
+    rows, dim = ext_keys2.shape
+    heads, _, feat = key_map.shape
+
+    def kernel(k_ref, m_ref, v_ref, mask_ref, phi_ref, st_ref, nm_ref):
+        logits = jnp.dot(k_ref[...], m_ref[0], preferred_element_type=jnp.float32)
+        live = mask_ref[...] > 0.0
+        values = v_ref[0:lag, :]
+        for place, sign in enumerate((1.0, -1.0)):
+            shifted = sign * logits
+            expo = jnp.exp(shifted - jnp.max(shifted, axis=-1, keepdims=True))
+            soft = expo / jnp.sum(expo, axis=-1, keepdims=True)
+            phi = jnp.where(live, soft, 0.0).astype(jnp.bfloat16)
+            cols = slice(place * feat, (place + 1) * feat)
+            phi_ref[0, :, cols] = phi
+            lagged = phi[0:lag, :]
+            st_ref[0, cols, :] = lax.dot_general(
+                lagged, values, (((0,), (0,)), ((), ())), preferred_element_type=jnp.float32
+            )
+            nm_ref[0, :, cols] = jnp.sum(lagged.astype(jnp.float32), axis=0, keepdims=True)
+
+    return pl.pallas_call(
+        kernel,
+        grid=(heads,),
+        in_specs=[
+            pl.BlockSpec((rows, dim), lambda h: (0, 0)),
+            pl.BlockSpec((1, dim, feat), lambda h: (h, 0, 0)),
+            pl.BlockSpec((rows, dim), lambda h: (0, 0)),
+            pl.BlockSpec((rows, 1), lambda h: (0, 0)),
+        ],
+        out_specs=[
+            pl.BlockSpec((1, rows, 2 * feat), lambda h: (h, 0, 0)),
+            pl.BlockSpec((1, 2 * feat, dim), lambda h: (h, 0, 0)),
+            pl.BlockSpec((1, 1, 2 * feat), lambda h: (h, 0, 0)),
+        ],
+        out_shape=[
+            jax.ShapeDtypeStruct((heads, rows, 2 * feat), jnp.bfloat16),
+            jax.ShapeDtypeStruct((heads, 2 * feat, dim), jnp.float32),
+            jax.ShapeDtypeStruct((heads, 1, 2 * feat), jnp.float32),
+        ],
+    )(ext_keys2, key_map, ext_values2, mask)
 
 
 def body(queries, keys, values, offsets, query_map, key_map, window_logit):
@@ -75,19 +119,17 @@
     ext_keys = jnp.concatenate([tail_keys, rot_k], axis=0)
     ext_values = jnp.concatenate([tail_values, value_rows], axis=0)
     valid = (jnp.arange(tokens + WINDOW) >= WINDOW) | (lax.axis_index("seq") > 0)
-    grouped_map = key_map.reshape(kv_local, group, head_dim, feat)
-    key_logits = jnp.einsum(
-        "ngd,gkdf->ngkf", ext_keys, grouped_map, preferred_element_type=jnp.float32
-    )
-    phi_key = jnp.where(valid[:, None, None, None], two_softmax(key_logits), 0.0).astype(
-        jnp.bfloat16
-    )
-    lag_phi = phi_key[:tokens].reshape(blocks, BLOCK, kv_local, group, 2 * feat)
-    lag_values = ext_values[:tokens].reshape(blocks, BLOCK, kv_local, head_dim)
-    block_states = jnp.einsum(
-        "bjgkf,bjgd->bgkfd", lag_phi, lag_values, preferred_element_type=jnp.float32
-    )
-    block_norms = jnp.sum(lag_phi, axis=1, dtype=jnp.float32)
+    ext_rows = tokens + WINDOW
+    phi_heads, state_heads, norm_heads = key_features(
+        ext_keys.reshape(ext_rows, head_dim),
+        key_map,
+        ext_values.reshape(ext_rows, head_dim),
+        valid.astype(jnp.float32)[:, None],
+        tokens,
+    )
+    phi_key = phi_heads.reshape(kv_local, group, ext_rows, 2 * feat)
+    block_states = state_heads.reshape(1, kv_local, group, 2 * feat, head_dim)
+    block_norms = norm_heads.reshape(1, kv_local, group, 2 * feat)
     total_state = jnp.sum(block_states, axis=0)
     total_norm = jnp.sum(block_norms, axis=0)
     before_state = jnp.concatenate(
@@ -145,7 +187,7 @@
     peak = jnp.max(jnp.where(near_window, scores, -jnp.inf), axis=-1, keepdims=True)
     weights = jnp.where(near_window, jnp.exp(scores - peak), 0.0)
     window_sum = jnp.sum(weights, axis=-1)
-    affinity = jnp.einsum("igkf,jgkf->gkij", phi_query, phi_key, preferred_element_type=jnp.float32)
+    affinity = jnp.einsum("igkf,gkjf->gkij", phi_query, phi_key, preferred_element_type=jnp.float32)
     affinity = jnp.where(linear_mask & live, affinity, 0.0)
     near_sum = jnp.sum(affinity, axis=-1)
     window_num = jnp.einsum(

time: 165 us -> 162 us (0.982)
  other arithmetic: 35.6 us -> 24.6 us
  Pallas kernels: 0 us -> 8.38 us
  waiting for transfers between devices: 32.2 us -> 36.6 us
  local copies, waits for them, and re-layouts: 15.1 us -> 12.7 us
  matrix products: 20.6 us -> 18.5 us
    pallas_call x0 -> x1, Pallas kernels: none -> 8.38 us  [key_features(): pl.pallas_call(kernel, grid=(heads,), in_specs=[pl.BlockSpec((rows, dim),...]
    reduce_sum x2 -> x0, other arithmetic: 7.57 us -> none  [the longest x1 3.97 us: body(): block_norms = jnp.sum(lag_phi, axis=1, dtype=jnp.float32)]
    ppermute x12, waiting for transfers between devices: 32.2 us -> 36.6 us  [passed_along(): lax.ppermute(value, axis, [(source, source + steps) for source in range(f...]
    convert_element_type x1, other arithmetic: 4.3 us -> 0.73 us  [body(): valid.astype(jnp.float32)[:, None]]
    div x1 -> x0, other arithmetic: 3.11 us -> none  [two_softmax(): jax.nn.softmax(logits, axis=-1)]
    another operation x3 -> x5, other arithmetic: 6.37 us -> 9.42 us
    dot_general x1 -> x0, local copies, waits for them, and re-layouts: 2.31 us -> none  [body(): jnp.einsum('ngd,gkdf->ngkf', ext_keys, grouped_map, preferred_element_typ...]
    unnamed x72 -> x58, local copies, waits for them, and re-layouts: 7.08 us -> 6.05 us
  transfers between devices with their start and end apart: 12 -> 12, of which waited for: 6 -> 6; matrix products, arithmetic and copies ran while one was open for 31% -> 21% of each run, Pallas kernels for 0% -> 0%
where the time goes in v8:
time: 162 us; the launch traced here: 160 us
  starting transfers between devices  38.7 us (24%)
  waiting for transfers between devices  36.6 us (23%)
  other arithmetic  24.6 us (15%)
  blocking collectives  20.3 us (13%)
  matrix products  18.5 us (11%)
  local copies, waits for them, and re-layouts  12.7 us (8%)
  Pallas kernels  8.38 us (5%)
    ppermute x12, starting transfers between devices, passed_along(): lax.ppermute(value, axis, [(source, source + steps) for source in range(f...  38.7 us
    ppermute x12, waiting for transfers between devices, passed_along(): lax.ppermute(value, axis, [(source, source + steps) for source in range(f...  36.6 us
    all_to_all x1, blocking collectives, body(): lax.all_to_all(result, 'head', split_axis=0, concat_axis=1, tiled=True)  20.3 us
    another operation x5, other arithmetic  9.42 us
    pallas_call x1, Pallas kernels, key_features(): pl.pallas_call(kernel, grid=(heads,), in_specs=[pl.BlockSpec((rows, dim),...  8.38 us
    unnamed x58, local copies, waits for them, and re-layouts  6.05 us
    add x8, other arithmetic, body(): inclusive = inclusive + received  4.83 us
    dot_general x1, matrix products, body(): jnp.einsum('gkij,jgd->igkd', affinity.astype(jnp.bfloat16), ext_values, p...  3.71 us
  transfers between devices with their start and end apart: 12, of which 6 were waited for; matrix products, arithmetic and copies ran while one was open for 21% of the time, Pallas kernels for 0%

profile of v8, /device:TPU:2, one launch (start us, length us, event | category | flops | bytes accessed | tf_op | source)
XLA Modules:
  0.0 160.3 jit_solution(10628523435817839078)
XLA Ops:
  0.0 0.8 add_bitcast_fusion
  0.8 0.9 bitcast_convert_fusion
  1.8 4.0 %subtract_convert_fusion.3 = (bf16[512,1,64]{2,0,1:T(8,128)(2,1)S(1)}, bf16[512,1,64]{2,0,1:T(8,128)(2,1)S(1)}) fusion(f32[512,1,128]{2,0,1:T(8,128)S(1)} %bitcast_convert_fusion, f32[64]{0:T(128)} %constant.75.clone, f32[512]{0:T(512)S(1)} %get-tuple-element.27, f32[64]{0:T(128)} %constant.74.clone, f32[512]{0:T(512)S(1)} %get-tuple-element.26, ...), kind=kLoop, calls=%fused_computation.70 | loop fusion | flops 753664 | bytes 400128 | tf_op jit(solution)/shard_map/convert.6
  5.9 3.8 %collective-permute-start.1 = (bf16[64,1,128]{2,0,1:T(8,128)(2,1)S(1)}, bf16[64,1,128]{2,0,1:T(8,128)(2,1)S(1)}, u32[]{:S(2)}, u32[]{:S(2)}) collective-permute-start(bf16[64,1,128]{2,0,1:T(8,128)(2,1)S(1)} %pad_maximum_fusion.15), channel_id=1, source_target_pairs={{0,8},{8,16},{16,24},{24,32},{32,40},{40,48},{48,56},{56,64},{64,7... | collective-permute-start | bytes 49160 | tf_op jit(solution)/shard_map/ppermute | solution.py:17
  9.7 0.7 slice_bitcast_fusion
  10.4 3.8 %collective-permute-start = (bf16[64,1,128]{2,0,1:T(8,128)(2,1)S(1)}, bf16[64,1,128]{2,0,1:T(8,128)(2,1)S(1)}, u32[]{:S(2)}, u32[]{:S(2)}) collective-permute-start(bf16[64,1,128]{2,0,1:T(8,128)(2,1)S(1)} %slice_bitcast_fusion), channel_id=1, source_target_pairs={{0,8},{8,16},{16,24},{24,32},{32,40},{40,48},{48,56},{56,64},{64,7... | collective-permute-start | bytes 49160 | tf_op jit(solution)/shard_map/ppermute | solution.py:17
  14.3 2.2 %fusion.53 = (f32[512,64]{0,1:T(8,128)S(1)}, f32[512,64]{0,1:T(8,128)S(1)}) fusion(f32[64]{0:T(128)} %constant.75.clone, f32[512]{0:T(512)S(1)} %get-tuple-element.27, f32[64]{0:T(128)} %constant.74.clone, f32[512]{0:T(512)S(1)} %get-tuple-element.26, f32[64]{0:T(128)} %constant.73.clone, f32[512]{0:T(512)S(1)} %get-tuple-element.25), kind=kLoop, calls=%fused_computation.91 | loop fusion | flops 491520 | bytes 269056 | tf_op jit(solution)/shard_map/sub | solution.py:30
  16.5 0.7 fusion.35.mask_ref
  17.2 0.6 broadcast_subtract_fusion
  17.8 0.8 copy.39.m_ref
  18.7 0.8 fusion.88.k_ref
  19.4 0.7 fusion.60.v_ref
  20.1 8.4 %shard_map.100 = (bf16[8,576,128]{2,1,0:T(8,128)(2,1)}, f32[8,128,128]{2,1,0:T(8,128)}, f32[8,1,128]{2,1,0:T(1,128)}) custom-call(bf16[576,128]{1,0:T(8,128)(2,1)} %fusion.88.k_ref, bf16[8,128,64]{2,1,0:T(8,128)(2,1)} %copy.39.m_ref, bf16[576,128]{1,0:T(8,128)(2,1)} %fusion.60.v_ref, f32[576,1]{1,0:T(8,128)} %fusion.35.mask_ref), custom_call_target="tpu_custom_call" | custom-call | tf_op jit(solution)/shard_map/pallas_call | solution.py:79
  28.5 1.0 slice.59
  29.4 3.8 %collective-permute-start.2 = (f32[66048]{0:T(1024)S(1)}, f32[66048]{0:T(1024)}, u32[]{:S(2)}, u32[]{:S(2)}) collective-permute-start(f32[66048]{0:T(1024)S(1)} %slice.59), channel_id=1, source_target_pairs={{0,8},{8,16},{16,24},{24,32},{32,40},{40,48},{48,56},{56,64},{64,7... | collective-permute-start | bytes 792584 | tf_op jit(solution)/shard_map/ppermute | solution.py:17
  33.3 0.8 copy.42
  34.1 0.8 copy.44
  35.0 1.2 fusion.22
  36.1 5.0 %collective-permute-done.2 = f32[66048]{0:T(1024)} collective-permute-done((f32[66048]{0:T(1024)S(1)}, f32[66048]{0:T(1024)}, u32[]{:S(2)}, u32[]{:S(2)}) %collective-permute-start.2) | collective-permute-done | bytes 264224 | tf_op jit(solution)/shard_map/ppermute | solution.py:17
  41.1 0.5 copy.40
  41.7 0.3 fusion.90
  41.9 1.9 %copy.59 = f32[512,8,64]{2,0,1:T(8,128)} copy(f32[512,8,64]{0,2,1:T(8,128)S(1)} %get-tuple-element.18) | data formatting | bytes 2097152
  43.9 2.0 %copy.60 = f32[512,8,64]{2,0,1:T(8,128)} copy(f32[512,8,64]{0,2,1:T(8,128)S(1)} %get-tuple-element.17) | data formatting | bytes 2097152
  45.9 1.0 slice_add_fusion
  46.9 3.4 %collective-permute-start.7 = (f32[66048]{0:T(1024)S(1)}, f32[66048]{0:T(1024)S(1)}, u32[]{:S(2)}, u32[]{:S(2)}) collective-permute-start(f32[66048]{0:T(1024)S(1)} %get-tuple-element.20), channel_id=1, source_target_pairs={{0,64},{8,72},{16,80},{24,88},{32,96},{40,104},{48,112},{56,120},{... | collective-permute-start | bytes 792584 | tf_op jit(solution)/shard_map/ppermute | solution.py:17
  50.3 4.6 %collective-permute-start.3 = (f32[66048]{0:T(1024)S(1)}, f32[66048]{0:T(1024)S(1)}, u32[]{:S(2)}, u32[]{:S(2)}) collective-permute-start(f32[66048]{0:T(1024)S(1)} %get-tuple-element.19), channel_id=1, source_target_pairs={{0,16},{8,24},{16,32},{24,40},{32,48},{40,56},{48,64},{56,72},{64,... | collective-permute-start | bytes 792584 | tf_op jit(solution)/shard_map/ppermute | solution.py:17
  54.9 2.8 %subtract_convert_fusion = (bf16[512,8,64]{2,0,1:T(8,128)(2,1)S(1)}, bf16[512,8,64]{2,0,1:T(8,128)(2,1)S(1)}) fusion(f32[512,8,64]{2,0,1:T(8,128)} %copy.60, f32[512,8,64]{2,0,1:T(8,128)} %copy.59, f32[512,64]{1,0:T(8,128)S(1)} %copy-done.10, f32[512,64]{1,0:T(8,128)S(1)} %copy-done.9), kind=kLoop, calls=%fused_computation.23 | loop fusion | flops 2097152 | bytes 3407872 | tf_op jit(solution)/shard_map/convert.4
  57.7 2.4 %fusion.2 = (f32[8,512]{1,0:T(8,128)S(1)}, f32[576,512,8]{1,0,2:T(8,128)S(1)}) fusion(pred[512,576]{0,1:T(8,128)(4,1)S(1)} %copy-done.1, bf16[512,8,64]{2,0,1:T(8,128)(2,1)S(1)} %get-tuple-element.16, bf16[512,8,64]{2,0,1:T(8,128)(2,1)S(1)} %get-tuple-element.15, bf16[512,1,64]{2,0,1:T(8,128)(2,1)S(1)} %get-tuple-element.22, ...), kind=kOutput, calls=%fused_computation.4 | convolution fusion | flops 613593088 | bytes 10944512 | tf_op jit(solution)/shard_map/igkd,jgd->gkij/dot_general | solution.py:183
  60.1 2.5 %fusion.5 = f32[8,512]{1,0:T(8,128)} fusion(f32[576,512,8]{1,0,2:T(8,128)S(1)} %get-tuple-element.35, f32[8,512]{1,0:T(8,128)S(1)} %get-tuple-element.34, pred[512,576]{0,1:T(8,128)(4,1)S(1)} %copy-done.1), kind=kLoop, calls=%fused_computation.9 | loop fusion | flops 9433088 | bytes 9764864 | tf_op jit(solution)/shard_map/reduce_sum | solution.py:189
  62.7 3.5 %fusion.10 = f32[128,8,512]{2,0,1:T(8,128)} fusion(f32[576,512,8]{1,0,2:T(8,128)S(1)} %get-tuple-element.35, f32[8,512]{1,0:T(8,128)S(1)} %get-tuple-element.34, pred[512,576]{0,1:T(8,128)(4,1)S(1)} %copy-done.1, bf16[512,1,128]{2,0,1:T(8,128)(2,1)S(1)} %bitcast.143, bf16[64,1,128]{2,0,1:T(8,128)(2,1)S(1)} %copy-done.19), kind=kOutput, calls=%fused_computation.14 | convolution fusion | flops 613711872 | bytes 11993088 | tf_op jit(solution)/shard_map/gkij,jgd->igkd/dot_general | solution.py:193
  66.2 0.8 add.210
  67.0 1.9 %collective-permute-start.8 = (f32[66048]{0:T(1024)}, f32[66048]{0:T(1024)S(1)}, u32[]{:S(2)}, u32[]{:S(2)}) collective-permute-start(f32[66048]{0:T(1024)} %add.210), channel_id=1, source_target_pairs={{0,128},{8,136},{16,144},{24,152},{32,160},{40,168},{48,176},{56,1... | collective-permute-start | bytes 792584 | tf_op jit(solution)/shard_map/ppermute | solution.py:17
  68.9 0.8 add.204
  69.7 4.0 %collective-permute-start.4 = (f32[66048]{0:T(1024)}, f32[66048]{0:T(1024)}, u32[]{:S(2)}, u32[]{:S(2)}) collective-permute-start(f32[66048]{0:T(1024)} %add.204), channel_id=1, source_target_pairs={{0,32},{8,40},{16,48},{24,56},{32,64},{40,72},{48,80},{56,88},{64,... | collective-permute-start | bytes 792584 | tf_op jit(solution)/shard_map/ppermute | solution.py:17
  73.8 1.5 fusion.92
  75.2 2.5 %fusion.91 = (f32[512,8]{0,1:T(8,128)}, f32[512,8,64]{0,2,1:T(8,128)}) fusion(bf16[8,128,64]{1,2,0:T(8,128)(2,1)S(1)} %copy-done, bf16[512,8,64]{2,0,1:T(8,128)(2,1)S(1)} %get-tuple-element.16, bf16[512,8,64]{2,0,1:T(8,128)(2,1)S(1)} %get-tuple-element.15), kind=kOutput, calls=%fused_computation.154 | convolution fusion | flops 69992512 | bytes 2244608 | tf_op jit(solution)/shard_map/sub | solution.py:48
  77.7 1.1 add.212
  78.8 1.9 %collective-permute-start.9 = (f32[66048]{0:T(1024)S(1)}, f32[66048]{0:T(1024)S(1)}, u32[]{:S(2)}, u32[]{:S(2)}) collective-permute-start(f32[66048]{0:T(1024)S(1)} %add.212), channel_id=1, source_target_pairs={{0,8},{8,16},{16,24},{24,32},{32,40},{40,48},{48,56},{56,64},{64,7... | collective-permute-start | bytes 792584 | tf_op jit(solution)/shard_map/ppermute | solution.py:17
  80.7 6.4 %collective-permute-done.4 = f32[66048]{0:T(1024)} collective-permute-done((f32[66048]{0:T(1024)}, f32[66048]{0:T(1024)}, u32[]{:S(2)}, u32[]{:S(2)}) %collective-permute-start.4) | collective-permute-done | bytes 264224 | tf_op jit(solution)/shard_map/ppermute | solution.py:17
  87.1 1.1 add.206
  88.2 1.9 %collective-permute-start.5 = (f32[66048]{0:T(1024)S(1)}, f32[66048]{0:T(1024)S(1)}, u32[]{:S(2)}, u32[]{:S(2)}) collective-permute-start(f32[66048]{0:T(1024)S(1)} %add.206), channel_id=1, source_target_pairs={{0,64},{8,72},{16,80},{24,88},{32,96},{40,104},{48,112},{56,120},{... | collective-permute-start | bytes 792584 | tf_op jit(solution)/shard_map/ppermute | solution.py:17
  90.1 1.2 divide_convert_fusion
  91.3 3.0 %collective-permute-done.9 = f32[66048]{0:T(1024)S(1)} collective-permute-done((f32[66048]{0:T(1024)S(1)}, f32[66048]{0:T(1024)S(1)}, u32[]{:S(2)}, u32[]{:S(2)}) %collective-permute-start.9) | collective-permute-done | bytes 264224 | tf_op jit(solution)/shard_map/ppermute | solution.py:17
  94.3 4.3 %collective-permute-start.10 = (f32[66048]{0:T(1024)S(1)}, f32[66048]{0:T(1024)S(1)}, u32[]{:S(2)}, u32[]{:S(2)}) collective-permute-start(f32[66048]{0:T(1024)S(1)} %add.214), channel_id=1, source_target_pairs={{0,16},{8,24},{16,32},{24,40},{32,48},{40,56},{48,64},{56,72},{64,... | collective-permute-start | bytes 792584 | tf_op jit(solution)/shard_map/ppermute | solution.py:17
  98.7 0.4 collective-permute-done.5
  99.1 2.8 %collective-permute-start.6 = (f32[66048]{0:T(1024)S(1)}, f32[66048]{0:T(1024)S(1)}, u32[]{:S(2)}, u32[]{:S(2)}) collective-permute-start(f32[66048]{0:T(1024)S(1)} %add.208), channel_id=1, source_target_pairs={{0,128},{8,136},{16,144},{24,152},{32,160},{40,168},{48,176},{56,1... | collective-permute-start | bytes 792584 | tf_op jit(solution)/shard_map/ppermute | solution.py:17
  101.9 3.7 %select_reduce_fusion = (f32[8,512]{1,0:T(8,128)S(1)}, bf16[8,512,576]{1,2,0:T(8,128)(2,1)}) fusion(pred[512,576]{0,1:T(8,128)(4,1)S(1)} %copy-done.11, bf16[8,576,128]{2,1,0:T(8,128)(2,1)S(1)} %copy-done.24, bf16[512,8,64]{0,2,1:T(8,128)(2,1)S(1)} %get-tuple-element.38, bf16[512,8,64]{0,2,1:T(8,128)(2,1)S(1)} %get-tuple-element.39), kind=kOutput, calls=%fused_computation.7 | convolution fusion | flops 613150720 | bytes 7258112 | tf_op jit(solution)/shard_map/igkf,gkjf->gkij/dot_general | solution.py:190
  105.5 5.7 %collective-permute-done.10 = f32[66048]{0:T(1024)S(1)} collective-permute-done((f32[66048]{0:T(1024)S(1)}, f32[66048]{0:T(1024)S(1)}, u32[]{:S(2)}, u32[]{:S(2)}) %collective-permute-start.10) | collective-permute-done | bytes 264224 | tf_op jit(solution)/shard_map/ppermute | solution.py:17
  111.2 2.4 %collective-permute-start.11 = (f32[66048]{0:T(1024)S(1)}, f32[66048]{0:T(1024)S(1)}, u32[]{:S(2)}, u32[]{:S(2)}) collective-permute-start(f32[66048]{0:T(1024)S(1)} %add.216), channel_id=1, source_target_pairs={{0,32},{8,40},{16,48},{24,56},{32,64},{40,72},{48,80},{56,88},{64,... | collective-permute-start | bytes 792584 | tf_op jit(solution)/shard_map/ppermute | solution.py:17
  113.6 1.1 add_add_fusion.1
  114.8 16.2 %collective-permute-done.11 = f32[66048]{0:T(1024)S(1)} collective-permute-done((f32[66048]{0:T(1024)S(1)}, f32[66048]{0:T(1024)S(1)}, u32[]{:S(2)}, u32[]{:S(2)}) %collective-permute-start.11) | collective-permute-done | bytes 264224 | tf_op jit(solution)/shard_map/ppermute | solution.py:17
  131.1 0.2 copy.46
  131.3 0.4 fusion.40
  131.7 0.4 fusion.58
  132.2 0.2 fusion.66
  132.5 0.2 fusion.64
  132.7 0.2 copy-done.17
  132.9 0.2 copy-done.12
  133.2 0.8 copy-done.26
  134.0 3.7 %fusion.17 = bf16[512,1,8,128]{0,3,2,1:T(8,128)(2,1)S(1)} fusion(f32[8,128,512]{2,1,0:T(8,128)S(1)} %fusion.58, f32[8,128,512]{2,1,0:T(8,128)S(1)} %fusion.40, f32[128,8,512]{2,0,1:T(8,128)S(1)} %copy-done.26, bf16[8,512,576]{1,2,0:T(8,128)(2,1)} %get-tuple-element.37, pred[512,576]{0,1:T(8,128)(4,1)S(1)} %copy-done.12, f32[512,8]{0,1:T(8,128)S(1)} %fusion.62, ...), kind=kOutput, calls=%fused_computation.24 | convolution fusion | flops 610304000 | bytes 12517440 | tf_op jit(solution)/shard_map/gkij,jgd->igkd/dot_general | solution.py:199
  137.7 0.8 copy.50
  138.5 0.5 all_to_all.14
  139.0 20.3 %all_to_all.19 = bf16[8,64,1024]{2,1,0:T(8,128)(2,1)S(1)} all-to-all(bf16[8,64,1024]{2,1,0:T(8,128)(2,1)S(1)} %all_to_all.14), channel_id=1, replica_groups=mesh['seq'=32,'head'=8] {'head'}, dimensions={0} | all-to-all | bytes 2097152 | tf_op jit(solution)/shard_map/all_to_all | solution.py:226
  159.3 1.1 copy.61
  (70 shorter events, 0.6 us)
Async XLA Ops:
  0.0 73.8 %copy-start = (bf16[8,128,64]{1,2,0:T(8,128)(2,1)S(1)}, bf16[8,128,64]{1,2,0:T(8,128)(2,1)}, u32[]{:S(2)}) copy-start(bf16[8,128,64]{1,2,0:T(8,128)(2,1)} %param.14) | copy-start | bytes 393220
  0.0 19.4 %copy-start.13 = (bf16[512,128]{1,0:T(8,128)(2,1)S(1)}, bf16[512,128]{1,0:T(8,128)(2,1)}, u32[]{:S(2)}) copy-start(bf16[512,128]{1,0:T(8,128)(2,1)} %param.12) | copy-start | bytes 393220
  0.0 17.2 %copy-start.25 = (f32[8]{0:T(128)S(1)}, f32[8]{0:T(128)}, u32[]{:S(2)}) copy-start(f32[8]{0:T(128)} %param.16) | copy-start | bytes 100
  0.0 17.8 %copy-start.16 = (bf16[8,128,64]{1,2,0:T(8,128)(2,1)S(1)}, bf16[8,128,64]{1,2,0:T(8,128)(2,1)}, u32[]{:S(2)}) copy-start(bf16[8,128,64]{1,2,0:T(8,128)(2,1)} %param.15) | copy-start | bytes 393220
  5.9 12.8 %collective-permute-start.1 = (bf16[64,1,128]{2,0,1:T(8,128)(2,1)S(1)}, bf16[64,1,128]{2,0,1:T(8,128)(2,1)S(1)}, u32[]{:S(2)}, u32[]{:S(2)}) collective-permute-start(bf16[64,1,128]{2,0,1:T(8,128)(2,1)S(1)} %pad_maximum_fusion.15), channel_id=1, source_target_pairs={{0,8},{8,16},{16,24},{24,32},{32,40},{40,48},{48,56},{56,64},{64,7... | collective-permute-start | bytes 49160 | tf_op jit(solution)/shard_map/ppermute | solution.py:17
  10.4 9.0 %collective-permute-start = (bf16[64,1,128]{2,0,1:T(8,128)(2,1)S(1)}, bf16[64,1,128]{2,0,1:T(8,128)(2,1)S(1)}, u32[]{:S(2)}, u32[]{:S(2)}) collective-permute-start(bf16[64,1,128]{2,0,1:T(8,128)(2,1)S(1)} %slice_bitcast_fusion), channel_id=1, source_target_pairs={{0,8},{8,16},{16,24},{24,32},{32,40},{40,48},{48,56},{56,64},{64,7... | collective-permute-start | bytes 49160 | tf_op jit(solution)/shard_map/ppermute | solution.py:17
  16.4 24.7 %copy-start.8 = (bf16[512,1024]{1,0:T(8,128)(2,1)S(1)}, bf16[512,1024]{1,0:T(8,128)(2,1)}, u32[]{:S(2)}) copy-start(bf16[512,1024]{1,0:T(8,128)(2,1)} %param.10) | copy-start | bytes 3145732
  19.4 16.7 %copy-start.18 = (bf16[64,1,128]{2,0,1:T(8,128)(2,1)}, bf16[64,1,128]{2,0,1:T(8,128)(2,1)S(1)}, u32[]{:S(2)}) copy-start(bf16[64,1,128]{2,0,1:T(8,128)(2,1)S(1)} %collective-permute-done) | copy-start | bytes 49156
  29.4 11.7 %collective-permute-start.2 = (f32[66048]{0:T(1024)S(1)}, f32[66048]{0:T(1024)}, u32[]{:S(2)}, u32[]{:S(2)}) collective-permute-start(f32[66048]{0:T(1024)S(1)} %slice.59), channel_id=1, source_target_pairs={{0,8},{8,16},{16,24},{24,32},{32,40},{40,48},{48,56},{56,64},{64,7... | collective-permute-start | bytes 792584 | tf_op jit(solution)/shard_map/ppermute | solution.py:17
  43.9 2.0 %copy-start.2 = (f32[8,128,128]{2,1,0:T(8,128)S(1)}, f32[8,128,128]{2,1,0:T(8,128)}, u32[]{:S(2)}) copy-start(f32[8,128,128]{2,1,0:T(8,128)} %get-tuple-element.9) | copy-start | bytes 1572868
  43.9 2.0 %copy-start.21 = (f32[8,1,128]{2,1,0:T(1,128)S(1)}, f32[8,1,128]{2,1,0:T(1,128)}, u32[]{:S(2)}) copy-start(f32[8,1,128]{2,1,0:T(1,128)} %get-tuple-element.12) | copy-start | bytes 12292
  43.9 11.0 %copy-start.9 = (f32[512,64]{1,0:T(8,128)S(1)}, f32[512,64]{1,0:T(8,128)}, u32[]{:S(2)}) copy-start(f32[512,64]{1,0:T(8,128)} %copy.42) | copy-start | bytes 393220
  43.9 11.0 %copy-start.10 = (f32[512,64]{1,0:T(8,128)S(1)}, f32[512,64]{1,0:T(8,128)}, u32[]{:S(2)}) copy-start(f32[512,64]{1,0:T(8,128)} %copy.44) | copy-start | bytes 393220
  46.9 19.3 %collective-permute-start.7 = (f32[66048]{0:T(1024)S(1)}, f32[66048]{0:T(1024)S(1)}, u32[]{:S(2)}, u32[]{:S(2)}) collective-permute-start(f32[66048]{0:T(1024)S(1)} %get-tuple-element.20), channel_id=1, source_target_pairs={{0,64},{8,72},{16,80},{24,88},{32,96},{40,104},{48,112},{56,120},{... | collective-permute-start | bytes 792584 | tf_op jit(solution)/shard_map/ppermute | solution.py:17
  50.3 7.4 %copy-start.1 = (pred[512,576]{0,1:T(8,128)(4,1)S(1)}, pred[512,576]{0,1:T(8,128)(4,1)}, u32[]{:S(2)}) copy-start(pred[512,576]{0,1:T(8,128)(4,1)} %get-tuple-element.29) | copy-start | bytes 884740
  50.3 18.6 %collective-permute-start.3 = (f32[66048]{0:T(1024)S(1)}, f32[66048]{0:T(1024)S(1)}, u32[]{:S(2)}, u32[]{:S(2)}) collective-permute-start(f32[66048]{0:T(1024)S(1)} %get-tuple-element.19), channel_id=1, source_target_pairs={{0,16},{8,24},{16,32},{24,40},{32,48},{40,56},{48,64},{56,72},{64,... | collective-permute-start | bytes 792584 | tf_op jit(solution)/shard_map/ppermute | solution.py:17
  60.1 2.6 %copy-start.14 = (bf16[512,128]{1,0:T(8,128)(2,1)S(1)}, bf16[512,128]{1,0:T(8,128)(2,1)}, u32[]{:S(2)}) copy-start(bf16[512,128]{1,0:T(8,128)(2,1)} %param.12) | copy-start | bytes 393220
  60.1 2.6 %copy-start.19 = (bf16[64,1,128]{2,0,1:T(8,128)(2,1)S(1)}, bf16[64,1,128]{2,0,1:T(8,128)(2,1)}, u32[]{:S(2)}) copy-start(bf16[64,1,128]{2,0,1:T(8,128)(2,1)} %copy-done.18) | copy-start | bytes 49156
  66.2 3.6 %copy-start.3 = (f32[66048]{0:T(1024)}, f32[66048]{0:T(1024)S(1)}, u32[]{:S(2)}) copy-start(f32[66048]{0:T(1024)S(1)} %collective-permute-done.7) | copy-start | bytes 792580
  67.0 10.7 %collective-permute-start.8 = (f32[66048]{0:T(1024)}, f32[66048]{0:T(1024)S(1)}, u32[]{:S(2)}, u32[]{:S(2)}) collective-permute-start(f32[66048]{0:T(1024)} %add.210), channel_id=1, source_target_pairs={{0,128},{8,136},{16,144},{24,152},{32,160},{40,168},{48,176},{56,1... | collective-permute-start | bytes 792584 | tf_op jit(solution)/shard_map/ppermute | solution.py:17
  68.9 0.8 copy-start.5
  69.7 17.4 %collective-permute-start.4 = (f32[66048]{0:T(1024)}, f32[66048]{0:T(1024)}, u32[]{:S(2)}, u32[]{:S(2)}) collective-permute-start(f32[66048]{0:T(1024)} %add.204), channel_id=1, source_target_pairs={{0,32},{8,40},{16,48},{24,56},{32,64},{40,72},{48,80},{56,88},{64,... | collective-permute-start | bytes 792584 | tf_op jit(solution)/shard_map/ppermute | solution.py:17
  77.7 12.4 %copy-start.7 = (f32[512,8,64]{0,2,1:T(8,128)S(1)}, f32[512,8,64]{0,2,1:T(8,128)}, u32[]{:S(2)}) copy-start(f32[512,8,64]{0,2,1:T(8,128)} %get-tuple-element.31) | copy-start | bytes 3145732
  78.8 15.5 %collective-permute-start.9 = (f32[66048]{0:T(1024)S(1)}, f32[66048]{0:T(1024)S(1)}, u32[]{:S(2)}, u32[]{:S(2)}) collective-permute-start(f32[66048]{0:T(1024)S(1)} %add.212), channel_id=1, source_target_pairs={{0,8},{8,16},{16,24},{24,32},{32,40},{40,48},{48,56},{56,64},{64,7... | collective-permute-start | bytes 792584 | tf_op jit(solution)/shard_map/ppermute | solution.py:17
  88.2 10.9 %collective-permute-start.5 = (f32[66048]{0:T(1024)S(1)}, f32[66048]{0:T(1024)S(1)}, u32[]{:S(2)}, u32[]{:S(2)}) collective-permute-start(f32[66048]{0:T(1024)S(1)} %add.206), channel_id=1, source_target_pairs={{0,64},{8,72},{16,80},{24,88},{32,96},{40,104},{48,112},{56,120},{... | collective-permute-start | bytes 792584 | tf_op jit(solution)/shard_map/ppermute | solution.py:17
  90.1 11.7 %copy-start.11 = (pred[512,576]{0,1:T(8,128)(4,1)S(1)}, pred[512,576]{0,1:T(8,128)(4,1)}, u32[]{:S(2)}) copy-start(pred[512,576]{0,1:T(8,128)(4,1)} %get-tuple-element.28) | copy-start | bytes 884740
  90.1 11.7 %copy-start.24 = (bf16[8,576,128]{2,1,0:T(8,128)(2,1)S(1)}, bf16[8,576,128]{2,1,0:T(8,128)(2,1)}, u32[]{:S(2)}) copy-start(bf16[8,576,128]{2,1,0:T(8,128)(2,1)} %get-tuple-element.11) | copy-start | bytes 3538948
  94.3 16.9 %collective-permute-start.10 = (f32[66048]{0:T(1024)S(1)}, f32[66048]{0:T(1024)S(1)}, u32[]{:S(2)}, u32[]{:S(2)}) collective-permute-start(f32[66048]{0:T(1024)S(1)} %add.214), channel_id=1, source_target_pairs={{0,16},{8,24},{16,32},{24,40},{32,48},{40,56},{48,64},{56,72},{64,... | collective-permute-start | bytes 792584 | tf_op jit(solution)/shard_map/ppermute | solution.py:17
  99.1 14.5 %collective-permute-start.6 = (f32[66048]{0:T(1024)S(1)}, f32[66048]{0:T(1024)S(1)}, u32[]{:S(2)}, u32[]{:S(2)}) collective-permute-start(f32[66048]{0:T(1024)S(1)} %add.208), channel_id=1, source_target_pairs={{0,128},{8,136},{16,144},{24,152},{32,160},{40,168},{48,176},{56,1... | collective-permute-start | bytes 792584 | tf_op jit(solution)/shard_map/ppermute | solution.py:17
  101.9 11.8 %copy-start.6 = (f32[66048]{0:T(1024)S(1)}, f32[66048]{0:T(1024)}, u32[]{:S(2)}) copy-start(f32[66048]{0:T(1024)} %copy-done.5) | copy-start | bytes 792580
  105.5 25.4 %copy-start.4 = (f32[66048]{0:T(1024)S(1)}, f32[66048]{0:T(1024)}, u32[]{:S(2)}) copy-start(f32[66048]{0:T(1024)} %copy-done.3) | copy-start | bytes 792580
  111.2 19.7 %collective-permute-start.11 = (f32[66048]{0:T(1024)S(1)}, f32[66048]{0:T(1024)S(1)}, u32[]{:S(2)}, u32[]{:S(2)}) collective-permute-start(f32[66048]{0:T(1024)S(1)} %add.216), channel_id=1, source_target_pairs={{0,32},{8,40},{16,48},{24,56},{32,64},{40,72},{48,80},{56,88},{64,... | collective-permute-start | bytes 792584 | tf_op jit(solution)/shard_map/ppermute | solution.py:17
  132.1 0.7 copy-start.17
  132.2 0.7 copy-start.22
  132.2 0.7 copy-start.23
  132.2 1.0 copy-start.12
  132.2 1.0 copy-start.15
  132.2 1.0 copy-start.20
  132.2 1.8 %copy-start.26 = (f32[128,8,512]{2,0,1:T(8,128)S(1)}, f32[128,8,512]{2,0,1:T(8,128)}, u32[]{:S(2)}) copy-start(f32[128,8,512]{2,0,1:T(8,128)} %fusion.10) | copy-start | bytes 6291460

commit v9 on v8

--- a/solution.py
+++ b/solution.py
@@ -60,35 +60,37 @@
     heads, _, feat = key_map.shape
 
     def kernel(k_ref, m_ref, v_ref, mask_ref, phi_ref, st_ref, nm_ref):
-        logits = jnp.dot(k_ref[...], m_ref[0], preferred_element_type=jnp.float32)
+        keys = k_ref[...]
         live = mask_ref[...] > 0.0
         values = v_ref[0:lag, :]
-        for place, sign in enumerate((1.0, -1.0)):
-            shifted = sign * logits
-            expo = jnp.exp(shifted - jnp.max(shifted, axis=-1, keepdims=True))
-            soft = expo / jnp.sum(expo, axis=-1, keepdims=True)
-            phi = jnp.where(live, soft, 0.0).astype(jnp.bfloat16)
-            cols = slice(place * feat, (place + 1) * feat)
-            phi_ref[0, :, cols] = phi
-            lagged = phi[0:lag, :]
-            st_ref[0, cols, :] = lax.dot_general(
-                lagged, values, (((0,), (0,)), ((), ())), preferred_element_type=jnp.float32
-            )
-            nm_ref[0, :, cols] = jnp.sum(lagged.astype(jnp.float32), axis=0, keepdims=True)
+        for head in range(heads):
+            logits = jnp.dot(keys, m_ref[head], preferred_element_type=jnp.float32)
+            for place, sign in enumerate((1.0, -1.0)):
+                shifted = sign * logits
+                expo = jnp.exp(shifted - jnp.max(shifted, axis=-1, keepdims=True))
+                soft = expo / jnp.sum(expo, axis=-1, keepdims=True)
+                phi = jnp.where(live, soft, 0.0).astype(jnp.bfloat16)
+                cols = slice(place * feat, (place + 1) * feat)
+                phi_ref[head, :, cols] = phi
+                lagged = phi[0:lag, :]
+                st_ref[head, cols, :] = lax.dot_general(
+                    lagged, values, (((0,), (0,)), ((), ())), preferred_element_type=jnp.float32
+                )
+                nm_ref[head, :, cols] = jnp.sum(lagged.astype(jnp.float32), axis=0, keepdims=True)
 
     return pl.pallas_call(
         kernel,
-        grid=(heads,),
+        grid=(1,),
         in_specs=[
             pl.BlockSpec((rows, dim), lambda h: (0, 0)),
-            pl.BlockSpec((1, dim, feat), lambda h: (h, 0, 0)),
+            pl.BlockSpec((heads, dim, feat), lambda h: (0, 0, 0)),
             pl.BlockSpec((rows, dim), lambda h: (0, 0)),
             pl.BlockSpec((rows, 1), lambda h: (0, 0)),
         ],
         out_specs=[
-            pl.BlockSpec((1, rows, 2 * feat), lambda h: (h, 0, 0)),
-            pl.BlockSpec((1, 2 * feat, dim), lambda h: (h, 0, 0)),
-            pl.BlockSpec((1, 1, 2 * feat), lambda h: (h, 0, 0)),
+            pl.BlockSpec((heads, rows, 2 * feat), lambda h: (0, 0, 0)),
+            pl.BlockSpec((heads, 2 * feat, dim), lambda h: (0, 0, 0)),
+            pl.BlockSpec((heads, 1, 2 * feat), lambda h: (0, 0, 0)),
         ],
         out_shape=[
             jax.ShapeDtypeStruct((heads, rows, 2 * feat), jnp.bfloat16),

time: 162 us -> 161 us (level)
  no operation moved by 1% of the time
where the time goes in v9:
time: 161 us; the launch traced here: 160 us
  starting transfers between devices  38.8 us (24%)
  waiting for transfers between devices  36.5 us (23%)
  other arithmetic  24.6 us (15%)
  blocking collectives  20.3 us (13%)
  matrix products  18.5 us (11%)
  local copies, waits for them, and re-layouts  12.7 us (8%)
  Pallas kernels  7.97 us (5%)
    ppermute x12, starting transfers between devices, passed_along(): lax.ppermute(value, axis, [(source, source + steps) for source in range(f...  38.8 us
    ppermute x12, waiting for transfers between devices, passed_along(): lax.ppermute(value, axis, [(source, source + steps) for source in range(f...  36.5 us
    all_to_all x1, blocking collectives, body(): lax.all_to_all(result, 'head', split_axis=0, concat_axis=1, tiled=True)  20.3 us
    another operation x5, other arithmetic  9.42 us
    pallas_call x1, Pallas kernels, key_features(): pl.pallas_call(kernel, grid=(1,), in_specs=[pl.BlockSpec((rows, dim), lam...  7.97 us
    unnamed x58, local copies, waits for them, and re-layouts  6.05 us
    add x8, other arithmetic, body(): inclusive = inclusive + received  4.83 us
    dot_general x1, matrix products, body(): jnp.einsum('gkij,jgd->igkd', affinity.astype(jnp.bfloat16), ext_values, p...  3.71 us
  transfers between devices with their start and end apart: 12, of which 6 were waited for; matrix products, arithmetic and copies ran while one was open for 21% of the time, Pallas kernels for 0%

profile of v9, /device:TPU:2, one launch (start us, length us, event | category | flops | bytes accessed | tf_op | source)
XLA Modules:
  0.0 159.9 jit_solution(3457945545166198722)
XLA Ops:
  0.0 0.8 add_bitcast_fusion
  0.8 0.9 bitcast_convert_fusion
  1.8 4.0 %subtract_convert_fusion.3 = (bf16[512,1,64]{2,0,1:T(8,128)(2,1)S(1)}, bf16[512,1,64]{2,0,1:T(8,128)(2,1)S(1)}) fusion(f32[512,1,128]{2,0,1:T(8,128)S(1)} %bitcast_convert_fusion, f32[64]{0:T(128)} %constant.75.clone, f32[512]{0:T(512)S(1)} %get-tuple-element.27, f32[64]{0:T(128)} %constant.74.clone, f32[512]{0:T(512)S(1)} %get-tuple-element.26, ...), kind=kLoop, calls=%fused_computation.70 | loop fusion | flops 753664 | bytes 400128 | tf_op jit(solution)/shard_map/convert.6
  5.9 3.8 %collective-permute-start.1 = (bf16[64,1,128]{2,0,1:T(8,128)(2,1)S(1)}, bf16[64,1,128]{2,0,1:T(8,128)(2,1)S(1)}, u32[]{:S(2)}, u32[]{:S(2)}) collective-permute-start(bf16[64,1,128]{2,0,1:T(8,128)(2,1)S(1)} %pad_maximum_fusion.15), channel_id=1, source_target_pairs={{0,8},{8,16},{16,24},{24,32},{32,40},{40,48},{48,56},{56,64},{64,7... | collective-permute-start | bytes 49160 | tf_op jit(solution)/shard_map/ppermute | solution.py:17
  9.7 0.7 slice_bitcast_fusion
  10.4 3.8 %collective-permute-start = (bf16[64,1,128]{2,0,1:T(8,128)(2,1)S(1)}, bf16[64,1,128]{2,0,1:T(8,128)(2,1)S(1)}, u32[]{:S(2)}, u32[]{:S(2)}) collective-permute-start(bf16[64,1,128]{2,0,1:T(8,128)(2,1)S(1)} %slice_bitcast_fusion), channel_id=1, source_target_pairs={{0,8},{8,16},{16,24},{24,32},{32,40},{40,48},{48,56},{56,64},{64,7... | collective-permute-start | bytes 49160 | tf_op jit(solution)/shard_map/ppermute | solution.py:17
  14.3 2.2 %fusion.53 = (f32[512,64]{0,1:T(8,128)S(1)}, f32[512,64]{0,1:T(8,128)S(1)}) fusion(f32[64]{0:T(128)} %constant.75.clone, f32[512]{0:T(512)S(1)} %get-tuple-element.27, f32[64]{0:T(128)} %constant.74.clone, f32[512]{0:T(512)S(1)} %get-tuple-element.26, f32[64]{0:T(128)} %constant.73.clone, f32[512]{0:T(512)S(1)} %get-tuple-element.25), kind=kLoop, calls=%fused_computation.91 | loop fusion | flops 491520 | bytes 269056 | tf_op jit(solution)/shard_map/sub | solution.py:30
  16.5 0.7 fusion.35.mask_ref
  17.2 0.6 broadcast_subtract_fusion
  17.8 0.8 copy.39.m_ref
  18.7 0.8 fusion.88.k_ref
  19.4 0.7 fusion.60.v_ref
  20.1 8.0 %shard_map.100 = (bf16[8,576,128]{2,1,0:T(8,128)(2,1)}, f32[8,128,128]{2,1,0:T(8,128)}, f32[8,1,128]{2,1,0:T(1,128)}) custom-call(bf16[576,128]{1,0:T(8,128)(2,1)} %fusion.88.k_ref, bf16[8,128,64]{2,1,0:T(8,128)(2,1)} %copy.39.m_ref, bf16[576,128]{1,0:T(8,128)(2,1)} %fusion.60.v_ref, f32[576,1]{1,0:T(8,128)} %fusion.35.mask_ref), custom_call_target="tpu_custom_call" | custom-call | tf_op jit(solution)/shard_map/pallas_call | solution.py:81
  28.1 1.0 slice.59
  29.0 3.8 %collective-permute-start.2 = (f32[66048]{0:T(1024)S(1)}, f32[66048]{0:T(1024)}, u32[]{:S(2)}, u32[]{:S(2)}) collective-permute-start(f32[66048]{0:T(1024)S(1)} %slice.59), channel_id=1, source_target_pairs={{0,8},{8,16},{16,24},{24,32},{32,40},{40,48},{48,56},{56,64},{64,7... | collective-permute-start | bytes 792584 | tf_op jit(solution)/shard_map/ppermute | solution.py:17
  32.9 0.8 copy.42
  33.7 0.8 copy.44
  34.6 1.2 fusion.22
  35.7 5.0 %collective-permute-done.2 = f32[66048]{0:T(1024)} collective-permute-done((f32[66048]{0:T(1024)S(1)}, f32[66048]{0:T(1024)}, u32[]{:S(2)}, u32[]{:S(2)}) %collective-permute-start.2) | collective-permute-done | bytes 264224 | tf_op jit(solution)/shard_map/ppermute | solution.py:17
  40.7 0.5 copy.40
  41.3 0.3 fusion.90
  41.5 1.9 %copy.59 = f32[512,8,64]{2,0,1:T(8,128)} copy(f32[512,8,64]{0,2,1:T(8,128)S(1)} %get-tuple-element.18) | data formatting | bytes 2097152
  43.5 2.0 %copy.60 = f32[512,8,64]{2,0,1:T(8,128)} copy(f32[512,8,64]{0,2,1:T(8,128)S(1)} %get-tuple-element.17) | data formatting | bytes 2097152
  45.5 1.0 slice_add_fusion
  46.5 3.4 %collective-permute-start.7 = (f32[66048]{0:T(1024)S(1)}, f32[66048]{0:T(1024)S(1)}, u32[]{:S(2)}, u32[]{:S(2)}) collective-permute-start(f32[66048]{0:T(1024)S(1)} %get-tuple-element.20), channel_id=1, source_target_pairs={{0,64},{8,72},{16,80},{24,88},{32,96},{40,104},{48,112},{56,120},{... | collective-permute-start | bytes 792584 | tf_op jit(solution)/shard_map/ppermute | solution.py:17
  49.9 4.6 %collective-permute-start.3 = (f32[66048]{0:T(1024)S(1)}, f32[66048]{0:T(1024)S(1)}, u32[]{:S(2)}, u32[]{:S(2)}) collective-permute-start(f32[66048]{0:T(1024)S(1)} %get-tuple-element.19), channel_id=1, source_target_pairs={{0,16},{8,24},{16,32},{24,40},{32,48},{40,56},{48,64},{56,72},{64,... | collective-permute-start | bytes 792584 | tf_op jit(solution)/shard_map/ppermute | solution.py:17
  54.5 2.8 %subtract_convert_fusion = (bf16[512,8,64]{2,0,1:T(8,128)(2,1)S(1)}, bf16[512,8,64]{2,0,1:T(8,128)(2,1)S(1)}) fusion(f32[512,8,64]{2,0,1:T(8,128)} %copy.60, f32[512,8,64]{2,0,1:T(8,128)} %copy.59, f32[512,64]{1,0:T(8,128)S(1)} %copy-done.10, f32[512,64]{1,0:T(8,128)S(1)} %copy-done.9), kind=kLoop, calls=%fused_computation.23 | loop fusion | flops 2097152 | bytes 3407872 | tf_op jit(solution)/shard_map/convert.4
  57.3 2.4 %fusion.2 = (f32[8,512]{1,0:T(8,128)S(1)}, f32[576,512,8]{1,0,2:T(8,128)S(1)}) fusion(pred[512,576]{0,1:T(8,128)(4,1)S(1)} %copy-done.1, bf16[512,8,64]{2,0,1:T(8,128)(2,1)S(1)} %get-tuple-element.16, bf16[512,8,64]{2,0,1:T(8,128)(2,1)S(1)} %get-tuple-element.15, bf16[512,1,64]{2,0,1:T(8,128)(2,1)S(1)} %get-tuple-element.22, ...), kind=kOutput, calls=%fused_computation.4 | convolution fusion | flops 613593088 | bytes 10944512 | tf_op jit(solution)/shard_map/igkd,jgd->gkij/dot_general | solution.py:185
  59.7 2.5 %fusion.5 = f32[8,512]{1,0:T(8,128)} fusion(f32[576,512,8]{1,0,2:T(8,128)S(1)} %get-tuple-element.35, f32[8,512]{1,0:T(8,128)S(1)} %get-tuple-element.34, pred[512,576]{0,1:T(8,128)(4,1)S(1)} %copy-done.1), kind=kLoop, calls=%fused_computation.9 | loop fusion | flops 9433088 | bytes 9764864 | tf_op jit(solution)/shard_map/reduce_sum | solution.py:191
  62.3 3.5 %fusion.10 = f32[128,8,512]{2,0,1:T(8,128)} fusion(f32[576,512,8]{1,0,2:T(8,128)S(1)} %get-tuple-element.35, f32[8,512]{1,0:T(8,128)S(1)} %get-tuple-element.34, pred[512,576]{0,1:T(8,128)(4,1)S(1)} %copy-done.1, bf16[512,1,128]{2,0,1:T(8,128)(2,1)S(1)} %bitcast.143, bf16[64,1,128]{2,0,1:T(8,128)(2,1)S(1)} %copy-done.19), kind=kOutput, calls=%fused_computation.14 | convolution fusion | flops 613711872 | bytes 11993088 | tf_op jit(solution)/shard_map/gkij,jgd->igkd/dot_general | solution.py:195
  65.8 0.8 add.210
  66.6 1.9 %collective-permute-start.8 = (f32[66048]{0:T(1024)}, f32[66048]{0:T(1024)S(1)}, u32[]{:S(2)}, u32[]{:S(2)}) collective-permute-start(f32[66048]{0:T(1024)} %add.210), channel_id=1, source_target_pairs={{0,128},{8,136},{16,144},{24,152},{32,160},{40,168},{48,176},{56,1... | collective-permute-start | bytes 792584 | tf_op jit(solution)/shard_map/ppermute | solution.py:17
  68.5 0.8 add.204
  69.3 4.0 %collective-permute-start.4 = (f32[66048]{0:T(1024)}, f32[66048]{0:T(1024)}, u32[]{:S(2)}, u32[]{:S(2)}) collective-permute-start(f32[66048]{0:T(1024)} %add.204), channel_id=1, source_target_pairs={{0,32},{8,40},{16,48},{24,56},{32,64},{40,72},{48,80},{56,88},{64,... | collective-permute-start | bytes 792584 | tf_op jit(solution)/shard_map/ppermute | solution.py:17
  73.4 1.5 fusion.92
  74.8 2.5 %fusion.91 = (f32[512,8]{0,1:T(8,128)}, f32[512,8,64]{0,2,1:T(8,128)}) fusion(bf16[8,128,64]{1,2,0:T(8,128)(2,1)S(1)} %copy-done, bf16[512,8,64]{2,0,1:T(8,128)(2,1)S(1)} %get-tuple-element.16, bf16[512,8,64]{2,0,1:T(8,128)(2,1)S(1)} %get-tuple-element.15), kind=kOutput, calls=%fused_computation.154 | convolution fusion | flops 69992512 | bytes 2244608 | tf_op jit(solution)/shard_map/sub | solution.py:48
  77.3 1.1 add.212
  78.4 1.9 %collective-permute-start.9 = (f32[66048]{0:T(1024)S(1)}, f32[66048]{0:T(1024)S(1)}, u32[]{:S(2)}, u32[]{:S(2)}) collective-permute-start(f32[66048]{0:T(1024)S(1)} %add.212), channel_id=1, source_target_pairs={{0,8},{8,16},{16,24},{24,32},{32,40},{40,48},{48,56},{56,64},{64,7... | collective-permute-start | bytes 792584 | tf_op jit(solution)/shard_map/ppermute | solution.py:17
  80.3 6.3 %collective-permute-done.4 = f32[66048]{0:T(1024)} collective-permute-done((f32[66048]{0:T(1024)}, f32[66048]{0:T(1024)}, u32[]{:S(2)}, u32[]{:S(2)}) %collective-permute-start.4) | collective-permute-done | bytes 264224 | tf_op jit(solution)/shard_map/ppermute | solution.py:17
  86.6 1.1 add.206
  87.7 1.9 %collective-permute-start.5 = (f32[66048]{0:T(1024)S(1)}, f32[66048]{0:T(1024)S(1)}, u32[]{:S(2)}, u32[]{:S(2)}) collective-permute-start(f32[66048]{0:T(1024)S(1)} %add.206), channel_id=1, source_target_pairs={{0,64},{8,72},{16,80},{24,88},{32,96},{40,104},{48,112},{56,120},{... | collective-permute-start | bytes 792584 | tf_op jit(solution)/shard_map/ppermute | solution.py:17
  89.7 1.2 divide_convert_fusion
  90.8 3.1 %collective-permute-done.9 = f32[66048]{0:T(1024)S(1)} collective-permute-done((f32[66048]{0:T(1024)S(1)}, f32[66048]{0:T(1024)S(1)}, u32[]{:S(2)}, u32[]{:S(2)}) %collective-permute-start.9) | collective-permute-done | bytes 264224 | tf_op jit(solution)/shard_map/ppermute | solution.py:17
  93.9 4.3 %collective-permute-start.10 = (f32[66048]{0:T(1024)S(1)}, f32[66048]{0:T(1024)S(1)}, u32[]{:S(2)}, u32[]{:S(2)}) collective-permute-start(f32[66048]{0:T(1024)S(1)} %add.214), channel_id=1, source_target_pairs={{0,16},{8,24},{16,32},{24,40},{32,48},{40,56},{48,64},{56,72},{64,... | collective-permute-start | bytes 792584 | tf_op jit(solution)/shard_map/ppermute | solution.py:17
  98.3 0.3 collective-permute-done.5
  98.6 2.8 %collective-permute-start.6 = (f32[66048]{0:T(1024)S(1)}, f32[66048]{0:T(1024)S(1)}, u32[]{:S(2)}, u32[]{:S(2)}) collective-permute-start(f32[66048]{0:T(1024)S(1)} %add.208), channel_id=1, source_target_pairs={{0,128},{8,136},{16,144},{24,152},{32,160},{40,168},{48,176},{56,1... | collective-permute-start | bytes 792584 | tf_op jit(solution)/shard_map/ppermute | solution.py:17
  101.5 3.7 %select_reduce_fusion = (f32[8,512]{1,0:T(8,128)S(1)}, bf16[8,512,576]{1,2,0:T(8,128)(2,1)}) fusion(pred[512,576]{0,1:T(8,128)(4,1)S(1)} %copy-done.11, bf16[8,576,128]{2,1,0:T(8,128)(2,1)S(1)} %copy-done.24, bf16[512,8,64]{0,2,1:T(8,128)(2,1)S(1)} %get-tuple-element.38, bf16[512,8,64]{0,2,1:T(8,128)(2,1)S(1)} %get-tuple-element.39), kind=kOutput, calls=%fused_computation.7 | convolution fusion | flops 613150720 | bytes 7258112 | tf_op jit(solution)/shard_map/igkf,gkjf->gkij/dot_general | solution.py:192
  105.1 5.6 %collective-permute-done.10 = f32[66048]{0:T(1024)S(1)} collective-permute-done((f32[66048]{0:T(1024)S(1)}, f32[66048]{0:T(1024)S(1)}, u32[]{:S(2)}, u32[]{:S(2)}) %collective-permute-start.10) | collective-permute-done | bytes 264224 | tf_op jit(solution)/shard_map/ppermute | solution.py:17
  110.8 2.4 %collective-permute-start.11 = (f32[66048]{0:T(1024)S(1)}, f32[66048]{0:T(1024)S(1)}, u32[]{:S(2)}, u32[]{:S(2)}) collective-permute-start(f32[66048]{0:T(1024)S(1)} %add.216), channel_id=1, source_target_pairs={{0,32},{8,40},{16,48},{24,56},{32,64},{40,72},{48,80},{56,88},{64,... | collective-permute-start | bytes 792584 | tf_op jit(solution)/shard_map/ppermute | solution.py:17
  113.2 1.1 add_add_fusion.1
  114.4 16.2 %collective-permute-done.11 = f32[66048]{0:T(1024)S(1)} collective-permute-done((f32[66048]{0:T(1024)S(1)}, f32[66048]{0:T(1024)S(1)}, u32[]{:S(2)}, u32[]{:S(2)}) %collective-permute-start.11) | collective-permute-done | bytes 264224 | tf_op jit(solution)/shard_map/ppermute | solution.py:17
  130.7 0.2 copy.46
  130.9 0.4 fusion.40
  131.3 0.4 fusion.58
  131.8 0.2 fusion.66
  132.1 0.2 fusion.64
  132.3 0.2 copy-done.17
  132.5 0.2 copy-done.12
  132.8 0.8 copy-done.26
  133.6 3.7 %fusion.17 = bf16[512,1,8,128]{0,3,2,1:T(8,128)(2,1)S(1)} fusion(f32[8,128,512]{2,1,0:T(8,128)S(1)} %fusion.58, f32[8,128,512]{2,1,0:T(8,128)S(1)} %fusion.40, f32[128,8,512]{2,0,1:T(8,128)S(1)} %copy-done.26, bf16[8,512,576]{1,2,0:T(8,128)(2,1)} %get-tuple-element.37, pred[512,576]{0,1:T(8,128)(4,1)S(1)} %copy-done.12, f32[512,8]{0,1:T(8,128)S(1)} %fusion.62, ...), kind=kOutput, calls=%fused_computation.24 | convolution fusion | flops 610304000 | bytes 12517440 | tf_op jit(solution)/shard_map/gkij,jgd->igkd/dot_general | solution.py:201
  137.3 0.8 copy.50
  138.1 0.5 all_to_all.14
  138.6 20.3 %all_to_all.19 = bf16[8,64,1024]{2,1,0:T(8,128)(2,1)S(1)} all-to-all(bf16[8,64,1024]{2,1,0:T(8,128)(2,1)S(1)} %all_to_all.14), channel_id=1, replica_groups=mesh['seq'=32,'head'=8] {'head'}, dimensions={0} | all-to-all | bytes 2097152 | tf_op jit(solution)/shard_map/all_to_all | solution.py:228
  158.8 1.1 copy.61
  (70 shorter events, 0.6 us)
Async XLA Ops:
  0.0 73.4 %copy-start = (bf16[8,128,64]{1,2,0:T(8,128)(2,1)S(1)}, bf16[8,128,64]{1,2,0:T(8,128)(2,1)}, u32[]{:S(2)}) copy-start(bf16[8,128,64]{1,2,0:T(8,128)(2,1)} %param.14) | copy-start | bytes 393220
  0.0 19.4 %copy-start.13 = (bf16[512,128]{1,0:T(8,128)(2,1)S(1)}, bf16[512,128]{1,0:T(8,128)(2,1)}, u32[]{:S(2)}) copy-start(bf16[512,128]{1,0:T(8,128)(2,1)} %param.12) | copy-start | bytes 393220
  0.0 17.2 %copy-start.25 = (f32[8]{0:T(128)S(1)}, f32[8]{0:T(128)}, u32[]{:S(2)}) copy-start(f32[8]{0:T(128)} %param.16) | copy-start | bytes 100
  0.0 17.8 %copy-start.16 = (bf16[8,128,64]{1,2,0:T(8,128)(2,1)S(1)}, bf16[8,128,64]{1,2,0:T(8,128)(2,1)}, u32[]{:S(2)}) copy-start(bf16[8,128,64]{1,2,0:T(8,128)(2,1)} %param.15) | copy-start | bytes 393220
  5.9 12.8 %collective-permute-start.1 = (bf16[64,1,128]{2,0,1:T(8,128)(2,1)S(1)}, bf16[64,1,128]{2,0,1:T(8,128)(2,1)S(1)}, u32[]{:S(2)}, u32[]{:S(2)}) collective-permute-start(bf16[64,1,128]{2,0,1:T(8,128)(2,1)S(1)} %pad_maximum_fusion.15), channel_id=1, source_target_pairs={{0,8},{8,16},{16,24},{24,32},{32,40},{40,48},{48,56},{56,64},{64,7... | collective-permute-start | bytes 49160 | tf_op jit(solution)/shard_map/ppermute | solution.py:17
  10.4 9.0 %collective-permute-start = (bf16[64,1,128]{2,0,1:T(8,128)(2,1)S(1)}, bf16[64,1,128]{2,0,1:T(8,128)(2,1)S(1)}, u32[]{:S(2)}, u32[]{:S(2)}) collective-permute-start(bf16[64,1,128]{2,0,1:T(8,128)(2,1)S(1)} %slice_bitcast_fusion), channel_id=1, source_target_pairs={{0,8},{8,16},{16,24},{24,32},{32,40},{40,48},{48,56},{56,64},{64,7... | collective-permute-start | bytes 49160 | tf_op jit(solution)/shard_map/ppermute | solution.py:17
  16.4 24.3 %copy-start.8 = (bf16[512,1024]{1,0:T(8,128)(2,1)S(1)}, bf16[512,1024]{1,0:T(8,128)(2,1)}, u32[]{:S(2)}) copy-start(bf16[512,1024]{1,0:T(8,128)(2,1)} %param.10) | copy-start | bytes 3145732
  19.4 16.3 %copy-start.18 = (bf16[64,1,128]{2,0,1:T(8,128)(2,1)}, bf16[64,1,128]{2,0,1:T(8,128)(2,1)S(1)}, u32[]{:S(2)}) copy-start(bf16[64,1,128]{2,0,1:T(8,128)(2,1)S(1)} %collective-permute-done) | copy-start | bytes 49156
  29.0 11.7 %collective-permute-start.2 = (f32[66048]{0:T(1024)S(1)}, f32[66048]{0:T(1024)}, u32[]{:S(2)}, u32[]{:S(2)}) collective-permute-start(f32[66048]{0:T(1024)S(1)} %slice.59), channel_id=1, source_target_pairs={{0,8},{8,16},{16,24},{24,32},{32,40},{40,48},{48,56},{56,64},{64,7... | collective-permute-start | bytes 792584 | tf_op jit(solution)/shard_map/ppermute | solution.py:17
  43.5 2.0 %copy-start.2 = (f32[8,128,128]{2,1,0:T(8,128)S(1)}, f32[8,128,128]{2,1,0:T(8,128)}, u32[]{:S(2)}) copy-start(f32[8,128,128]{2,1,0:T(8,128)} %get-tuple-element.9) | copy-start | bytes 1572868
  43.5 2.0 %copy-start.21 = (f32[8,1,128]{2,1,0:T(1,128)S(1)}, f32[8,1,128]{2,1,0:T(1,128)}, u32[]{:S(2)}) copy-start(f32[8,1,128]{2,1,0:T(1,128)} %get-tuple-element.12) | copy-start | bytes 12292
  43.5 11.0 %copy-start.9 = (f32[512,64]{1,0:T(8,128)S(1)}, f32[512,64]{1,0:T(8,128)}, u32[]{:S(2)}) copy-start(f32[512,64]{1,0:T(8,128)} %copy.42) | copy-start | bytes 393220
  43.5 11.0 %copy-start.10 = (f32[512,64]{1,0:T(8,128)S(1)}, f32[512,64]{1,0:T(8,128)}, u32[]{:S(2)}) copy-start(f32[512,64]{1,0:T(8,128)} %copy.44) | copy-start | bytes 393220
  46.5 19.3 %collective-permute-start.7 = (f32[66048]{0:T(1024)S(1)}, f32[66048]{0:T(1024)S(1)}, u32[]{:S(2)}, u32[]{:S(2)}) collective-permute-start(f32[66048]{0:T(1024)S(1)} %get-tuple-element.20), channel_id=1, source_target_pairs={{0,64},{8,72},{16,80},{24,88},{32,96},{40,104},{48,112},{56,120},{... | collective-permute-start | bytes 792584 | tf_op jit(solution)/shard_map/ppermute | solution.py:17
  49.9 7.4 %copy-start.1 = (pred[512,576]{0,1:T(8,128)(4,1)S(1)}, pred[512,576]{0,1:T(8,128)(4,1)}, u32[]{:S(2)}) copy-start(pred[512,576]{0,1:T(8,128)(4,1)} %get-tuple-element.29) | copy-start | bytes 884740
  49.9 18.6 %collective-permute-start.3 = (f32[66048]{0:T(1024)S(1)}, f32[66048]{0:T(1024)S(1)}, u32[]{:S(2)}, u32[]{:S(2)}) collective-permute-start(f32[66048]{0:T(1024)S(1)} %get-tuple-element.19), channel_id=1, source_target_pairs={{0,16},{8,24},{16,32},{24,40},{32,48},{40,56},{48,64},{56,72},{64,... | collective-permute-start | bytes 792584 | tf_op jit(solution)/shard_map/ppermute | solution.py:17
  59.7 2.6 %copy-start.14 = (bf16[512,128]{1,0:T(8,128)(2,1)S(1)}, bf16[512,128]{1,0:T(8,128)(2,1)}, u32[]{:S(2)}) copy-start(bf16[512,128]{1,0:T(8,128)(2,1)} %param.12) | copy-start | bytes 393220
  59.7 2.6 %copy-start.19 = (bf16[64,1,128]{2,0,1:T(8,128)(2,1)S(1)}, bf16[64,1,128]{2,0,1:T(8,128)(2,1)}, u32[]{:S(2)}) copy-start(bf16[64,1,128]{2,0,1:T(8,128)(2,1)} %copy-done.18) | copy-start | bytes 49156
  65.8 3.6 %copy-start.3 = (f32[66048]{0:T(1024)}, f32[66048]{0:T(1024)S(1)}, u32[]{:S(2)}) copy-start(f32[66048]{0:T(1024)S(1)} %collective-permute-done.7) | copy-start | bytes 792580
  66.6 10.7 %collective-permute-start.8 = (f32[66048]{0:T(1024)}, f32[66048]{0:T(1024)S(1)}, u32[]{:S(2)}, u32[]{:S(2)}) collective-permute-start(f32[66048]{0:T(1024)} %add.210), channel_id=1, source_target_pairs={{0,128},{8,136},{16,144},{24,152},{32,160},{40,168},{48,176},{56,1... | collective-permute-start | bytes 792584 | tf_op jit(solution)/shard_map/ppermute | solution.py:17
  68.5 0.8 copy-start.5
  69.3 17.3 %collective-permute-start.4 = (f32[66048]{0:T(1024)}, f32[66048]{0:T(1024)}, u32[]{:S(2)}, u32[]{:S(2)}) collective-permute-start(f32[66048]{0:T(1024)} %add.204), channel_id=1, source_target_pairs={{0,32},{8,40},{16,48},{24,56},{32,64},{40,72},{48,80},{56,88},{64,... | collective-permute-start | bytes 792584 | tf_op jit(solution)/shard_map/ppermute | solution.py:17
  77.3 12.3 %copy-start.7 = (f32[512,8,64]{0,2,1:T(8,128)S(1)}, f32[512,8,64]{0,2,1:T(8,128)}, u32[]{:S(2)}) copy-start(f32[512,8,64]{0,2,1:T(8,128)} %get-tuple-element.31) | copy-start | bytes 3145732
  78.4 15.5 %collective-permute-start.9 = (f32[66048]{0:T(1024)S(1)}, f32[66048]{0:T(1024)S(1)}, u32[]{:S(2)}, u32[]{:S(2)}) collective-permute-start(f32[66048]{0:T(1024)S(1)} %add.212), channel_id=1, source_target_pairs={{0,8},{8,16},{16,24},{24,32},{32,40},{40,48},{48,56},{56,64},{64,7... | collective-permute-start | bytes 792584 | tf_op jit(solution)/shard_map/ppermute | solution.py:17
  87.7 10.9 %collective-permute-start.5 = (f32[66048]{0:T(1024)S(1)}, f32[66048]{0:T(1024)S(1)}, u32[]{:S(2)}, u32[]{:S(2)}) collective-permute-start(f32[66048]{0:T(1024)S(1)} %add.206), channel_id=1, source_target_pairs={{0,64},{8,72},{16,80},{24,88},{32,96},{40,104},{48,112},{56,120},{... | collective-permute-start | bytes 792584 | tf_op jit(solution)/shard_map/ppermute | solution.py:17
  89.6 11.8 %copy-start.11 = (pred[512,576]{0,1:T(8,128)(4,1)S(1)}, pred[512,576]{0,1:T(8,128)(4,1)}, u32[]{:S(2)}) copy-start(pred[512,576]{0,1:T(8,128)(4,1)} %get-tuple-element.28) | copy-start | bytes 884740
  89.6 11.8 %copy-start.24 = (bf16[8,576,128]{2,1,0:T(8,128)(2,1)S(1)}, bf16[8,576,128]{2,1,0:T(8,128)(2,1)}, u32[]{:S(2)}) copy-start(bf16[8,576,128]{2,1,0:T(8,128)(2,1)} %get-tuple-element.11) | copy-start | bytes 3538948
  93.9 16.9 %collective-permute-start.10 = (f32[66048]{0:T(1024)S(1)}, f32[66048]{0:T(1024)S(1)}, u32[]{:S(2)}, u32[]{:S(2)}) collective-permute-start(f32[66048]{0:T(1024)S(1)} %add.214), channel_id=1, source_target_pairs={{0,16},{8,24},{16,32},{24,40},{32,48},{40,56},{48,64},{56,72},{64,... | collective-permute-start | bytes 792584 | tf_op jit(solution)/shard_map/ppermute | solution.py:17
  98.6 14.6 %collective-permute-start.6 = (f32[66048]{0:T(1024)S(1)}, f32[66048]{0:T(1024)S(1)}, u32[]{:S(2)}, u32[]{:S(2)}) collective-permute-start(f32[66048]{0:T(1024)S(1)} %add.208), channel_id=1, source_target_pairs={{0,128},{8,136},{16,144},{24,152},{32,160},{40,168},{48,176},{56,1... | collective-permute-start | bytes 792584 | tf_op jit(solution)/shard_map/ppermute | solution.py:17
  101.5 11.8 %copy-start.6 = (f32[66048]{0:T(1024)S(1)}, f32[66048]{0:T(1024)}, u32[]{:S(2)}) copy-start(f32[66048]{0:T(1024)} %copy-done.5) | copy-start | bytes 792580
  105.1 25.4 %copy-start.4 = (f32[66048]{0:T(1024)S(1)}, f32[66048]{0:T(1024)}, u32[]{:S(2)}) copy-start(f32[66048]{0:T(1024)} %copy-done.3) | copy-start | bytes 792580
  110.8 19.7 %collective-permute-start.11 = (f32[66048]{0:T(1024)S(1)}, f32[66048]{0:T(1024)S(1)}, u32[]{:S(2)}, u32[]{:S(2)}) collective-permute-start(f32[66048]{0:T(1024)S(1)} %add.216), channel_id=1, source_target_pairs={{0,32},{8,40},{16,48},{24,56},{32,64},{40,72},{48,80},{56,88},{64,... | collective-permute-start | bytes 792584 | tf_op jit(solution)/shard_map/ppermute | solution.py:17
  131.7 0.7 copy-start.17
  131.8 0.7 copy-start.22
  131.8 0.7 copy-start.23
  131.8 1.0 copy-start.12
  131.8 1.0 copy-start.15
  131.8 1.0 copy-start.20
  131.8 1.8 %copy-start.26 = (f32[128,8,512]{2,0,1:T(8,128)S(1)}, f32[128,8,512]{2,0,1:T(8,128)}, u32[]{:S(2)}) copy-start(f32[128,8,512]{2,0,1:T(8,128)} %fusion.10) | copy-start | bytes 6291460

commit v10 on v9

--- a/solution.py
+++ b/solution.py
@@ -55,50 +55,49 @@
     return (high_part, rest_part)
 
 
-def key_features(ext_keys2, key_map, ext_values2, mask, lag):
+def key_features(ext_keys2, key_map_t, ext_values2, mask, lag):
     rows, dim = ext_keys2.shape
-    heads, _, feat = key_map.shape
+    heads, feat, _ = key_map_t.shape
 
     def kernel(k_ref, m_ref, v_ref, mask_ref, phi_ref, st_ref, nm_ref):
         keys = k_ref[...]
         live = mask_ref[...] > 0.0
         values = v_ref[0:lag, :]
         for head in range(heads):
-            logits = jnp.dot(keys, m_ref[head], preferred_element_type=jnp.float32)
+            logits = lax.dot_general(
+                m_ref[head], keys, (((1,), (1,)), ((), ())), preferred_element_type=jnp.float32
+            )
             for place, sign in enumerate((1.0, -1.0)):
                 shifted = sign * logits
-                expo = jnp.exp(shifted - jnp.max(shifted, axis=-1, keepdims=True))
-                soft = expo / jnp.sum(expo, axis=-1, keepdims=True)
+                expo = jnp.exp(shifted - jnp.max(shifted, axis=0, keepdims=True))
+                soft = expo / jnp.sum(expo, axis=0, keepdims=True)
                 phi = jnp.where(live, soft, 0.0).astype(jnp.bfloat16)
-                cols = slice(place * feat, (place + 1) * feat)
-                phi_ref[head, :, cols] = phi
-                lagged = phi[0:lag, :]
-                st_ref[head, cols, :] = lax.dot_general(
-                    lagged, values, (((0,), (0,)), ((), ())), preferred_element_type=jnp.float32
-                )
-                nm_ref[head, :, cols] = jnp.sum(lagged.astype(jnp.float32), axis=0, keepdims=True)
+                band = slice(place * feat, (place + 1) * feat)
+                phi_ref[head, band, :] = phi
+                lagged = phi[:, 0:lag]
+                st_ref[head, band, :] = jnp.dot(lagged, values, preferred_element_type=jnp.float32)
+                nm_ref[head, band, :] = jnp.sum(lagged.astype(jnp.float32), axis=1, keepdims=True)
 
     return pl.pallas_call(
         kernel,
         grid=(1,),
         in_specs=[
             pl.BlockSpec((rows, dim), lambda h: (0, 0)),
-            pl.BlockSpec((heads, dim, feat), lambda h: (0, 0, 0)),
+            pl.BlockSpec((heads, feat, dim), lambda h: (0, 0, 0)),
             pl.BlockSpec((rows, dim), lambda h: (0, 0)),
-            pl.BlockSpec((rows, 1), lambda h: (0, 0)),
+            pl.BlockSpec((1, rows), lambda h: (0, 0)),
         ],
         out_specs=[
-            pl.BlockSpec((heads, rows, 2 * feat), lambda h: (0, 0, 0)),
+            pl.BlockSpec((heads, 2 * feat, rows), lambda h: (0, 0, 0)),
             pl.BlockSpec((heads, 2 * feat, dim), lambda h: (0, 0, 0)),
-            pl.BlockSpec((heads, 1, 2 * feat), lambda h: (0, 0, 0)),
+            pl.BlockSpec((heads, 2 * feat, 1), lambda h: (0, 0, 0)),
         ],
         out_shape=[
-            jax.ShapeDtypeStruct((heads, rows, 2 * feat), jnp.bfloat16),
+            jax.ShapeDtypeStruct((heads, 2 * feat, rows), jnp.bfloat16),
             jax.ShapeDtypeStruct((heads, 2 * feat, dim), jnp.float32),
-            jax.ShapeDtypeStruct((heads, 1, 2 * feat), jnp.float32),
+            jax.ShapeDtypeStruct((heads, 2 * feat, 1), jnp.float32),
         ],
-    )(ext_keys2, key_map, ext_values2, mask)
-
+    )(ext_keys2, key_map_t, ext_values2, mask)
 
 def body(queries, keys, values, offsets, query_map, key_map, window_logit):
     tokens = queries.shape[0]
@@ -124,12 +123,12 @@
     ext_rows = tokens + WINDOW
     phi_heads, state_heads, norm_heads = key_features(
         ext_keys.reshape(ext_rows, head_dim),
-        key_map,
+        jnp.transpose(key_map, (0, 2, 1)),
         ext_values.reshape(ext_rows, head_dim),
-        valid.astype(jnp.float32)[:, None],
+        valid.astype(jnp.float32)[None, :],
         tokens,
     )
-    phi_key = phi_heads.reshape(kv_local, group, ext_rows, 2 * feat)
+    phi_key = phi_heads.reshape(kv_local, group, 2 * feat, ext_rows)
     block_states = state_heads.reshape(1, kv_local, group, 2 * feat, head_dim)
     block_norms = norm_heads.reshape(1, kv_local, group, 2 * feat)
     total_state = jnp.sum(block_states, axis=0)
@@ -189,7 +188,7 @@
     peak = jnp.max(jnp.where(near_window, scores, -jnp.inf), axis=-1, keepdims=True)
     weights = jnp.where(near_window, jnp.exp(scores - peak), 0.0)
     window_sum = jnp.sum(weights, axis=-1)
-    affinity = jnp.einsum("igkf,gkjf->gkij", phi_query, phi_key, preferred_element_type=jnp.float32)
+    affinity = jnp.einsum("igkf,gkfj->gkij", phi_query, phi_key, preferred_element_type=jnp.float32)
     affinity = jnp.where(linear_mask & live, affinity, 0.0)
     near_sum = jnp.sum(affinity, axis=-1)
     window_num = jnp.einsum(

time: 161 us -> 157 us (0.975)
  Pallas kernels: 7.97 us -> 4.59 us
    pallas_call x1, Pallas kernels: 7.97 us -> 4.59 us  [key_features(): pl.pallas_call(kernel, grid=(1,), in_specs=[pl.BlockSpec((rows, dim), lam...]
    unnamed x58 -> x55, local copies, waits for them, and re-layouts: 6.05 us -> 5.17 us
  transfers between devices with their start and end apart: 12 -> 12, of which waited for: 6 -> 6; matrix products, arithmetic and copies ran while one was open for 21% -> 22% of each run, Pallas kernels for 0% -> 0%
where the time goes in v10:
time: 157 us; the launch traced here: 156 us
  starting transfers between devices  38.9 us (25%)
  waiting for transfers between devices  35.6 us (23%)
  other arithmetic  25.9 us (16%)
  blocking collectives  20.4 us (13%)
  matrix products  18.6 us (12%)
  local copies, waits for them, and re-layouts  11.9 us (8%)
  Pallas kernels  4.59 us (3%)
    ppermute x12, starting transfers between devices, passed_along(): lax.ppermute(value, axis, [(source, source + steps) for source in range(f...  38.9 us
    ppermute x12, waiting for transfers between devices, passed_along(): lax.ppermute(value, axis, [(source, source + steps) for source in range(f...  35.6 us
    all_to_all x1, blocking collectives, body(): lax.all_to_all(result, 'head', split_axis=0, concat_axis=1, tiled=True)  20.4 us
    another operation x5, other arithmetic  9.44 us
    unnamed x55, local copies, waits for them, and re-layouts  5.17 us
    add x8, other arithmetic, body(): inclusive = inclusive + received  4.81 us
    pallas_call x1, Pallas kernels, key_features(): pl.pallas_call(kernel, grid=(1,), in_specs=[pl.BlockSpec((rows, dim), lam...  4.59 us
    dot_general x1, matrix products, body(): jnp.einsum('igkf,gkfj->gkij', phi_query, phi_key, preferred_element_type=...  3.75 us
  transfers between devices with their start and end apart: 12, of which 6 were waited for; matrix products, arithmetic and copies ran while one was open for 22% of the time, Pallas kernels for 0%

profile of v10, /device:TPU:2, one launch (start us, length us, event | category | flops | bytes accessed | tf_op | source)
XLA Modules:
  0.0 156.4 jit_solution(13263485078199033735)
XLA Ops:
  0.0 0.8 add_bitcast_fusion
  0.8 0.9 bitcast_convert_fusion
  1.7 4.0 %subtract_convert_fusion.3 = (bf16[512,1,64]{2,0,1:T(8,128)(2,1)S(1)}, bf16[512,1,64]{2,0,1:T(8,128)(2,1)S(1)}) fusion(f32[512,1,128]{2,0,1:T(8,128)S(1)} %bitcast_convert_fusion, f32[64]{0:T(128)} %constant.75.clone, f32[512]{0:T(512)S(1)} %get-tuple-element.27, f32[64]{0:T(128)} %constant.74.clone, f32[512]{0:T(512)S(1)} %get-tuple-element.26, ...), kind=kLoop, calls=%fused_computation.67 | loop fusion | flops 753664 | bytes 400128 | tf_op jit(solution)/shard_map/convert.6
  5.9 3.9 %collective-permute-start.1 = (bf16[64,1,128]{2,0,1:T(8,128)(2,1)S(1)}, bf16[64,1,128]{2,0,1:T(8,128)(2,1)S(1)}, u32[]{:S(2)}, u32[]{:S(2)}) collective-permute-start(bf16[64,1,128]{2,0,1:T(8,128)(2,1)S(1)} %pad_maximum_fusion.15), channel_id=1, source_target_pairs={{0,8},{8,16},{16,24},{24,32},{32,40},{40,48},{48,56},{56,64},{64,7... | collective-permute-start | bytes 49160 | tf_op jit(solution)/shard_map/ppermute | solution.py:17
  9.8 0.7 slice_bitcast_fusion
  10.6 3.8 %collective-permute-start = (bf16[64,1,128]{2,0,1:T(8,128)(2,1)S(1)}, bf16[64,1,128]{2,0,1:T(8,128)(2,1)S(1)}, u32[]{:S(2)}, u32[]{:S(2)}) collective-permute-start(bf16[64,1,128]{2,0,1:T(8,128)(2,1)S(1)} %slice_bitcast_fusion), channel_id=1, source_target_pairs={{0,8},{8,16},{16,24},{24,32},{32,40},{40,48},{48,56},{56,64},{64,7... | collective-permute-start | bytes 49160 | tf_op jit(solution)/shard_map/ppermute | solution.py:17
  14.4 2.2 %fusion.51 = (f32[512,64]{0,1:T(8,128)S(1)}, f32[512,64]{0,1:T(8,128)S(1)}) fusion(f32[64]{0:T(128)} %constant.75.clone, f32[512]{0:T(512)S(1)} %get-tuple-element.27, f32[64]{0:T(128)} %constant.74.clone, f32[512]{0:T(512)S(1)} %get-tuple-element.26, f32[64]{0:T(128)} %constant.73.clone, f32[512]{0:T(512)S(1)} %get-tuple-element.25), kind=kLoop, calls=%fused_computation.88 | loop fusion | flops 491520 | bytes 269056 | tf_op jit(solution)/shard_map/sub | solution.py:30
  16.6 0.6 or_convert_fusion.mask_ref
  17.2 1.3 broadcast_subtract_fusion
  18.4 0.8 fusion.86.k_ref
  19.2 0.7 fusion.58.v_ref
  19.9 4.6 %shard_map.100 = (bf16[8,128,576]{2,1,0:T(8,128)(2,1)}, f32[8,128,128]{2,1,0:T(8,128)}, f32[8,128,1]{2,1,0:T(8,128)}) custom-call(bf16[576,128]{1,0:T(8,128)(2,1)} %fusion.86.k_ref, bf16[8,64,128]{2,1,0:T(8,128)(2,1)} %bitcast.146, bf16[576,128]{1,0:T(8,128)(2,1)} %fusion.58.v_ref, f32[1,576]{1,0:T(1,128)} %or_convert_fusion.mask_ref), custom_call_target="tpu_custom_call" | custom-call | tf_op jit(solution)/shard_map/pallas_call | solution.py:81
  24.5 1.0 slice.59
  25.5 3.8 %collective-permute-start.2 = (f32[66048]{0:T(1024)S(1)}, f32[66048]{0:T(1024)}, u32[]{:S(2)}, u32[]{:S(2)}) collective-permute-start(f32[66048]{0:T(1024)S(1)} %slice.59), channel_id=1, source_target_pairs={{0,8},{8,16},{16,24},{24,32},{32,40},{40,48},{48,56},{56,64},{64,7... | collective-permute-start | bytes 792584 | tf_op jit(solution)/shard_map/ppermute | solution.py:17
  29.3 0.8 copy.40
  30.2 0.9 copy.42
  31.0 1.2 fusion.22
  32.2 0.8 reduce.4
  33.0 4.2 %collective-permute-done.2 = f32[66048]{0:T(1024)} collective-permute-done((f32[66048]{0:T(1024)S(1)}, f32[66048]{0:T(1024)}, u32[]{:S(2)}, u32[]{:S(2)}) %collective-permute-start.2) | collective-permute-done | bytes 264224 | tf_op jit(solution)/shard_map/ppermute | solution.py:17
  37.2 0.5 copy.38
  37.7 0.3 fusion.88
  38.0 1.9 %copy.59 = f32[512,8,64]{2,0,1:T(8,128)} copy(f32[512,8,64]{0,2,1:T(8,128)S(1)} %get-tuple-element.18) | data formatting | bytes 2097152
  39.9 2.0 %copy.60 = f32[512,8,64]{2,0,1:T(8,128)} copy(f32[512,8,64]{0,2,1:T(8,128)S(1)} %get-tuple-element.17) | data formatting | bytes 2097152
  41.9 1.0 slice_add_fusion
  42.9 3.4 %collective-permute-start.7 = (f32[66048]{0:T(1024)S(1)}, f32[66048]{0:T(1024)S(1)}, u32[]{:S(2)}, u32[]{:S(2)}) collective-permute-start(f32[66048]{0:T(1024)S(1)} %get-tuple-element.20), channel_id=1, source_target_pairs={{0,64},{8,72},{16,80},{24,88},{32,96},{40,104},{48,112},{56,120},{... | collective-permute-start | bytes 792584 | tf_op jit(solution)/shard_map/ppermute | solution.py:17
  46.3 4.6 %collective-permute-start.3 = (f32[66048]{0:T(1024)S(1)}, f32[66048]{0:T(1024)S(1)}, u32[]{:S(2)}, u32[]{:S(2)}) collective-permute-start(f32[66048]{0:T(1024)S(1)} %get-tuple-element.19), channel_id=1, source_target_pairs={{0,16},{8,24},{16,32},{24,40},{32,48},{40,56},{48,64},{56,72},{64,... | collective-permute-start | bytes 792584 | tf_op jit(solution)/shard_map/ppermute | solution.py:17
  50.9 2.8 %subtract_convert_fusion = (bf16[512,8,64]{2,0,1:T(8,128)(2,1)S(1)}, bf16[512,8,64]{2,0,1:T(8,128)(2,1)S(1)}) fusion(f32[512,8,64]{2,0,1:T(8,128)} %copy.60, f32[512,8,64]{2,0,1:T(8,128)} %copy.59, f32[512,64]{1,0:T(8,128)S(1)} %copy-done.10, f32[512,64]{1,0:T(8,128)S(1)} %copy-done.9), kind=kLoop, calls=%fused_computation.23 | loop fusion | flops 2097152 | bytes 3407872 | tf_op jit(solution)/shard_map/convert.4
  53.7 2.4 %fusion.2 = (f32[8,512]{1,0:T(8,128)S(1)}, f32[576,512,8]{1,0,2:T(8,128)S(1)}) fusion(pred[512,576]{0,1:T(8,128)(4,1)S(1)} %copy-done.1, bf16[512,8,64]{2,0,1:T(8,128)(2,1)S(1)} %get-tuple-element.16, bf16[512,8,64]{2,0,1:T(8,128)(2,1)S(1)} %get-tuple-element.15, bf16[512,1,64]{2,0,1:T(8,128)(2,1)S(1)} %get-tuple-element.22, ...), kind=kOutput, calls=%fused_computation.4 | convolution fusion | flops 613593088 | bytes 10944512 | tf_op jit(solution)/shard_map/igkd,jgd->gkij/dot_general | solution.py:184
  56.1 2.5 %fusion.5 = f32[8,512]{1,0:T(8,128)} fusion(f32[576,512,8]{1,0,2:T(8,128)S(1)} %get-tuple-element.35, f32[8,512]{1,0:T(8,128)S(1)} %get-tuple-element.34, pred[512,576]{0,1:T(8,128)(4,1)S(1)} %copy-done.1), kind=kLoop, calls=%fused_computation.9 | loop fusion | flops 9433088 | bytes 9764864 | tf_op jit(solution)/shard_map/reduce_sum | solution.py:190
  58.7 3.5 %fusion.10 = f32[128,8,512]{2,0,1:T(8,128)} fusion(f32[576,512,8]{1,0,2:T(8,128)S(1)} %get-tuple-element.35, f32[8,512]{1,0:T(8,128)S(1)} %get-tuple-element.34, pred[512,576]{0,1:T(8,128)(4,1)S(1)} %copy-done.1, bf16[512,1,128]{2,0,1:T(8,128)(2,1)S(1)} %bitcast.144, bf16[64,1,128]{2,0,1:T(8,128)(2,1)S(1)} %copy-done.20), kind=kOutput, calls=%fused_computation.14 | convolution fusion | flops 613711872 | bytes 11993088 | tf_op jit(solution)/shard_map/gkij,jgd->igkd/dot_general | solution.py:194
  62.2 0.8 add.210
  63.0 1.9 %collective-permute-start.8 = (f32[66048]{0:T(1024)}, f32[66048]{0:T(1024)S(1)}, u32[]{:S(2)}, u32[]{:S(2)}) collective-permute-start(f32[66048]{0:T(1024)} %add.210), channel_id=1, source_target_pairs={{0,128},{8,136},{16,144},{24,152},{32,160},{40,168},{48,176},{56,1... | collective-permute-start | bytes 792584 | tf_op jit(solution)/shard_map/ppermute | solution.py:17
  64.9 0.8 add.204
  65.7 4.0 %collective-permute-start.4 = (f32[66048]{0:T(1024)}, f32[66048]{0:T(1024)}, u32[]{:S(2)}, u32[]{:S(2)}) collective-permute-start(f32[66048]{0:T(1024)} %add.204), channel_id=1, source_target_pairs={{0,32},{8,40},{16,48},{24,56},{32,64},{40,72},{48,80},{56,88},{64,... | collective-permute-start | bytes 792584 | tf_op jit(solution)/shard_map/ppermute | solution.py:17
  69.8 1.5 fusion.90
  71.2 2.5 %fusion.89 = (f32[512,8]{0,1:T(8,128)}, f32[512,8,64]{0,2,1:T(8,128)}) fusion(bf16[8,128,64]{1,2,0:T(8,128)(2,1)S(1)} %copy-done, bf16[512,8,64]{2,0,1:T(8,128)(2,1)S(1)} %get-tuple-element.16, bf16[512,8,64]{2,0,1:T(8,128)(2,1)S(1)} %get-tuple-element.15), kind=kOutput, calls=%fused_computation.152 | convolution fusion | flops 69992512 | bytes 2244608 | tf_op jit(solution)/shard_map/sub | solution.py:48
  73.7 1.1 add.212
  74.8 1.9 %collective-permute-start.9 = (f32[66048]{0:T(1024)S(1)}, f32[66048]{0:T(1024)S(1)}, u32[]{:S(2)}, u32[]{:S(2)}) collective-permute-start(f32[66048]{0:T(1024)S(1)} %add.212), channel_id=1, source_target_pairs={{0,8},{8,16},{16,24},{24,32},{32,40},{40,48},{48,56},{56,64},{64,7... | collective-permute-start | bytes 792584 | tf_op jit(solution)/shard_map/ppermute | solution.py:17
  76.7 6.3 %collective-permute-done.4 = f32[66048]{0:T(1024)} collective-permute-done((f32[66048]{0:T(1024)}, f32[66048]{0:T(1024)}, u32[]{:S(2)}, u32[]{:S(2)}) %collective-permute-start.4) | collective-permute-done | bytes 264224 | tf_op jit(solution)/shard_map/ppermute | solution.py:17
  83.0 1.1 add.206
  84.1 1.9 %collective-permute-start.5 = (f32[66048]{0:T(1024)S(1)}, f32[66048]{0:T(1024)S(1)}, u32[]{:S(2)}, u32[]{:S(2)}) collective-permute-start(f32[66048]{0:T(1024)S(1)} %add.206), channel_id=1, source_target_pairs={{0,64},{8,72},{16,80},{24,88},{32,96},{40,104},{48,112},{56,120},{... | collective-permute-start | bytes 792584 | tf_op jit(solution)/shard_map/ppermute | solution.py:17
  86.0 1.2 divide_convert_fusion
  87.2 3.1 %collective-permute-done.9 = f32[66048]{0:T(1024)S(1)} collective-permute-done((f32[66048]{0:T(1024)S(1)}, f32[66048]{0:T(1024)S(1)}, u32[]{:S(2)}, u32[]{:S(2)}) %collective-permute-start.9) | collective-permute-done | bytes 264224 | tf_op jit(solution)/shard_map/ppermute | solution.py:17
  90.3 4.3 %collective-permute-start.10 = (f32[66048]{0:T(1024)S(1)}, f32[66048]{0:T(1024)S(1)}, u32[]{:S(2)}, u32[]{:S(2)}) collective-permute-start(f32[66048]{0:T(1024)S(1)} %add.214), channel_id=1, source_target_pairs={{0,16},{8,24},{16,32},{24,40},{32,48},{40,56},{48,64},{56,72},{64,... | collective-permute-start | bytes 792584 | tf_op jit(solution)/shard_map/ppermute | solution.py:17
  94.7 0.3 collective-permute-done.5
  95.0 2.8 %collective-permute-start.6 = (f32[66048]{0:T(1024)S(1)}, f32[66048]{0:T(1024)S(1)}, u32[]{:S(2)}, u32[]{:S(2)}) collective-permute-start(f32[66048]{0:T(1024)S(1)} %add.208), channel_id=1, source_target_pairs={{0,128},{8,136},{16,144},{24,152},{32,160},{40,168},{48,176},{56,1... | collective-permute-start | bytes 792584 | tf_op jit(solution)/shard_map/ppermute | solution.py:17
  97.9 3.7 %select_reduce_fusion = (f32[8,512]{1,0:T(8,128)S(1)}, bf16[8,512,576]{1,2,0:T(8,128)(2,1)}) fusion(pred[512,576]{0,1:T(8,128)(4,1)S(1)} %copy-done.12, bf16[8,128,576]{2,1,0:T(8,128)(2,1)S(1)} %copy-done.24, bf16[512,8,64]{0,2,1:T(8,128)(2,1)S(1)} %get-tuple-element.38, bf16[512,8,64]{0,2,1:T(8,128)(2,1)S(1)} %get-tuple-element.39), kind=kOutput, calls=%fused_computation.7 | convolution fusion | flops 613150720 | bytes 7258112 | tf_op jit(solution)/shard_map/igkf,gkfj->gkij/dot_general | solution.py:191
  101.6 5.6 %collective-permute-done.10 = f32[66048]{0:T(1024)S(1)} collective-permute-done((f32[66048]{0:T(1024)S(1)}, f32[66048]{0:T(1024)S(1)}, u32[]{:S(2)}, u32[]{:S(2)}) %collective-permute-start.10) | collective-permute-done | bytes 264224 | tf_op jit(solution)/shard_map/ppermute | solution.py:17
  107.2 2.4 %collective-permute-start.11 = (f32[66048]{0:T(1024)S(1)}, f32[66048]{0:T(1024)S(1)}, u32[]{:S(2)}, u32[]{:S(2)}) collective-permute-start(f32[66048]{0:T(1024)S(1)} %add.216), channel_id=1, source_target_pairs={{0,32},{8,40},{16,48},{24,56},{32,64},{40,72},{48,80},{56,88},{64,... | collective-permute-start | bytes 792584 | tf_op jit(solution)/shard_map/ppermute | solution.py:17
  109.6 1.1 add_add_fusion.1
  110.7 16.1 %collective-permute-done.11 = f32[66048]{0:T(1024)S(1)} collective-permute-done((f32[66048]{0:T(1024)S(1)}, f32[66048]{0:T(1024)S(1)}, u32[]{:S(2)}, u32[]{:S(2)}) %collective-permute-start.11) | collective-permute-done | bytes 264224 | tf_op jit(solution)/shard_map/ppermute | solution.py:17
  127.0 0.2 copy.45
  127.2 0.4 fusion.38
  127.7 0.4 fusion.56
  128.2 0.2 fusion.64
  128.4 0.2 fusion.62
  128.6 0.2 copy-done.17
  128.9 0.2 copy-done.13
  129.1 0.8 copy-done.25
  129.9 3.7 %fusion.17 = bf16[512,1,8,128]{0,3,2,1:T(8,128)(2,1)S(1)} fusion(f32[8,128,512]{2,1,0:T(8,128)S(1)} %fusion.56, f32[8,128,512]{2,1,0:T(8,128)S(1)} %fusion.38, f32[128,8,512]{2,0,1:T(8,128)S(1)} %copy-done.25, bf16[8,512,576]{1,2,0:T(8,128)(2,1)} %get-tuple-element.37, pred[512,576]{0,1:T(8,128)(4,1)S(1)} %copy-done.13, f32[512,8]{0,1:T(8,128)S(1)} %fusion.60, ...), kind=kOutput, calls=%fused_computation.24 | convolution fusion | flops 610304000 | bytes 12517440 | tf_op jit(solution)/shard_map/gkij,jgd->igkd/dot_general | solution.py:200
  133.6 0.8 copy.49
  134.4 0.5 all_to_all.14
  134.9 20.4 %all_to_all.19 = bf16[8,64,1024]{2,1,0:T(8,128)(2,1)S(1)} all-to-all(bf16[8,64,1024]{2,1,0:T(8,128)(2,1)S(1)} %all_to_all.14), channel_id=1, replica_groups=mesh['seq'=32,'head'=8] {'head'}, dimensions={0} | all-to-all | bytes 2097152 | tf_op jit(solution)/shard_map/all_to_all | solution.py:227
  155.3 1.1 copy.61
  (68 shorter events, 0.6 us)
Async XLA Ops:
  0.0 69.8 %copy-start = (bf16[8,128,64]{1,2,0:T(8,128)(2,1)S(1)}, bf16[8,128,64]{1,2,0:T(8,128)(2,1)}, u32[]{:S(2)}) copy-start(bf16[8,128,64]{1,2,0:T(8,128)(2,1)} %param.14) | copy-start | bytes 393220
  0.0 19.2 %copy-start.14 = (bf16[512,128]{1,0:T(8,128)(2,1)S(1)}, bf16[512,128]{1,0:T(8,128)(2,1)}, u32[]{:S(2)}) copy-start(bf16[512,128]{1,0:T(8,128)(2,1)} %param.12) | copy-start | bytes 393220
  5.8 31.4 %copy-start.8 = (bf16[512,1024]{1,0:T(8,128)(2,1)S(1)}, bf16[512,1024]{1,0:T(8,128)(2,1)}, u32[]{:S(2)}) copy-start(bf16[512,1024]{1,0:T(8,128)(2,1)} %param.10) | copy-start | bytes 3145732
  5.9 12.5 %collective-permute-start.1 = (bf16[64,1,128]{2,0,1:T(8,128)(2,1)S(1)}, bf16[64,1,128]{2,0,1:T(8,128)(2,1)S(1)}, u32[]{:S(2)}, u32[]{:S(2)}) collective-permute-start(bf16[64,1,128]{2,0,1:T(8,128)(2,1)S(1)} %pad_maximum_fusion.15), channel_id=1, source_target_pairs={{0,8},{8,16},{16,24},{24,32},{32,40},{40,48},{48,56},{56,64},{64,7... | collective-permute-start | bytes 49160 | tf_op jit(solution)/shard_map/ppermute | solution.py:17
  10.6 8.6 %collective-permute-start = (bf16[64,1,128]{2,0,1:T(8,128)(2,1)S(1)}, bf16[64,1,128]{2,0,1:T(8,128)(2,1)S(1)}, u32[]{:S(2)}, u32[]{:S(2)}) collective-permute-start(bf16[64,1,128]{2,0,1:T(8,128)(2,1)S(1)} %slice_bitcast_fusion), channel_id=1, source_target_pairs={{0,8},{8,16},{16,24},{24,32},{32,40},{40,48},{48,56},{56,64},{64,7... | collective-permute-start | bytes 49160 | tf_op jit(solution)/shard_map/ppermute | solution.py:17
  19.2 0.7 copy-start.19
  24.5 7.8 %copy-start.11 = (f32[8,128,1]{2,1,0:T(8,128)S(1)}, f32[8,128,1]{2,1,0:T(8,128)}, u32[]{:S(2)}) copy-start(f32[8,128,1]{2,1,0:T(8,128)} %get-tuple-element.12) | copy-start | bytes 12292
  25.5 11.7 %collective-permute-start.2 = (f32[66048]{0:T(1024)S(1)}, f32[66048]{0:T(1024)}, u32[]{:S(2)}, u32[]{:S(2)}) collective-permute-start(f32[66048]{0:T(1024)S(1)} %slice.59), channel_id=1, source_target_pairs={{0,8},{8,16},{16,24},{24,32},{32,40},{40,48},{48,56},{56,64},{64,7... | collective-permute-start | bytes 792584 | tf_op jit(solution)/shard_map/ppermute | solution.py:17
  39.9 2.0 %copy-start.2 = (f32[8,128,128]{2,1,0:T(8,128)S(1)}, f32[8,128,128]{2,1,0:T(8,128)}, u32[]{:S(2)}) copy-start(f32[8,128,128]{2,1,0:T(8,128)} %get-tuple-element.9) | copy-start | bytes 1572868
  39.9 2.0 %copy-start.18 = (f32[8,128]{1,0:T(8,128)S(1)}, f32[8,128]{1,0:T(8,128)}, u32[]{:S(2)}) copy-start(f32[8,128]{1,0:T(8,128)} %reduce.4) | copy-start | bytes 12292
  39.9 11.0 %copy-start.9 = (f32[512,64]{1,0:T(8,128)S(1)}, f32[512,64]{1,0:T(8,128)}, u32[]{:S(2)}) copy-start(f32[512,64]{1,0:T(8,128)} %copy.40) | copy-start | bytes 393220
  39.9 11.0 %copy-start.10 = (f32[512,64]{1,0:T(8,128)S(1)}, f32[512,64]{1,0:T(8,128)}, u32[]{:S(2)}) copy-start(f32[512,64]{1,0:T(8,128)} %copy.42) | copy-start | bytes 393220
  42.9 19.3 %collective-permute-start.7 = (f32[66048]{0:T(1024)S(1)}, f32[66048]{0:T(1024)S(1)}, u32[]{:S(2)}, u32[]{:S(2)}) collective-permute-start(f32[66048]{0:T(1024)S(1)} %get-tuple-element.20), channel_id=1, source_target_pairs={{0,64},{8,72},{16,80},{24,88},{32,96},{40,104},{48,112},{56,120},{... | collective-permute-start | bytes 792584 | tf_op jit(solution)/shard_map/ppermute | solution.py:17
  46.3 7.4 %copy-start.1 = (pred[512,576]{0,1:T(8,128)(4,1)S(1)}, pred[512,576]{0,1:T(8,128)(4,1)}, u32[]{:S(2)}) copy-start(pred[512,576]{0,1:T(8,128)(4,1)} %get-tuple-element.29) | copy-start | bytes 884740
  46.3 18.6 %collective-permute-start.3 = (f32[66048]{0:T(1024)S(1)}, f32[66048]{0:T(1024)S(1)}, u32[]{:S(2)}, u32[]{:S(2)}) collective-permute-start(f32[66048]{0:T(1024)S(1)} %get-tuple-element.19), channel_id=1, source_target_pairs={{0,16},{8,24},{16,32},{24,40},{32,48},{40,56},{48,64},{56,72},{64,... | collective-permute-start | bytes 792584 | tf_op jit(solution)/shard_map/ppermute | solution.py:17
  56.1 2.6 %copy-start.15 = (bf16[512,128]{1,0:T(8,128)(2,1)S(1)}, bf16[512,128]{1,0:T(8,128)(2,1)}, u32[]{:S(2)}) copy-start(bf16[512,128]{1,0:T(8,128)(2,1)} %param.12) | copy-start | bytes 393220
  56.1 2.6 %copy-start.20 = (bf16[64,1,128]{2,0,1:T(8,128)(2,1)S(1)}, bf16[64,1,128]{2,0,1:T(8,128)(2,1)}, u32[]{:S(2)}) copy-start(bf16[64,1,128]{2,0,1:T(8,128)(2,1)} %copy-done.19) | copy-start | bytes 49156
  62.2 3.5 %copy-start.3 = (f32[66048]{0:T(1024)}, f32[66048]{0:T(1024)S(1)}, u32[]{:S(2)}) copy-start(f32[66048]{0:T(1024)S(1)} %collective-permute-done.7) | copy-start | bytes 792580
  63.0 10.7 %collective-permute-start.8 = (f32[66048]{0:T(1024)}, f32[66048]{0:T(1024)S(1)}, u32[]{:S(2)}, u32[]{:S(2)}) collective-permute-start(f32[66048]{0:T(1024)} %add.210), channel_id=1, source_target_pairs={{0,128},{8,136},{16,144},{24,152},{32,160},{40,168},{48,176},{56,1... | collective-permute-start | bytes 792584 | tf_op jit(solution)/shard_map/ppermute | solution.py:17
  64.9 0.8 copy-start.5
  65.7 17.3 %collective-permute-start.4 = (f32[66048]{0:T(1024)}, f32[66048]{0:T(1024)}, u32[]{:S(2)}, u32[]{:S(2)}) collective-permute-start(f32[66048]{0:T(1024)} %add.204), channel_id=1, source_target_pairs={{0,32},{8,40},{16,48},{24,56},{32,64},{40,72},{48,80},{56,88},{64,... | collective-permute-start | bytes 792584 | tf_op jit(solution)/shard_map/ppermute | solution.py:17
  73.7 12.3 %copy-start.7 = (f32[512,8,64]{0,2,1:T(8,128)S(1)}, f32[512,8,64]{0,2,1:T(8,128)}, u32[]{:S(2)}) copy-start(f32[512,8,64]{0,2,1:T(8,128)} %get-tuple-element.31) | copy-start | bytes 3145732
  74.8 15.5 %collective-permute-start.9 = (f32[66048]{0:T(1024)S(1)}, f32[66048]{0:T(1024)S(1)}, u32[]{:S(2)}, u32[]{:S(2)}) collective-permute-start(f32[66048]{0:T(1024)S(1)} %add.212), channel_id=1, source_target_pairs={{0,8},{8,16},{16,24},{24,32},{32,40},{40,48},{48,56},{56,64},{64,7... | collective-permute-start | bytes 792584 | tf_op jit(solution)/shard_map/ppermute | solution.py:17
  84.1 10.9 %collective-permute-start.5 = (f32[66048]{0:T(1024)S(1)}, f32[66048]{0:T(1024)S(1)}, u32[]{:S(2)}, u32[]{:S(2)}) collective-permute-start(f32[66048]{0:T(1024)S(1)} %add.206), channel_id=1, source_target_pairs={{0,64},{8,72},{16,80},{24,88},{32,96},{40,104},{48,112},{56,120},{... | collective-permute-start | bytes 792584 | tf_op jit(solution)/shard_map/ppermute | solution.py:17
  86.0 11.8 %copy-start.12 = (pred[512,576]{0,1:T(8,128)(4,1)S(1)}, pred[512,576]{0,1:T(8,128)(4,1)}, u32[]{:S(2)}) copy-start(pred[512,576]{0,1:T(8,128)(4,1)} %get-tuple-element.28) | copy-start | bytes 884740
  86.0 11.8 %copy-start.24 = (bf16[8,128,576]{2,1,0:T(8,128)(2,1)S(1)}, bf16[8,128,576]{2,1,0:T(8,128)(2,1)}, u32[]{:S(2)}) copy-start(bf16[8,128,576]{2,1,0:T(8,128)(2,1)} %get-tuple-element.11) | copy-start | bytes 3538948
  90.3 16.9 %collective-permute-start.10 = (f32[66048]{0:T(1024)S(1)}, f32[66048]{0:T(1024)S(1)}, u32[]{:S(2)}, u32[]{:S(2)}) collective-permute-start(f32[66048]{0:T(1024)S(1)} %add.214), channel_id=1, source_target_pairs={{0,16},{8,24},{16,32},{24,40},{32,48},{40,56},{48,64},{56,72},{64,... | collective-permute-start | bytes 792584 | tf_op jit(solution)/shard_map/ppermute | solution.py:17
  95.0 14.6 %collective-permute-start.6 = (f32[66048]{0:T(1024)S(1)}, f32[66048]{0:T(1024)S(1)}, u32[]{:S(2)}, u32[]{:S(2)}) collective-permute-start(f32[66048]{0:T(1024)S(1)} %add.208), channel_id=1, source_target_pairs={{0,128},{8,136},{16,144},{24,152},{32,160},{40,168},{48,176},{56,1... | collective-permute-start | bytes 792584 | tf_op jit(solution)/shard_map/ppermute | solution.py:17
  97.9 11.8 %copy-start.6 = (f32[66048]{0:T(1024)S(1)}, f32[66048]{0:T(1024)}, u32[]{:S(2)}) copy-start(f32[66048]{0:T(1024)} %copy-done.5) | copy-start | bytes 792580
  101.6 25.3 %copy-start.4 = (f32[66048]{0:T(1024)S(1)}, f32[66048]{0:T(1024)}, u32[]{:S(2)}) copy-start(f32[66048]{0:T(1024)} %copy-done.3) | copy-start | bytes 792580
  107.2 19.7 %collective-permute-start.11 = (f32[66048]{0:T(1024)S(1)}, f32[66048]{0:T(1024)S(1)}, u32[]{:S(2)}, u32[]{:S(2)}) collective-permute-start(f32[66048]{0:T(1024)S(1)} %add.216), channel_id=1, source_target_pairs={{0,32},{8,40},{16,48},{24,56},{32,64},{40,72},{48,80},{56,88},{64,... | collective-permute-start | bytes 792584 | tf_op jit(solution)/shard_map/ppermute | solution.py:17
  128.1 0.7 copy-start.17
  128.1 0.7 copy-start.22
  128.1 0.7 copy-start.23
  128.1 1.0 copy-start.13
  128.1 1.0 copy-start.16
  128.1 1.0 copy-start.21
  128.1 1.8 %copy-start.25 = (f32[128,8,512]{2,0,1:T(8,128)S(1)}, f32[128,8,512]{2,0,1:T(8,128)}, u32[]{:S(2)}) copy-start(f32[128,8,512]{2,0,1:T(8,128)} %fusion.10) | copy-start | bytes 6291460

commit v11 on v10

--- a/solution.py
+++ b/solution.py
@@ -30,6 +30,29 @@
     cosine = cos_high * jnp.cos(lower) - sin_high * jnp.sin(lower)
     sine = sin_high * jnp.cos(lower) + cos_high * jnp.sin(lower)
     return (cosine, sine)
+
+
+def span_tables(offsets, half):
+    frequency = [500000.0 ** (-float(order) / half) for order in range(half)]
+    coarse = jnp.asarray([4096.0 * value % (2.0 * math.pi) for value in frequency], jnp.float32)
+    medium = jnp.asarray([64.0 * value % (2.0 * math.pi) for value in frequency], jnp.float32)
+    finest = jnp.asarray(frequency, jnp.float32)
+    quarters = SPAN // 64
+    upper = (offsets // 4096).astype(jnp.float32)[:, None] * coarse[None, :]
+    middle_index = (offsets[:, None] // 64 + jnp.arange(quarters, dtype=jnp.int32)[None, :]) % 64
+    middle = middle_index.astype(jnp.float32)[:, :, None] * medium[None, None, :]
+    lower = jnp.arange(64, dtype=jnp.float32)[:, None] * finest[None, :]
+    cos_upper = jnp.cos(upper)[:, None, :]
+    sin_upper = jnp.sin(upper)[:, None, :]
+    cos_high = cos_upper * jnp.cos(middle) - sin_upper * jnp.sin(middle)
+    sin_high = sin_upper * jnp.cos(middle) + cos_upper * jnp.sin(middle)
+    cos_high = cos_high[:, :, None, :]
+    sin_high = sin_high[:, :, None, :]
+    cos_lower = jnp.cos(lower)[None, None]
+    sin_lower = jnp.sin(lower)[None, None]
+    cosine = cos_high * cos_lower - sin_high * sin_lower
+    sine = sin_high * cos_lower + cos_high * sin_lower
+    return (cosine.reshape(-1, half), sine.reshape(-1, half))
 
 
 def rotate(rows, cosine, sine):
@@ -108,8 +131,7 @@
     group = heads // kv_local
     blocks = tokens // BLOCK
     extent = BLOCK + WINDOW
-    positions = (offsets[:, None] + jnp.arange(SPAN, dtype=jnp.int32)[None, :]).reshape(tokens)
-    cosine, sine = angle_tables(positions, head_dim // 2)
+    cosine, sine = span_tables(offsets, head_dim // 2)
     rot_k = rotate(
         keys.reshape(tokens, kv_local, head_dim).astype(jnp.float32), cosine, sine
     ).astype(jnp.bfloat16)

time: 157 us -> 153 us (0.975)
  other arithmetic: 25.9 us -> 22.8 us
  waiting for transfers between devices: 35.6 us -> 38.3 us
  starting transfers between devices: 38.9 us -> 36.9 us
  local copies, waits for them, and re-layouts: 11.9 us -> 10 us
    another operation x5, other arithmetic: 9.44 us -> 5.6 us
    ppermute x12, waiting for transfers between devices: 35.6 us -> 38.3 us  [passed_along(): lax.ppermute(value, axis, [(source, source + steps) for source in range(f...]
    ppermute x12, starting transfers between devices: 38.9 us -> 36.9 us  [passed_along(): lax.ppermute(value, axis, [(source, source + steps) for source in range(f...]
    unnamed x55 -> x62, local copies, waits for them, and re-layouts: 5.17 us -> 5.72 us
  transfers between devices with their start and end apart: 12 -> 12, of which waited for: 6 -> 7; matrix products, arithmetic and copies ran while one was open for 22% -> 20% of each run, Pallas kernels for 0% -> 0%
where the time goes in v11:
time: 153 us; the launch traced here: 152 us
  waiting for transfers between devices  38.3 us (25%)
  starting transfers between devices  36.9 us (24%)
  other arithmetic  22.8 us (15%)
  blocking collectives  20.2 us (13%)
  matrix products  18.5 us (12%)
  local copies, waits for them, and re-layouts  10 us (7%)
  Pallas kernels  4.56 us (3%)
    ppermute x12, waiting for transfers between devices, passed_along(): lax.ppermute(value, axis, [(source, source + steps) for source in range(f...  38.3 us
    ppermute x12, starting transfers between devices, passed_along(): lax.ppermute(value, axis, [(source, source + steps) for source in range(f...  36.9 us
    all_to_all x1, blocking collectives, body(): lax.all_to_all(result, 'head', split_axis=0, concat_axis=1, tiled=True)  20.2 us
    unnamed x62, local copies, waits for them, and re-layouts  5.72 us
    another operation x5, other arithmetic  5.6 us
    add x8, other arithmetic, body(): inclusive = inclusive + received  4.83 us
    pallas_call x1, Pallas kernels, key_features(): pl.pallas_call(kernel, grid=(1,), in_specs=[pl.BlockSpec((rows, dim), lam...  4.56 us
    dot_general x1, matrix products, body(): jnp.einsum('gkij,jgd->igkd', affinity.astype(jnp.bfloat16), ext_values, p...  3.71 us
  transfers between devices with their start and end apart: 12, of which 7 were waited for; matrix products, arithmetic and copies ran while one was open for 20% of the time, Pallas kernels for 0%

profile of v11, /device:TPU:2, one launch (start us, length us, event | category | flops | bytes accessed | tf_op | source)
XLA Modules:
  0.0 151.8 jit_solution(6460352098775546804)
XLA Ops:
  0.0 0.7 and_select_fusion.1
  0.8 0.8 fusion.36
  1.6 0.9 bitcast_convert_fusion
  2.5 0.8 multiply_cosine_fusion.1
  3.3 0.8 fusion.44
  4.2 0.2 subtract_convert_fusion.3
  4.3 0.5 copy-done.2
  4.9 3.8 %collective-permute-start.1 = (bf16[64,1,128]{2,0,1:T(8,128)(2,1)S(1)}, bf16[64,1,128]{2,0,1:T(8,128)(2,1)S(1)}, u32[]{:S(2)}, u32[]{:S(2)}) collective-permute-start(bf16[64,1,128]{2,0,1:T(8,128)(2,1)S(1)} %pad_maximum_fusion.15), channel_id=1, source_target_pairs={{0,8},{8,16},{16,24},{24,32},{32,40},{40,48},{48,56},{56,64},{64,7... | collective-permute-start | bytes 49160 | tf_op jit(solution)/shard_map/ppermute | solution.py:17
  8.8 3.8 %collective-permute-start = (bf16[64,1,128]{2,0,1:T(8,128)(2,1)S(1)}, bf16[64,1,128]{2,0,1:T(8,128)(2,1)S(1)}, u32[]{:S(2)}, u32[]{:S(2)}) collective-permute-start(bf16[64,1,128]{2,0,1:T(8,128)(2,1)S(1)} %slice_bitcast_fusion), channel_id=1, source_target_pairs={{0,8},{8,16},{16,24},{24,32},{32,40},{40,48},{48,56},{56,64},{64,7... | collective-permute-start | bytes 49160 | tf_op jit(solution)/shard_map/ppermute | solution.py:17
  12.6 0.6 or_convert_fusion.mask_ref
  13.2 0.6 broadcast_subtract_fusion
  13.8 0.6 collective-permute-done.1
  14.4 0.8 fusion.68.k_ref
  15.1 1.4 collective-permute-done
  16.5 0.7 fusion.34.v_ref
  17.2 4.6 %shard_map.100 = (bf16[8,128,576]{2,1,0:T(8,128)(2,1)}, f32[8,128,128]{2,1,0:T(8,128)}, f32[8,128,1]{2,1,0:T(8,128)}) custom-call(bf16[576,128]{1,0:T(8,128)(2,1)} %fusion.68.k_ref, bf16[8,64,128]{2,1,0:T(8,128)(2,1)} %bitcast.151, bf16[576,128]{1,0:T(8,128)(2,1)} %fusion.34.v_ref, f32[1,576]{1,0:T(1,128)} %or_convert_fusion.mask_ref), custom_call_target="tpu_custom_call" | custom-call | tf_op jit(solution)/shard_map/pallas_call | solution.py:104
  21.8 1.0 slice.59
  22.7 1.9 %collective-permute-start.2 = (f32[66048]{0:T(1024)S(1)}, f32[66048]{0:T(1024)}, u32[]{:S(2)}, u32[]{:S(2)}) collective-permute-start(f32[66048]{0:T(1024)S(1)} %slice.59), channel_id=1, source_target_pairs={{0,8},{8,16},{16,24},{24,32},{32,40},{40,48},{48,56},{56,64},{64,7... | collective-permute-start | bytes 792584 | tf_op jit(solution)/shard_map/ppermute | solution.py:17
  24.7 1.2 fusion.22
  25.8 1.8 %reduce.4 = f32[8,128]{1,0:T(8,128)} reduce(f32[8,128,1]{2,1,0:T(8,128)} %get-tuple-element.12, f32[]{:T(128)} %constant.74), dimensions={2}, to_apply=%get-tuple-element.12.reduce_sub_computation | reduce | bytes 8196 | tf_op jit(solution)/shard_map/pallas_call | solution.py:104
  27.7 6.2 %collective-permute-done.2 = f32[66048]{0:T(1024)} collective-permute-done((f32[66048]{0:T(1024)S(1)}, f32[66048]{0:T(1024)}, u32[]{:S(2)}, u32[]{:S(2)}) %collective-permute-start.2) | collective-permute-done | bytes 264224 | tf_op jit(solution)/shard_map/ppermute | solution.py:17
  33.9 0.5 copy.26
  34.5 0.3 fusion.70
  34.7 1.9 %copy.45 = f32[512,8,64]{2,0,1:T(8,128)} copy(f32[512,8,64]{0,2,1:T(8,128)S(1)} %get-tuple-element.18) | data formatting | bytes 2097152
  36.7 2.0 %copy.46 = f32[512,8,64]{2,0,1:T(8,128)} copy(f32[512,8,64]{0,2,1:T(8,128)S(1)} %get-tuple-element.17) | data formatting | bytes 2097152
  38.6 1.0 slice_add_fusion
  39.6 3.4 %collective-permute-start.7 = (f32[66048]{0:T(1024)S(1)}, f32[66048]{0:T(1024)S(1)}, u32[]{:S(2)}, u32[]{:S(2)}) collective-permute-start(f32[66048]{0:T(1024)S(1)} %get-tuple-element.22), channel_id=1, source_target_pairs={{0,64},{8,72},{16,80},{24,88},{32,96},{40,104},{48,112},{56,120},{... | collective-permute-start | bytes 792584 | tf_op jit(solution)/shard_map/ppermute | solution.py:17
  43.1 2.8 %collective-permute-start.3 = (f32[66048]{0:T(1024)S(1)}, f32[66048]{0:T(1024)S(1)}, u32[]{:S(2)}, u32[]{:S(2)}) collective-permute-start(f32[66048]{0:T(1024)S(1)} %get-tuple-element.21), channel_id=1, source_target_pairs={{0,16},{8,24},{16,32},{24,40},{32,48},{40,56},{48,64},{56,72},{64,... | collective-permute-start | bytes 792584 | tf_op jit(solution)/shard_map/ppermute | solution.py:17
  46.0 2.9 %subtract_convert_fusion = (bf16[512,8,64]{2,0,1:T(8,128)(2,1)S(1)}, bf16[512,8,64]{2,0,1:T(8,128)(2,1)S(1)}) fusion(f32[512,8,64]{2,0,1:T(8,128)} %copy.46, f32[512,8,64]{2,0,1:T(8,128)} %copy.45, f32[512,64]{1,0:T(8,128)S(1)} %bitcast.144, f32[512,64]{1,0:T(8,128)S(1)} %bitcast.142), kind=kLoop, calls=%fused_computation.23 | loop fusion | flops 2097152 | bytes 3407872 | tf_op jit(solution)/shard_map/convert.4
  48.8 2.3 %fusion.2 = (f32[8,512]{1,0:T(8,128)S(1)}, f32[576,512,8]{1,0,2:T(8,128)S(1)}) fusion(pred[512,576]{0,1:T(8,128)(4,1)S(1)} %copy-done.1, bf16[512,8,64]{2,0,1:T(8,128)(2,1)S(1)} %get-tuple-element.16, bf16[512,8,64]{2,0,1:T(8,128)(2,1)S(1)} %get-tuple-element.15, bf16[512,1,64]{2,0,1:T(8,128)(2,1)S(1)} %copy-done.8, bf16[512,1,64]{2,0,1:T(8,128)(2,1)S(1)} %copy-done.6, ...), kind=kOutput, calls=%fused_computation.4 | convolution fusion | flops 613593088 | bytes 10944512 | tf_op jit(solution)/shard_map/igkd,jgd->gkij/dot_general | solution.py:206
  51.2 2.5 %fusion.5 = f32[8,512]{1,0:T(8,128)} fusion(f32[576,512,8]{1,0,2:T(8,128)S(1)} %get-tuple-element.40, f32[8,512]{1,0:T(8,128)S(1)} %get-tuple-element.39, pred[512,576]{0,1:T(8,128)(4,1)S(1)} %copy-done.1), kind=kLoop, calls=%fused_computation.9 | loop fusion | flops 9433088 | bytes 9764864 | tf_op jit(solution)/shard_map/reduce_sum | solution.py:212
  53.7 3.5 %fusion.10 = f32[128,8,512]{2,0,1:T(8,128)} fusion(f32[576,512,8]{1,0,2:T(8,128)S(1)} %get-tuple-element.40, f32[8,512]{1,0:T(8,128)S(1)} %get-tuple-element.39, pred[512,576]{0,1:T(8,128)(4,1)S(1)} %copy-done.1, bf16[512,1,128]{2,0,1:T(8,128)(2,1)S(1)} %bitcast.149, bf16[64,1,128]{2,0,1:T(8,128)(2,1)S(1)} %copy-done.23), kind=kOutput, calls=%fused_computation.14 | convolution fusion | flops 613711872 | bytes 11993088 | tf_op jit(solution)/shard_map/gkij,jgd->igkd/dot_general | solution.py:216
  57.2 0.8 add.176
  58.0 1.9 %collective-permute-start.8 = (f32[66048]{0:T(1024)}, f32[66048]{0:T(1024)S(1)}, u32[]{:S(2)}, u32[]{:S(2)}) collective-permute-start(f32[66048]{0:T(1024)} %add.176), channel_id=1, source_target_pairs={{0,128},{8,136},{16,144},{24,152},{32,160},{40,168},{48,176},{56,1... | collective-permute-start | bytes 792584 | tf_op jit(solution)/shard_map/ppermute | solution.py:17
  60.0 0.8 add.170
  60.8 5.3 %collective-permute-start.4 = (f32[66048]{0:T(1024)}, f32[66048]{0:T(1024)}, u32[]{:S(2)}, u32[]{:S(2)}) collective-permute-start(f32[66048]{0:T(1024)} %add.170), channel_id=1, source_target_pairs={{0,32},{8,40},{16,48},{24,56},{32,64},{40,72},{48,80},{56,88},{64,... | collective-permute-start | bytes 792584 | tf_op jit(solution)/shard_map/ppermute | solution.py:17
  66.1 1.5 fusion.72
  67.6 2.5 %fusion.71 = (f32[512,8]{0,1:T(8,128)}, f32[512,8,64]{0,2,1:T(8,128)}) fusion(bf16[8,128,64]{1,2,0:T(8,128)(2,1)S(1)} %copy-done, bf16[512,8,64]{2,0,1:T(8,128)(2,1)S(1)} %get-tuple-element.16, bf16[512,8,64]{2,0,1:T(8,128)(2,1)S(1)} %get-tuple-element.15), kind=kOutput, calls=%fused_computation.125 | convolution fusion | flops 69992512 | bytes 2244608 | tf_op jit(solution)/shard_map/sub | solution.py:71
  70.0 1.1 add.178
  71.1 1.9 %collective-permute-start.9 = (f32[66048]{0:T(1024)S(1)}, f32[66048]{0:T(1024)S(1)}, u32[]{:S(2)}, u32[]{:S(2)}) collective-permute-start(f32[66048]{0:T(1024)S(1)} %add.178), channel_id=1, source_target_pairs={{0,8},{8,16},{16,24},{24,32},{32,40},{40,48},{48,56},{56,64},{64,7... | collective-permute-start | bytes 792584 | tf_op jit(solution)/shard_map/ppermute | solution.py:17
  73.0 1.7 %collective-permute-done.4 = f32[66048]{0:T(1024)} collective-permute-done((f32[66048]{0:T(1024)}, f32[66048]{0:T(1024)}, u32[]{:S(2)}, u32[]{:S(2)}) %collective-permute-start.4) | collective-permute-done | bytes 264224 | tf_op jit(solution)/shard_map/ppermute | solution.py:17
  74.7 1.1 add.172
  75.8 3.0 %collective-permute-start.5 = (f32[66048]{0:T(1024)S(1)}, f32[66048]{0:T(1024)S(1)}, u32[]{:S(2)}, u32[]{:S(2)}) collective-permute-start(f32[66048]{0:T(1024)S(1)} %add.172), channel_id=1, source_target_pairs={{0,64},{8,72},{16,80},{24,88},{32,96},{40,104},{48,112},{56,120},{... | collective-permute-start | bytes 792584 | tf_op jit(solution)/shard_map/ppermute | solution.py:17
  78.8 1.1 divide_convert_fusion
  80.0 5.4 %collective-permute-done.9 = f32[66048]{0:T(1024)S(1)} collective-permute-done((f32[66048]{0:T(1024)S(1)}, f32[66048]{0:T(1024)S(1)}, u32[]{:S(2)}, u32[]{:S(2)}) %collective-permute-start.9) | collective-permute-done | bytes 264224 | tf_op jit(solution)/shard_map/ppermute | solution.py:17
  85.4 3.9 %collective-permute-start.10 = (f32[66048]{0:T(1024)S(1)}, f32[66048]{0:T(1024)S(1)}, u32[]{:S(2)}, u32[]{:S(2)}) collective-permute-start(f32[66048]{0:T(1024)S(1)} %add.180), channel_id=1, source_target_pairs={{0,16},{8,24},{16,32},{24,40},{32,48},{40,56},{48,64},{56,72},{64,... | collective-permute-start | bytes 792584 | tf_op jit(solution)/shard_map/ppermute | solution.py:17
  89.3 1.4 collective-permute-start.6
  90.8 3.7 %select_reduce_fusion = (f32[8,512]{1,0:T(8,128)S(1)}, bf16[8,512,576]{1,2,0:T(8,128)(2,1)}) fusion(pred[512,576]{0,1:T(8,128)(4,1)S(1)} %copy-done.15, bf16[8,128,576]{2,1,0:T(8,128)(2,1)S(1)} %copy-done.27, bf16[512,8,64]{0,2,1:T(8,128)(2,1)S(1)} %get-tuple-element.43, bf16[512,8,64]{0,2,1:T(8,128)(2,1)S(1)} %get-tuple-element.44), kind=kOutput, calls=%fused_computation.7 | convolution fusion | flops 613150720 | bytes 7258112 | tf_op jit(solution)/shard_map/igkf,gkfj->gkij/dot_general | solution.py:213
  94.5 7.3 %collective-permute-done.10 = f32[66048]{0:T(1024)S(1)} collective-permute-done((f32[66048]{0:T(1024)S(1)}, f32[66048]{0:T(1024)S(1)}, u32[]{:S(2)}, u32[]{:S(2)}) %collective-permute-start.10) | collective-permute-done | bytes 264224 | tf_op jit(solution)/shard_map/ppermute | solution.py:17
  101.8 3.7 %collective-permute-start.11 = (f32[66048]{0:T(1024)S(1)}, f32[66048]{0:T(1024)S(1)}, u32[]{:S(2)}, u32[]{:S(2)}) collective-permute-start(f32[66048]{0:T(1024)S(1)} %add.182), channel_id=1, source_target_pairs={{0,32},{8,40},{16,48},{24,56},{32,64},{40,72},{48,80},{56,88},{64,... | collective-permute-start | bytes 792584 | tf_op jit(solution)/shard_map/ppermute | solution.py:17
  105.5 1.2 add_add_fusion.1
  106.7 15.7 %collective-permute-done.11 = f32[66048]{0:T(1024)S(1)} collective-permute-done((f32[66048]{0:T(1024)S(1)}, f32[66048]{0:T(1024)S(1)}, u32[]{:S(2)}, u32[]{:S(2)}) %collective-permute-start.11) | collective-permute-done | bytes 264224 | tf_op jit(solution)/shard_map/ppermute | solution.py:17
  122.6 0.2 copy.31
  122.8 0.4 fusion.26
  123.2 0.4 fusion.32
  123.7 0.2 fusion.48
  124.0 0.2 fusion.46
  124.5 0.2 copy-done.16
  124.7 0.8 copy-done.29
  125.5 3.7 %fusion.17 = bf16[512,1,8,128]{0,3,2,1:T(8,128)(2,1)S(1)} fusion(f32[8,128,512]{2,1,0:T(8,128)S(1)} %fusion.32, f32[8,128,512]{2,1,0:T(8,128)S(1)} %fusion.26, f32[128,8,512]{2,0,1:T(8,128)S(1)} %copy-done.29, bf16[8,512,576]{1,2,0:T(8,128)(2,1)} %get-tuple-element.42, pred[512,576]{0,1:T(8,128)(4,1)S(1)} %copy-done.16, f32[512,8]{0,1:T(8,128)S(1)} %fusion.38, ...), kind=kOutput, calls=%fused_computation.24 | convolution fusion | flops 610304000 | bytes 12517440 | tf_op jit(solution)/shard_map/gkij,jgd->igkd/dot_general | solution.py:222
  129.2 0.8 copy.35
  130.0 0.5 all_to_all.14
  130.5 20.2 %all_to_all.19 = bf16[8,64,1024]{2,1,0:T(8,128)(2,1)S(1)} all-to-all(bf16[8,64,1024]{2,1,0:T(8,128)(2,1)S(1)} %all_to_all.14), channel_id=1, replica_groups=mesh['seq'=32,'head'=8] {'head'}, dimensions={0} | all-to-all | bytes 2097152 | tf_op jit(solution)/shard_map/all_to_all | solution.py:249
  150.7 1.1 copy.47
  (76 shorter events, 0.9 us)
Async XLA Ops:
  0.0 66.1 %copy-start = (bf16[8,128,64]{1,2,0:T(8,128)(2,1)S(1)}, bf16[8,128,64]{1,2,0:T(8,128)(2,1)}, u32[]{:S(2)}) copy-start(bf16[8,128,64]{1,2,0:T(8,128)(2,1)} %param.14) | copy-start | bytes 393220
  0.0 8.8 %copy-start.17 = (bf16[512,128]{1,0:T(8,128)(2,1)S(1)}, bf16[512,128]{1,0:T(8,128)(2,1)}, u32[]{:S(2)}) copy-start(bf16[512,128]{1,0:T(8,128)(2,1)} %param.12) | copy-start | bytes 393220
  0.0 13.2 %copy-start.28 = (f32[8]{0:T(128)S(1)}, f32[8]{0:T(128)}, u32[]{:S(2)}) copy-start(f32[8]{0:T(128)} %param.16) | copy-start | bytes 100
  4.1 0.7 copy-start.2
  4.2 29.8 %copy-start.14 = (bf16[512,1024]{1,0:T(8,128)(2,1)S(1)}, bf16[512,1024]{1,0:T(8,128)(2,1)}, u32[]{:S(2)}) copy-start(bf16[512,1024]{1,0:T(8,128)(2,1)} %param.10) | copy-start | bytes 3145732
  4.9 22.8 %copy-start.5 = (bf16[512,1,64]{2,0,1:T(8,128)(2,1)}, bf16[512,1,64]{2,0,1:T(8,128)(2,1)S(1)}, u32[]{:S(2)}) copy-start(bf16[512,1,64]{2,0,1:T(8,128)(2,1)S(1)} %get-tuple-element.19) | copy-start | bytes 196612
  4.9 22.8 %copy-start.7 = (bf16[512,1,64]{2,0,1:T(8,128)(2,1)}, bf16[512,1,64]{2,0,1:T(8,128)(2,1)S(1)}, u32[]{:S(2)}) copy-start(bf16[512,1,64]{2,0,1:T(8,128)(2,1)S(1)} %get-tuple-element.20) | copy-start | bytes 196612
  4.9 9.4 %collective-permute-start.1 = (bf16[64,1,128]{2,0,1:T(8,128)(2,1)S(1)}, bf16[64,1,128]{2,0,1:T(8,128)(2,1)S(1)}, u32[]{:S(2)}, u32[]{:S(2)}) collective-permute-start(bf16[64,1,128]{2,0,1:T(8,128)(2,1)S(1)} %pad_maximum_fusion.15), channel_id=1, source_target_pairs={{0,8},{8,16},{16,24},{24,32},{32,40},{40,48},{48,56},{56,64},{64,7... | collective-permute-start | bytes 49160 | tf_op jit(solution)/shard_map/ppermute | solution.py:17
  8.8 7.7 %collective-permute-start = (bf16[64,1,128]{2,0,1:T(8,128)(2,1)S(1)}, bf16[64,1,128]{2,0,1:T(8,128)(2,1)S(1)}, u32[]{:S(2)}, u32[]{:S(2)}) collective-permute-start(bf16[64,1,128]{2,0,1:T(8,128)(2,1)S(1)} %slice_bitcast_fusion), channel_id=1, source_target_pairs={{0,8},{8,16},{16,24},{24,32},{32,40},{40,48},{48,56},{56,64},{64,7... | collective-permute-start | bytes 49160 | tf_op jit(solution)/shard_map/ppermute | solution.py:17
  16.5 5.2 %copy-start.22 = (bf16[64,1,128]{2,0,1:T(8,128)(2,1)}, bf16[64,1,128]{2,0,1:T(8,128)(2,1)S(1)}, u32[]{:S(2)}) copy-start(bf16[64,1,128]{2,0,1:T(8,128)(2,1)S(1)} %collective-permute-done) | copy-start | bytes 49156
  22.7 11.2 %collective-permute-start.2 = (f32[66048]{0:T(1024)S(1)}, f32[66048]{0:T(1024)}, u32[]{:S(2)}, u32[]{:S(2)}) collective-permute-start(f32[66048]{0:T(1024)S(1)} %slice.59), channel_id=1, source_target_pairs={{0,8},{8,16},{16,24},{24,32},{32,40},{40,48},{48,56},{56,64},{64,7... | collective-permute-start | bytes 792584 | tf_op jit(solution)/shard_map/ppermute | solution.py:17
  36.7 2.0 %copy-start.4 = (f32[8,128,128]{2,1,0:T(8,128)S(1)}, f32[8,128,128]{2,1,0:T(8,128)}, u32[]{:S(2)}) copy-start(f32[8,128,128]{2,1,0:T(8,128)} %get-tuple-element.9) | copy-start | bytes 1572868
  36.7 2.0 %copy-start.21 = (f32[8,128]{1,0:T(8,128)S(1)}, f32[8,128]{1,0:T(8,128)}, u32[]{:S(2)}) copy-start(f32[8,128]{1,0:T(8,128)} %reduce.4) | copy-start | bytes 12292
  36.7 9.2 %copy-start.3 = (f32[2,4,64,64]{3,2,1,0:T(8,128)S(1)}, f32[2,4,64,64]{3,2,1,0:T(8,128)}, u32[]{:S(2)}) copy-start(f32[2,4,64,64]{3,2,1,0:T(8,128)} %copy-done.2) | copy-start | bytes 393220
  39.6 17.6 %collective-permute-start.7 = (f32[66048]{0:T(1024)S(1)}, f32[66048]{0:T(1024)S(1)}, u32[]{:S(2)}, u32[]{:S(2)}) collective-permute-start(f32[66048]{0:T(1024)S(1)} %get-tuple-element.22), channel_id=1, source_target_pairs={{0,64},{8,72},{16,80},{24,88},{32,96},{40,104},{48,112},{56,120},{... | collective-permute-start | bytes 792584 | tf_op jit(solution)/shard_map/ppermute | solution.py:17
  43.1 16.9 %collective-permute-start.3 = (f32[66048]{0:T(1024)S(1)}, f32[66048]{0:T(1024)S(1)}, u32[]{:S(2)}, u32[]{:S(2)}) collective-permute-start(f32[66048]{0:T(1024)S(1)} %get-tuple-element.21), channel_id=1, source_target_pairs={{0,16},{8,24},{16,32},{24,40},{32,48},{40,56},{48,64},{56,72},{64,... | collective-permute-start | bytes 792584 | tf_op jit(solution)/shard_map/ppermute | solution.py:17
  45.9 2.9 %copy-start.1 = (pred[512,576]{0,1:T(8,128)(4,1)S(1)}, pred[512,576]{0,1:T(8,128)(4,1)}, u32[]{:S(2)}) copy-start(pred[512,576]{0,1:T(8,128)(4,1)} %get-tuple-element.28) | copy-start | bytes 884740
  45.9 2.9 %copy-start.6 = (bf16[512,1,64]{2,0,1:T(8,128)(2,1)S(1)}, bf16[512,1,64]{2,0,1:T(8,128)(2,1)}, u32[]{:S(2)}) copy-start(bf16[512,1,64]{2,0,1:T(8,128)(2,1)} %copy-done.5) | copy-start | bytes 196612
  45.9 2.9 %copy-start.8 = (bf16[512,1,64]{2,0,1:T(8,128)(2,1)S(1)}, bf16[512,1,64]{2,0,1:T(8,128)(2,1)}, u32[]{:S(2)}) copy-start(bf16[512,1,64]{2,0,1:T(8,128)(2,1)} %copy-done.7) | copy-start | bytes 196612
  51.2 2.6 %copy-start.18 = (bf16[512,128]{1,0:T(8,128)(2,1)S(1)}, bf16[512,128]{1,0:T(8,128)(2,1)}, u32[]{:S(2)}) copy-start(bf16[512,128]{1,0:T(8,128)(2,1)} %param.12) | copy-start | bytes 393220
  51.2 2.6 %copy-start.23 = (bf16[64,1,128]{2,0,1:T(8,128)(2,1)S(1)}, bf16[64,1,128]{2,0,1:T(8,128)(2,1)}, u32[]{:S(2)}) copy-start(bf16[64,1,128]{2,0,1:T(8,128)(2,1)} %copy-done.22) | copy-start | bytes 49156
  57.2 3.6 %copy-start.9 = (f32[66048]{0:T(1024)}, f32[66048]{0:T(1024)S(1)}, u32[]{:S(2)}) copy-start(f32[66048]{0:T(1024)S(1)} %collective-permute-done.7) | copy-start | bytes 792580
  58.0 12.0 %collective-permute-start.8 = (f32[66048]{0:T(1024)}, f32[66048]{0:T(1024)S(1)}, u32[]{:S(2)}, u32[]{:S(2)}) collective-permute-start(f32[66048]{0:T(1024)} %add.176), channel_id=1, source_target_pairs={{0,128},{8,136},{16,144},{24,152},{32,160},{40,168},{48,176},{56,1... | collective-permute-start | bytes 792584 | tf_op jit(solution)/shard_map/ppermute | solution.py:17
  60.0 0.8 copy-start.11
  60.8 13.9 %collective-permute-start.4 = (f32[66048]{0:T(1024)}, f32[66048]{0:T(1024)}, u32[]{:S(2)}, u32[]{:S(2)}) collective-permute-start(f32[66048]{0:T(1024)} %add.170), channel_id=1, source_target_pairs={{0,32},{8,40},{16,48},{24,56},{32,64},{40,72},{48,80},{56,88},{64,... | collective-permute-start | bytes 792584 | tf_op jit(solution)/shard_map/ppermute | solution.py:17
  70.0 8.8 %copy-start.13 = (f32[512,8,64]{0,2,1:T(8,128)S(1)}, f32[512,8,64]{0,2,1:T(8,128)}, u32[]{:S(2)}) copy-start(f32[512,8,64]{0,2,1:T(8,128)} %get-tuple-element.36) | copy-start | bytes 3145732
  71.1 14.3 %collective-permute-start.9 = (f32[66048]{0:T(1024)S(1)}, f32[66048]{0:T(1024)S(1)}, u32[]{:S(2)}, u32[]{:S(2)}) collective-permute-start(f32[66048]{0:T(1024)S(1)} %add.178), channel_id=1, source_target_pairs={{0,8},{8,16},{16,24},{24,32},{32,40},{40,48},{48,56},{56,64},{64,7... | collective-permute-start | bytes 792584 | tf_op jit(solution)/shard_map/ppermute | solution.py:17
  75.8 13.5 %collective-permute-start.5 = (f32[66048]{0:T(1024)S(1)}, f32[66048]{0:T(1024)S(1)}, u32[]{:S(2)}, u32[]{:S(2)}) collective-permute-start(f32[66048]{0:T(1024)S(1)} %add.172), channel_id=1, source_target_pairs={{0,64},{8,72},{16,80},{24,88},{32,96},{40,104},{48,112},{56,120},{... | collective-permute-start | bytes 792584 | tf_op jit(solution)/shard_map/ppermute | solution.py:17
  78.8 12.0 %copy-start.15 = (pred[512,576]{0,1:T(8,128)(4,1)S(1)}, pred[512,576]{0,1:T(8,128)(4,1)}, u32[]{:S(2)}) copy-start(pred[512,576]{0,1:T(8,128)(4,1)} %get-tuple-element.27) | copy-start | bytes 884740
  78.8 12.0 %copy-start.27 = (bf16[8,128,576]{2,1,0:T(8,128)(2,1)S(1)}, bf16[8,128,576]{2,1,0:T(8,128)(2,1)}, u32[]{:S(2)}) copy-start(bf16[8,128,576]{2,1,0:T(8,128)(2,1)} %get-tuple-element.11) | copy-start | bytes 3538948
  85.4 16.4 %collective-permute-start.10 = (f32[66048]{0:T(1024)S(1)}, f32[66048]{0:T(1024)S(1)}, u32[]{:S(2)}, u32[]{:S(2)}) collective-permute-start(f32[66048]{0:T(1024)S(1)} %add.180), channel_id=1, source_target_pairs={{0,16},{8,24},{16,32},{24,40},{32,48},{40,56},{48,64},{56,72},{64,... | collective-permute-start | bytes 792584 | tf_op jit(solution)/shard_map/ppermute | solution.py:17
  89.3 16.2 %collective-permute-start.6 = (f32[66048]{0:T(1024)S(1)}, f32[66048]{0:T(1024)S(1)}, u32[]{:S(2)}, u32[]{:S(2)}) collective-permute-start(f32[66048]{0:T(1024)S(1)} %add.174), channel_id=1, source_target_pairs={{0,128},{8,136},{16,144},{24,152},{32,160},{40,168},{48,176},{56,1... | collective-permute-start | bytes 792584 | tf_op jit(solution)/shard_map/ppermute | solution.py:17
  90.8 14.7 %copy-start.12 = (f32[66048]{0:T(1024)S(1)}, f32[66048]{0:T(1024)}, u32[]{:S(2)}) copy-start(f32[66048]{0:T(1024)} %copy-done.11) | copy-start | bytes 792580
  94.5 27.9 %copy-start.10 = (f32[66048]{0:T(1024)S(1)}, f32[66048]{0:T(1024)}, u32[]{:S(2)}) copy-start(f32[66048]{0:T(1024)} %copy-done.9) | copy-start | bytes 792580
  101.8 20.6 %collective-permute-start.11 = (f32[66048]{0:T(1024)S(1)}, f32[66048]{0:T(1024)S(1)}, u32[]{:S(2)}, u32[]{:S(2)}) collective-permute-start(f32[66048]{0:T(1024)S(1)} %add.182), channel_id=1, source_target_pairs={{0,32},{8,40},{16,48},{24,56},{32,64},{40,72},{48,80},{56,88},{64,... | collective-permute-start | bytes 792584 | tf_op jit(solution)/shard_map/ppermute | solution.py:17
  123.7 0.7 copy-start.20
  123.7 0.7 copy-start.25
  123.7 0.7 copy-start.26
  123.7 1.0 copy-start.16
  123.7 1.0 copy-start.19
  123.7 1.0 copy-start.24
  123.7 1.8 %copy-start.29 = (f32[128,8,512]{2,0,1:T(8,128)S(1)}, f32[128,8,512]{2,0,1:T(8,128)}, u32[]{:S(2)}) copy-start(f32[128,8,512]{2,0,1:T(8,128)} %fusion.10) | copy-start | bytes 6291460

commit v12 on v11

--- a/solution.py
+++ b/solution.py
@@ -174,7 +174,7 @@
     orders = (shifts, shifts[half:] + shifts[:half])
     middle = packed.size // 2
     pieces = []
-    for order, piece in zip(orders, (packed[:middle], packed[middle:])):
+    for order, piece in zip(orders, lax.optimization_barrier((packed[:middle], packed[middle:]))):
         inclusive = piece
         exclusive = jnp.zeros_like(piece)
         for place, shift in enumerate(order):

time: 153 us -> 153 us (level)
  the two profiles are of different devices: /device:TPU:2 before, /device:TPU:36 now
where the time goes in v12:
time: 153 us
  starting transfers between devices  43.2 us (28%)
  waiting for transfers between devices  30.7 us (20%)
  other arithmetic  25.7 us (17%)
  blocking collectives  20.3 us (13%)
  matrix products  18.5 us (12%)
  local copies, waits for them, and re-layouts  9.04 us (6%)
  Pallas kernels  4.56 us (3%)
    ppermute x12, starting transfers between devices, passed_along(): lax.ppermute(value, axis, [(source, source + steps) for source in range(f...  43.2 us
    ppermute x12, waiting for transfers between devices, passed_along(): lax.ppermute(value, axis, [(source, source + steps) for source in range(f...  30.7 us
    all_to_all x1, blocking collectives, body(): lax.all_to_all(result, 'head', split_axis=0, concat_axis=1, tiled=True)  20.3 us
    add x8, other arithmetic, body(): inclusive = inclusive + received  5.74 us
    unnamed x58, local copies, waits for them, and re-layouts  5.72 us
    another operation x5, other arithmetic  5.6 us
    pallas_call x1, Pallas kernels, key_features(): pl.pallas_call(kernel, grid=(1,), in_specs=[pl.BlockSpec((rows, dim), lam...  4.56 us
    dot_general x1, matrix products, body(): jnp.einsum('igkf,gkfj->gkij', phi_query, phi_key, preferred_element_type=...  3.73 us
  transfers between devices with their start and end apart: 12, of which 6 were waited for; matrix products, arithmetic and copies ran while one was open for 22% of the time, Pallas kernels for 0%

profile of v12, /device:TPU:36, one launch (start us, length us, event | category | flops | bytes accessed | tf_op | source)
XLA Modules:
  0.0 152.6 jit_solution(8889033024427594116)
XLA Ops:
  0.0 0.7 and_select_fusion.1
  0.8 0.8 fusion.36
  1.6 0.9 bitcast_convert_fusion
  2.5 0.8 multiply_cosine_fusion.1
  3.3 0.8 fusion.44
  4.2 0.2 subtract_convert_fusion.3
  4.3 0.5 copy-done.2
  4.9 3.9 %collective-permute-start.1 = (bf16[64,1,128]{2,0,1:T(8,128)(2,1)S(1)}, bf16[64,1,128]{2,0,1:T(8,128)(2,1)S(1)}, u32[]{:S(2)}, u32[]{:S(2)}) collective-permute-start(bf16[64,1,128]{2,0,1:T(8,128)(2,1)S(1)} %pad_maximum_fusion.15), channel_id=1, source_target_pairs={{0,8},{8,16},{16,24},{24,32},{32,40},{40,48},{48,56},{56,64},{64,7... | collective-permute-start | bytes 49160 | tf_op jit(solution)/shard_map/ppermute | solution.py:17
  8.9 3.8 %collective-permute-start = (bf16[64,1,128]{2,0,1:T(8,128)(2,1)S(1)}, bf16[64,1,128]{2,0,1:T(8,128)(2,1)S(1)}, u32[]{:S(2)}, u32[]{:S(2)}) collective-permute-start(bf16[64,1,128]{2,0,1:T(8,128)(2,1)S(1)} %slice_bitcast_fusion), channel_id=1, source_target_pairs={{0,8},{8,16},{16,24},{24,32},{32,40},{40,48},{48,56},{56,64},{64,7... | collective-permute-start | bytes 49160 | tf_op jit(solution)/shard_map/ppermute | solution.py:17
  12.7 0.6 or_convert_fusion.mask_ref
  13.3 0.6 broadcast_subtract_fusion
  13.9 0.8 fusion.68.k_ref
  14.7 0.7 fusion.34.v_ref
  15.4 4.6 %shard_map.100 = (bf16[8,128,576]{2,1,0:T(8,128)(2,1)}, f32[8,128,128]{2,1,0:T(8,128)}, f32[8,128,1]{2,1,0:T(8,128)}) custom-call(bf16[576,128]{1,0:T(8,128)(2,1)} %fusion.68.k_ref, bf16[8,64,128]{2,1,0:T(8,128)(2,1)} %bitcast.150, bf16[576,128]{1,0:T(8,128)(2,1)} %fusion.34.v_ref, f32[1,576]{1,0:T(1,128)} %or_convert_fusion.mask_ref), custom_call_target="tpu_custom_call" | custom-call | tf_op jit(solution)/shard_map/pallas_call | solution.py:104
  19.9 1.2 reduce.4
  21.2 1.8 %pad_maximum_fusion.3 = (f32[66048]{0:T(1024)}, f32[66048]{0:T(1024)S(1)}) fusion(f32[1024]{0:T(1024)S(1)} %bitcast.151, f32[131072]{0:T(1024)} %bitcast.146), kind=kLoop, calls=%fused_computation.44 | loop fusion | flops 66048 | bytes 1323008 | tf_op jit(solution)/shard_map/concatenate | solution.py:166
  22.9 5.0 %collective-permute-start.2 = (f32[66048]{0:T(1024)S(1)}, f32[66048]{0:T(1024)}, u32[]{:S(2)}, u32[]{:S(2)}) collective-permute-start(f32[66048]{0:T(1024)S(1)} %get-tuple-element.13), channel_id=1, source_target_pairs={{0,8},{8,16},{16,24},{24,32},{32,40},{40,48},{48,56},{56,64},{64,7... | collective-permute-start | bytes 792584 | tf_op jit(solution)/shard_map/ppermute | solution.py:17
  28.0 1.1 fusion.22
  29.1 3.1 %collective-permute-start.7 = (f32[66048]{0:T(1024)}, f32[66048]{0:T(1024)}, u32[]{:S(2)}, u32[]{:S(2)}) collective-permute-start(f32[66048]{0:T(1024)} %get-tuple-element.16), channel_id=1, source_target_pairs={{0,64},{8,72},{16,80},{24,88},{32,96},{40,104},{48,112},{56,120},{... | collective-permute-start | bytes 792584 | tf_op jit(solution)/shard_map/ppermute | solution.py:17
  32.3 0.8 collective-permute-done.2
  33.1 0.5 copy.26
  33.6 0.3 fusion.70
  33.9 1.9 %copy.45 = f32[512,8,64]{2,0,1:T(8,128)} copy(f32[512,8,64]{0,2,1:T(8,128)S(1)} %get-tuple-element.22) | data formatting | bytes 2097152
  35.8 2.0 %copy.46 = f32[512,8,64]{2,0,1:T(8,128)} copy(f32[512,8,64]{0,2,1:T(8,128)S(1)} %get-tuple-element.21) | data formatting | bytes 2097152
  37.8 0.8 collective-permute-done.7
  38.6 1.1 add.176
  39.7 1.3 collective-permute-start.8
  41.0 1.7 %add.168 = f32[66048]{0:T(1024)} add(f32[66048]{0:T(1024)S(1)} %copy-done.11, f32[66048]{0:T(1024)} %collective-permute-done.2) | non-fusion elementwise | flops 66048 | bytes 792576 | tf_op jit(solution)/shard_map/add | solution.py:186
  42.7 4.5 %collective-permute-start.3 = (f32[66048]{0:T(1024)}, f32[66048]{0:T(1024)}, u32[]{:S(2)}, u32[]{:S(2)}) collective-permute-start(f32[66048]{0:T(1024)} %add.168), channel_id=1, source_target_pairs={{0,16},{8,24},{16,32},{24,40},{32,48},{40,56},{48,64},{56,72},{64,... | collective-permute-start | bytes 792584 | tf_op jit(solution)/shard_map/ppermute | solution.py:17
  47.2 2.9 %subtract_convert_fusion = (bf16[512,8,64]{2,0,1:T(8,128)(2,1)S(1)}, bf16[512,8,64]{2,0,1:T(8,128)(2,1)S(1)}) fusion(f32[512,8,64]{2,0,1:T(8,128)} %copy.46, f32[512,8,64]{2,0,1:T(8,128)} %copy.45, f32[512,64]{1,0:T(8,128)S(1)} %bitcast.144, f32[512,64]{1,0:T(8,128)S(1)} %bitcast.142), kind=kLoop, calls=%fused_computation.23 | loop fusion | flops 2097152 | bytes 3407872 | tf_op jit(solution)/shard_map/convert.4
  50.1 2.3 %fusion.2 = (f32[8,512]{1,0:T(8,128)S(1)}, f32[576,512,8]{1,0,2:T(8,128)S(1)}) fusion(pred[512,576]{0,1:T(8,128)(4,1)S(1)} %copy-done.1, bf16[512,8,64]{2,0,1:T(8,128)(2,1)S(1)} %get-tuple-element.20, bf16[512,8,64]{2,0,1:T(8,128)(2,1)S(1)} %get-tuple-element.19, bf16[512,1,64]{2,0,1:T(8,128)(2,1)S(1)} %copy-done.7, bf16[512,1,64]{2,0,1:T(8,128)(2,1)S(1)} %copy-done.5, ...), kind=kOutput, calls=%fused_computation.4 | convolution fusion | flops 613593088 | bytes 10944512 | tf_op jit(solution)/shard_map/igkd,jgd->gkij/dot_general | solution.py:206
  52.4 2.5 %fusion.5 = f32[8,512]{1,0:T(8,128)} fusion(f32[576,512,8]{1,0,2:T(8,128)S(1)} %get-tuple-element.44, f32[8,512]{1,0:T(8,128)S(1)} %get-tuple-element.43, pred[512,576]{0,1:T(8,128)(4,1)S(1)} %copy-done.1), kind=kLoop, calls=%fused_computation.9 | loop fusion | flops 9433088 | bytes 9764864 | tf_op jit(solution)/shard_map/reduce_sum | solution.py:212
  55.0 3.5 %fusion.10 = f32[128,8,512]{2,0,1:T(8,128)} fusion(f32[576,512,8]{1,0,2:T(8,128)S(1)} %get-tuple-element.44, f32[8,512]{1,0:T(8,128)S(1)} %get-tuple-element.43, pred[512,576]{0,1:T(8,128)(4,1)S(1)} %copy-done.1, bf16[512,1,128]{2,0,1:T(8,128)(2,1)S(1)} %bitcast.148, bf16[64,1,128]{2,0,1:T(8,128)(2,1)S(1)} %copy-done.21), kind=kOutput, calls=%fused_computation.14 | convolution fusion | flops 613711872 | bytes 11993088 | tf_op jit(solution)/shard_map/gkij,jgd->igkd/dot_general | solution.py:216
  58.5 0.8 add.178
  59.3 5.0 %collective-permute-start.9 = (f32[66048]{0:T(1024)}, f32[66048]{0:T(1024)S(1)}, u32[]{:S(2)}, u32[]{:S(2)}) collective-permute-start(f32[66048]{0:T(1024)} %add.178), channel_id=1, source_target_pairs={{0,8},{8,16},{16,24},{24,32},{32,40},{40,48},{48,56},{56,64},{64,7... | collective-permute-start | bytes 792584 | tf_op jit(solution)/shard_map/ppermute | solution.py:17
  64.3 1.5 fusion.72
  65.8 2.5 %fusion.71 = (f32[512,8]{0,1:T(8,128)}, f32[512,8,64]{0,2,1:T(8,128)}) fusion(bf16[8,128,64]{1,2,0:T(8,128)(2,1)S(1)} %copy-done, bf16[512,8,64]{2,0,1:T(8,128)(2,1)S(1)} %get-tuple-element.20, bf16[512,8,64]{2,0,1:T(8,128)(2,1)S(1)} %get-tuple-element.19), kind=kOutput, calls=%fused_computation.124 | convolution fusion | flops 69992512 | bytes 2244608 | tf_op jit(solution)/shard_map/sub | solution.py:71
  68.2 1.1 add.170
  69.4 5.6 %collective-permute-start.4 = (f32[66048]{0:T(1024)S(1)}, f32[66048]{0:T(1024)S(1)}, u32[]{:S(2)}, u32[]{:S(2)}) collective-permute-start(f32[66048]{0:T(1024)S(1)} %add.170), channel_id=1, source_target_pairs={{0,32},{8,40},{16,48},{24,56},{32,64},{40,72},{48,80},{56,88},{64,... | collective-permute-start | bytes 792584 | tf_op jit(solution)/shard_map/ppermute | solution.py:17
  75.0 1.0 add.180
  76.0 1.9 %collective-permute-start.10 = (f32[66048]{0:T(1024)S(1)}, f32[66048]{0:T(1024)S(1)}, u32[]{:S(2)}, u32[]{:S(2)}) collective-permute-start(f32[66048]{0:T(1024)S(1)} %add.180), channel_id=1, source_target_pairs={{0,16},{8,24},{16,32},{24,40},{32,48},{40,56},{48,64},{56,72},{64,... | collective-permute-start | bytes 792584 | tf_op jit(solution)/shard_map/ppermute | solution.py:17
  77.9 1.1 divide_convert_fusion
  79.1 7.8 %collective-permute-done.4 = f32[66048]{0:T(1024)S(1)} collective-permute-done((f32[66048]{0:T(1024)S(1)}, f32[66048]{0:T(1024)S(1)}, u32[]{:S(2)}, u32[]{:S(2)}) %collective-permute-start.4) | collective-permute-done | bytes 264224 | tf_op jit(solution)/shard_map/ppermute | solution.py:17
  87.0 4.1 %collective-permute-start.5 = (f32[66048]{0:T(1024)S(1)}, f32[66048]{0:T(1024)S(1)}, u32[]{:S(2)}, u32[]{:S(2)}) collective-permute-start(f32[66048]{0:T(1024)S(1)} %add.172), channel_id=1, source_target_pairs={{0,64},{8,72},{16,80},{24,88},{32,96},{40,104},{48,112},{56,120},{... | collective-permute-start | bytes 792584 | tf_op jit(solution)/shard_map/ppermute | solution.py:17
  91.1 6.4 %collective-permute-done.10 = f32[66048]{0:T(1024)S(1)} collective-permute-done((f32[66048]{0:T(1024)S(1)}, f32[66048]{0:T(1024)S(1)}, u32[]{:S(2)}, u32[]{:S(2)}) %collective-permute-start.10) | collective-permute-done | bytes 264224 | tf_op jit(solution)/shard_map/ppermute | solution.py:17
  97.6 3.6 %collective-permute-start.11 = (f32[66048]{0:T(1024)S(1)}, f32[66048]{0:T(1024)S(1)}, u32[]{:S(2)}, u32[]{:S(2)}) collective-permute-start(f32[66048]{0:T(1024)S(1)} %add.182), channel_id=1, source_target_pairs={{0,32},{8,40},{16,48},{24,56},{32,64},{40,72},{48,80},{56,88},{64,... | collective-permute-start | bytes 792584 | tf_op jit(solution)/shard_map/ppermute | solution.py:17
  101.2 3.7 %select_reduce_fusion = (f32[8,512]{1,0:T(8,128)S(1)}, bf16[8,512,576]{1,2,0:T(8,128)(2,1)}) fusion(pred[512,576]{0,1:T(8,128)(4,1)S(1)} %copy-done.14, bf16[8,128,576]{2,1,0:T(8,128)(2,1)S(1)} %copy-done.25, bf16[512,8,64]{0,2,1:T(8,128)(2,1)S(1)} %get-tuple-element.47, bf16[512,8,64]{0,2,1:T(8,128)(2,1)S(1)} %get-tuple-element.48), kind=kOutput, calls=%fused_computation.7 | convolution fusion | flops 613150720 | bytes 7258112 | tf_op jit(solution)/shard_map/igkf,gkfj->gkij/dot_general | solution.py:213
  105.0 1.3 collective-permute-start.6
  106.3 11.2 %collective-permute-done.11 = f32[66048]{0:T(1024)S(1)} collective-permute-done((f32[66048]{0:T(1024)S(1)}, f32[66048]{0:T(1024)S(1)}, u32[]{:S(2)}, u32[]{:S(2)}) %collective-permute-start.11) | collective-permute-done | bytes 264224 | tf_op jit(solution)/shard_map/ppermute | solution.py:17
  117.5 1.1 add_add_fusion
  118.6 3.6 %collective-permute-done.6 = f32[66048]{0:T(1024)S(1)} collective-permute-done((f32[66048]{0:T(1024)S(1)}, f32[66048]{0:T(1024)S(1)}, u32[]{:S(2)}, u32[]{:S(2)}) %collective-permute-start.6) | collective-permute-done | bytes 264224 | tf_op jit(solution)/shard_map/ppermute | solution.py:17
  122.2 1.1 add_add_fusion.1
  123.3 0.2 copy.31
  123.5 0.4 fusion.26
  124.0 0.4 fusion.32
  124.5 0.2 fusion.48
  124.7 0.2 fusion.46
  125.2 0.2 copy-done.15
  125.4 0.8 copy-done.27
  126.2 3.7 %fusion.17 = bf16[512,1,8,128]{0,3,2,1:T(8,128)(2,1)S(1)} fusion(f32[8,128,512]{2,1,0:T(8,128)S(1)} %fusion.32, f32[8,128,512]{2,1,0:T(8,128)S(1)} %fusion.26, f32[128,8,512]{2,0,1:T(8,128)S(1)} %copy-done.27, bf16[8,512,576]{1,2,0:T(8,128)(2,1)} %get-tuple-element.46, pred[512,576]{0,1:T(8,128)(4,1)S(1)} %copy-done.15, f32[512,8]{0,1:T(8,128)S(1)} %fusion.38, ...), kind=kOutput, calls=%fused_computation.24 | convolution fusion | flops 610304000 | bytes 12517440 | tf_op jit(solution)/shard_map/gkij,jgd->igkd/dot_general | solution.py:222
  129.9 0.8 copy.35
  130.7 0.5 all_to_all.14
  131.2 20.3 %all_to_all.19 = bf16[8,64,1024]{2,1,0:T(8,128)(2,1)S(1)} all-to-all(bf16[8,64,1024]{2,1,0:T(8,128)(2,1)S(1)} %all_to_all.14), channel_id=1, replica_groups=mesh['seq'=32,'head'=8] {'head'}, dimensions={0} | all-to-all | bytes 2097152 | tf_op jit(solution)/shard_map/all_to_all | solution.py:249
  151.5 1.1 copy.47
  (72 shorter events, 0.8 us)
Async XLA Ops:
  0.0 64.3 %copy-start = (bf16[8,128,64]{1,2,0:T(8,128)(2,1)S(1)}, bf16[8,128,64]{1,2,0:T(8,128)(2,1)}, u32[]{:S(2)}) copy-start(bf16[8,128,64]{1,2,0:T(8,128)(2,1)} %param.14) | copy-start | bytes 393220
  0.0 8.9 %copy-start.16 = (bf16[512,128]{1,0:T(8,128)(2,1)S(1)}, bf16[512,128]{1,0:T(8,128)(2,1)}, u32[]{:S(2)}) copy-start(bf16[512,128]{1,0:T(8,128)(2,1)} %param.12) | copy-start | bytes 393220
  0.0 13.3 %copy-start.26 = (f32[8]{0:T(128)S(1)}, f32[8]{0:T(128)}, u32[]{:S(2)}) copy-start(f32[8]{0:T(128)} %param.16) | copy-start | bytes 100
  4.1 0.7 copy-start.2
  4.8 27.4 %copy-start.4 = (bf16[512,1,64]{2,0,1:T(8,128)(2,1)}, bf16[512,1,64]{2,0,1:T(8,128)(2,1)S(1)}, u32[]{:S(2)}) copy-start(bf16[512,1,64]{2,0,1:T(8,128)(2,1)S(1)} %get-tuple-element.23) | copy-start | bytes 196612
  4.8 27.4 %copy-start.6 = (bf16[512,1,64]{2,0,1:T(8,128)(2,1)}, bf16[512,1,64]{2,0,1:T(8,128)(2,1)S(1)}, u32[]{:S(2)}) copy-start(bf16[512,1,64]{2,0,1:T(8,128)(2,1)S(1)} %get-tuple-element.24) | copy-start | bytes 196612
  4.8 28.2 %copy-start.13 = (bf16[512,1024]{1,0:T(8,128)(2,1)S(1)}, bf16[512,1024]{1,0:T(8,128)(2,1)}, u32[]{:S(2)}) copy-start(bf16[512,1024]{1,0:T(8,128)(2,1)} %param.10) | copy-start | bytes 3145732
  4.9 9.0 %collective-permute-start.1 = (bf16[64,1,128]{2,0,1:T(8,128)(2,1)S(1)}, bf16[64,1,128]{2,0,1:T(8,128)(2,1)S(1)}, u32[]{:S(2)}, u32[]{:S(2)}) collective-permute-start(bf16[64,1,128]{2,0,1:T(8,128)(2,1)S(1)} %pad_maximum_fusion.15), channel_id=1, source_target_pairs={{0,8},{8,16},{16,24},{24,32},{32,40},{40,48},{48,56},{56,64},{64,7... | collective-permute-start | bytes 49160 | tf_op jit(solution)/shard_map/ppermute | solution.py:17
  8.9 5.8 %collective-permute-start = (bf16[64,1,128]{2,0,1:T(8,128)(2,1)S(1)}, bf16[64,1,128]{2,0,1:T(8,128)(2,1)S(1)}, u32[]{:S(2)}, u32[]{:S(2)}) collective-permute-start(bf16[64,1,128]{2,0,1:T(8,128)(2,1)S(1)} %slice_bitcast_fusion), channel_id=1, source_target_pairs={{0,8},{8,16},{16,24},{24,32},{32,40},{40,48},{48,56},{56,64},{64,7... | collective-permute-start | bytes 49160 | tf_op jit(solution)/shard_map/ppermute | solution.py:17
  14.7 6.5 %copy-start.20 = (bf16[64,1,128]{2,0,1:T(8,128)(2,1)}, bf16[64,1,128]{2,0,1:T(8,128)(2,1)S(1)}, u32[]{:S(2)}) copy-start(bf16[64,1,128]{2,0,1:T(8,128)(2,1)S(1)} %collective-permute-done) | copy-start | bytes 49156
  22.9 9.3 %copy-start.10 = (f32[66048]{0:T(1024)}, f32[66048]{0:T(1024)S(1)}, u32[]{:S(2)}) copy-start(f32[66048]{0:T(1024)S(1)} %get-tuple-element.13) | copy-start | bytes 792580
  22.9 10.1 %collective-permute-start.2 = (f32[66048]{0:T(1024)S(1)}, f32[66048]{0:T(1024)}, u32[]{:S(2)}, u32[]{:S(2)}) collective-permute-start(f32[66048]{0:T(1024)S(1)} %get-tuple-element.13), channel_id=1, source_target_pairs={{0,8},{8,16},{16,24},{24,32},{32,40},{40,48},{48,56},{56,64},{64,7... | collective-permute-start | bytes 792584 | tf_op jit(solution)/shard_map/ppermute | solution.py:17
  29.1 9.5 %collective-permute-start.7 = (f32[66048]{0:T(1024)}, f32[66048]{0:T(1024)}, u32[]{:S(2)}, u32[]{:S(2)}) collective-permute-start(f32[66048]{0:T(1024)} %get-tuple-element.16), channel_id=1, source_target_pairs={{0,64},{8,72},{16,80},{24,88},{32,96},{40,104},{48,112},{56,120},{... | collective-permute-start | bytes 792584 | tf_op jit(solution)/shard_map/ppermute | solution.py:17
  35.8 5.2 %copy-start.11 = (f32[66048]{0:T(1024)S(1)}, f32[66048]{0:T(1024)}, u32[]{:S(2)}) copy-start(f32[66048]{0:T(1024)} %copy-done.10) | copy-start | bytes 792580
  35.8 11.3 %copy-start.3 = (f32[2,4,64,64]{3,2,1,0:T(8,128)S(1)}, f32[2,4,64,64]{3,2,1,0:T(8,128)}, u32[]{:S(2)}) copy-start(f32[2,4,64,64]{3,2,1,0:T(8,128)} %copy-done.2) | copy-start | bytes 393220
  39.7 18.8 %collective-permute-start.8 = (f32[66048]{0:T(1024)S(1)}, f32[66048]{0:T(1024)S(1)}, u32[]{:S(2)}, u32[]{:S(2)}) collective-permute-start(f32[66048]{0:T(1024)S(1)} %add.176), channel_id=1, source_target_pairs={{0,128},{8,136},{16,144},{24,152},{32,160},{40,168},{48,176},{56,1... | collective-permute-start | bytes 792584 | tf_op jit(solution)/shard_map/ppermute | solution.py:17
  42.7 25.6 %collective-permute-start.3 = (f32[66048]{0:T(1024)}, f32[66048]{0:T(1024)}, u32[]{:S(2)}, u32[]{:S(2)}) collective-permute-start(f32[66048]{0:T(1024)} %add.168), channel_id=1, source_target_pairs={{0,16},{8,24},{16,32},{24,40},{32,48},{40,56},{48,64},{56,72},{64,... | collective-permute-start | bytes 792584 | tf_op jit(solution)/shard_map/ppermute | solution.py:17
  47.1 2.9 %copy-start.1 = (pred[512,576]{0,1:T(8,128)(4,1)S(1)}, pred[512,576]{0,1:T(8,128)(4,1)}, u32[]{:S(2)}) copy-start(pred[512,576]{0,1:T(8,128)(4,1)} %get-tuple-element.32) | copy-start | bytes 884740
  47.2 2.9 %copy-start.5 = (bf16[512,1,64]{2,0,1:T(8,128)(2,1)S(1)}, bf16[512,1,64]{2,0,1:T(8,128)(2,1)}, u32[]{:S(2)}) copy-start(bf16[512,1,64]{2,0,1:T(8,128)(2,1)} %copy-done.4) | copy-start | bytes 196612
  47.2 2.9 %copy-start.7 = (bf16[512,1,64]{2,0,1:T(8,128)(2,1)S(1)}, bf16[512,1,64]{2,0,1:T(8,128)(2,1)}, u32[]{:S(2)}) copy-start(bf16[512,1,64]{2,0,1:T(8,128)(2,1)} %copy-done.6) | copy-start | bytes 196612
  52.4 2.6 %copy-start.17 = (bf16[512,128]{1,0:T(8,128)(2,1)S(1)}, bf16[512,128]{1,0:T(8,128)(2,1)}, u32[]{:S(2)}) copy-start(bf16[512,128]{1,0:T(8,128)(2,1)} %param.12) | copy-start | bytes 393220
  52.4 2.6 %copy-start.21 = (bf16[64,1,128]{2,0,1:T(8,128)(2,1)S(1)}, bf16[64,1,128]{2,0,1:T(8,128)(2,1)}, u32[]{:S(2)}) copy-start(bf16[64,1,128]{2,0,1:T(8,128)(2,1)} %copy-done.20) | copy-start | bytes 49156
  58.5 0.8 copy-start.8
  59.3 15.7 %collective-permute-start.9 = (f32[66048]{0:T(1024)}, f32[66048]{0:T(1024)S(1)}, u32[]{:S(2)}, u32[]{:S(2)}) collective-permute-start(f32[66048]{0:T(1024)} %add.178), channel_id=1, source_target_pairs={{0,8},{8,16},{16,24},{24,32},{32,40},{40,48},{48,56},{56,64},{64,7... | collective-permute-start | bytes 792584 | tf_op jit(solution)/shard_map/ppermute | solution.py:17
  68.2 9.7 %copy-start.12 = (f32[512,8,64]{0,2,1:T(8,128)S(1)}, f32[512,8,64]{0,2,1:T(8,128)}, u32[]{:S(2)}) copy-start(f32[512,8,64]{0,2,1:T(8,128)} %get-tuple-element.40) | copy-start | bytes 3145732
  69.4 17.5 %collective-permute-start.4 = (f32[66048]{0:T(1024)S(1)}, f32[66048]{0:T(1024)S(1)}, u32[]{:S(2)}, u32[]{:S(2)}) collective-permute-start(f32[66048]{0:T(1024)S(1)} %add.170), channel_id=1, source_target_pairs={{0,32},{8,40},{16,48},{24,56},{32,64},{40,72},{48,80},{56,88},{64,... | collective-permute-start | bytes 792584 | tf_op jit(solution)/shard_map/ppermute | solution.py:17
  76.0 21.5 %collective-permute-start.10 = (f32[66048]{0:T(1024)S(1)}, f32[66048]{0:T(1024)S(1)}, u32[]{:S(2)}, u32[]{:S(2)}) collective-permute-start(f32[66048]{0:T(1024)S(1)} %add.180), channel_id=1, source_target_pairs={{0,16},{8,24},{16,32},{24,40},{32,48},{40,56},{48,64},{56,72},{64,... | collective-permute-start | bytes 792584 | tf_op jit(solution)/shard_map/ppermute | solution.py:17
  77.9 23.3 %copy-start.14 = (pred[512,576]{0,1:T(8,128)(4,1)S(1)}, pred[512,576]{0,1:T(8,128)(4,1)}, u32[]{:S(2)}) copy-start(pred[512,576]{0,1:T(8,128)(4,1)} %get-tuple-element.31) | copy-start | bytes 884740
  77.9 23.3 %copy-start.25 = (bf16[8,128,576]{2,1,0:T(8,128)(2,1)S(1)}, bf16[8,128,576]{2,1,0:T(8,128)(2,1)}, u32[]{:S(2)}) copy-start(bf16[8,128,576]{2,1,0:T(8,128)(2,1)} %get-tuple-element.15) | copy-start | bytes 3538948
  87.0 18.0 %collective-permute-start.5 = (f32[66048]{0:T(1024)S(1)}, f32[66048]{0:T(1024)S(1)}, u32[]{:S(2)}, u32[]{:S(2)}) collective-permute-start(f32[66048]{0:T(1024)S(1)} %add.172), channel_id=1, source_target_pairs={{0,64},{8,72},{16,80},{24,88},{32,96},{40,104},{48,112},{56,120},{... | collective-permute-start | bytes 792584 | tf_op jit(solution)/shard_map/ppermute | solution.py:17
  97.6 19.9 %collective-permute-start.11 = (f32[66048]{0:T(1024)S(1)}, f32[66048]{0:T(1024)S(1)}, u32[]{:S(2)}, u32[]{:S(2)}) collective-permute-start(f32[66048]{0:T(1024)S(1)} %add.182), channel_id=1, source_target_pairs={{0,32},{8,40},{16,48},{24,56},{32,64},{40,72},{48,80},{56,88},{64,... | collective-permute-start | bytes 792584 | tf_op jit(solution)/shard_map/ppermute | solution.py:17
  101.2 16.3 %copy-start.9 = (f32[66048]{0:T(1024)S(1)}, f32[66048]{0:T(1024)}, u32[]{:S(2)}) copy-start(f32[66048]{0:T(1024)} %copy-done.8) | copy-start | bytes 792580
  105.0 17.2 %collective-permute-start.6 = (f32[66048]{0:T(1024)S(1)}, f32[66048]{0:T(1024)S(1)}, u32[]{:S(2)}, u32[]{:S(2)}) collective-permute-start(f32[66048]{0:T(1024)S(1)} %add.174), channel_id=1, source_target_pairs={{0,128},{8,136},{16,144},{24,152},{32,160},{40,168},{48,176},{56,1... | collective-permute-start | bytes 792584 | tf_op jit(solution)/shard_map/ppermute | solution.py:17
  124.4 0.7 copy-start.19
  124.4 0.7 copy-start.23
  124.4 0.7 copy-start.24
  124.4 1.0 copy-start.15
  124.4 1.0 copy-start.18
  124.4 1.0 copy-start.22
  124.4 1.8 %copy-start.27 = (f32[128,8,512]{2,0,1:T(8,128)S(1)}, f32[128,8,512]{2,0,1:T(8,128)}, u32[]{:S(2)}) copy-start(f32[128,8,512]{2,0,1:T(8,128)} %fusion.10) | copy-start | bytes 6291460

commit v13 on v12

--- a/solution.py
+++ b/solution.py
@@ -246,18 +246,32 @@
     )
     outputs = (numerator / denominator[..., None]).astype(jnp.bfloat16)
     result = outputs.reshape(tokens, heads * head_dim)
-    return lax.all_to_all(result, "head", split_axis=0, concat_axis=1, tiled=True)
+    outer = lax.axis_size("hy")
+    pair = lax.axis_size("hc")
+    staged = result.reshape(outer, pair, tokens // (outer * pair), heads * head_dim)
+    staged = lax.all_to_all(staged, "hc", split_axis=1, concat_axis=1, tiled=True)
+    staged = lax.all_to_all(staged, "hy", split_axis=0, concat_axis=0, tiled=True)
+    staged = jnp.transpose(staged, (2, 0, 1, 3))
+    return staged.reshape(staged.shape[0], -1)
 
 
 def solution(mesh):
+    head_count = mesh.shape["head"]
+    pair = math.gcd(head_count, 2)
+    split_mesh = jax.sharding.Mesh(
+        mesh.devices.reshape(mesh.shape["seq"], head_count // pair, pair), ("seq", "hy", "hc")
+    )
+    cols = ("hy", "hc")
     in_specs = (
-        P("seq", "head"),
-        P("seq", "head"),
-        P("seq", "head"),
+        P("seq", cols),
+        P("seq", cols),
+        P("seq", cols),
         P("seq"),
-        P("head", None, None),
-        P("head", None, None),
-        P("head"),
-    )
-    out_specs = P(("seq", "head"), None)
-    return jax.shard_map(body, mesh=mesh, in_specs=in_specs, out_specs=out_specs, check_vma=False)
+        P(cols, None, None),
+        P(cols, None, None),
+        P(cols),
+    )
+    out_specs = P(("seq", "hy", "hc"), None)
+    return jax.shard_map(
+        body, mesh=split_mesh, in_specs=in_specs, out_specs=out_specs, check_vma=False
+    )

time: 153 us -> 162 us (1.059)
  local copies, waits for them, and re-layouts: 9.04 us -> 13.4 us
  blocking collectives: 20.3 us -> 24.3 us
    all_to_all x1 -> x2, blocking collectives: 20.3 us -> 24.3 us  [the longest x1 19.7 us: body(): lax.all_to_all(staged, 'hy', split_axis=0, concat_axis=0, tiled=True)]
    another operation x0 -> x2, local copies, waits for them, and re-layouts: none -> 3.86 us  [body(): result.reshape(outer, pair, tokens // (outer * pair), heads * head_dim)]
  transfers between devices with their start and end apart: 12 -> 12, of which waited for: 6 -> 6; matrix products, arithmetic and copies ran while one was open for 22% -> 21% of each run, Pallas kernels for 0% -> 0%
where the time goes in v13:
time: 162 us; the launch traced here: 161 us
  starting transfers between devices  43.2 us (27%)
  waiting for transfers between devices  30.7 us (19%)
  other arithmetic  25.7 us (16%)
  blocking collectives  24.3 us (15%)
  matrix products  18.5 us (11%)
  local copies, waits for them, and re-layouts  13.4 us (8%)
  Pallas kernels  4.56 us (3%)
    ppermute x12, starting transfers between devices, passed_along(): lax.ppermute(value, axis, [(source, source + steps) for source in range(f...  43.2 us
    ppermute x12, waiting for transfers between devices, passed_along(): lax.ppermute(value, axis, [(source, source + steps) for source in range(f...  30.7 us
    all_to_all x1, blocking collectives, body(): lax.all_to_all(staged, 'hy', split_axis=0, concat_axis=0, tiled=True)  19.7 us
    add x8, other arithmetic, body(): inclusive = inclusive + received  5.74 us
    unnamed x58, local copies, waits for them, and re-layouts  5.72 us
    another operation x5, other arithmetic  5.6 us
    all_to_all x1, blocking collectives, body(): lax.all_to_all(staged, 'hc', split_axis=1, concat_axis=1, tiled=True)  4.58 us
    pallas_call x1, Pallas kernels, key_features(): pl.pallas_call(kernel, grid=(1,), in_specs=[pl.BlockSpec((rows, dim), lam...  4.56 us
  transfers between devices with their start and end apart: 12, of which 6 were waited for; matrix products, arithmetic and copies ran while one was open for 21% of the time, Pallas kernels for 0%

profile of v13, /device:TPU:36, one launch (start us, length us, event | category | flops | bytes accessed | tf_op | source)
XLA Modules:
  0.0 160.9 jit_solution(1666907665869086842)
XLA Ops:
  0.0 0.7 and_select_fusion.1
  0.8 0.8 fusion.36
  1.6 0.9 bitcast_convert_fusion
  2.5 0.8 multiply_cosine_fusion.1
  3.3 0.8 fusion.44
  4.3 0.5 copy-done.2
  4.9 3.9 %collective-permute-start.1 = (bf16[64,1,128]{2,0,1:T(8,128)(2,1)S(1)}, bf16[64,1,128]{2,0,1:T(8,128)(2,1)S(1)}, u32[]{:S(2)}, u32[]{:S(2)}) collective-permute-start(bf16[64,1,128]{2,0,1:T(8,128)(2,1)S(1)} %pad_maximum_fusion.15), channel_id=1, source_target_pairs={{0,8},{8,16},{16,24},{24,32},{32,40},{40,48},{48,56},{56,64},{64,7... | collective-permute-start | bytes 49160 | tf_op jit(solution)/shard_map/ppermute | solution.py:17
  8.9 3.8 %collective-permute-start = (bf16[64,1,128]{2,0,1:T(8,128)(2,1)S(1)}, bf16[64,1,128]{2,0,1:T(8,128)(2,1)S(1)}, u32[]{:S(2)}, u32[]{:S(2)}) collective-permute-start(bf16[64,1,128]{2,0,1:T(8,128)(2,1)S(1)} %slice_bitcast_fusion), channel_id=1, source_target_pairs={{0,8},{8,16},{16,24},{24,32},{32,40},{40,48},{48,56},{56,64},{64,7... | collective-permute-start | bytes 49160 | tf_op jit(solution)/shard_map/ppermute | solution.py:17
  12.7 0.6 or_convert_fusion.mask_ref
  13.3 0.6 broadcast_subtract_fusion
  13.9 0.8 fusion.68.k_ref
  14.7 0.7 fusion.34.v_ref
  15.4 4.6 %shard_map.100 = (bf16[8,128,576]{2,1,0:T(8,128)(2,1)}, f32[8,128,128]{2,1,0:T(8,128)}, f32[8,128,1]{2,1,0:T(8,128)}) custom-call(bf16[576,128]{1,0:T(8,128)(2,1)} %fusion.68.k_ref, bf16[8,64,128]{2,1,0:T(8,128)(2,1)} %bitcast.148, bf16[576,128]{1,0:T(8,128)(2,1)} %fusion.34.v_ref, f32[1,576]{1,0:T(1,128)} %or_convert_fusion.mask_ref), custom_call_target="tpu_custom_call" | custom-call | tf_op jit(solution)/shard_map/pallas_call | solution.py:104
  19.9 1.2 reduce.4
  21.2 1.8 %pad_maximum_fusion.3 = (f32[66048]{0:T(1024)}, f32[66048]{0:T(1024)S(1)}) fusion(f32[1024]{0:T(1024)S(1)} %bitcast.149, f32[131072]{0:T(1024)} %bitcast.144), kind=kLoop, calls=%fused_computation.44 | loop fusion | flops 66048 | bytes 1323008 | tf_op jit(solution)/shard_map/concatenate | solution.py:166
  22.9 5.0 %collective-permute-start.2 = (f32[66048]{0:T(1024)S(1)}, f32[66048]{0:T(1024)}, u32[]{:S(2)}, u32[]{:S(2)}) collective-permute-start(f32[66048]{0:T(1024)S(1)} %get-tuple-element.13), channel_id=1, source_target_pairs={{0,8},{8,16},{16,24},{24,32},{32,40},{40,48},{48,56},{56,64},{64,7... | collective-permute-start | bytes 792584 | tf_op jit(solution)/shard_map/ppermute | solution.py:17
  28.0 1.1 fusion.22
  29.1 3.1 %collective-permute-start.7 = (f32[66048]{0:T(1024)}, f32[66048]{0:T(1024)}, u32[]{:S(2)}, u32[]{:S(2)}) collective-permute-start(f32[66048]{0:T(1024)} %get-tuple-element.16), channel_id=1, source_target_pairs={{0,64},{8,72},{16,80},{24,88},{32,96},{40,104},{48,112},{56,120},{... | collective-permute-start | bytes 792584 | tf_op jit(solution)/shard_map/ppermute | solution.py:17
  32.3 0.8 collective-permute-done.2
  33.1 0.5 copy.49
  33.6 0.3 fusion.70
  33.9 1.9 %copy.72 = f32[512,8,64]{2,0,1:T(8,128)} copy(f32[512,8,64]{0,2,1:T(8,128)S(1)} %get-tuple-element.22) | data formatting | bytes 2097152
  35.8 2.0 %copy.73 = f32[512,8,64]{2,0,1:T(8,128)} copy(f32[512,8,64]{0,2,1:T(8,128)S(1)} %get-tuple-element.21) | data formatting | bytes 2097152
  37.8 0.8 collective-permute-done.7
  38.6 1.1 add.176
  39.7 1.3 collective-permute-start.8
  41.0 1.7 %add.168 = f32[66048]{0:T(1024)} add(f32[66048]{0:T(1024)S(1)} %copy-done.11, f32[66048]{0:T(1024)} %collective-permute-done.2) | non-fusion elementwise | flops 66048 | bytes 792576 | tf_op jit(solution)/shard_map/add | solution.py:186
  42.7 4.5 %collective-permute-start.3 = (f32[66048]{0:T(1024)}, f32[66048]{0:T(1024)}, u32[]{:S(2)}, u32[]{:S(2)}) collective-permute-start(f32[66048]{0:T(1024)} %add.168), channel_id=1, source_target_pairs={{0,16},{8,24},{16,32},{24,40},{32,48},{40,56},{48,64},{56,72},{64,... | collective-permute-start | bytes 792584 | tf_op jit(solution)/shard_map/ppermute | solution.py:17
  47.2 2.9 %subtract_convert_fusion = (bf16[512,8,64]{2,0,1:T(8,128)(2,1)S(1)}, bf16[512,8,64]{2,0,1:T(8,128)(2,1)S(1)}) fusion(f32[512,8,64]{2,0,1:T(8,128)} %copy.73, f32[512,8,64]{2,0,1:T(8,128)} %copy.72, f32[512,64]{1,0:T(8,128)S(1)} %bitcast.142, f32[512,64]{1,0:T(8,128)S(1)} %bitcast.140), kind=kLoop, calls=%fused_computation.23 | loop fusion | flops 2097152 | bytes 3407872 | tf_op jit(solution)/shard_map/convert.4
  50.1 2.3 %fusion.2 = (f32[8,512]{1,0:T(8,128)S(1)}, f32[576,512,8]{1,0,2:T(8,128)S(1)}) fusion(pred[512,576]{0,1:T(8,128)(4,1)S(1)} %copy-done.1, bf16[512,8,64]{2,0,1:T(8,128)(2,1)S(1)} %get-tuple-element.20, bf16[512,8,64]{2,0,1:T(8,128)(2,1)S(1)} %get-tuple-element.19, bf16[512,1,64]{2,0,1:T(8,128)(2,1)S(1)} %copy-done.7, bf16[512,1,64]{2,0,1:T(8,128)(2,1)S(1)} %copy-done.5, ...), kind=kOutput, calls=%fused_computation.4 | convolution fusion | flops 613593088 | bytes 10944512 | tf_op jit(solution)/shard_map/igkd,jgd->gkij/dot_general | solution.py:206
  52.4 2.5 %fusion.5 = f32[8,512]{1,0:T(8,128)} fusion(f32[576,512,8]{1,0,2:T(8,128)S(1)} %get-tuple-element.44, f32[8,512]{1,0:T(8,128)S(1)} %get-tuple-element.43, pred[512,576]{0,1:T(8,128)(4,1)S(1)} %copy-done.1), kind=kLoop, calls=%fused_computation.9 | loop fusion | flops 9433088 | bytes 9764864 | tf_op jit(solution)/shard_map/reduce_sum | solution.py:212
  55.0 3.5 %fusion.10 = f32[128,8,512]{2,0,1:T(8,128)} fusion(f32[576,512,8]{1,0,2:T(8,128)S(1)} %get-tuple-element.44, f32[8,512]{1,0:T(8,128)S(1)} %get-tuple-element.43, pred[512,576]{0,1:T(8,128)(4,1)S(1)} %copy-done.1, bf16[512,1,128]{2,0,1:T(8,128)(2,1)S(1)} %bitcast.146, bf16[64,1,128]{2,0,1:T(8,128)(2,1)S(1)} %copy-done.21), kind=kOutput, calls=%fused_computation.14 | convolution fusion | flops 613711872 | bytes 11993088 | tf_op jit(solution)/shard_map/gkij,jgd->igkd/dot_general | solution.py:216
  58.5 0.8 add.178
  59.3 5.0 %collective-permute-start.9 = (f32[66048]{0:T(1024)}, f32[66048]{0:T(1024)S(1)}, u32[]{:S(2)}, u32[]{:S(2)}) collective-permute-start(f32[66048]{0:T(1024)} %add.178), channel_id=1, source_target_pairs={{0,8},{8,16},{16,24},{24,32},{32,40},{40,48},{48,56},{56,64},{64,7... | collective-permute-start | bytes 792584 | tf_op jit(solution)/shard_map/ppermute | solution.py:17
  64.3 1.5 fusion.72
  65.8 2.5 %fusion.71 = (f32[512,8]{0,1:T(8,128)}, f32[512,8,64]{0,2,1:T(8,128)}) fusion(bf16[8,128,64]{1,2,0:T(8,128)(2,1)S(1)} %copy-done, bf16[512,8,64]{2,0,1:T(8,128)(2,1)S(1)} %get-tuple-element.20, bf16[512,8,64]{2,0,1:T(8,128)(2,1)S(1)} %get-tuple-element.19), kind=kOutput, calls=%fused_computation.124 | convolution fusion | flops 69992512 | bytes 2244608 | tf_op jit(solution)/shard_map/sub | solution.py:71
  68.2 1.1 add.170
  69.4 5.6 %collective-permute-start.4 = (f32[66048]{0:T(1024)S(1)}, f32[66048]{0:T(1024)S(1)}, u32[]{:S(2)}, u32[]{:S(2)}) collective-permute-start(f32[66048]{0:T(1024)S(1)} %add.170), channel_id=1, source_target_pairs={{0,32},{8,40},{16,48},{24,56},{32,64},{40,72},{48,80},{56,88},{64,... | collective-permute-start | bytes 792584 | tf_op jit(solution)/shard_map/ppermute | solution.py:17
  75.0 1.0 add.180
  76.0 1.9 %collective-permute-start.10 = (f32[66048]{0:T(1024)S(1)}, f32[66048]{0:T(1024)S(1)}, u32[]{:S(2)}, u32[]{:S(2)}) collective-permute-start(f32[66048]{0:T(1024)S(1)} %add.180), channel_id=1, source_target_pairs={{0,16},{8,24},{16,32},{24,40},{32,48},{40,56},{48,64},{56,72},{64,... | collective-permute-start | bytes 792584 | tf_op jit(solution)/shard_map/ppermute | solution.py:17
  77.9 1.1 divide_convert_fusion
  79.1 7.8 %collective-permute-done.4 = f32[66048]{0:T(1024)S(1)} collective-permute-done((f32[66048]{0:T(1024)S(1)}, f32[66048]{0:T(1024)S(1)}, u32[]{:S(2)}, u32[]{:S(2)}) %collective-permute-start.4) | collective-permute-done | bytes 264224 | tf_op jit(solution)/shard_map/ppermute | solution.py:17
  87.0 4.1 %collective-permute-start.5 = (f32[66048]{0:T(1024)S(1)}, f32[66048]{0:T(1024)S(1)}, u32[]{:S(2)}, u32[]{:S(2)}) collective-permute-start(f32[66048]{0:T(1024)S(1)} %add.172), channel_id=1, source_target_pairs={{0,64},{8,72},{16,80},{24,88},{32,96},{40,104},{48,112},{56,120},{... | collective-permute-start | bytes 792584 | tf_op jit(solution)/shard_map/ppermute | solution.py:17
  91.1 6.4 %collective-permute-done.10 = f32[66048]{0:T(1024)S(1)} collective-permute-done((f32[66048]{0:T(1024)S(1)}, f32[66048]{0:T(1024)S(1)}, u32[]{:S(2)}, u32[]{:S(2)}) %collective-permute-start.10) | collective-permute-done | bytes 264224 | tf_op jit(solution)/shard_map/ppermute | solution.py:17
  97.6 3.6 %collective-permute-start.11 = (f32[66048]{0:T(1024)S(1)}, f32[66048]{0:T(1024)S(1)}, u32[]{:S(2)}, u32[]{:S(2)}) collective-permute-start(f32[66048]{0:T(1024)S(1)} %add.182), channel_id=1, source_target_pairs={{0,32},{8,40},{16,48},{24,56},{32,64},{40,72},{48,80},{56,88},{64,... | collective-permute-start | bytes 792584 | tf_op jit(solution)/shard_map/ppermute | solution.py:17
  101.2 3.7 %select_reduce_fusion = (f32[8,512]{1,0:T(8,128)S(1)}, bf16[8,512,576]{1,2,0:T(8,128)(2,1)}) fusion(pred[512,576]{0,1:T(8,128)(4,1)S(1)} %copy-done.14, bf16[8,128,576]{2,1,0:T(8,128)(2,1)S(1)} %copy-done.25, bf16[512,8,64]{0,2,1:T(8,128)(2,1)S(1)} %get-tuple-element.47, bf16[512,8,64]{0,2,1:T(8,128)(2,1)S(1)} %get-tuple-element.48), kind=kOutput, calls=%fused_computation.7 | convolution fusion | flops 613150720 | bytes 7258112 | tf_op jit(solution)/shard_map/igkf,gkfj->gkij/dot_general | solution.py:213
  105.0 1.3 collective-permute-start.6
  106.3 11.2 %collective-permute-done.11 = f32[66048]{0:T(1024)S(1)} collective-permute-done((f32[66048]{0:T(1024)S(1)}, f32[66048]{0:T(1024)S(1)}, u32[]{:S(2)}, u32[]{:S(2)}) %collective-permute-start.11) | collective-permute-done | bytes 264224 | tf_op jit(solution)/shard_map/ppermute | solution.py:17
  117.5 1.1 add_add_fusion
  118.6 3.6 %collective-permute-done.6 = f32[66048]{0:T(1024)S(1)} collective-permute-done((f32[66048]{0:T(1024)S(1)}, f32[66048]{0:T(1024)S(1)}, u32[]{:S(2)}, u32[]{:S(2)}) %collective-permute-start.6) | collective-permute-done | bytes 264224 | tf_op jit(solution)/shard_map/ppermute | solution.py:17
  122.2 1.1 add_add_fusion.1
  123.3 0.2 copy.54
  123.5 0.4 fusion.26
  124.0 0.4 fusion.32
  124.5 0.2 fusion.48
  124.7 0.2 fusion.46
  125.4 0.8 copy-done.27
  126.2 3.7 %fusion.17 = bf16[512,1,8,128]{0,3,2,1:T(8,128)(2,1)S(1)} fusion(f32[8,128,512]{2,1,0:T(8,128)S(1)} %fusion.32, f32[8,128,512]{2,1,0:T(8,128)S(1)} %fusion.26, f32[128,8,512]{2,0,1:T(8,128)S(1)} %copy-done.27, bf16[8,512,576]{1,2,0:T(8,128)(2,1)} %get-tuple-element.46, pred[512,576]{0,1:T(8,128)(4,1)S(1)} %copy-done.15, f32[512,8]{0,1:T(8,128)S(1)} %fusion.38, ...), kind=kOutput, calls=%fused_computation.24 | convolution fusion | flops 610304000 | bytes 12517440 | tf_op jit(solution)/shard_map/gkij,jgd->igkd/dot_general | solution.py:222
  129.9 1.1 reshape.479
  131.0 2.8 %copy.59 = bf16[4,2,64,1024]{3,2,0,1:T(8,128)(2,1)S(1)} copy(bf16[4,2,64,1024]{2,1,0,3:T(2,128)(2,1)S(1)} %reshape.479) | data formatting | bytes 2097152 | tf_op jit(solution)/shard_map/reshape;reshape | solution.py:251
  133.8 4.6 %all_to_all.10 = bf16[4,2,64,1024]{3,2,0,1:T(8,128)(2,1)S(1)} all-to-all(bf16[4,2,64,1024]{3,2,0,1:T(8,128)(2,1)S(1)} %copy.59), channel_id=1, replica_groups=mesh['seq'=32,'hy'=4,'hc'=2] {'hc'}, dimensions={1} | all-to-all | bytes 2097152 | tf_op jit(solution)/shard_map/all_to_all | solution.py:252
  138.4 19.7 %all_to_all.11 = bf16[4,2,64,1024]{3,2,1,0:T(8,128)(2,1)S(1)} all-to-all(bf16[4,2,64,1024]{3,2,1,0:T(8,128)(2,1)S(1)} %copy.60), channel_id=1, replica_groups=mesh['seq'=32,'hy'=4,'hc'=2] {'hy'}, dimensions={0} | all-to-all | bytes 2097152 | tf_op jit(solution)/shard_map/all_to_all | solution.py:253
  158.2 1.1 copy.61
  159.3 1.6 reshape.470
  (75 shorter events, 1.2 us)
Async XLA Ops:
  0.0 64.3 %copy-start = (bf16[8,128,64]{1,2,0:T(8,128)(2,1)S(1)}, bf16[8,128,64]{1,2,0:T(8,128)(2,1)}, u32[]{:S(2)}) copy-start(bf16[8,128,64]{1,2,0:T(8,128)(2,1)} %param.14) | copy-start | bytes 393220
  0.0 8.9 %copy-start.16 = (bf16[512,128]{1,0:T(8,128)(2,1)S(1)}, bf16[512,128]{1,0:T(8,128)(2,1)}, u32[]{:S(2)}) copy-start(bf16[512,128]{1,0:T(8,128)(2,1)} %param.12) | copy-start | bytes 393220
  0.0 13.3 %copy-start.26 = (f32[8]{0:T(128)S(1)}, f32[8]{0:T(128)}, u32[]{:S(2)}) copy-start(f32[8]{0:T(128)} %param.16) | copy-start | bytes 100
  4.1 0.7 copy-start.2
  4.8 27.4 %copy-start.4 = (bf16[512,1,64]{2,0,1:T(8,128)(2,1)}, bf16[512,1,64]{2,0,1:T(8,128)(2,1)S(1)}, u32[]{:S(2)}) copy-start(bf16[512,1,64]{2,0,1:T(8,128)(2,1)S(1)} %get-tuple-element.23) | copy-start | bytes 196612
  4.8 27.4 %copy-start.6 = (bf16[512,1,64]{2,0,1:T(8,128)(2,1)}, bf16[512,1,64]{2,0,1:T(8,128)(2,1)S(1)}, u32[]{:S(2)}) copy-start(bf16[512,1,64]{2,0,1:T(8,128)(2,1)S(1)} %get-tuple-element.24) | copy-start | bytes 196612
  4.8 28.2 %copy-start.13 = (bf16[512,1024]{1,0:T(8,128)(2,1)S(1)}, bf16[512,1024]{1,0:T(8,128)(2,1)}, u32[]{:S(2)}) copy-start(bf16[512,1024]{1,0:T(8,128)(2,1)} %param.10) | copy-start | bytes 3145732
  4.9 9.0 %collective-permute-start.1 = (bf16[64,1,128]{2,0,1:T(8,128)(2,1)S(1)}, bf16[64,1,128]{2,0,1:T(8,128)(2,1)S(1)}, u32[]{:S(2)}, u32[]{:S(2)}) collective-permute-start(bf16[64,1,128]{2,0,1:T(8,128)(2,1)S(1)} %pad_maximum_fusion.15), channel_id=1, source_target_pairs={{0,8},{8,16},{16,24},{24,32},{32,40},{40,48},{48,56},{56,64},{64,7... | collective-permute-start | bytes 49160 | tf_op jit(solution)/shard_map/ppermute | solution.py:17
  8.9 5.8 %collective-permute-start = (bf16[64,1,128]{2,0,1:T(8,128)(2,1)S(1)}, bf16[64,1,128]{2,0,1:T(8,128)(2,1)S(1)}, u32[]{:S(2)}, u32[]{:S(2)}) collective-permute-start(bf16[64,1,128]{2,0,1:T(8,128)(2,1)S(1)} %slice_bitcast_fusion), channel_id=1, source_target_pairs={{0,8},{8,16},{16,24},{24,32},{32,40},{40,48},{48,56},{56,64},{64,7... | collective-permute-start | bytes 49160 | tf_op jit(solution)/shard_map/ppermute | solution.py:17
  14.7 6.5 %copy-start.20 = (bf16[64,1,128]{2,0,1:T(8,128)(2,1)}, bf16[64,1,128]{2,0,1:T(8,128)(2,1)S(1)}, u32[]{:S(2)}) copy-start(bf16[64,1,128]{2,0,1:T(8,128)(2,1)S(1)} %collective-permute-done) | copy-start | bytes 49156
  22.9 9.3 %copy-start.10 = (f32[66048]{0:T(1024)}, f32[66048]{0:T(1024)S(1)}, u32[]{:S(2)}) copy-start(f32[66048]{0:T(1024)S(1)} %get-tuple-element.13) | copy-start | bytes 792580
  22.9 10.1 %collective-permute-start.2 = (f32[66048]{0:T(1024)S(1)}, f32[66048]{0:T(1024)}, u32[]{:S(2)}, u32[]{:S(2)}) collective-permute-start(f32[66048]{0:T(1024)S(1)} %get-tuple-element.13), channel_id=1, source_target_pairs={{0,8},{8,16},{16,24},{24,32},{32,40},{40,48},{48,56},{56,64},{64,7... | collective-permute-start | bytes 792584 | tf_op jit(solution)/shard_map/ppermute | solution.py:17
  29.1 9.5 %collective-permute-start.7 = (f32[66048]{0:T(1024)}, f32[66048]{0:T(1024)}, u32[]{:S(2)}, u32[]{:S(2)}) collective-permute-start(f32[66048]{0:T(1024)} %get-tuple-element.16), channel_id=1, source_target_pairs={{0,64},{8,72},{16,80},{24,88},{32,96},{40,104},{48,112},{56,120},{... | collective-permute-start | bytes 792584 | tf_op jit(solution)/shard_map/ppermute | solution.py:17
  35.8 5.2 %copy-start.11 = (f32[66048]{0:T(1024)S(1)}, f32[66048]{0:T(1024)}, u32[]{:S(2)}) copy-start(f32[66048]{0:T(1024)} %copy-done.10) | copy-start | bytes 792580
  35.8 11.3 %copy-start.3 = (f32[2,4,64,64]{3,2,1,0:T(8,128)S(1)}, f32[2,4,64,64]{3,2,1,0:T(8,128)}, u32[]{:S(2)}) copy-start(f32[2,4,64,64]{3,2,1,0:T(8,128)} %copy-done.2) | copy-start | bytes 393220
  39.7 18.8 %collective-permute-start.8 = (f32[66048]{0:T(1024)S(1)}, f32[66048]{0:T(1024)S(1)}, u32[]{:S(2)}, u32[]{:S(2)}) collective-permute-start(f32[66048]{0:T(1024)S(1)} %add.176), channel_id=1, source_target_pairs={{0,128},{8,136},{16,144},{24,152},{32,160},{40,168},{48,176},{56,1... | collective-permute-start | bytes 792584 | tf_op jit(solution)/shard_map/ppermute | solution.py:17
  42.7 25.6 %collective-permute-start.3 = (f32[66048]{0:T(1024)}, f32[66048]{0:T(1024)}, u32[]{:S(2)}, u32[]{:S(2)}) collective-permute-start(f32[66048]{0:T(1024)} %add.168), channel_id=1, source_target_pairs={{0,16},{8,24},{16,32},{24,40},{32,48},{40,56},{48,64},{56,72},{64,... | collective-permute-start | bytes 792584 | tf_op jit(solution)/shard_map/ppermute | solution.py:17
  47.1 2.9 %copy-start.1 = (pred[512,576]{0,1:T(8,128)(4,1)S(1)}, pred[512,576]{0,1:T(8,128)(4,1)}, u32[]{:S(2)}) copy-start(pred[512,576]{0,1:T(8,128)(4,1)} %get-tuple-element.32) | copy-start | bytes 884740
  47.2 2.9 %copy-start.5 = (bf16[512,1,64]{2,0,1:T(8,128)(2,1)S(1)}, bf16[512,1,64]{2,0,1:T(8,128)(2,1)}, u32[]{:S(2)}) copy-start(bf16[512,1,64]{2,0,1:T(8,128)(2,1)} %copy-done.4) | copy-start | bytes 196612
  47.2 2.9 %copy-start.7 = (bf16[512,1,64]{2,0,1:T(8,128)(2,1)S(1)}, bf16[512,1,64]{2,0,1:T(8,128)(2,1)}, u32[]{:S(2)}) copy-start(bf16[512,1,64]{2,0,1:T(8,128)(2,1)} %copy-done.6) | copy-start | bytes 196612
  52.4 2.6 %copy-start.17 = (bf16[512,128]{1,0:T(8,128)(2,1)S(1)}, bf16[512,128]{1,0:T(8,128)(2,1)}, u32[]{:S(2)}) copy-start(bf16[512,128]{1,0:T(8,128)(2,1)} %param.12) | copy-start | bytes 393220
  52.4 2.6 %copy-start.21 = (bf16[64,1,128]{2,0,1:T(8,128)(2,1)S(1)}, bf16[64,1,128]{2,0,1:T(8,128)(2,1)}, u32[]{:S(2)}) copy-start(bf16[64,1,128]{2,0,1:T(8,128)(2,1)} %copy-done.20) | copy-start | bytes 49156
  58.5 0.8 copy-start.8
  59.3 15.7 %collective-permute-start.9 = (f32[66048]{0:T(1024)}, f32[66048]{0:T(1024)S(1)}, u32[]{:S(2)}, u32[]{:S(2)}) collective-permute-start(f32[66048]{0:T(1024)} %add.178), channel_id=1, source_target_pairs={{0,8},{8,16},{16,24},{24,32},{32,40},{40,48},{48,56},{56,64},{64,7... | collective-permute-start | bytes 792584 | tf_op jit(solution)/shard_map/ppermute | solution.py:17
  68.2 9.7 %copy-start.12 = (f32[512,8,64]{0,2,1:T(8,128)S(1)}, f32[512,8,64]{0,2,1:T(8,128)}, u32[]{:S(2)}) copy-start(f32[512,8,64]{0,2,1:T(8,128)} %get-tuple-element.40) | copy-start | bytes 3145732
  69.4 17.5 %collective-permute-start.4 = (f32[66048]{0:T(1024)S(1)}, f32[66048]{0:T(1024)S(1)}, u32[]{:S(2)}, u32[]{:S(2)}) collective-permute-start(f32[66048]{0:T(1024)S(1)} %add.170), channel_id=1, source_target_pairs={{0,32},{8,40},{16,48},{24,56},{32,64},{40,72},{48,80},{56,88},{64,... | collective-permute-start | bytes 792584 | tf_op jit(solution)/shard_map/ppermute | solution.py:17
  76.0 21.5 %collective-permute-start.10 = (f32[66048]{0:T(1024)S(1)}, f32[66048]{0:T(1024)S(1)}, u32[]{:S(2)}, u32[]{:S(2)}) collective-permute-start(f32[66048]{0:T(1024)S(1)} %add.180), channel_id=1, source_target_pairs={{0,16},{8,24},{16,32},{24,40},{32,48},{40,56},{48,64},{56,72},{64,... | collective-permute-start | bytes 792584 | tf_op jit(solution)/shard_map/ppermute | solution.py:17
  77.9 23.3 %copy-start.14 = (pred[512,576]{0,1:T(8,128)(4,1)S(1)}, pred[512,576]{0,1:T(8,128)(4,1)}, u32[]{:S(2)}) copy-start(pred[512,576]{0,1:T(8,128)(4,1)} %get-tuple-element.31) | copy-start | bytes 884740
  77.9 23.3 %copy-start.25 = (bf16[8,128,576]{2,1,0:T(8,128)(2,1)S(1)}, bf16[8,128,576]{2,1,0:T(8,128)(2,1)}, u32[]{:S(2)}) copy-start(bf16[8,128,576]{2,1,0:T(8,128)(2,1)} %get-tuple-element.15) | copy-start | bytes 3538948
  87.0 18.0 %collective-permute-start.5 = (f32[66048]{0:T(1024)S(1)}, f32[66048]{0:T(1024)S(1)}, u32[]{:S(2)}, u32[]{:S(2)}) collective-permute-start(f32[66048]{0:T(1024)S(1)} %add.172), channel_id=1, source_target_pairs={{0,64},{8,72},{16,80},{24,88},{32,96},{40,104},{48,112},{56,120},{... | collective-permute-start | bytes 792584 | tf_op jit(solution)/shard_map/ppermute | solution.py:17
  97.6 19.9 %collective-permute-start.11 = (f32[66048]{0:T(1024)S(1)}, f32[66048]{0:T(1024)S(1)}, u32[]{:S(2)}, u32[]{:S(2)}) collective-permute-start(f32[66048]{0:T(1024)S(1)} %add.182), channel_id=1, source_target_pairs={{0,32},{8,40},{16,48},{24,56},{32,64},{40,72},{48,80},{56,88},{64,... | collective-permute-start | bytes 792584 | tf_op jit(solution)/shard_map/ppermute | solution.py:17
  101.2 16.3 %copy-start.9 = (f32[66048]{0:T(1024)S(1)}, f32[66048]{0:T(1024)}, u32[]{:S(2)}) copy-start(f32[66048]{0:T(1024)} %copy-done.8) | copy-start | bytes 792580
  105.0 17.2 %collective-permute-start.6 = (f32[66048]{0:T(1024)S(1)}, f32[66048]{0:T(1024)S(1)}, u32[]{:S(2)}, u32[]{:S(2)}) collective-permute-start(f32[66048]{0:T(1024)S(1)} %add.174), channel_id=1, source_target_pairs={{0,128},{8,136},{16,144},{24,152},{32,160},{40,168},{48,176},{56,1... | collective-permute-start | bytes 792584 | tf_op jit(solution)/shard_map/ppermute | solution.py:17
  124.4 0.7 copy-start.19
  124.4 0.7 copy-start.23
  124.4 0.7 copy-start.24
  124.4 1.0 copy-start.15
  124.4 1.0 copy-start.18
  124.4 1.0 copy-start.22
  124.4 1.8 %copy-start.27 = (f32[128,8,512]{2,0,1:T(8,128)S(1)}, f32[128,8,512]{2,0,1:T(8,128)}, u32[]{:S(2)}) copy-start(f32[128,8,512]{2,0,1:T(8,128)} %fusion.10) | copy-start | bytes 6291460

commit v14 on v12

--- a/solution.py
+++ b/solution.py
@@ -136,9 +136,13 @@
         keys.reshape(tokens, kv_local, head_dim).astype(jnp.float32), cosine, sine
     ).astype(jnp.bfloat16)
     value_rows = values.reshape(tokens, kv_local, head_dim)
-    tail_keys, tail_values = passed_along(
-        (rot_k[tokens - WINDOW :], value_rows[tokens - WINDOW :]), "seq", 1
-    )
+    tail_both = passed_along(
+        jnp.concatenate([rot_k[tokens - WINDOW :], value_rows[tokens - WINDOW :]], axis=-1),
+        "seq",
+        1,
+    )
+    tail_keys = tail_both[..., :head_dim]
+    tail_values = tail_both[..., head_dim:]
     ext_keys = jnp.concatenate([tail_keys, rot_k], axis=0)
     ext_values = jnp.concatenate([tail_values, value_rows], axis=0)
     valid = (jnp.arange(tokens + WINDOW) >= WINDOW) | (lax.axis_index("seq") > 0)

time: 153 us -> 159 us (1.039)
  waiting for transfers between devices: 30.7 us -> 43 us
  starting transfers between devices: 43.2 us -> 37.2 us
    ppermute x12 -> x11, waiting for transfers between devices: 30.7 us -> 43 us  [passed_along(): lax.ppermute(value, axis, [(source, source + steps) for source in range(f...]
    ppermute x12 -> x11, starting transfers between devices: 43.2 us -> 37.2 us  [passed_along(): lax.ppermute(value, axis, [(source, source + steps) for source in range(f...]
    unnamed x58 -> x54, local copies, waits for them, and re-layouts: 5.72 us -> 5.59 us
  transfers between devices with their start and end apart: 12 -> 11, of which waited for: 6 -> 7; matrix products, arithmetic and copies ran while one was open for 22% -> 20% of each run, Pallas kernels for 0% -> 0%
where the time goes in v14:
time: 159 us; the launch traced here: 158 us
  waiting for transfers between devices  43 us (27%)
  starting transfers between devices  37.2 us (23%)
  other arithmetic  24.8 us (16%)
  blocking collectives  20.3 us (13%)
  matrix products  18.5 us (12%)
  local copies, waits for them, and re-layouts  9.64 us (6%)
  Pallas kernels  4.59 us (3%)
    ppermute x11, waiting for transfers between devices, passed_along(): lax.ppermute(value, axis, [(source, source + steps) for source in range(f...  43 us
    ppermute x11, starting transfers between devices, passed_along(): lax.ppermute(value, axis, [(source, source + steps) for source in range(f...  37.2 us
    all_to_all x1, blocking collectives, body(): lax.all_to_all(result, 'head', split_axis=0, concat_axis=1, tiled=True)  20.3 us
    add x8, other arithmetic, body(): inclusive = inclusive + received  5.77 us
    unnamed x54, local copies, waits for them, and re-layouts  5.59 us
    another operation x5, other arithmetic  4.76 us
    pallas_call x1, Pallas kernels, key_features(): pl.pallas_call(kernel, grid=(1,), in_specs=[pl.BlockSpec((rows, dim), lam...  4.59 us
    dot_general x1, matrix products, body(): jnp.einsum('igkf,gkfj->gkij', phi_query, phi_key, preferred_element_type=...  3.74 us
  transfers between devices with their start and end apart: 11, of which 7 were waited for; matrix products, arithmetic and copies ran while one was open for 20% of the time, Pallas kernels for 0%

profile of v14, /device:TPU:36, one launch (start us, length us, event | category | flops | bytes accessed | tf_op | source)
XLA Modules:
  0.0 158.4 jit_solution(13216369882887742594)
XLA Ops:
  0.0 0.7 and_select_fusion.1
  0.8 0.8 fusion.37
  1.6 0.9 bitcast_convert_fusion
  2.5 0.7 slice_bitcast_fusion
  3.3 0.8 multiply_cosine_fusion.1
  4.0 0.8 fusion.45
  4.9 0.2 subtract_convert_fusion.3
  5.0 0.5 copy-done.2
  5.7 4.0 %collective-permute-start = (bf16[64,1,256]{2,0,1:T(8,128)(2,1)S(1)}, bf16[64,1,256]{2,0,1:T(8,128)(2,1)S(1)}, u32[]{:S(2)}, u32[]{:S(2)}) collective-permute-start(bf16[64,1,256]{2,0,1:T(8,128)(2,1)S(1)} %fusion.35), channel_id=1, source_target_pairs={{0,8},{8,16},{16,24},{24,32},{32,40},{40,48},{48,56},{56,64},{64,7... | collective-permute-start | bytes 98312 | tf_op jit(solution)/shard_map/ppermute | solution.py:17
  9.6 0.6 or_convert_fusion.mask_ref
  10.2 0.6 broadcast_subtract_fusion
  10.8 0.8 collective-permute-done
  11.6 0.8 fusion.34
  12.4 4.6 %shard_map.100 = (bf16[8,128,576]{2,1,0:T(8,128)(2,1)}, f32[8,128,128]{2,1,0:T(8,128)}, f32[8,128,1]{2,1,0:T(8,128)}) custom-call(bf16[576,128]{1,0:T(8,128)(2,1)} %get-tuple-element.50.k_ref, bf16[8,64,128]{2,1,0:T(8,128)(2,1)} %bitcast.150, bf16[576,128]{1,0:T(8,128)(2,1)} %get-tuple-element.49.v_ref, f32[1,576]{1,0:T(1,128)} %or_convert_fusion.mask_ref), custom_call_target="tpu_custom_call" | custom-call | tf_op jit(solution)/shard_map/pallas_call | solution.py:104
  17.0 1.2 reduce.4
  18.2 1.8 %pad_maximum_fusion.3 = (f32[66048]{0:T(1024)}, f32[66048]{0:T(1024)S(1)}) fusion(f32[1024]{0:T(1024)S(1)} %bitcast.151, f32[131072]{0:T(1024)} %bitcast.146), kind=kLoop, calls=%fused_computation.44 | loop fusion | flops 66048 | bytes 1323008 | tf_op jit(solution)/shard_map/concatenate | solution.py:170
  20.0 3.8 %collective-permute-start.1 = (f32[66048]{0:T(1024)S(1)}, f32[66048]{0:T(1024)}, u32[]{:S(2)}, u32[]{:S(2)}) collective-permute-start(f32[66048]{0:T(1024)S(1)} %get-tuple-element.13), channel_id=1, source_target_pairs={{0,8},{8,16},{16,24},{24,32},{32,40},{40,48},{48,56},{56,64},{64,7... | collective-permute-start | bytes 792584 | tf_op jit(solution)/shard_map/ppermute | solution.py:17
  23.8 1.1 fusion.22
  25.0 3.1 %collective-permute-start.6 = (f32[66048]{0:T(1024)}, f32[66048]{0:T(1024)}, u32[]{:S(2)}, u32[]{:S(2)}) collective-permute-start(f32[66048]{0:T(1024)} %get-tuple-element.16), channel_id=1, source_target_pairs={{0,64},{8,72},{16,80},{24,88},{32,96},{40,104},{48,112},{56,120},{... | collective-permute-start | bytes 792584 | tf_op jit(solution)/shard_map/ppermute | solution.py:17
  28.1 3.3 %collective-permute-done.1 = f32[66048]{0:T(1024)} collective-permute-done((f32[66048]{0:T(1024)S(1)}, f32[66048]{0:T(1024)}, u32[]{:S(2)}, u32[]{:S(2)}) %collective-permute-start.1) | collective-permute-done | bytes 264224 | tf_op jit(solution)/shard_map/ppermute | solution.py:17
  31.4 0.5 copy.26
  32.0 0.3 fusion.71
  32.3 1.9 %copy.45 = f32[512,8,64]{2,0,1:T(8,128)} copy(f32[512,8,64]{0,2,1:T(8,128)S(1)} %get-tuple-element.22) | data formatting | bytes 2097152
  34.2 2.0 %copy.46 = f32[512,8,64]{2,0,1:T(8,128)} copy(f32[512,8,64]{0,2,1:T(8,128)S(1)} %get-tuple-element.21) | data formatting | bytes 2097152
  36.2 2.9 %subtract_convert_fusion = (bf16[512,8,64]{2,0,1:T(8,128)(2,1)S(1)}, bf16[512,8,64]{2,0,1:T(8,128)(2,1)S(1)}) fusion(f32[512,8,64]{2,0,1:T(8,128)} %copy.46, f32[512,8,64]{2,0,1:T(8,128)} %copy.45, f32[512,64]{1,0:T(8,128)S(1)} %bitcast.144, f32[512,64]{1,0:T(8,128)S(1)} %bitcast.142), kind=kLoop, calls=%fused_computation.23 | loop fusion | flops 2097152 | bytes 3407872 | tf_op jit(solution)/shard_map/convert.4
  39.0 2.3 %fusion.2 = (f32[8,512]{1,0:T(8,128)S(1)}, f32[576,512,8]{1,0,2:T(8,128)S(1)}) fusion(pred[512,576]{0,1:T(8,128)(4,1)S(1)} %copy-done.1, bf16[512,8,64]{2,0,1:T(8,128)(2,1)S(1)} %get-tuple-element.20, bf16[512,8,64]{2,0,1:T(8,128)(2,1)S(1)} %get-tuple-element.19, bf16[512,1,64]{2,0,1:T(8,128)(2,1)S(1)} %copy-done.7, bf16[512,1,64]{2,0,1:T(8,128)(2,1)S(1)} %copy-done.5, ...), kind=kOutput, calls=%fused_computation.4 | convolution fusion | flops 613593088 | bytes 10944512 | tf_op jit(solution)/shard_map/igkd,jgd->gkij/dot_general | solution.py:210
  41.4 2.5 %fusion.5 = f32[8,512]{1,0:T(8,128)} fusion(f32[576,512,8]{1,0,2:T(8,128)S(1)} %get-tuple-element.46, f32[8,512]{1,0:T(8,128)S(1)} %get-tuple-element.45, pred[512,576]{0,1:T(8,128)(4,1)S(1)} %copy-done.1), kind=kLoop, calls=%fused_computation.9 | loop fusion | flops 9433088 | bytes 9764864 | tf_op jit(solution)/shard_map/reduce_sum | solution.py:216
  43.9 3.5 %fusion.10 = f32[128,8,512]{2,0,1:T(8,128)} fusion(f32[576,512,8]{1,0,2:T(8,128)S(1)} %get-tuple-element.46, f32[8,512]{1,0:T(8,128)S(1)} %get-tuple-element.45, pred[512,576]{0,1:T(8,128)(4,1)S(1)} %copy-done.1, bf16[512,1,128]{2,0,1:T(8,128)(2,1)S(1)} %bitcast.148, bf16[64,1,128]{2,0,1:T(8,128)(2,1)S(1)} %copy-done.18), kind=kOutput, calls=%fused_computation.14 | convolution fusion | flops 613711872 | bytes 11993088 | tf_op jit(solution)/shard_map/gkij,jgd->igkd/dot_general | solution.py:220
  47.4 1.8 %add.176 = f32[66048]{0:T(1024)} add(f32[66048]{0:T(1024)} %get-tuple-element.16, f32[66048]{0:T(1024)} %collective-permute-done.6) | non-fusion elementwise | flops 66048 | bytes 792576 | tf_op jit(solution)/shard_map/add | solution.py:190
  49.2 1.5 collective-permute-start.7
  50.7 1.5 fusion.74
  52.2 1.7 %add.168 = f32[66048]{0:T(1024)} add(f32[66048]{0:T(1024)S(1)} %copy-done.9, f32[66048]{0:T(1024)} %collective-permute-done.1) | non-fusion elementwise | flops 66048 | bytes 792576 | tf_op jit(solution)/shard_map/add | solution.py:190
  53.9 4.5 %collective-permute-start.2 = (f32[66048]{0:T(1024)}, f32[66048]{0:T(1024)S(1)}, u32[]{:S(2)}, u32[]{:S(2)}) collective-permute-start(f32[66048]{0:T(1024)} %add.168), channel_id=1, source_target_pairs={{0,16},{8,24},{16,32},{24,40},{32,48},{40,56},{48,64},{56,72},{64,... | collective-permute-start | bytes 792584 | tf_op jit(solution)/shard_map/ppermute | solution.py:17
  58.3 2.5 %fusion.73 = (f32[512,8]{0,1:T(8,128)}, f32[512,8,64]{0,2,1:T(8,128)}) fusion(bf16[8,128,64]{1,2,0:T(8,128)(2,1)S(1)} %copy-done, bf16[512,8,64]{2,0,1:T(8,128)(2,1)S(1)} %get-tuple-element.20, bf16[512,8,64]{2,0,1:T(8,128)(2,1)S(1)} %get-tuple-element.19), kind=kOutput, calls=%fused_computation.126 | convolution fusion | flops 69992512 | bytes 2244608 | tf_op jit(solution)/shard_map/sub | solution.py:71
  60.8 1.1 add.178
  62.0 5.7 %collective-permute-start.8 = (f32[66048]{0:T(1024)S(1)}, f32[66048]{0:T(1024)S(1)}, u32[]{:S(2)}, u32[]{:S(2)}) collective-permute-start(f32[66048]{0:T(1024)S(1)} %add.178), channel_id=1, source_target_pairs={{0,8},{8,16},{16,24},{24,32},{32,40},{40,48},{48,56},{56,64},{64,7... | collective-permute-start | bytes 792584 | tf_op jit(solution)/shard_map/ppermute | solution.py:17
  67.7 0.8 divide_convert_fusion.1
  68.5 1.0 add.170
  69.5 5.6 %collective-permute-start.3 = (f32[66048]{0:T(1024)S(1)}, f32[66048]{0:T(1024)S(1)}, u32[]{:S(2)}, u32[]{:S(2)}) collective-permute-start(f32[66048]{0:T(1024)S(1)} %add.170), channel_id=1, source_target_pairs={{0,32},{8,40},{16,48},{24,56},{32,64},{40,72},{48,80},{56,88},{64,... | collective-permute-start | bytes 792584 | tf_op jit(solution)/shard_map/ppermute | solution.py:17
  75.1 0.9 collective-permute-done.8
  76.0 4.0 %collective-permute-start.9 = (f32[66048]{0:T(1024)S(1)}, f32[66048]{0:T(1024)S(1)}, u32[]{:S(2)}, u32[]{:S(2)}) collective-permute-start(f32[66048]{0:T(1024)S(1)} %add.180), channel_id=1, source_target_pairs={{0,16},{8,24},{16,32},{24,40},{32,48},{40,56},{48,64},{56,72},{64,... | collective-permute-start | bytes 792584 | tf_op jit(solution)/shard_map/ppermute | solution.py:17
  80.2 7.7 %collective-permute-done.3 = f32[66048]{0:T(1024)S(1)} collective-permute-done((f32[66048]{0:T(1024)S(1)}, f32[66048]{0:T(1024)S(1)}, u32[]{:S(2)}, u32[]{:S(2)}) %collective-permute-start.3) | collective-permute-done | bytes 264224 | tf_op jit(solution)/shard_map/ppermute | solution.py:17
  88.0 1.9 %collective-permute-start.4 = (f32[66048]{0:T(1024)S(1)}, f32[66048]{0:T(1024)S(1)}, u32[]{:S(2)}, u32[]{:S(2)}) collective-permute-start(f32[66048]{0:T(1024)S(1)} %add.172), channel_id=1, source_target_pairs={{0,64},{8,72},{16,80},{24,88},{32,96},{40,104},{48,112},{56,120},{... | collective-permute-start | bytes 792584 | tf_op jit(solution)/shard_map/ppermute | solution.py:17
  89.9 12.7 %collective-permute-done.9 = f32[66048]{0:T(1024)S(1)} collective-permute-done((f32[66048]{0:T(1024)S(1)}, f32[66048]{0:T(1024)S(1)}, u32[]{:S(2)}, u32[]{:S(2)}) %collective-permute-start.9) | collective-permute-done | bytes 264224 | tf_op jit(solution)/shard_map/ppermute | solution.py:17
  102.7 1.9 %collective-permute-start.10 = (f32[66048]{0:T(1024)S(1)}, f32[66048]{0:T(1024)S(1)}, u32[]{:S(2)}, u32[]{:S(2)}) collective-permute-start(f32[66048]{0:T(1024)S(1)} %add.182), channel_id=1, source_target_pairs={{0,32},{8,40},{16,48},{24,56},{32,64},{40,72},{48,80},{56,88},{64,... | collective-permute-start | bytes 792584 | tf_op jit(solution)/shard_map/ppermute | solution.py:17
  104.6 3.7 %select_reduce_fusion = (f32[8,512]{1,0:T(8,128)S(1)}, bf16[8,512,576]{1,2,0:T(8,128)(2,1)}) fusion(pred[512,576]{0,1:T(8,128)(4,1)S(1)} %copy-done.12, bf16[8,128,576]{2,1,0:T(8,128)(2,1)S(1)} %copy-done.23, bf16[512,8,64]{0,2,1:T(8,128)(2,1)S(1)} %divide_convert_fusion, bf16[512,8,64]{0,2,1:T(8,128)(2,1)S(1)} %divide_convert_fusion.1), kind=kOutput, calls=%fused_computation.7 | convolution fusion | flops 613150720 | bytes 7258112 | tf_op jit(solution)/shard_map/igkf,gkfj->gkij/dot_general | solution.py:217
  108.4 1.3 collective-permute-start.5
  109.7 15.0 %collective-permute-done.10 = f32[66048]{0:T(1024)S(1)} collective-permute-done((f32[66048]{0:T(1024)S(1)}, f32[66048]{0:T(1024)S(1)}, u32[]{:S(2)}, u32[]{:S(2)}) %collective-permute-start.10) | collective-permute-done | bytes 264224 | tf_op jit(solution)/shard_map/ppermute | solution.py:17
  124.7 1.1 add_add_fusion
  125.8 2.5 %collective-permute-done.5 = f32[66048]{0:T(1024)S(1)} collective-permute-done((f32[66048]{0:T(1024)S(1)}, f32[66048]{0:T(1024)S(1)}, u32[]{:S(2)}, u32[]{:S(2)}) %collective-permute-start.5) | collective-permute-done | bytes 264224 | tf_op jit(solution)/shard_map/ppermute | solution.py:17
  128.3 1.0 add_add_fusion.1
  129.4 0.2 copy.31
  129.6 0.4 fusion.26
  130.0 0.4 fusion.32
  130.5 0.2 fusion.49
  130.7 0.2 fusion.47
  131.0 0.2 copy-done.16
  131.2 0.1 copy-done.15
  131.4 0.8 copy-done.25
  132.2 3.7 %fusion.17 = bf16[512,1,8,128]{0,3,2,1:T(8,128)(2,1)S(1)} fusion(f32[8,128,512]{2,1,0:T(8,128)S(1)} %fusion.32, f32[8,128,512]{2,1,0:T(8,128)S(1)} %fusion.26, f32[128,8,512]{2,0,1:T(8,128)S(1)} %copy-done.25, bf16[8,512,576]{1,2,0:T(8,128)(2,1)} %get-tuple-element.48, pred[512,576]{0,1:T(8,128)(4,1)S(1)} %copy-done.12, f32[512,8]{0,1:T(8,128)S(1)} %fusion.39, ...), kind=kOutput, calls=%fused_computation.24 | convolution fusion | flops 610304000 | bytes 12517440 | tf_op jit(solution)/shard_map/gkij,jgd->igkd/dot_general | solution.py:226
  135.9 0.8 copy.35
  136.6 0.5 all_to_all.14
  137.1 20.3 %all_to_all.19 = bf16[8,64,1024]{2,1,0:T(8,128)(2,1)S(1)} all-to-all(bf16[8,64,1024]{2,1,0:T(8,128)(2,1)S(1)} %all_to_all.14), channel_id=1, replica_groups=mesh['seq'=32,'head'=8] {'head'}, dimensions={0} | all-to-all | bytes 2097152 | tf_op jit(solution)/shard_map/all_to_all | solution.py:253
  157.4 1.1 copy.47
  (67 shorter events, 0.7 us)
Async XLA Ops:
  0.0 50.7 %copy-start = (bf16[8,128,64]{1,2,0:T(8,128)(2,1)S(1)}, bf16[8,128,64]{1,2,0:T(8,128)(2,1)}, u32[]{:S(2)}) copy-start(bf16[8,128,64]{1,2,0:T(8,128)(2,1)} %param.14) | copy-start | bytes 393220
  0.0 11.6 %copy-start.13 = (bf16[512,128]{1,0:T(8,128)(2,1)S(1)}, bf16[512,128]{1,0:T(8,128)(2,1)}, u32[]{:S(2)}) copy-start(bf16[512,128]{1,0:T(8,128)(2,1)} %param.12) | copy-start | bytes 393220
  0.0 10.2 %copy-start.24 = (f32[8]{0:T(128)S(1)}, f32[8]{0:T(128)}, u32[]{:S(2)}) copy-start(f32[8]{0:T(128)} %param.16) | copy-start | bytes 100
  4.9 0.7 copy-start.2
  5.6 22.5 %copy-start.4 = (bf16[512,1,64]{2,0,1:T(8,128)(2,1)}, bf16[512,1,64]{2,0,1:T(8,128)(2,1)S(1)}, u32[]{:S(2)}) copy-start(bf16[512,1,64]{2,0,1:T(8,128)(2,1)S(1)} %get-tuple-element.23) | copy-start | bytes 196612
  5.6 22.5 %copy-start.6 = (bf16[512,1,64]{2,0,1:T(8,128)(2,1)}, bf16[512,1,64]{2,0,1:T(8,128)(2,1)S(1)}, u32[]{:S(2)}) copy-start(bf16[512,1,64]{2,0,1:T(8,128)(2,1)S(1)} %get-tuple-element.24) | copy-start | bytes 196612
  5.6 25.9 %copy-start.11 = (bf16[512,1024]{1,0:T(8,128)(2,1)S(1)}, bf16[512,1024]{1,0:T(8,128)(2,1)}, u32[]{:S(2)}) copy-start(bf16[512,1024]{1,0:T(8,128)(2,1)} %param.10) | copy-start | bytes 3145732
  5.7 5.9 %collective-permute-start = (bf16[64,1,256]{2,0,1:T(8,128)(2,1)S(1)}, bf16[64,1,256]{2,0,1:T(8,128)(2,1)S(1)}, u32[]{:S(2)}, u32[]{:S(2)}) collective-permute-start(bf16[64,1,256]{2,0,1:T(8,128)(2,1)S(1)} %fusion.35), channel_id=1, source_target_pairs={{0,8},{8,16},{16,24},{24,32},{32,40},{40,48},{48,56},{56,64},{64,7... | collective-permute-start | bytes 98312 | tf_op jit(solution)/shard_map/ppermute | solution.py:17
  11.6 6.6 %copy-start.17 = (bf16[64,1,128]{2,0,1:T(8,128)(2,1)}, bf16[64,1,128]{2,0,1:T(8,128)(2,1)S(1)}, u32[]{:S(2)}) copy-start(bf16[64,1,128]{2,0,1:T(8,128)(2,1)S(1)} %get-tuple-element.29) | copy-start | bytes 49156
  20.0 8.1 %copy-start.8 = (f32[66048]{0:T(1024)}, f32[66048]{0:T(1024)S(1)}, u32[]{:S(2)}) copy-start(f32[66048]{0:T(1024)S(1)} %get-tuple-element.13) | copy-start | bytes 792580
  20.0 11.4 %collective-permute-start.1 = (f32[66048]{0:T(1024)S(1)}, f32[66048]{0:T(1024)}, u32[]{:S(2)}, u32[]{:S(2)}) collective-permute-start(f32[66048]{0:T(1024)S(1)} %get-tuple-element.13), channel_id=1, source_target_pairs={{0,8},{8,16},{16,24},{24,32},{32,40},{40,48},{48,56},{56,64},{64,7... | collective-permute-start | bytes 792584 | tf_op jit(solution)/shard_map/ppermute | solution.py:17
  25.0 22.5 %collective-permute-start.6 = (f32[66048]{0:T(1024)}, f32[66048]{0:T(1024)}, u32[]{:S(2)}, u32[]{:S(2)}) collective-permute-start(f32[66048]{0:T(1024)} %get-tuple-element.16), channel_id=1, source_target_pairs={{0,64},{8,72},{16,80},{24,88},{32,96},{40,104},{48,112},{56,120},{... | collective-permute-start | bytes 792584 | tf_op jit(solution)/shard_map/ppermute | solution.py:17
  34.2 2.0 %copy-start.3 = (f32[2,4,64,64]{3,2,1,0:T(8,128)S(1)}, f32[2,4,64,64]{3,2,1,0:T(8,128)}, u32[]{:S(2)}) copy-start(f32[2,4,64,64]{3,2,1,0:T(8,128)} %copy-done.2) | copy-start | bytes 393220
  36.1 2.9 %copy-start.1 = (pred[512,576]{0,1:T(8,128)(4,1)S(1)}, pred[512,576]{0,1:T(8,128)(4,1)}, u32[]{:S(2)}) copy-start(pred[512,576]{0,1:T(8,128)(4,1)} %get-tuple-element.34) | copy-start | bytes 884740
  36.1 2.9 %copy-start.5 = (bf16[512,1,64]{2,0,1:T(8,128)(2,1)S(1)}, bf16[512,1,64]{2,0,1:T(8,128)(2,1)}, u32[]{:S(2)}) copy-start(bf16[512,1,64]{2,0,1:T(8,128)(2,1)} %copy-done.4) | copy-start | bytes 196612
  36.1 2.9 %copy-start.7 = (bf16[512,1,64]{2,0,1:T(8,128)(2,1)S(1)}, bf16[512,1,64]{2,0,1:T(8,128)(2,1)}, u32[]{:S(2)}) copy-start(bf16[512,1,64]{2,0,1:T(8,128)(2,1)} %copy-done.6) | copy-start | bytes 196612
  41.4 2.6 %copy-start.14 = (bf16[512,128]{1,0:T(8,128)(2,1)S(1)}, bf16[512,128]{1,0:T(8,128)(2,1)}, u32[]{:S(2)}) copy-start(bf16[512,128]{1,0:T(8,128)(2,1)} %param.12) | copy-start | bytes 393220
  41.4 2.6 %copy-start.18 = (bf16[64,1,128]{2,0,1:T(8,128)(2,1)S(1)}, bf16[64,1,128]{2,0,1:T(8,128)(2,1)}, u32[]{:S(2)}) copy-start(bf16[64,1,128]{2,0,1:T(8,128)(2,1)} %copy-done.17) | copy-start | bytes 49156
  47.4 4.8 %copy-start.9 = (f32[66048]{0:T(1024)S(1)}, f32[66048]{0:T(1024)}, u32[]{:S(2)}) copy-start(f32[66048]{0:T(1024)} %copy-done.8) | copy-start | bytes 792580
  49.2 11.6 %collective-permute-start.7 = (f32[66048]{0:T(1024)}, f32[66048]{0:T(1024)}, u32[]{:S(2)}, u32[]{:S(2)}) collective-permute-start(f32[66048]{0:T(1024)} %add.176), channel_id=1, source_target_pairs={{0,128},{8,136},{16,144},{24,152},{32,160},{40,168},{48,176},{56,1... | collective-permute-start | bytes 792584 | tf_op jit(solution)/shard_map/ppermute | solution.py:17
  53.9 14.6 %collective-permute-start.2 = (f32[66048]{0:T(1024)}, f32[66048]{0:T(1024)S(1)}, u32[]{:S(2)}, u32[]{:S(2)}) collective-permute-start(f32[66048]{0:T(1024)} %add.168), channel_id=1, source_target_pairs={{0,16},{8,24},{16,32},{24,40},{32,48},{40,56},{48,64},{56,72},{64,... | collective-permute-start | bytes 792584 | tf_op jit(solution)/shard_map/ppermute | solution.py:17
  60.8 19.2 %copy-start.10 = (f32[512,8,64]{0,2,1:T(8,128)S(1)}, f32[512,8,64]{0,2,1:T(8,128)}, u32[]{:S(2)}) copy-start(f32[512,8,64]{0,2,1:T(8,128)} %get-tuple-element.42) | copy-start | bytes 3145732
  60.8 19.2 %copy-start.20 = (f32[512,8]{0,1:T(8,128)S(1)}, f32[512,8]{0,1:T(8,128)}, u32[]{:S(2)}) copy-start(f32[512,8]{0,1:T(8,128)} %get-tuple-element.41) | copy-start | bytes 49156
  62.0 14.0 %collective-permute-start.8 = (f32[66048]{0:T(1024)S(1)}, f32[66048]{0:T(1024)S(1)}, u32[]{:S(2)}, u32[]{:S(2)}) collective-permute-start(f32[66048]{0:T(1024)S(1)} %add.178), channel_id=1, source_target_pairs={{0,8},{8,16},{16,24},{24,32},{32,40},{40,48},{48,56},{56,64},{64,7... | collective-permute-start | bytes 792584 | tf_op jit(solution)/shard_map/ppermute | solution.py:17
  69.5 35.1 %copy-start.12 = (pred[512,576]{0,1:T(8,128)(4,1)S(1)}, pred[512,576]{0,1:T(8,128)(4,1)}, u32[]{:S(2)}) copy-start(pred[512,576]{0,1:T(8,128)(4,1)} %get-tuple-element.33) | copy-start | bytes 884740
  69.5 35.1 %copy-start.23 = (bf16[8,128,576]{2,1,0:T(8,128)(2,1)S(1)}, bf16[8,128,576]{2,1,0:T(8,128)(2,1)}, u32[]{:S(2)}) copy-start(bf16[8,128,576]{2,1,0:T(8,128)(2,1)} %get-tuple-element.15) | copy-start | bytes 3538948
  69.5 18.4 %collective-permute-start.3 = (f32[66048]{0:T(1024)S(1)}, f32[66048]{0:T(1024)S(1)}, u32[]{:S(2)}, u32[]{:S(2)}) collective-permute-start(f32[66048]{0:T(1024)S(1)} %add.170), channel_id=1, source_target_pairs={{0,32},{8,40},{16,48},{24,56},{32,64},{40,72},{48,80},{56,88},{64,... | collective-permute-start | bytes 792584 | tf_op jit(solution)/shard_map/ppermute | solution.py:17
  76.0 26.6 %collective-permute-start.9 = (f32[66048]{0:T(1024)S(1)}, f32[66048]{0:T(1024)S(1)}, u32[]{:S(2)}, u32[]{:S(2)}) collective-permute-start(f32[66048]{0:T(1024)S(1)} %add.180), channel_id=1, source_target_pairs={{0,16},{8,24},{16,32},{24,40},{32,48},{40,56},{48,64},{56,72},{64,... | collective-permute-start | bytes 792584 | tf_op jit(solution)/shard_map/ppermute | solution.py:17
  88.0 20.4 %collective-permute-start.4 = (f32[66048]{0:T(1024)S(1)}, f32[66048]{0:T(1024)S(1)}, u32[]{:S(2)}, u32[]{:S(2)}) collective-permute-start(f32[66048]{0:T(1024)S(1)} %add.172), channel_id=1, source_target_pairs={{0,64},{8,72},{16,80},{24,88},{32,96},{40,104},{48,112},{56,120},{... | collective-permute-start | bytes 792584 | tf_op jit(solution)/shard_map/ppermute | solution.py:17
  102.7 22.0 %collective-permute-start.10 = (f32[66048]{0:T(1024)S(1)}, f32[66048]{0:T(1024)S(1)}, u32[]{:S(2)}, u32[]{:S(2)}) collective-permute-start(f32[66048]{0:T(1024)S(1)} %add.182), channel_id=1, source_target_pairs={{0,32},{8,40},{16,48},{24,56},{32,64},{40,72},{48,80},{56,88},{64,... | collective-permute-start | bytes 792584 | tf_op jit(solution)/shard_map/ppermute | solution.py:17
  108.4 19.9 %collective-permute-start.5 = (f32[66048]{0:T(1024)S(1)}, f32[66048]{0:T(1024)S(1)}, u32[]{:S(2)}, u32[]{:S(2)}) collective-permute-start(f32[66048]{0:T(1024)S(1)} %add.174), channel_id=1, source_target_pairs={{0,128},{8,136},{16,144},{24,152},{32,160},{40,168},{48,176},{56,1... | collective-permute-start | bytes 792584 | tf_op jit(solution)/shard_map/ppermute | solution.py:17
  130.4 0.7 copy-start.16
  130.4 0.7 copy-start.21
  130.5 0.7 copy-start.22
  130.5 0.9 copy-start.15
  130.5 0.9 copy-start.19
  130.5 1.7 %copy-start.25 = (f32[128,8,512]{2,0,1:T(8,128)S(1)}, f32[128,8,512]{2,0,1:T(8,128)}, u32[]{:S(2)}) copy-start(f32[128,8,512]{2,0,1:T(8,128)} %fusion.10) | copy-start | bytes 6291460

commit v15 on v14

--- a/solution.py
+++ b/solution.py
@@ -183,7 +183,7 @@
         exclusive = jnp.zeros_like(piece)
         for place, shift in enumerate(order):
             received = passed_along(inclusive, "seq", shift)
-            if not pieces and place == 0:
+            if not pieces and place == 1:
                 first_received = received
             exclusive = exclusive + received
             if place + 1 < len(order):

time: 159 us -> 159 us (level)
  the two profiles are of different devices: /device:TPU:36 before, /device:TPU:2 now
where the time goes in v15:
time: 159 us; the launch traced here: 156 us
  starting transfers between devices  42.2 us (27%)
  waiting for transfers between devices  38.3 us (24%)
  other arithmetic  21.5 us (14%)
  blocking collectives  20.2 us (13%)
  matrix products  18.6 us (12%)
  local copies, waits for them, and re-layouts  9.67 us (6%)
  Pallas kernels  4.56 us (3%)
    ppermute x11, starting transfers between devices, passed_along(): lax.ppermute(value, axis, [(source, source + steps) for source in range(f...  42.2 us
    ppermute x11, waiting for transfers between devices, passed_along(): lax.ppermute(value, axis, [(source, source + steps) for source in range(f...  38.3 us
    all_to_all x1, blocking collectives, body(): lax.all_to_all(result, 'head', split_axis=0, concat_axis=1, tiled=True)  20.2 us
    unnamed x62, local copies, waits for them, and re-layouts  5.62 us
    another operation x5, other arithmetic  4.78 us
    pallas_call x1, Pallas kernels, key_features(): pl.pallas_call(kernel, grid=(1,), in_specs=[pl.BlockSpec((rows, dim), lam...  4.56 us
    dot_general x1, matrix products, body(): jnp.einsum('gkij,jgd->igkd', affinity.astype(jnp.bfloat16), ext_values, p...  3.78 us
    dot_general x1, matrix products, body(): jnp.einsum('igkf,gkfj->gkij', phi_query, phi_key, preferred_element_type=...  3.72 us
  transfers between devices with their start and end apart: 11, of which 9 were waited for; matrix products, arithmetic and copies ran while one was open for 19% of the time, Pallas kernels for 0%

profile of v15, /device:TPU:2, one launch (start us, length us, event | category | flops | bytes accessed | tf_op | source)
XLA Modules:
  0.0 155.6 jit_solution(8706899929944702088)
XLA Ops:
  0.0 0.7 and_select_fusion.1
  0.8 0.8 fusion.37
  1.6 0.9 bitcast_convert_fusion
  2.5 0.7 slice_bitcast_fusion
  3.2 0.8 multiply_cosine_fusion.1
  4.0 0.8 fusion.45
  4.9 0.2 subtract_convert_fusion.3
  5.0 0.5 copy-done.2
  5.7 3.8 %collective-permute-start = (bf16[64,1,256]{2,0,1:T(8,128)(2,1)S(1)}, bf16[64,1,256]{2,0,1:T(8,128)(2,1)S(1)}, u32[]{:S(2)}, u32[]{:S(2)}) collective-permute-start(bf16[64,1,256]{2,0,1:T(8,128)(2,1)S(1)} %fusion.35), channel_id=1, source_target_pairs={{0,8},{8,16},{16,24},{24,32},{32,40},{40,48},{48,56},{56,64},{64,7... | collective-permute-start | bytes 98312 | tf_op jit(solution)/shard_map/ppermute | solution.py:17
  9.5 0.6 or_convert_fusion.mask_ref
  10.1 5.2 %collective-permute-done = bf16[64,1,256]{2,0,1:T(8,128)(2,1)S(1)} collective-permute-done((bf16[64,1,256]{2,0,1:T(8,128)(2,1)S(1)}, bf16[64,1,256]{2,0,1:T(8,128)(2,1)S(1)}, u32[]{:S(2)}, u32[]{:S(2)}) %collective-permute-start) | collective-permute-done | bytes 32800 | tf_op jit(solution)/shard_map/ppermute | solution.py:17
  15.3 0.8 fusion.34
  16.1 4.6 %shard_map.100 = (bf16[8,128,576]{2,1,0:T(8,128)(2,1)}, f32[8,128,128]{2,1,0:T(8,128)}, f32[8,128,1]{2,1,0:T(8,128)}) custom-call(bf16[576,128]{1,0:T(8,128)(2,1)} %get-tuple-element.50.k_ref, bf16[8,64,128]{2,1,0:T(8,128)(2,1)} %bitcast.150, bf16[576,128]{1,0:T(8,128)(2,1)} %get-tuple-element.49.v_ref, f32[1,576]{1,0:T(1,128)} %or_convert_fusion.mask_ref), custom_call_target="tpu_custom_call" | custom-call | tf_op jit(solution)/shard_map/pallas_call | solution.py:104
  20.6 1.3 reduce.4
  22.0 1.1 pad_maximum_fusion.3
  23.0 1.9 %collective-permute-start.1 = (f32[66048]{0:T(1024)S(1)}, f32[66048]{0:T(1024)S(1)}, u32[]{:S(2)}, u32[]{:S(2)}) collective-permute-start(f32[66048]{0:T(1024)S(1)} %get-tuple-element.13), channel_id=1, source_target_pairs={{0,8},{8,16},{16,24},{24,32},{32,40},{40,48},{48,56},{56,64},{64,7... | collective-permute-start | bytes 792584 | tf_op jit(solution)/shard_map/ppermute | solution.py:17
  25.0 0.5 broadcast_subtract_fusion
  25.5 3.4 %collective-permute-start.6 = (f32[66048]{0:T(1024)S(1)}, f32[66048]{0:T(1024)S(1)}, u32[]{:S(2)}, u32[]{:S(2)}) collective-permute-start(f32[66048]{0:T(1024)S(1)} %get-tuple-element.16), channel_id=1, source_target_pairs={{0,64},{8,72},{16,80},{24,88},{32,96},{40,104},{48,112},{56,120},{... | collective-permute-start | bytes 792584 | tf_op jit(solution)/shard_map/ppermute | solution.py:17
  28.9 5.5 %collective-permute-done.1 = f32[66048]{0:T(1024)S(1)} collective-permute-done((f32[66048]{0:T(1024)S(1)}, f32[66048]{0:T(1024)S(1)}, u32[]{:S(2)}, u32[]{:S(2)}) %collective-permute-start.1) | collective-permute-done | bytes 264224 | tf_op jit(solution)/shard_map/ppermute | solution.py:17
  34.5 1.9 %collective-permute-start.2 = (f32[66048]{0:T(1024)S(1)}, f32[66048]{0:T(1024)}, u32[]{:S(2)}, u32[]{:S(2)}) collective-permute-start(f32[66048]{0:T(1024)S(1)} %add.166), channel_id=1, source_target_pairs={{0,16},{8,24},{16,32},{24,40},{32,48},{40,56},{48,64},{56,72},{64,... | collective-permute-start | bytes 792584 | tf_op jit(solution)/shard_map/ppermute | solution.py:17
  36.4 1.1 fusion.22
  37.6 2.5 %collective-permute-done.6 = f32[66048]{0:T(1024)S(1)} collective-permute-done((f32[66048]{0:T(1024)S(1)}, f32[66048]{0:T(1024)S(1)}, u32[]{:S(2)}, u32[]{:S(2)}) %collective-permute-start.6) | collective-permute-done | bytes 264224 | tf_op jit(solution)/shard_map/ppermute | solution.py:17
  40.0 0.8 add.176
  40.9 5.0 %collective-permute-start.7 = (f32[66048]{0:T(1024)}, f32[66048]{0:T(1024)}, u32[]{:S(2)}, u32[]{:S(2)}) collective-permute-start(f32[66048]{0:T(1024)} %add.176), channel_id=1, source_target_pairs={{0,128},{8,136},{16,144},{24,152},{32,160},{40,168},{48,176},{56,1... | collective-permute-start | bytes 792584 | tf_op jit(solution)/shard_map/ppermute | solution.py:17
  45.9 3.9 %collective-permute-done.2 = f32[66048]{0:T(1024)} collective-permute-done((f32[66048]{0:T(1024)S(1)}, f32[66048]{0:T(1024)}, u32[]{:S(2)}, u32[]{:S(2)}) %collective-permute-start.2) | collective-permute-done | bytes 264224 | tf_op jit(solution)/shard_map/ppermute | solution.py:17
  49.8 0.5 copy.26
  50.3 0.3 fusion.71
  50.6 1.9 %copy.45 = f32[512,8,64]{2,0,1:T(8,128)} copy(f32[512,8,64]{0,2,1:T(8,128)S(1)} %get-tuple-element.22) | data formatting | bytes 2097152
  52.5 2.0 %copy.46 = f32[512,8,64]{2,0,1:T(8,128)} copy(f32[512,8,64]{0,2,1:T(8,128)S(1)} %get-tuple-element.21) | data formatting | bytes 2097152
  54.5 2.9 %subtract_convert_fusion = (bf16[512,8,64]{2,0,1:T(8,128)(2,1)S(1)}, bf16[512,8,64]{2,0,1:T(8,128)(2,1)S(1)}) fusion(f32[512,8,64]{2,0,1:T(8,128)} %copy.46, f32[512,8,64]{2,0,1:T(8,128)} %copy.45, f32[512,64]{1,0:T(8,128)S(1)} %bitcast.144, f32[512,64]{1,0:T(8,128)S(1)} %bitcast.142), kind=kLoop, calls=%fused_computation.23 | loop fusion | flops 2097152 | bytes 3407872 | tf_op jit(solution)/shard_map/convert.4
  57.4 2.3 %fusion.2 = (f32[8,512]{1,0:T(8,128)S(1)}, f32[576,512,8]{1,0,2:T(8,128)S(1)}) fusion(pred[512,576]{0,1:T(8,128)(4,1)S(1)} %copy-done.1, bf16[512,8,64]{2,0,1:T(8,128)(2,1)S(1)} %get-tuple-element.20, bf16[512,8,64]{2,0,1:T(8,128)(2,1)S(1)} %get-tuple-element.19, bf16[512,1,64]{2,0,1:T(8,128)(2,1)S(1)} %copy-done.7, bf16[512,1,64]{2,0,1:T(8,128)(2,1)S(1)} %copy-done.5, ...), kind=kOutput, calls=%fused_computation.4 | convolution fusion | flops 613593088 | bytes 10944512 | tf_op jit(solution)/shard_map/igkd,jgd->gkij/dot_general | solution.py:210
  59.7 2.5 %fusion.5 = f32[8,512]{1,0:T(8,128)} fusion(f32[576,512,8]{1,0,2:T(8,128)S(1)} %get-tuple-element.46, f32[8,512]{1,0:T(8,128)S(1)} %get-tuple-element.45, pred[512,576]{0,1:T(8,128)(4,1)S(1)} %copy-done.1), kind=kLoop, calls=%fused_computation.9 | loop fusion | flops 9433088 | bytes 9764864 | tf_op jit(solution)/shard_map/reduce_sum | solution.py:216
  62.3 3.5 %fusion.10 = f32[128,8,512]{2,0,1:T(8,128)} fusion(f32[576,512,8]{1,0,2:T(8,128)S(1)} %get-tuple-element.46, f32[8,512]{1,0:T(8,128)S(1)} %get-tuple-element.45, pred[512,576]{0,1:T(8,128)(4,1)S(1)} %copy-done.1, bf16[512,1,128]{2,0,1:T(8,128)(2,1)S(1)} %bitcast.148, bf16[64,1,128]{2,0,1:T(8,128)(2,1)S(1)} %copy-done.22), kind=kOutput, calls=%fused_computation.14 | convolution fusion | flops 613711872 | bytes 11993088 | tf_op jit(solution)/shard_map/gkij,jgd->igkd/dot_general | solution.py:220
  65.8 1.5 fusion.74
  67.2 2.5 %fusion.73 = (f32[512,8]{0,1:T(8,128)}, f32[512,8,64]{0,2,1:T(8,128)}) fusion(bf16[8,128,64]{1,2,0:T(8,128)(2,1)S(1)} %copy-done, bf16[512,8,64]{2,0,1:T(8,128)(2,1)S(1)} %get-tuple-element.20, bf16[512,8,64]{2,0,1:T(8,128)(2,1)S(1)} %get-tuple-element.19), kind=kOutput, calls=%fused_computation.126 | convolution fusion | flops 69992512 | bytes 2244608 | tf_op jit(solution)/shard_map/sub | solution.py:71
  69.7 1.1 add.178
  70.9 1.9 %collective-permute-start.8 = (f32[66048]{0:T(1024)S(1)}, f32[66048]{0:T(1024)S(1)}, u32[]{:S(2)}, u32[]{:S(2)}) collective-permute-start(f32[66048]{0:T(1024)S(1)} %add.178), channel_id=1, source_target_pairs={{0,8},{8,16},{16,24},{24,32},{32,40},{40,48},{48,56},{56,64},{64,7... | collective-permute-start | bytes 792584 | tf_op jit(solution)/shard_map/ppermute | solution.py:17
  72.8 1.0 add.170
  73.8 4.6 %collective-permute-start.3 = (f32[66048]{0:T(1024)S(1)}, f32[66048]{0:T(1024)S(1)}, u32[]{:S(2)}, u32[]{:S(2)}) collective-permute-start(f32[66048]{0:T(1024)S(1)} %add.170), channel_id=1, source_target_pairs={{0,32},{8,40},{16,48},{24,56},{32,64},{40,72},{48,80},{56,88},{64,... | collective-permute-start | bytes 792584 | tf_op jit(solution)/shard_map/ppermute | solution.py:17
  78.3 0.8 divide_convert_fusion.1
  79.2 10.3 %collective-permute-done.8 = f32[66048]{0:T(1024)S(1)} collective-permute-done((f32[66048]{0:T(1024)S(1)}, f32[66048]{0:T(1024)S(1)}, u32[]{:S(2)}, u32[]{:S(2)}) %collective-permute-start.8) | collective-permute-done | bytes 264224 | tf_op jit(solution)/shard_map/ppermute | solution.py:17
  89.5 1.9 %collective-permute-start.9 = (f32[66048]{0:T(1024)S(1)}, f32[66048]{0:T(1024)S(1)}, u32[]{:S(2)}, u32[]{:S(2)}) collective-permute-start(f32[66048]{0:T(1024)S(1)} %add.180), channel_id=1, source_target_pairs={{0,16},{8,24},{16,32},{24,40},{32,48},{40,56},{48,64},{56,72},{64,... | collective-permute-start | bytes 792584 | tf_op jit(solution)/shard_map/ppermute | solution.py:17
  91.6 3.7 %collective-permute-done.3 = f32[66048]{0:T(1024)S(1)} collective-permute-done((f32[66048]{0:T(1024)S(1)}, f32[66048]{0:T(1024)S(1)}, u32[]{:S(2)}, u32[]{:S(2)}) %collective-permute-start.3) | collective-permute-done | bytes 264224 | tf_op jit(solution)/shard_map/ppermute | solution.py:17
  95.4 8.4 %collective-permute-start.4 = (f32[66048]{0:T(1024)S(1)}, f32[66048]{0:T(1024)S(1)}, u32[]{:S(2)}, u32[]{:S(2)}) collective-permute-start(f32[66048]{0:T(1024)S(1)} %add.172), channel_id=1, source_target_pairs={{0,64},{8,72},{16,80},{24,88},{32,96},{40,104},{48,112},{56,120},{... | collective-permute-start | bytes 792584 | tf_op jit(solution)/shard_map/ppermute | solution.py:17
  103.8 2.8 %collective-permute-done.9 = f32[66048]{0:T(1024)S(1)} collective-permute-done((f32[66048]{0:T(1024)S(1)}, f32[66048]{0:T(1024)S(1)}, u32[]{:S(2)}, u32[]{:S(2)}) %collective-permute-start.9) | collective-permute-done | bytes 264224 | tf_op jit(solution)/shard_map/ppermute | solution.py:17
  106.6 2.1 %collective-permute-start.10 = (f32[66048]{0:T(1024)S(1)}, f32[66048]{0:T(1024)S(1)}, u32[]{:S(2)}, u32[]{:S(2)}) collective-permute-start(f32[66048]{0:T(1024)S(1)} %add.182), channel_id=1, source_target_pairs={{0,32},{8,40},{16,48},{24,56},{32,64},{40,72},{48,80},{56,88},{64,... | collective-permute-start | bytes 792584 | tf_op jit(solution)/shard_map/ppermute | solution.py:17
  108.8 3.7 %select_reduce_fusion = (f32[8,512]{1,0:T(8,128)S(1)}, bf16[8,512,576]{1,2,0:T(8,128)(2,1)}) fusion(pred[512,576]{0,1:T(8,128)(4,1)S(1)} %copy-done.16, bf16[8,128,576]{2,1,0:T(8,128)(2,1)S(1)} %copy-done.27, bf16[512,8,64]{0,2,1:T(8,128)(2,1)S(1)} %divide_convert_fusion, bf16[512,8,64]{0,2,1:T(8,128)(2,1)S(1)} %divide_convert_fusion.1), kind=kOutput, calls=%fused_computation.7 | convolution fusion | flops 613150720 | bytes 7258112 | tf_op jit(solution)/shard_map/igkf,gkfj->gkij/dot_general | solution.py:217
  112.5 0.9 collective-permute-done.4
  113.4 7.2 %collective-permute-start.5 = (f32[66048]{0:T(1024)S(1)}, f32[66048]{0:T(1024)S(1)}, u32[]{:S(2)}, u32[]{:S(2)}) collective-permute-start(f32[66048]{0:T(1024)S(1)} %add.174), channel_id=1, source_target_pairs={{0,128},{8,136},{16,144},{24,152},{32,160},{40,168},{48,176},{56,1... | collective-permute-start | bytes 792584 | tf_op jit(solution)/shard_map/ppermute | solution.py:17
  120.7 3.6 %collective-permute-done.10 = f32[66048]{0:T(1024)S(1)} collective-permute-done((f32[66048]{0:T(1024)S(1)}, f32[66048]{0:T(1024)S(1)}, u32[]{:S(2)}, u32[]{:S(2)}) %collective-permute-start.10) | collective-permute-done | bytes 264224 | tf_op jit(solution)/shard_map/ppermute | solution.py:17
  124.3 1.0 add_add_fusion
  125.3 1.1 add_add_fusion.1
  126.4 0.2 copy.31
  126.7 0.4 fusion.26
  127.1 0.4 fusion.32
  127.6 0.2 fusion.49
  127.8 0.2 fusion.47
  128.0 0.2 copy-done.20
  128.4 0.8 copy-done.29
  129.2 3.8 %fusion.17 = bf16[512,1,8,128]{0,3,2,1:T(8,128)(2,1)S(1)} fusion(f32[8,128,512]{2,1,0:T(8,128)S(1)} %fusion.32, f32[8,128,512]{2,1,0:T(8,128)S(1)} %fusion.26, f32[128,8,512]{2,0,1:T(8,128)S(1)} %copy-done.29, bf16[8,512,576]{1,2,0:T(8,128)(2,1)} %get-tuple-element.48, pred[512,576]{0,1:T(8,128)(4,1)S(1)} %copy-done.16, f32[512,8]{0,1:T(8,128)S(1)} %fusion.39, ...), kind=kOutput, calls=%fused_computation.24 | convolution fusion | flops 610304000 | bytes 12517440 | tf_op jit(solution)/shard_map/gkij,jgd->igkd/dot_general | solution.py:226
  133.0 0.8 copy.35
  133.8 0.5 all_to_all.14
  134.3 20.2 %all_to_all.19 = bf16[8,64,1024]{2,1,0:T(8,128)(2,1)S(1)} all-to-all(bf16[8,64,1024]{2,1,0:T(8,128)(2,1)S(1)} %all_to_all.14), channel_id=1, replica_groups=mesh['seq'=32,'head'=8] {'head'}, dimensions={0} | all-to-all | bytes 2097152 | tf_op jit(solution)/shard_map/all_to_all | solution.py:253
  154.5 1.1 copy.47
  (75 shorter events, 0.9 us)
Async XLA Ops:
  0.0 65.8 %copy-start = (bf16[8,128,64]{1,2,0:T(8,128)(2,1)S(1)}, bf16[8,128,64]{1,2,0:T(8,128)(2,1)}, u32[]{:S(2)}) copy-start(bf16[8,128,64]{1,2,0:T(8,128)(2,1)} %param.14) | copy-start | bytes 393220
  0.0 15.3 %copy-start.17 = (bf16[512,128]{1,0:T(8,128)(2,1)S(1)}, bf16[512,128]{1,0:T(8,128)(2,1)}, u32[]{:S(2)}) copy-start(bf16[512,128]{1,0:T(8,128)(2,1)} %param.12) | copy-start | bytes 393220
  4.9 0.7 copy-start.2
  4.9 20.1 %copy-start.28 = (f32[8]{0:T(128)S(1)}, f32[8]{0:T(128)}, u32[]{:S(2)}) copy-start(f32[8]{0:T(128)} %param.16) | copy-start | bytes 100
  5.6 28.9 %copy-start.4 = (bf16[512,1,64]{2,0,1:T(8,128)(2,1)}, bf16[512,1,64]{2,0,1:T(8,128)(2,1)S(1)}, u32[]{:S(2)}) copy-start(bf16[512,1,64]{2,0,1:T(8,128)(2,1)S(1)} %get-tuple-element.23) | copy-start | bytes 196612
  5.6 28.9 %copy-start.6 = (bf16[512,1,64]{2,0,1:T(8,128)(2,1)}, bf16[512,1,64]{2,0,1:T(8,128)(2,1)S(1)}, u32[]{:S(2)}) copy-start(bf16[512,1,64]{2,0,1:T(8,128)(2,1)S(1)} %get-tuple-element.24) | copy-start | bytes 196612
  5.7 9.6 %collective-permute-start = (bf16[64,1,256]{2,0,1:T(8,128)(2,1)S(1)}, bf16[64,1,256]{2,0,1:T(8,128)(2,1)S(1)}, u32[]{:S(2)}, u32[]{:S(2)}) collective-permute-start(bf16[64,1,256]{2,0,1:T(8,128)(2,1)S(1)} %fusion.35), channel_id=1, source_target_pairs={{0,8},{8,16},{16,24},{24,32},{32,40},{40,48},{48,56},{56,64},{64,7... | collective-permute-start | bytes 98312 | tf_op jit(solution)/shard_map/ppermute | solution.py:17
  15.3 7.8 %copy-start.21 = (bf16[64,1,128]{2,0,1:T(8,128)(2,1)}, bf16[64,1,128]{2,0,1:T(8,128)(2,1)S(1)}, u32[]{:S(2)}) copy-start(bf16[64,1,128]{2,0,1:T(8,128)(2,1)S(1)} %get-tuple-element.29) | copy-start | bytes 49156
  20.6 29.1 %copy-start.15 = (bf16[512,1024]{1,0:T(8,128)(2,1)S(1)}, bf16[512,1024]{1,0:T(8,128)(2,1)}, u32[]{:S(2)}) copy-start(bf16[512,1024]{1,0:T(8,128)(2,1)} %param.10) | copy-start | bytes 3145732
  23.0 11.4 %collective-permute-start.1 = (f32[66048]{0:T(1024)S(1)}, f32[66048]{0:T(1024)S(1)}, u32[]{:S(2)}, u32[]{:S(2)}) collective-permute-start(f32[66048]{0:T(1024)S(1)} %get-tuple-element.13), channel_id=1, source_target_pairs={{0,8},{8,16},{16,24},{24,32},{32,40},{40,48},{48,56},{56,64},{64,7... | collective-permute-start | bytes 792584 | tf_op jit(solution)/shard_map/ppermute | solution.py:17
  25.5 14.5 %collective-permute-start.6 = (f32[66048]{0:T(1024)S(1)}, f32[66048]{0:T(1024)S(1)}, u32[]{:S(2)}, u32[]{:S(2)}) collective-permute-start(f32[66048]{0:T(1024)S(1)} %get-tuple-element.16), channel_id=1, source_target_pairs={{0,64},{8,72},{16,80},{24,88},{32,96},{40,104},{48,112},{56,120},{... | collective-permute-start | bytes 792584 | tf_op jit(solution)/shard_map/ppermute | solution.py:17
  34.4 11.5 %copy-start.8 = (f32[66048]{0:T(1024)}, f32[66048]{0:T(1024)S(1)}, u32[]{:S(2)}) copy-start(f32[66048]{0:T(1024)S(1)} %collective-permute-done.1) | copy-start | bytes 792580
  34.5 11.4 %copy-start.12 = (f32[66048]{0:T(1024)}, f32[66048]{0:T(1024)S(1)}, u32[]{:S(2)}) copy-start(f32[66048]{0:T(1024)S(1)} %add.166) | copy-start | bytes 792580
  34.5 15.3 %collective-permute-start.2 = (f32[66048]{0:T(1024)S(1)}, f32[66048]{0:T(1024)}, u32[]{:S(2)}, u32[]{:S(2)}) collective-permute-start(f32[66048]{0:T(1024)S(1)} %add.166), channel_id=1, source_target_pairs={{0,16},{8,24},{16,32},{24,40},{32,48},{40,56},{48,64},{56,72},{64,... | collective-permute-start | bytes 792584 | tf_op jit(solution)/shard_map/ppermute | solution.py:17
  40.0 5.9 %copy-start.10 = (f32[66048]{0:T(1024)}, f32[66048]{0:T(1024)S(1)}, u32[]{:S(2)}) copy-start(f32[66048]{0:T(1024)S(1)} %collective-permute-done.6) | copy-start | bytes 792580
  40.9 28.8 %collective-permute-start.7 = (f32[66048]{0:T(1024)}, f32[66048]{0:T(1024)}, u32[]{:S(2)}, u32[]{:S(2)}) collective-permute-start(f32[66048]{0:T(1024)} %add.176), channel_id=1, source_target_pairs={{0,128},{8,136},{16,144},{24,152},{32,160},{40,168},{48,176},{56,1... | collective-permute-start | bytes 792584 | tf_op jit(solution)/shard_map/ppermute | solution.py:17
  52.5 2.0 %copy-start.3 = (f32[2,4,64,64]{3,2,1,0:T(8,128)S(1)}, f32[2,4,64,64]{3,2,1,0:T(8,128)}, u32[]{:S(2)}) copy-start(f32[2,4,64,64]{3,2,1,0:T(8,128)} %copy-done.2) | copy-start | bytes 393220
  54.5 2.9 %copy-start.1 = (pred[512,576]{0,1:T(8,128)(4,1)S(1)}, pred[512,576]{0,1:T(8,128)(4,1)}, u32[]{:S(2)}) copy-start(pred[512,576]{0,1:T(8,128)(4,1)} %get-tuple-element.34) | copy-start | bytes 884740
  54.5 2.9 %copy-start.5 = (bf16[512,1,64]{2,0,1:T(8,128)(2,1)S(1)}, bf16[512,1,64]{2,0,1:T(8,128)(2,1)}, u32[]{:S(2)}) copy-start(bf16[512,1,64]{2,0,1:T(8,128)(2,1)} %copy-done.4) | copy-start | bytes 196612
  54.5 2.9 %copy-start.7 = (bf16[512,1,64]{2,0,1:T(8,128)(2,1)S(1)}, bf16[512,1,64]{2,0,1:T(8,128)(2,1)}, u32[]{:S(2)}) copy-start(bf16[512,1,64]{2,0,1:T(8,128)(2,1)} %copy-done.6) | copy-start | bytes 196612
  59.7 2.6 %copy-start.18 = (bf16[512,128]{1,0:T(8,128)(2,1)S(1)}, bf16[512,128]{1,0:T(8,128)(2,1)}, u32[]{:S(2)}) copy-start(bf16[512,128]{1,0:T(8,128)(2,1)} %param.12) | copy-start | bytes 393220
  59.7 2.6 %copy-start.22 = (bf16[64,1,128]{2,0,1:T(8,128)(2,1)S(1)}, bf16[64,1,128]{2,0,1:T(8,128)(2,1)}, u32[]{:S(2)}) copy-start(bf16[64,1,128]{2,0,1:T(8,128)(2,1)} %copy-done.21) | copy-start | bytes 49156
  67.2 5.5 %copy-start.13 = (f32[66048]{0:T(1024)S(1)}, f32[66048]{0:T(1024)}, u32[]{:S(2)}) copy-start(f32[66048]{0:T(1024)} %copy-done.12) | copy-start | bytes 792580
  69.7 21.8 %copy-start.14 = (f32[512,8,64]{0,2,1:T(8,128)S(1)}, f32[512,8,64]{0,2,1:T(8,128)}, u32[]{:S(2)}) copy-start(f32[512,8,64]{0,2,1:T(8,128)} %get-tuple-element.42) | copy-start | bytes 3145732
  69.7 21.8 %copy-start.24 = (f32[512,8]{0,1:T(8,128)S(1)}, f32[512,8]{0,1:T(8,128)}, u32[]{:S(2)}) copy-start(f32[512,8]{0,1:T(8,128)} %get-tuple-element.41) | copy-start | bytes 49156
  70.9 18.6 %collective-permute-start.8 = (f32[66048]{0:T(1024)S(1)}, f32[66048]{0:T(1024)S(1)}, u32[]{:S(2)}, u32[]{:S(2)}) collective-permute-start(f32[66048]{0:T(1024)S(1)} %add.178), channel_id=1, source_target_pairs={{0,8},{8,16},{16,24},{24,32},{32,40},{40,48},{48,56},{56,64},{64,7... | collective-permute-start | bytes 792584 | tf_op jit(solution)/shard_map/ppermute | solution.py:17
  73.8 21.6 %collective-permute-start.3 = (f32[66048]{0:T(1024)S(1)}, f32[66048]{0:T(1024)S(1)}, u32[]{:S(2)}, u32[]{:S(2)}) collective-permute-start(f32[66048]{0:T(1024)S(1)} %add.170), channel_id=1, source_target_pairs={{0,32},{8,40},{16,48},{24,56},{32,64},{40,72},{48,80},{56,88},{64,... | collective-permute-start | bytes 792584 | tf_op jit(solution)/shard_map/ppermute | solution.py:17
  79.2 29.5 %copy-start.16 = (pred[512,576]{0,1:T(8,128)(4,1)S(1)}, pred[512,576]{0,1:T(8,128)(4,1)}, u32[]{:S(2)}) copy-start(pred[512,576]{0,1:T(8,128)(4,1)} %get-tuple-element.33) | copy-start | bytes 884740
  79.2 29.5 %copy-start.27 = (bf16[8,128,576]{2,1,0:T(8,128)(2,1)S(1)}, bf16[8,128,576]{2,1,0:T(8,128)(2,1)}, u32[]{:S(2)}) copy-start(bf16[8,128,576]{2,1,0:T(8,128)(2,1)} %get-tuple-element.15) | copy-start | bytes 3538948
  89.5 17.0 %collective-permute-start.9 = (f32[66048]{0:T(1024)S(1)}, f32[66048]{0:T(1024)S(1)}, u32[]{:S(2)}, u32[]{:S(2)}) collective-permute-start(f32[66048]{0:T(1024)S(1)} %add.180), channel_id=1, source_target_pairs={{0,16},{8,24},{16,32},{24,40},{32,48},{40,56},{48,64},{56,72},{64,... | collective-permute-start | bytes 792584 | tf_op jit(solution)/shard_map/ppermute | solution.py:17
  95.4 18.0 %collective-permute-start.4 = (f32[66048]{0:T(1024)S(1)}, f32[66048]{0:T(1024)S(1)}, u32[]{:S(2)}, u32[]{:S(2)}) collective-permute-start(f32[66048]{0:T(1024)S(1)} %add.172), channel_id=1, source_target_pairs={{0,64},{8,72},{16,80},{24,88},{32,96},{40,104},{48,112},{56,120},{... | collective-permute-start | bytes 792584 | tf_op jit(solution)/shard_map/ppermute | solution.py:17
  106.6 17.7 %collective-permute-start.10 = (f32[66048]{0:T(1024)S(1)}, f32[66048]{0:T(1024)S(1)}, u32[]{:S(2)}, u32[]{:S(2)}) collective-permute-start(f32[66048]{0:T(1024)S(1)} %add.182), channel_id=1, source_target_pairs={{0,32},{8,40},{16,48},{24,56},{32,64},{40,72},{48,80},{56,88},{64,... | collective-permute-start | bytes 792584 | tf_op jit(solution)/shard_map/ppermute | solution.py:17
  108.7 15.5 %copy-start.11 = (f32[66048]{0:T(1024)S(1)}, f32[66048]{0:T(1024)}, u32[]{:S(2)}) copy-start(f32[66048]{0:T(1024)} %copy-done.10) | copy-start | bytes 792580
  112.5 12.9 %copy-start.9 = (f32[66048]{0:T(1024)S(1)}, f32[66048]{0:T(1024)}, u32[]{:S(2)}) copy-start(f32[66048]{0:T(1024)} %copy-done.8) | copy-start | bytes 792580
  113.4 11.9 %collective-permute-start.5 = (f32[66048]{0:T(1024)S(1)}, f32[66048]{0:T(1024)S(1)}, u32[]{:S(2)}, u32[]{:S(2)}) collective-permute-start(f32[66048]{0:T(1024)S(1)} %add.174), channel_id=1, source_target_pairs={{0,128},{8,136},{16,144},{24,152},{32,160},{40,168},{48,176},{56,1... | collective-permute-start | bytes 792584 | tf_op jit(solution)/shard_map/ppermute | solution.py:17
  127.5 0.7 copy-start.20
  127.5 0.7 copy-start.25
  127.5 0.7 copy-start.26
  127.5 0.9 copy-start.19
  127.5 0.9 copy-start.23
  127.5 1.7 %copy-start.29 = (f32[128,8,512]{2,0,1:T(8,128)S(1)}, f32[128,8,512]{2,0,1:T(8,128)}, u32[]{:S(2)}) copy-start(f32[128,8,512]{2,0,1:T(8,128)} %fusion.10) | copy-start | bytes 6291460

commit v16 on v11

--- a/solution.py
+++ b/solution.py
@@ -225,6 +225,11 @@
         ext_values,
         preferred_element_type=jnp.float32,
     )
+    head_factor = factor[None, :, :, None]
+    local_num = head_factor * window_num + (1.0 - head_factor) * near_num
+    local_den = factor[None] * jnp.transpose(window_sum, (2, 0, 1)) + (1.0 - factor[None]) * (
+        jnp.transpose(near_sum, (2, 0, 1))
+    )
     state_now = prior_state + before_state[0]
     norm_now = prior_norm + before_norm[0]
     state_high, state_rest = split_parts(state_now)
@@ -239,11 +244,8 @@
     far_sum = far_sum + jnp.einsum(
         "igkf,gkf->igk", phi_query, norm_rest, preferred_element_type=jnp.float32
     )
-    head_factor = factor[None, :, :, None]
-    numerator = head_factor * window_num + (1.0 - head_factor) * (near_num + far_num)
-    denominator = factor[None] * jnp.transpose(window_sum, (2, 0, 1)) + (1.0 - factor[None]) * (
-        jnp.transpose(near_sum, (2, 0, 1)) + far_sum
-    )
+    numerator = local_num + (1.0 - head_factor) * far_num
+    denominator = local_den + (1.0 - factor[None]) * far_sum
     outputs = (numerator / denominator[..., None]).astype(jnp.bfloat16)
     result = outputs.reshape(tokens, heads * head_dim)
     return lax.all_to_all(result, "head", split_axis=0, concat_axis=1, tiled=True)

time: 153 us -> 153 us (level)
  no operation moved by 1% of the time
where the time goes in v16:
time: 153 us; the launch traced here: 152 us
  waiting for transfers between devices  38.3 us (25%)
  starting transfers between devices  36.9 us (24%)
  other arithmetic  22.7 us (15%)
  blocking collectives  20.2 us (13%)
  matrix products  18.5 us (12%)
  local copies, waits for them, and re-layouts  10.7 us (7%)
  Pallas kernels  4.56 us (3%)
    ppermute x12, waiting for transfers between devices, passed_along(): lax.ppermute(value, axis, [(source, source + steps) for source in range(f...  38.3 us
    ppermute x12, starting transfers between devices, passed_along(): lax.ppermute(value, axis, [(source, source + steps) for source in range(f...  36.9 us
    all_to_all x1, blocking collectives, body(): lax.all_to_all(result, 'head', split_axis=0, concat_axis=1, tiled=True)  20.2 us
    unnamed x62, local copies, waits for them, and re-layouts  6.41 us
    another operation x5, other arithmetic  5.6 us
    add x8, other arithmetic, body(): inclusive = inclusive + received  4.76 us
    pallas_call x1, Pallas kernels, key_features(): pl.pallas_call(kernel, grid=(1,), in_specs=[pl.BlockSpec((rows, dim), lam...  4.56 us
    dot_general x1, matrix products, body(): jnp.einsum('gkij,jgd->igkd', affinity.astype(jnp.bfloat16), ext_values, p...  3.73 us
  transfers between devices with their start and end apart: 12, of which 7 were waited for; matrix products, arithmetic and copies ran while one was open for 20% of the time, Pallas kernels for 0%

profile of v16, /device:TPU:2, one launch (start us, length us, event | category | flops | bytes accessed | tf_op | source)
XLA Modules:
  0.0 152.4 jit_solution(15377900692958718030)
XLA Ops:
  0.0 0.7 and_select_fusion.1
  0.8 0.8 fusion.35
  1.6 0.9 bitcast_convert_fusion
  2.5 0.8 multiply_cosine_fusion.1
  3.3 0.8 fusion.43
  4.3 0.5 copy-done.2
  4.9 3.8 %collective-permute-start.1 = (bf16[64,1,128]{2,0,1:T(8,128)(2,1)S(1)}, bf16[64,1,128]{2,0,1:T(8,128)(2,1)S(1)}, u32[]{:S(2)}, u32[]{:S(2)}) collective-permute-start(bf16[64,1,128]{2,0,1:T(8,128)(2,1)S(1)} %pad_maximum_fusion.15), channel_id=1, source_target_pairs={{0,8},{8,16},{16,24},{24,32},{32,40},{40,48},{48,56},{56,64},{64,7... | collective-permute-start | bytes 49160 | tf_op jit(solution)/shard_map/ppermute | solution.py:17
  8.8 3.8 %collective-permute-start = (bf16[64,1,128]{2,0,1:T(8,128)(2,1)S(1)}, bf16[64,1,128]{2,0,1:T(8,128)(2,1)S(1)}, u32[]{:S(2)}, u32[]{:S(2)}) collective-permute-start(bf16[64,1,128]{2,0,1:T(8,128)(2,1)S(1)} %slice_bitcast_fusion), channel_id=1, source_target_pairs={{0,8},{8,16},{16,24},{24,32},{32,40},{40,48},{48,56},{56,64},{64,7... | collective-permute-start | bytes 49160 | tf_op jit(solution)/shard_map/ppermute | solution.py:17
  12.6 0.6 or_convert_fusion.mask_ref
  13.2 0.6 broadcast_subtract_fusion
  13.8 0.6 collective-permute-done.1
  14.4 0.8 fusion.67.k_ref
  15.1 1.4 collective-permute-done
  16.5 0.7 fusion.33.v_ref
  17.2 4.6 %shard_map.100 = (bf16[8,128,576]{2,1,0:T(8,128)(2,1)}, f32[8,128,128]{2,1,0:T(8,128)}, f32[8,128,1]{2,1,0:T(8,128)}) custom-call(bf16[576,128]{1,0:T(8,128)(2,1)} %fusion.67.k_ref, bf16[8,64,128]{2,1,0:T(8,128)(2,1)} %bitcast.149, bf16[576,128]{1,0:T(8,128)(2,1)} %fusion.33.v_ref, f32[1,576]{1,0:T(1,128)} %or_convert_fusion.mask_ref), custom_call_target="tpu_custom_call" | custom-call | tf_op jit(solution)/shard_map/pallas_call | solution.py:104
  21.8 1.0 slice.59
  22.7 1.9 %collective-permute-start.2 = (f32[66048]{0:T(1024)S(1)}, f32[66048]{0:T(1024)}, u32[]{:S(2)}, u32[]{:S(2)}) collective-permute-start(f32[66048]{0:T(1024)S(1)} %slice.59), channel_id=1, source_target_pairs={{0,8},{8,16},{16,24},{24,32},{32,40},{40,48},{48,56},{56,64},{64,7... | collective-permute-start | bytes 792584 | tf_op jit(solution)/shard_map/ppermute | solution.py:17
  24.7 1.2 fusion.21
  25.8 1.8 %reduce.4 = f32[8,128]{1,0:T(8,128)} reduce(f32[8,128,1]{2,1,0:T(8,128)} %get-tuple-element.12, f32[]{:T(128)} %constant.74), dimensions={2}, to_apply=%get-tuple-element.12.reduce_sub_computation | reduce | bytes 8196 | tf_op jit(solution)/shard_map/pallas_call | solution.py:104
  27.7 6.2 %collective-permute-done.2 = f32[66048]{0:T(1024)} collective-permute-done((f32[66048]{0:T(1024)S(1)}, f32[66048]{0:T(1024)}, u32[]{:S(2)}, u32[]{:S(2)}) %collective-permute-start.2) | collective-permute-done | bytes 264224 | tf_op jit(solution)/shard_map/ppermute | solution.py:17
  33.9 0.5 copy.26
  34.5 0.3 fusion.69
  34.7 1.9 %copy.45 = f32[512,8,64]{2,0,1:T(8,128)} copy(f32[512,8,64]{0,2,1:T(8,128)S(1)} %get-tuple-element.18) | data formatting | bytes 2097152
  36.7 2.0 %copy.46 = f32[512,8,64]{2,0,1:T(8,128)} copy(f32[512,8,64]{0,2,1:T(8,128)S(1)} %get-tuple-element.17) | data formatting | bytes 2097152
  38.6 1.0 slice_add_fusion
  39.6 3.4 %collective-permute-start.7 = (f32[66048]{0:T(1024)S(1)}, f32[66048]{0:T(1024)S(1)}, u32[]{:S(2)}, u32[]{:S(2)}) collective-permute-start(f32[66048]{0:T(1024)S(1)} %get-tuple-element.22), channel_id=1, source_target_pairs={{0,64},{8,72},{16,80},{24,88},{32,96},{40,104},{48,112},{56,120},{... | collective-permute-start | bytes 792584 | tf_op jit(solution)/shard_map/ppermute | solution.py:17
  43.1 2.8 %collective-permute-start.3 = (f32[66048]{0:T(1024)S(1)}, f32[66048]{0:T(1024)S(1)}, u32[]{:S(2)}, u32[]{:S(2)}) collective-permute-start(f32[66048]{0:T(1024)S(1)} %get-tuple-element.21), channel_id=1, source_target_pairs={{0,16},{8,24},{16,32},{24,40},{32,48},{40,56},{48,64},{56,72},{64,... | collective-permute-start | bytes 792584 | tf_op jit(solution)/shard_map/ppermute | solution.py:17
  46.0 2.9 %subtract_convert_fusion = (bf16[512,8,64]{2,0,1:T(8,128)(2,1)S(1)}, bf16[512,8,64]{2,0,1:T(8,128)(2,1)S(1)}) fusion(f32[512,8,64]{2,0,1:T(8,128)} %copy.46, f32[512,8,64]{2,0,1:T(8,128)} %copy.45, f32[512,64]{1,0:T(8,128)S(1)} %bitcast.142, f32[512,64]{1,0:T(8,128)S(1)} %bitcast.140), kind=kLoop, calls=%fused_computation.25 | loop fusion | flops 2097152 | bytes 3407872 | tf_op jit(solution)/shard_map/convert.4
  48.8 2.3 %fusion.2 = (f32[8,512]{1,0:T(8,128)S(1)}, f32[576,512,8]{1,0,2:T(8,128)S(1)}) fusion(pred[512,576]{0,1:T(8,128)(4,1)S(1)} %copy-done.1, bf16[512,8,64]{2,0,1:T(8,128)(2,1)S(1)} %get-tuple-element.16, bf16[512,8,64]{2,0,1:T(8,128)(2,1)S(1)} %get-tuple-element.15, bf16[512,1,64]{2,0,1:T(8,128)(2,1)S(1)} %copy-done.8, bf16[512,1,64]{2,0,1:T(8,128)(2,1)S(1)} %copy-done.6, ...), kind=kOutput, calls=%fused_computation.4 | convolution fusion | flops 613593088 | bytes 10944512 | tf_op jit(solution)/shard_map/igkd,jgd->gkij/dot_general | solution.py:206
  51.2 2.5 %fusion.5 = f32[8,512]{1,0:T(8,128)} fusion(f32[576,512,8]{1,0,2:T(8,128)S(1)} %get-tuple-element.36, f32[8,512]{1,0:T(8,128)S(1)} %get-tuple-element.35, pred[512,576]{0,1:T(8,128)(4,1)S(1)} %copy-done.1), kind=kLoop, calls=%fused_computation.9 | loop fusion | flops 9433088 | bytes 9764864 | tf_op jit(solution)/shard_map/reduce_sum | solution.py:212
  53.7 3.5 %fusion.10 = f32[128,8,512]{2,0,1:T(8,128)} fusion(f32[576,512,8]{1,0,2:T(8,128)S(1)} %get-tuple-element.36, f32[8,512]{1,0:T(8,128)S(1)} %get-tuple-element.35, pred[512,576]{0,1:T(8,128)(4,1)S(1)} %copy-done.1, bf16[512,1,128]{2,0,1:T(8,128)(2,1)S(1)} %bitcast.147, bf16[64,1,128]{2,0,1:T(8,128)(2,1)S(1)} %copy-done.23), kind=kOutput, calls=%fused_computation.14 | convolution fusion | flops 613711872 | bytes 11993088 | tf_op jit(solution)/shard_map/gkij,jgd->igkd/dot_general | solution.py:216
  57.2 0.8 add.178
  58.0 1.9 %collective-permute-start.8 = (f32[66048]{0:T(1024)}, f32[66048]{0:T(1024)S(1)}, u32[]{:S(2)}, u32[]{:S(2)}) collective-permute-start(f32[66048]{0:T(1024)} %add.178), channel_id=1, source_target_pairs={{0,128},{8,136},{16,144},{24,152},{32,160},{40,168},{48,176},{56,1... | collective-permute-start | bytes 792584 | tf_op jit(solution)/shard_map/ppermute | solution.py:17
  60.0 0.7 copy-done.11
  60.7 0.7 add.172
  61.4 5.3 %collective-permute-start.4 = (f32[66048]{0:T(1024)}, f32[66048]{0:T(1024)}, u32[]{:S(2)}, u32[]{:S(2)}) collective-permute-start(f32[66048]{0:T(1024)} %add.172), channel_id=1, source_target_pairs={{0,32},{8,40},{16,48},{24,56},{32,64},{40,72},{48,80},{56,88},{64,... | collective-permute-start | bytes 792584 | tf_op jit(solution)/shard_map/ppermute | solution.py:17
  66.7 2.5 %fusion.70 = (f32[512,8]{0,1:T(8,128)}, f32[512,8,64]{0,2,1:T(8,128)}) fusion(bf16[8,128,64]{1,2,0:T(8,128)(2,1)S(1)} %copy-done, bf16[512,8,64]{2,0,1:T(8,128)(2,1)S(1)} %get-tuple-element.16, bf16[512,8,64]{2,0,1:T(8,128)(2,1)S(1)} %get-tuple-element.15), kind=kOutput, calls=%fused_computation.127 | convolution fusion | flops 69992512 | bytes 2244608 | tf_op jit(solution)/shard_map/sub | solution.py:71
  69.2 1.5 fusion.71
  70.7 1.1 add.180
  71.7 1.9 %collective-permute-start.9 = (f32[66048]{0:T(1024)S(1)}, f32[66048]{0:T(1024)S(1)}, u32[]{:S(2)}, u32[]{:S(2)}) collective-permute-start(f32[66048]{0:T(1024)S(1)} %add.180), channel_id=1, source_target_pairs={{0,8},{8,16},{16,24},{24,32},{32,40},{40,48},{48,56},{56,64},{64,7... | collective-permute-start | bytes 792584 | tf_op jit(solution)/shard_map/ppermute | solution.py:17
  73.7 1.7 %collective-permute-done.4 = f32[66048]{0:T(1024)} collective-permute-done((f32[66048]{0:T(1024)}, f32[66048]{0:T(1024)}, u32[]{:S(2)}, u32[]{:S(2)}) %collective-permute-start.4) | collective-permute-done | bytes 264224 | tf_op jit(solution)/shard_map/ppermute | solution.py:17
  75.3 1.1 add.174
  76.4 2.9 %collective-permute-start.5 = (f32[66048]{0:T(1024)S(1)}, f32[66048]{0:T(1024)S(1)}, u32[]{:S(2)}, u32[]{:S(2)}) collective-permute-start(f32[66048]{0:T(1024)S(1)} %add.174), channel_id=1, source_target_pairs={{0,64},{8,72},{16,80},{24,88},{32,96},{40,104},{48,112},{56,120},{... | collective-permute-start | bytes 792584 | tf_op jit(solution)/shard_map/ppermute | solution.py:17
  79.4 1.1 divide_convert_fusion
  80.5 5.5 %collective-permute-done.9 = f32[66048]{0:T(1024)S(1)} collective-permute-done((f32[66048]{0:T(1024)S(1)}, f32[66048]{0:T(1024)S(1)}, u32[]{:S(2)}, u32[]{:S(2)}) %collective-permute-start.9) | collective-permute-done | bytes 264224 | tf_op jit(solution)/shard_map/ppermute | solution.py:17
  86.0 3.8 %collective-permute-start.10 = (f32[66048]{0:T(1024)S(1)}, f32[66048]{0:T(1024)S(1)}, u32[]{:S(2)}, u32[]{:S(2)}) collective-permute-start(f32[66048]{0:T(1024)S(1)} %add.182), channel_id=1, source_target_pairs={{0,16},{8,24},{16,32},{24,40},{32,48},{40,56},{48,64},{56,72},{64,... | collective-permute-start | bytes 792584 | tf_op jit(solution)/shard_map/ppermute | solution.py:17
  89.9 1.5 %collective-permute-start.6 = (f32[66048]{0:T(1024)S(1)}, f32[66048]{0:T(1024)S(1)}, u32[]{:S(2)}, u32[]{:S(2)}) collective-permute-start(f32[66048]{0:T(1024)S(1)} %add.176), channel_id=1, source_target_pairs={{0,128},{8,136},{16,144},{24,152},{32,160},{40,168},{48,176},{56,1... | collective-permute-start | bytes 792584 | tf_op jit(solution)/shard_map/ppermute | solution.py:17
  91.4 3.7 %select_reduce_fusion = (f32[8,512]{1,0:T(8,128)S(1)}, bf16[8,512,576]{1,2,0:T(8,128)(2,1)}) fusion(pred[512,576]{0,1:T(8,128)(4,1)S(1)} %copy-done.15, bf16[8,128,576]{2,1,0:T(8,128)(2,1)S(1)} %copy-done.27, bf16[512,8,64]{0,2,1:T(8,128)(2,1)S(1)} %get-tuple-element.43, bf16[512,8,64]{0,2,1:T(8,128)(2,1)S(1)} %get-tuple-element.44), kind=kOutput, calls=%fused_computation.7 | convolution fusion | flops 613150720 | bytes 7258112 | tf_op jit(solution)/shard_map/igkf,gkfj->gkij/dot_general | solution.py:213
  95.1 7.3 %collective-permute-done.10 = f32[66048]{0:T(1024)S(1)} collective-permute-done((f32[66048]{0:T(1024)S(1)}, f32[66048]{0:T(1024)S(1)}, u32[]{:S(2)}, u32[]{:S(2)}) %collective-permute-start.10) | collective-permute-done | bytes 264224 | tf_op jit(solution)/shard_map/ppermute | solution.py:17
  102.4 3.7 %collective-permute-start.11 = (f32[66048]{0:T(1024)S(1)}, f32[66048]{0:T(1024)S(1)}, u32[]{:S(2)}, u32[]{:S(2)}) collective-permute-start(f32[66048]{0:T(1024)S(1)} %add.184), channel_id=1, source_target_pairs={{0,32},{8,40},{16,48},{24,56},{32,64},{40,72},{48,80},{56,88},{64,... | collective-permute-start | bytes 792584 | tf_op jit(solution)/shard_map/ppermute | solution.py:17
  106.2 1.2 add_add_fusion.1
  107.3 15.7 %collective-permute-done.11 = f32[66048]{0:T(1024)S(1)} collective-permute-done((f32[66048]{0:T(1024)S(1)}, f32[66048]{0:T(1024)S(1)}, u32[]{:S(2)}, u32[]{:S(2)}) %collective-permute-start.11) | collective-permute-done | bytes 264224 | tf_op jit(solution)/shard_map/ppermute | solution.py:17
  123.2 0.2 copy.31
  123.5 0.4 fusion.25
  123.9 0.4 fusion.31
  124.4 0.2 fusion.47
  124.6 0.2 fusion.45
  125.1 0.2 copy-done.16
  125.3 0.8 copy-done.29
  126.1 3.7 %fusion.15 = bf16[512,1,8,128]{0,3,2,1:T(8,128)(2,1)S(1)} fusion(f32[128,8,512]{2,0,1:T(8,128)S(1)} %copy-done.29, f32[8,128,512]{2,1,0:T(8,128)S(1)} %fusion.31, f32[8,128,512]{2,1,0:T(8,128)S(1)} %fusion.25, bf16[8,512,576]{1,2,0:T(8,128)(2,1)} %get-tuple-element.42, pred[512,576]{0,1:T(8,128)(4,1)S(1)} %copy-done.16, f32[512,8]{0,1:T(8,128)S(1)} %fusion.37, ...), kind=kOutput, calls=%fused_computation.19 | convolution fusion | flops 610828288 | bytes 12517440 | tf_op jit(solution)/shard_map/gkij,jgd->igkd/dot_general | solution.py:222
  129.9 0.8 copy.35
  130.6 0.5 all_to_all.14
  131.1 20.2 %all_to_all.19 = bf16[8,64,1024]{2,1,0:T(8,128)(2,1)S(1)} all-to-all(bf16[8,64,1024]{2,1,0:T(8,128)(2,1)S(1)} %all_to_all.14), channel_id=1, replica_groups=mesh['seq'=32,'head'=8] {'head'}, dimensions={0} | all-to-all | bytes 2097152 | tf_op jit(solution)/shard_map/all_to_all | solution.py:251
  151.4 1.1 copy.47
  (76 shorter events, 1.1 us)
Async XLA Ops:
  0.0 66.7 %copy-start = (bf16[8,128,64]{1,2,0:T(8,128)(2,1)S(1)}, bf16[8,128,64]{1,2,0:T(8,128)(2,1)}, u32[]{:S(2)}) copy-start(bf16[8,128,64]{1,2,0:T(8,128)(2,1)} %param.14) | copy-start | bytes 393220
  0.0 8.8 %copy-start.17 = (bf16[512,128]{1,0:T(8,128)(2,1)S(1)}, bf16[512,128]{1,0:T(8,128)(2,1)}, u32[]{:S(2)}) copy-start(bf16[512,128]{1,0:T(8,128)(2,1)} %param.12) | copy-start | bytes 393220
  0.0 13.2 %copy-start.28 = (f32[8]{0:T(128)S(1)}, f32[8]{0:T(128)}, u32[]{:S(2)}) copy-start(f32[8]{0:T(128)} %param.16) | copy-start | bytes 100
  4.1 0.7 copy-start.2
  4.2 29.8 %copy-start.14 = (bf16[512,1024]{1,0:T(8,128)(2,1)S(1)}, bf16[512,1024]{1,0:T(8,128)(2,1)}, u32[]{:S(2)}) copy-start(bf16[512,1024]{1,0:T(8,128)(2,1)} %param.10) | copy-start | bytes 3145732
  4.9 22.8 %copy-start.5 = (bf16[512,1,64]{2,0,1:T(8,128)(2,1)}, bf16[512,1,64]{2,0,1:T(8,128)(2,1)S(1)}, u32[]{:S(2)}) copy-start(bf16[512,1,64]{2,0,1:T(8,128)(2,1)S(1)} %get-tuple-element.19) | copy-start | bytes 196612
  4.9 22.8 %copy-start.7 = (bf16[512,1,64]{2,0,1:T(8,128)(2,1)}, bf16[512,1,64]{2,0,1:T(8,128)(2,1)S(1)}, u32[]{:S(2)}) copy-start(bf16[512,1,64]{2,0,1:T(8,128)(2,1)S(1)} %get-tuple-element.20) | copy-start | bytes 196612
  4.9 9.4 %collective-permute-start.1 = (bf16[64,1,128]{2,0,1:T(8,128)(2,1)S(1)}, bf16[64,1,128]{2,0,1:T(8,128)(2,1)S(1)}, u32[]{:S(2)}, u32[]{:S(2)}) collective-permute-start(bf16[64,1,128]{2,0,1:T(8,128)(2,1)S(1)} %pad_maximum_fusion.15), channel_id=1, source_target_pairs={{0,8},{8,16},{16,24},{24,32},{32,40},{40,48},{48,56},{56,64},{64,7... | collective-permute-start | bytes 49160 | tf_op jit(solution)/shard_map/ppermute | solution.py:17
  8.8 7.7 %collective-permute-start = (bf16[64,1,128]{2,0,1:T(8,128)(2,1)S(1)}, bf16[64,1,128]{2,0,1:T(8,128)(2,1)S(1)}, u32[]{:S(2)}, u32[]{:S(2)}) collective-permute-start(bf16[64,1,128]{2,0,1:T(8,128)(2,1)S(1)} %slice_bitcast_fusion), channel_id=1, source_target_pairs={{0,8},{8,16},{16,24},{24,32},{32,40},{40,48},{48,56},{56,64},{64,7... | collective-permute-start | bytes 49160 | tf_op jit(solution)/shard_map/ppermute | solution.py:17
  16.5 5.2 %copy-start.22 = (bf16[64,1,128]{2,0,1:T(8,128)(2,1)}, bf16[64,1,128]{2,0,1:T(8,128)(2,1)S(1)}, u32[]{:S(2)}) copy-start(bf16[64,1,128]{2,0,1:T(8,128)(2,1)S(1)} %collective-permute-done) | copy-start | bytes 49156
  22.7 11.2 %collective-permute-start.2 = (f32[66048]{0:T(1024)S(1)}, f32[66048]{0:T(1024)}, u32[]{:S(2)}, u32[]{:S(2)}) collective-permute-start(f32[66048]{0:T(1024)S(1)} %slice.59), channel_id=1, source_target_pairs={{0,8},{8,16},{16,24},{24,32},{32,40},{40,48},{48,56},{56,64},{64,7... | collective-permute-start | bytes 792584 | tf_op jit(solution)/shard_map/ppermute | solution.py:17
  36.7 2.0 %copy-start.4 = (f32[8,128,128]{2,1,0:T(8,128)S(1)}, f32[8,128,128]{2,1,0:T(8,128)}, u32[]{:S(2)}) copy-start(f32[8,128,128]{2,1,0:T(8,128)} %get-tuple-element.9) | copy-start | bytes 1572868
  36.7 2.0 %copy-start.21 = (f32[8,128]{1,0:T(8,128)S(1)}, f32[8,128]{1,0:T(8,128)}, u32[]{:S(2)}) copy-start(f32[8,128]{1,0:T(8,128)} %reduce.4) | copy-start | bytes 12292
  36.7 9.2 %copy-start.3 = (f32[2,4,64,64]{3,2,1,0:T(8,128)S(1)}, f32[2,4,64,64]{3,2,1,0:T(8,128)}, u32[]{:S(2)}) copy-start(f32[2,4,64,64]{3,2,1,0:T(8,128)} %copy-done.2) | copy-start | bytes 393220
  39.6 17.6 %collective-permute-start.7 = (f32[66048]{0:T(1024)S(1)}, f32[66048]{0:T(1024)S(1)}, u32[]{:S(2)}, u32[]{:S(2)}) collective-permute-start(f32[66048]{0:T(1024)S(1)} %get-tuple-element.22), channel_id=1, source_target_pairs={{0,64},{8,72},{16,80},{24,88},{32,96},{40,104},{48,112},{56,120},{... | collective-permute-start | bytes 792584 | tf_op jit(solution)/shard_map/ppermute | solution.py:17
  43.1 16.9 %collective-permute-start.3 = (f32[66048]{0:T(1024)S(1)}, f32[66048]{0:T(1024)S(1)}, u32[]{:S(2)}, u32[]{:S(2)}) collective-permute-start(f32[66048]{0:T(1024)S(1)} %get-tuple-element.21), channel_id=1, source_target_pairs={{0,16},{8,24},{16,32},{24,40},{32,48},{40,56},{48,64},{56,72},{64,... | collective-permute-start | bytes 792584 | tf_op jit(solution)/shard_map/ppermute | solution.py:17
  45.9 2.9 %copy-start.1 = (pred[512,576]{0,1:T(8,128)(4,1)S(1)}, pred[512,576]{0,1:T(8,128)(4,1)}, u32[]{:S(2)}) copy-start(pred[512,576]{0,1:T(8,128)(4,1)} %get-tuple-element.28) | copy-start | bytes 884740
  45.9 2.9 %copy-start.6 = (bf16[512,1,64]{2,0,1:T(8,128)(2,1)S(1)}, bf16[512,1,64]{2,0,1:T(8,128)(2,1)}, u32[]{:S(2)}) copy-start(bf16[512,1,64]{2,0,1:T(8,128)(2,1)} %copy-done.5) | copy-start | bytes 196612
  45.9 2.9 %copy-start.8 = (bf16[512,1,64]{2,0,1:T(8,128)(2,1)S(1)}, bf16[512,1,64]{2,0,1:T(8,128)(2,1)}, u32[]{:S(2)}) copy-start(bf16[512,1,64]{2,0,1:T(8,128)(2,1)} %copy-done.7) | copy-start | bytes 196612
  51.2 2.6 %copy-start.18 = (bf16[512,128]{1,0:T(8,128)(2,1)S(1)}, bf16[512,128]{1,0:T(8,128)(2,1)}, u32[]{:S(2)}) copy-start(bf16[512,128]{1,0:T(8,128)(2,1)} %param.12) | copy-start | bytes 393220
  51.2 2.6 %copy-start.23 = (bf16[64,1,128]{2,0,1:T(8,128)(2,1)S(1)}, bf16[64,1,128]{2,0,1:T(8,128)(2,1)}, u32[]{:S(2)}) copy-start(bf16[64,1,128]{2,0,1:T(8,128)(2,1)} %copy-done.22) | copy-start | bytes 49156
  57.2 9.5 %copy-start.9 = (f32[66048]{0:T(1024)}, f32[66048]{0:T(1024)S(1)}, u32[]{:S(2)}) copy-start(f32[66048]{0:T(1024)S(1)} %collective-permute-done.7) | copy-start | bytes 792580
  58.0 12.6 %collective-permute-start.8 = (f32[66048]{0:T(1024)}, f32[66048]{0:T(1024)S(1)}, u32[]{:S(2)}, u32[]{:S(2)}) collective-permute-start(f32[66048]{0:T(1024)} %add.178), channel_id=1, source_target_pairs={{0,128},{8,136},{16,144},{24,152},{32,160},{40,168},{48,176},{56,1... | collective-permute-start | bytes 792584 | tf_op jit(solution)/shard_map/ppermute | solution.py:17
  60.0 0.7 copy-start.11
  61.4 13.9 %collective-permute-start.4 = (f32[66048]{0:T(1024)}, f32[66048]{0:T(1024)}, u32[]{:S(2)}, u32[]{:S(2)}) collective-permute-start(f32[66048]{0:T(1024)} %add.172), channel_id=1, source_target_pairs={{0,32},{8,40},{16,48},{24,56},{32,64},{40,72},{48,80},{56,88},{64,... | collective-permute-start | bytes 792584 | tf_op jit(solution)/shard_map/ppermute | solution.py:17
  70.7 8.7 %copy-start.13 = (f32[512,8,64]{0,2,1:T(8,128)S(1)}, f32[512,8,64]{0,2,1:T(8,128)}, u32[]{:S(2)}) copy-start(f32[512,8,64]{0,2,1:T(8,128)} %get-tuple-element.38) | copy-start | bytes 3145732
  71.7 14.3 %collective-permute-start.9 = (f32[66048]{0:T(1024)S(1)}, f32[66048]{0:T(1024)S(1)}, u32[]{:S(2)}, u32[]{:S(2)}) collective-permute-start(f32[66048]{0:T(1024)S(1)} %add.180), channel_id=1, source_target_pairs={{0,8},{8,16},{16,24},{24,32},{32,40},{40,48},{48,56},{56,64},{64,7... | collective-permute-start | bytes 792584 | tf_op jit(solution)/shard_map/ppermute | solution.py:17
  76.4 13.4 %collective-permute-start.5 = (f32[66048]{0:T(1024)S(1)}, f32[66048]{0:T(1024)S(1)}, u32[]{:S(2)}, u32[]{:S(2)}) collective-permute-start(f32[66048]{0:T(1024)S(1)} %add.174), channel_id=1, source_target_pairs={{0,64},{8,72},{16,80},{24,88},{32,96},{40,104},{48,112},{56,120},{... | collective-permute-start | bytes 792584 | tf_op jit(solution)/shard_map/ppermute | solution.py:17
  79.4 12.1 %copy-start.15 = (pred[512,576]{0,1:T(8,128)(4,1)S(1)}, pred[512,576]{0,1:T(8,128)(4,1)}, u32[]{:S(2)}) copy-start(pred[512,576]{0,1:T(8,128)(4,1)} %get-tuple-element.27) | copy-start | bytes 884740
  79.4 12.1 %copy-start.27 = (bf16[8,128,576]{2,1,0:T(8,128)(2,1)S(1)}, bf16[8,128,576]{2,1,0:T(8,128)(2,1)}, u32[]{:S(2)}) copy-start(bf16[8,128,576]{2,1,0:T(8,128)(2,1)} %get-tuple-element.11) | copy-start | bytes 3538948
  86.0 16.4 %collective-permute-start.10 = (f32[66048]{0:T(1024)S(1)}, f32[66048]{0:T(1024)S(1)}, u32[]{:S(2)}, u32[]{:S(2)}) collective-permute-start(f32[66048]{0:T(1024)S(1)} %add.182), channel_id=1, source_target_pairs={{0,16},{8,24},{16,32},{24,40},{32,48},{40,56},{48,64},{56,72},{64,... | collective-permute-start | bytes 792584 | tf_op jit(solution)/shard_map/ppermute | solution.py:17
  89.9 16.3 %collective-permute-start.6 = (f32[66048]{0:T(1024)S(1)}, f32[66048]{0:T(1024)S(1)}, u32[]{:S(2)}, u32[]{:S(2)}) collective-permute-start(f32[66048]{0:T(1024)S(1)} %add.176), channel_id=1, source_target_pairs={{0,128},{8,136},{16,144},{24,152},{32,160},{40,168},{48,176},{56,1... | collective-permute-start | bytes 792584 | tf_op jit(solution)/shard_map/ppermute | solution.py:17
  91.4 14.7 %copy-start.12 = (f32[66048]{0:T(1024)S(1)}, f32[66048]{0:T(1024)}, u32[]{:S(2)}) copy-start(f32[66048]{0:T(1024)} %copy-done.11) | copy-start | bytes 792580
  95.1 27.9 %copy-start.10 = (f32[66048]{0:T(1024)S(1)}, f32[66048]{0:T(1024)}, u32[]{:S(2)}) copy-start(f32[66048]{0:T(1024)} %copy-done.9) | copy-start | bytes 792580
  102.4 20.6 %collective-permute-start.11 = (f32[66048]{0:T(1024)S(1)}, f32[66048]{0:T(1024)S(1)}, u32[]{:S(2)}, u32[]{:S(2)}) collective-permute-start(f32[66048]{0:T(1024)S(1)} %add.184), channel_id=1, source_target_pairs={{0,32},{8,40},{16,48},{24,56},{32,64},{40,72},{48,80},{56,88},{64,... | collective-permute-start | bytes 792584 | tf_op jit(solution)/shard_map/ppermute | solution.py:17
  124.3 0.7 copy-start.20
  124.3 0.7 copy-start.25
  124.3 0.7 copy-start.26
  124.3 1.0 copy-start.16
  124.3 1.0 copy-start.19
  124.4 1.0 copy-start.24
  124.4 1.8 %copy-start.29 = (f32[128,8,512]{2,0,1:T(8,128)S(1)}, f32[128,8,512]{2,0,1:T(8,128)}, u32[]{:S(2)}) copy-start(f32[128,8,512]{2,0,1:T(8,128)} %fusion.10) | copy-start | bytes 6291460

commit v17 on v16

--- a/solution.py
+++ b/solution.py
@@ -230,6 +230,7 @@
     local_den = factor[None] * jnp.transpose(window_sum, (2, 0, 1)) + (1.0 - factor[None]) * (
         jnp.transpose(near_sum, (2, 0, 1))
     )
+    local_num, local_den = lax.optimization_barrier((local_num, local_den))
     state_now = prior_state + before_state[0]
     norm_now = prior_norm + before_norm[0]
     state_high, state_rest = split_parts(state_now)

time: 153 us -> 152 us (level)
  waiting for transfers between devices: 38.3 us -> 46.6 us
  matrix products: 18.5 us -> 13.9 us
  other arithmetic: 22.7 us -> 20.1 us
  starting transfers between devices: 36.9 us -> 35.1 us
    ppermute x12, waiting for transfers between devices: 38.3 us -> 46.6 us  [passed_along(): lax.ppermute(value, axis, [(source, source + steps) for source in range(f...]
    dot_general x1, matrix products: 3.69 us -> 1.6 us  [body(): jnp.einsum('igkf,gkfj->gkij', phi_query, phi_key, preferred_element_type=...]
    ppermute x12, starting transfers between devices: 36.9 us -> 35.1 us  [passed_along(): lax.ppermute(value, axis, [(source, source + steps) for source in range(f...]
    unnamed x62 -> x50, local copies, waits for them, and re-layouts: 6.41 us -> 5.57 us
where the time goes in v17:
time: 152 us; the launch traced here: 151 us
  waiting for transfers between devices  46.6 us (31%)
  starting transfers between devices  35.1 us (23%)
  blocking collectives  20.2 us (13%)
  other arithmetic  20.1 us (13%)
  matrix products  13.9 us (9%)
  local copies, waits for them, and re-layouts  9.95 us (7%)
  Pallas kernels  4.59 us (3%)
    ppermute x12, waiting for transfers between devices, passed_along(): lax.ppermute(value, axis, [(source, source + steps) for source in range(f...  46.6 us
    ppermute x12, starting transfers between devices, passed_along(): lax.ppermute(value, axis, [(source, source + steps) for source in range(f...  35.1 us
    all_to_all x1, blocking collectives, body(): lax.all_to_all(result, 'head', split_axis=0, concat_axis=1, tiled=True)  20.2 us
    unnamed x50, local copies, waits for them, and re-layouts  5.57 us
    another operation x5, other arithmetic  4.76 us
    pallas_call x1, Pallas kernels, key_features(): pl.pallas_call(kernel, grid=(1,), in_specs=[pl.BlockSpec((rows, dim), lam...  4.59 us
    dot_general x1, matrix products, body(): jnp.einsum('gkij,jgd->igkd', weights.astype(jnp.bfloat16), ext_values, pr...  3.48 us
    add x8, other arithmetic, body(): inclusive = inclusive + received  3.27 us
  transfers between devices with their start and end apart: 12, of which 7 were waited for; matrix products, arithmetic and copies ran while one was open for 20% of the time, Pallas kernels for 0%

profile of v17, /device:TPU:2, one launch (start us, length us, event | category | flops | bytes accessed | tf_op | source)
XLA Modules:
  0.0 151.1 jit_solution(16295298600366078148)
XLA Ops:
  0.0 0.7 and_select_fusion.1
  0.7 0.1 fusion.52
  0.8 0.8 fusion.35
  1.6 0.9 bitcast_convert_fusion
  2.5 0.8 multiply_cosine_fusion.1
  3.3 0.8 fusion.43
  4.2 0.2 subtract_convert_fusion.3
  4.3 0.5 copy-done.2
  4.8 0.1 pad_maximum_fusion.15
  4.9 3.8 %collective-permute-start.1 = (bf16[64,1,128]{2,0,1:T(8,128)(2,1)S(1)}, bf16[64,1,128]{2,0,1:T(8,128)(2,1)S(1)}, u32[]{:S(2)}, u32[]{:S(2)}) collective-permute-start(bf16[64,1,128]{2,0,1:T(8,128)(2,1)S(1)} %pad_maximum_fusion.15), channel_id=1, source_target_pairs={{0,8},{8,16},{16,24},{24,32},{32,40},{40,48},{48,56},{56,64},{64,7... | collective-permute-start | bytes 49160 | tf_op jit(solution)/shard_map/ppermute | solution.py:17
  8.8 3.8 %collective-permute-start = (bf16[64,1,128]{2,0,1:T(8,128)(2,1)S(1)}, bf16[64,1,128]{2,0,1:T(8,128)(2,1)S(1)}, u32[]{:S(2)}, u32[]{:S(2)}) collective-permute-start(bf16[64,1,128]{2,0,1:T(8,128)(2,1)S(1)} %slice_bitcast_fusion), channel_id=1, source_target_pairs={{0,8},{8,16},{16,24},{24,32},{32,40},{40,48},{48,56},{56,64},{64,7... | collective-permute-start | bytes 49160 | tf_op jit(solution)/shard_map/ppermute | solution.py:17
  12.6 0.6 or_convert_fusion.mask_ref
  13.2 0.6 broadcast_subtract_fusion
  13.8 0.6 collective-permute-done.1
  14.4 0.8 fusion.67.k_ref
  15.1 1.4 collective-permute-done
  16.5 0.7 fusion.33.v_ref
  17.2 4.6 %shard_map.100 = (bf16[8,128,576]{2,1,0:T(8,128)(2,1)}, f32[8,128,128]{2,1,0:T(8,128)}, f32[8,128,1]{2,1,0:T(8,128)}) custom-call(bf16[576,128]{1,0:T(8,128)(2,1)} %fusion.67.k_ref, bf16[8,64,128]{2,1,0:T(8,128)(2,1)} %bitcast.151, bf16[576,128]{1,0:T(8,128)(2,1)} %fusion.33.v_ref, f32[1,576]{1,0:T(1,128)} %or_convert_fusion.mask_ref), custom_call_target="tpu_custom_call" | custom-call | tf_op jit(solution)/shard_map/pallas_call | solution.py:104
  21.8 1.0 slice.59
  22.8 1.9 %collective-permute-start.2 = (f32[66048]{0:T(1024)S(1)}, f32[66048]{0:T(1024)S(1)}, u32[]{:S(2)}, u32[]{:S(2)}) collective-permute-start(f32[66048]{0:T(1024)S(1)} %slice.59), channel_id=1, source_target_pairs={{0,8},{8,16},{16,24},{24,32},{32,40},{40,48},{48,56},{56,64},{64,7... | collective-permute-start | bytes 792584 | tf_op jit(solution)/shard_map/ppermute | solution.py:17
  24.8 1.2 fusion.22
  25.9 1.2 reduce.4
  27.2 6.7 %collective-permute-done.2 = f32[66048]{0:T(1024)S(1)} collective-permute-done((f32[66048]{0:T(1024)S(1)}, f32[66048]{0:T(1024)S(1)}, u32[]{:S(2)}, u32[]{:S(2)}) %collective-permute-start.2) | collective-permute-done | bytes 264224 | tf_op jit(solution)/shard_map/ppermute | solution.py:17
  33.9 0.9 slice_add_fusion
  34.8 3.4 %collective-permute-start.7 = (f32[66048]{0:T(1024)}, f32[66048]{0:T(1024)}, u32[]{:S(2)}, u32[]{:S(2)}) collective-permute-start(f32[66048]{0:T(1024)} %get-tuple-element.26), channel_id=1, source_target_pairs={{0,64},{8,72},{16,80},{24,88},{32,96},{40,104},{48,112},{56,120},{... | collective-permute-start | bytes 792584 | tf_op jit(solution)/shard_map/ppermute | solution.py:17
  38.2 0.5 copy.26
  38.8 0.3 fusion.69
  39.0 1.9 %copy.45 = f32[512,8,64]{2,0,1:T(8,128)} copy(f32[512,8,64]{0,2,1:T(8,128)S(1)} %get-tuple-element.22) | data formatting | bytes 2097152
  41.0 1.9 %copy.46 = f32[512,8,64]{2,0,1:T(8,128)} copy(f32[512,8,64]{0,2,1:T(8,128)S(1)} %get-tuple-element.21) | data formatting | bytes 2097152
  42.9 3.0 %collective-permute-start.3 = (f32[66048]{0:T(1024)}, f32[66048]{0:T(1024)}, u32[]{:S(2)}, u32[]{:S(2)}) collective-permute-start(f32[66048]{0:T(1024)} %get-tuple-element.25), channel_id=1, source_target_pairs={{0,16},{8,24},{16,32},{24,40},{32,48},{40,56},{48,64},{56,72},{64,... | collective-permute-start | bytes 792584 | tf_op jit(solution)/shard_map/ppermute | solution.py:17
  46.0 2.9 %subtract_convert_fusion = (bf16[512,8,64]{2,0,1:T(8,128)(2,1)S(1)}, bf16[512,8,64]{2,0,1:T(8,128)(2,1)S(1)}) fusion(f32[512,8,64]{2,0,1:T(8,128)} %copy.46, f32[512,8,64]{2,0,1:T(8,128)} %copy.45, f32[512,64]{1,0:T(8,128)S(1)} %bitcast.144, f32[512,64]{1,0:T(8,128)S(1)} %bitcast.142), kind=kLoop, calls=%fused_computation.26 | loop fusion | flops 2097152 | bytes 3407872 | tf_op jit(solution)/shard_map/convert.4
  48.9 2.3 %fusion.2 = (f32[8,512]{1,0:T(8,128)S(1)}, f32[576,512,8]{1,0,2:T(8,128)S(1)}) fusion(pred[512,576]{0,1:T(8,128)(4,1)S(1)} %copy-done.1, bf16[512,8,64]{2,0,1:T(8,128)(2,1)S(1)} %get-tuple-element.20, bf16[512,8,64]{2,0,1:T(8,128)(2,1)S(1)} %get-tuple-element.19, bf16[512,1,64]{2,0,1:T(8,128)(2,1)S(1)} %copy-done.8, bf16[512,1,64]{2,0,1:T(8,128)(2,1)S(1)} %copy-done.6, ...), kind=kOutput, calls=%fused_computation.4 | convolution fusion | flops 613593088 | bytes 10944512 | tf_op jit(solution)/shard_map/igkd,jgd->gkij/dot_general | solution.py:206
  51.2 1.9 %fusion.5 = f32[8,512]{1,0:T(8,128)S(1)} fusion(f32[576,512,8]{1,0,2:T(8,128)S(1)} %get-tuple-element.40, f32[8,512]{1,0:T(8,128)S(1)} %get-tuple-element.39, pred[512,576]{0,1:T(8,128)(4,1)S(1)} %copy-done.1), kind=kLoop, calls=%fused_computation.9 | loop fusion | flops 9433088 | bytes 9764864 | tf_op jit(solution)/shard_map/reduce_sum | solution.py:212
  53.2 3.5 %fusion.10 = f32[128,8,512]{2,0,1:T(8,128)} fusion(f32[576,512,8]{1,0,2:T(8,128)S(1)} %get-tuple-element.40, f32[8,512]{1,0:T(8,128)S(1)} %get-tuple-element.39, pred[512,576]{0,1:T(8,128)(4,1)S(1)} %copy-done.1, bf16[512,1,128]{2,0,1:T(8,128)(2,1)S(1)} %bitcast.149, bf16[64,1,128]{2,0,1:T(8,128)(2,1)S(1)} %copy-done.17), kind=kOutput, calls=%fused_computation.14 | convolution fusion | flops 613711872 | bytes 11993088 | tf_op jit(solution)/shard_map/gkij,jgd->igkd/dot_general | solution.py:216
  56.7 0.9 fusion.71
  57.5 1.9 %fusion.70 = (f32[512,8]{0,1:T(8,128)S(1)}, f32[512,8,64]{0,2,1:T(8,128)}) fusion(bf16[8,128,64]{1,2,0:T(8,128)(2,1)S(1)} %copy-done, bf16[512,8,64]{2,0,1:T(8,128)(2,1)S(1)} %get-tuple-element.20, bf16[512,8,64]{2,0,1:T(8,128)(2,1)S(1)} %get-tuple-element.19), kind=kOutput, calls=%fused_computation.128 | convolution fusion | flops 69992512 | bytes 2244608 | tf_op jit(solution)/shard_map/sub | solution.py:71
  59.4 1.1 add.179
  60.6 1.9 %collective-permute-start.8 = (f32[66048]{0:T(1024)S(1)}, f32[66048]{0:T(1024)S(1)}, u32[]{:S(2)}, u32[]{:S(2)}) collective-permute-start(f32[66048]{0:T(1024)S(1)} %add.179), channel_id=1, source_target_pairs={{0,128},{8,136},{16,144},{24,152},{32,160},{40,168},{48,176},{56,1... | collective-permute-start | bytes 792584 | tf_op jit(solution)/shard_map/ppermute | solution.py:17
  62.5 1.1 add.173
  63.6 5.1 %collective-permute-start.4 = (f32[66048]{0:T(1024)S(1)}, f32[66048]{0:T(1024)S(1)}, u32[]{:S(2)}, u32[]{:S(2)}) collective-permute-start(f32[66048]{0:T(1024)S(1)} %add.173), channel_id=1, source_target_pairs={{0,32},{8,40},{16,48},{24,56},{32,64},{40,72},{48,80},{56,88},{64,... | collective-permute-start | bytes 792584 | tf_op jit(solution)/shard_map/ppermute | solution.py:17
  68.7 0.3 divide_convert_fusion
  69.1 2.1 %collective-permute-start.9 = (f32[66048]{0:T(1024)S(1)}, f32[66048]{0:T(1024)S(1)}, u32[]{:S(2)}, u32[]{:S(2)}) collective-permute-start(f32[66048]{0:T(1024)S(1)} %add.181), channel_id=1, source_target_pairs={{0,8},{8,16},{16,24},{24,32},{32,40},{40,48},{48,56},{56,64},{64,7... | collective-permute-start | bytes 792584 | tf_op jit(solution)/shard_map/ppermute | solution.py:17
  71.1 14.0 %collective-permute-done.4 = f32[66048]{0:T(1024)S(1)} collective-permute-done((f32[66048]{0:T(1024)S(1)}, f32[66048]{0:T(1024)S(1)}, u32[]{:S(2)}, u32[]{:S(2)}) %collective-permute-start.4) | collective-permute-done | bytes 264224 | tf_op jit(solution)/shard_map/ppermute | solution.py:17
  85.1 2.5 %collective-permute-start.5 = (f32[66048]{0:T(1024)S(1)}, f32[66048]{0:T(1024)S(1)}, u32[]{:S(2)}, u32[]{:S(2)}) collective-permute-start(f32[66048]{0:T(1024)S(1)} %add.175), channel_id=1, source_target_pairs={{0,64},{8,72},{16,80},{24,88},{32,96},{40,104},{48,112},{56,120},{... | collective-permute-start | bytes 792584 | tf_op jit(solution)/shard_map/ppermute | solution.py:17
  87.7 1.6 %select_reduce_fusion = (f32[8,512]{1,0:T(8,128)S(1)}, bf16[8,512,576]{1,2,0:T(8,128)(2,1)S(1)}) fusion(pred[512,576]{0,1:T(8,128)(4,1)S(1)} %copy-done.13, bf16[8,128,576]{2,1,0:T(8,128)(2,1)S(1)} %copy-done.20, bf16[512,8,64]{0,2,1:T(8,128)(2,1)S(1)} %get-tuple-element.47, bf16[512,8,64]{0,2,1:T(8,128)(2,1)S(1)} %get-tuple-element.48), kind=kOutput, calls=%fused_computation.7 | convolution fusion | flops 613150720 | bytes 7258112 | tf_op jit(solution)/shard_map/igkf,gkfj->gkij/dot_general | solution.py:213
  89.3 1.9 %collective-permute-start.10 = (f32[66048]{0:T(1024)S(1)}, f32[66048]{0:T(1024)S(1)}, u32[]{:S(2)}, u32[]{:S(2)}) collective-permute-start(f32[66048]{0:T(1024)S(1)} %add.183), channel_id=1, source_target_pairs={{0,16},{8,24},{16,32},{24,40},{32,48},{40,56},{48,64},{56,72},{64,... | collective-permute-start | bytes 792584 | tf_op jit(solution)/shard_map/ppermute | solution.py:17
  91.2 2.2 %collective-permute-done.5 = f32[66048]{0:T(1024)S(1)} collective-permute-done((f32[66048]{0:T(1024)S(1)}, f32[66048]{0:T(1024)S(1)}, u32[]{:S(2)}, u32[]{:S(2)}) %collective-permute-start.5) | collective-permute-done | bytes 264224 | tf_op jit(solution)/shard_map/ppermute | solution.py:17
  93.5 2.1 %collective-permute-start.6 = (f32[66048]{0:T(1024)S(1)}, f32[66048]{0:T(1024)S(1)}, u32[]{:S(2)}, u32[]{:S(2)}) collective-permute-start(f32[66048]{0:T(1024)S(1)} %add.177), channel_id=1, source_target_pairs={{0,128},{8,136},{16,144},{24,152},{32,160},{40,168},{48,176},{56,1... | collective-permute-start | bytes 792584 | tf_op jit(solution)/shard_map/ppermute | solution.py:17
  95.7 2.4 %fusion.17 = f32[512,1,8,128]{0,3,2,1:T(8,128)} fusion(f32[128,8,512]{2,0,1:T(8,128)S(1)} %copy-done.22, bf16[8,512,576]{1,2,0:T(8,128)(2,1)S(1)} %get-tuple-element.46, pred[512,576]{0,1:T(8,128)(4,1)S(1)} %copy-done.13, f32[8]{0:T(128)S(1)} %copy-done.18, f32[8]{0:T(128)S(1)} %copy-done.19, bf16[512,1,128]{2,0,1:T(8,128)(2,1)S(1)} %bitcast.150, ...), kind=kOutput, calls=%fused_computation.23 | convolution fusion | flops 608206848 | bytes 9355328 | tf_op jit(solution)/shard_map/gkij,jgd->igkd/dot_general | solution.py:222
  98.2 5.7 %collective-permute-done.10 = f32[66048]{0:T(1024)S(1)} collective-permute-done((f32[66048]{0:T(1024)S(1)}, f32[66048]{0:T(1024)S(1)}, u32[]{:S(2)}, u32[]{:S(2)}) %collective-permute-start.10) | collective-permute-done | bytes 264224 | tf_op jit(solution)/shard_map/ppermute | solution.py:17
  103.9 3.5 %collective-permute-start.11 = (f32[66048]{0:T(1024)S(1)}, f32[66048]{0:T(1024)S(1)}, u32[]{:S(2)}, u32[]{:S(2)}) collective-permute-start(f32[66048]{0:T(1024)S(1)} %add.185), channel_id=1, source_target_pairs={{0,32},{8,40},{16,48},{24,56},{32,64},{40,72},{48,80},{56,88},{64,... | collective-permute-start | bytes 792584 | tf_op jit(solution)/shard_map/ppermute | solution.py:17
  107.5 1.0 add_add_fusion.1
  108.5 16.0 %collective-permute-done.11 = f32[66048]{0:T(1024)S(1)} collective-permute-done((f32[66048]{0:T(1024)S(1)}, f32[66048]{0:T(1024)S(1)}, u32[]{:S(2)}, u32[]{:S(2)}) %collective-permute-start.11) | collective-permute-done | bytes 264224 | tf_op jit(solution)/shard_map/ppermute | solution.py:17
  124.5 1.1 add_add_fusion
  125.6 0.2 fusion.47
  125.9 0.2 fusion.45
  126.2 0.2 copy.31
  126.4 0.4 fusion.31
  126.9 1.1 copy-done.23
  128.0 0.5 fusion.15
  128.5 0.8 copy.35
  129.3 0.5 all_to_all.14
  129.8 20.2 %all_to_all.19 = bf16[8,64,1024]{2,1,0:T(8,128)(2,1)S(1)} all-to-all(bf16[8,64,1024]{2,1,0:T(8,128)(2,1)S(1)} %all_to_all.14), channel_id=1, replica_groups=mesh['seq'=32,'head'=8] {'head'}, dimensions={0} | all-to-all | bytes 2097152 | tf_op jit(solution)/shard_map/all_to_all | solution.py:252
  150.0 1.1 copy.47
  (65 shorter events, 0.6 us)
Async XLA Ops:
  0.0 56.7 %copy-start = (bf16[8,128,64]{1,2,0:T(8,128)(2,1)S(1)}, bf16[8,128,64]{1,2,0:T(8,128)(2,1)}, u32[]{:S(2)}) copy-start(bf16[8,128,64]{1,2,0:T(8,128)(2,1)} %param.14) | copy-start | bytes 393220
  0.0 8.8 %copy-start.14 = (bf16[512,128]{1,0:T(8,128)(2,1)S(1)}, bf16[512,128]{1,0:T(8,128)(2,1)}, u32[]{:S(2)}) copy-start(bf16[512,128]{1,0:T(8,128)(2,1)} %param.12) | copy-start | bytes 393220
  0.0 13.2 %copy-start.21 = (f32[8]{0:T(128)S(1)}, f32[8]{0:T(128)}, u32[]{:S(2)}) copy-start(f32[8]{0:T(128)} %param.16) | copy-start | bytes 100
  4.1 0.7 copy-start.2
  4.8 12.4 %copy-start.5 = (bf16[512,1,64]{2,0,1:T(8,128)(2,1)}, bf16[512,1,64]{2,0,1:T(8,128)(2,1)S(1)}, u32[]{:S(2)}) copy-start(bf16[512,1,64]{2,0,1:T(8,128)(2,1)S(1)} %get-tuple-element.23) | copy-start | bytes 196612
  4.8 12.4 %copy-start.7 = (bf16[512,1,64]{2,0,1:T(8,128)(2,1)}, bf16[512,1,64]{2,0,1:T(8,128)(2,1)S(1)}, u32[]{:S(2)}) copy-start(bf16[512,1,64]{2,0,1:T(8,128)(2,1)S(1)} %get-tuple-element.24) | copy-start | bytes 196612
  4.9 9.4 %collective-permute-start.1 = (bf16[64,1,128]{2,0,1:T(8,128)(2,1)S(1)}, bf16[64,1,128]{2,0,1:T(8,128)(2,1)S(1)}, u32[]{:S(2)}, u32[]{:S(2)}) collective-permute-start(bf16[64,1,128]{2,0,1:T(8,128)(2,1)S(1)} %pad_maximum_fusion.15), channel_id=1, source_target_pairs={{0,8},{8,16},{16,24},{24,32},{32,40},{40,48},{48,56},{56,64},{64,7... | collective-permute-start | bytes 49160 | tf_op jit(solution)/shard_map/ppermute | solution.py:17
  8.8 7.7 %collective-permute-start = (bf16[64,1,128]{2,0,1:T(8,128)(2,1)S(1)}, bf16[64,1,128]{2,0,1:T(8,128)(2,1)S(1)}, u32[]{:S(2)}, u32[]{:S(2)}) collective-permute-start(bf16[64,1,128]{2,0,1:T(8,128)(2,1)S(1)} %slice_bitcast_fusion), channel_id=1, source_target_pairs={{0,8},{8,16},{16,24},{24,32},{32,40},{40,48},{48,56},{56,64},{64,7... | collective-permute-start | bytes 49160 | tf_op jit(solution)/shard_map/ppermute | solution.py:17
  15.1 23.1 %copy-start.12 = (bf16[512,1024]{1,0:T(8,128)(2,1)S(1)}, bf16[512,1024]{1,0:T(8,128)(2,1)}, u32[]{:S(2)}) copy-start(bf16[512,1024]{1,0:T(8,128)(2,1)} %param.10) | copy-start | bytes 3145732
  16.5 0.7 copy-start.16
  21.8 12.1 %copy-start.4 = (f32[8,128,128]{2,1,0:T(8,128)S(1)}, f32[8,128,128]{2,1,0:T(8,128)}, u32[]{:S(2)}) copy-start(f32[8,128,128]{2,1,0:T(8,128)} %get-tuple-element.11) | copy-start | bytes 1572868
  22.8 11.1 %collective-permute-start.2 = (f32[66048]{0:T(1024)S(1)}, f32[66048]{0:T(1024)S(1)}, u32[]{:S(2)}, u32[]{:S(2)}) collective-permute-start(f32[66048]{0:T(1024)S(1)} %slice.59), channel_id=1, source_target_pairs={{0,8},{8,16},{16,24},{24,32},{32,40},{40,48},{48,56},{56,64},{64,7... | collective-permute-start | bytes 792584 | tf_op jit(solution)/shard_map/ppermute | solution.py:17
  33.9 0.9 copy-start.9
  34.8 24.6 %collective-permute-start.7 = (f32[66048]{0:T(1024)}, f32[66048]{0:T(1024)}, u32[]{:S(2)}, u32[]{:S(2)}) collective-permute-start(f32[66048]{0:T(1024)} %get-tuple-element.26), channel_id=1, source_target_pairs={{0,64},{8,72},{16,80},{24,88},{32,96},{40,104},{48,112},{56,120},{... | collective-permute-start | bytes 792584 | tf_op jit(solution)/shard_map/ppermute | solution.py:17
  41.0 5.0 %copy-start.3 = (f32[2,4,64,64]{3,2,1,0:T(8,128)S(1)}, f32[2,4,64,64]{3,2,1,0:T(8,128)}, u32[]{:S(2)}) copy-start(f32[2,4,64,64]{3,2,1,0:T(8,128)} %copy-done.2) | copy-start | bytes 393220
  42.9 19.6 %collective-permute-start.3 = (f32[66048]{0:T(1024)}, f32[66048]{0:T(1024)}, u32[]{:S(2)}, u32[]{:S(2)}) collective-permute-start(f32[66048]{0:T(1024)} %get-tuple-element.25), channel_id=1, source_target_pairs={{0,16},{8,24},{16,32},{24,40},{32,48},{40,56},{48,64},{56,72},{64,... | collective-permute-start | bytes 792584 | tf_op jit(solution)/shard_map/ppermute | solution.py:17
  46.0 2.9 %copy-start.1 = (pred[512,576]{0,1:T(8,128)(4,1)S(1)}, pred[512,576]{0,1:T(8,128)(4,1)}, u32[]{:S(2)}) copy-start(pred[512,576]{0,1:T(8,128)(4,1)} %get-tuple-element.32) | copy-start | bytes 884740
  46.0 2.9 %copy-start.6 = (bf16[512,1,64]{2,0,1:T(8,128)(2,1)S(1)}, bf16[512,1,64]{2,0,1:T(8,128)(2,1)}, u32[]{:S(2)}) copy-start(bf16[512,1,64]{2,0,1:T(8,128)(2,1)} %copy-done.5) | copy-start | bytes 196612
  46.0 2.9 %copy-start.8 = (bf16[512,1,64]{2,0,1:T(8,128)(2,1)S(1)}, bf16[512,1,64]{2,0,1:T(8,128)(2,1)}, u32[]{:S(2)}) copy-start(bf16[512,1,64]{2,0,1:T(8,128)(2,1)} %copy-done.7) | copy-start | bytes 196612
  51.2 2.0 %copy-start.15 = (bf16[512,128]{1,0:T(8,128)(2,1)S(1)}, bf16[512,128]{1,0:T(8,128)(2,1)}, u32[]{:S(2)}) copy-start(bf16[512,128]{1,0:T(8,128)(2,1)} %param.12) | copy-start | bytes 393220
  51.2 2.0 %copy-start.17 = (bf16[64,1,128]{2,0,1:T(8,128)(2,1)S(1)}, bf16[64,1,128]{2,0,1:T(8,128)(2,1)}, u32[]{:S(2)}) copy-start(bf16[64,1,128]{2,0,1:T(8,128)(2,1)} %copy-done.16) | copy-start | bytes 49156
  59.4 9.3 %copy-start.11 = (f32[512,8,64]{0,2,1:T(8,128)S(1)}, f32[512,8,64]{0,2,1:T(8,128)}, u32[]{:S(2)}) copy-start(f32[512,8,64]{0,2,1:T(8,128)} %get-tuple-element.42) | copy-start | bytes 3145732
  60.6 8.5 %collective-permute-start.8 = (f32[66048]{0:T(1024)S(1)}, f32[66048]{0:T(1024)S(1)}, u32[]{:S(2)}, u32[]{:S(2)}) collective-permute-start(f32[66048]{0:T(1024)S(1)} %add.179), channel_id=1, source_target_pairs={{0,128},{8,136},{16,144},{24,152},{32,160},{40,168},{48,176},{56,1... | collective-permute-start | bytes 792584 | tf_op jit(solution)/shard_map/ppermute | solution.py:17
  63.6 21.5 %collective-permute-start.4 = (f32[66048]{0:T(1024)S(1)}, f32[66048]{0:T(1024)S(1)}, u32[]{:S(2)}, u32[]{:S(2)}) collective-permute-start(f32[66048]{0:T(1024)S(1)} %add.173), channel_id=1, source_target_pairs={{0,32},{8,40},{16,48},{24,56},{32,64},{40,72},{48,80},{56,88},{64,... | collective-permute-start | bytes 792584 | tf_op jit(solution)/shard_map/ppermute | solution.py:17
  68.7 18.9 %copy-start.13 = (pred[512,576]{0,1:T(8,128)(4,1)S(1)}, pred[512,576]{0,1:T(8,128)(4,1)}, u32[]{:S(2)}) copy-start(pred[512,576]{0,1:T(8,128)(4,1)} %get-tuple-element.31) | copy-start | bytes 884740
  68.7 18.9 %copy-start.20 = (bf16[8,128,576]{2,1,0:T(8,128)(2,1)S(1)}, bf16[8,128,576]{2,1,0:T(8,128)(2,1)}, u32[]{:S(2)}) copy-start(bf16[8,128,576]{2,1,0:T(8,128)(2,1)} %get-tuple-element.13) | copy-start | bytes 3538948
  69.1 20.2 %collective-permute-start.9 = (f32[66048]{0:T(1024)S(1)}, f32[66048]{0:T(1024)S(1)}, u32[]{:S(2)}, u32[]{:S(2)}) collective-permute-start(f32[66048]{0:T(1024)S(1)} %add.181), channel_id=1, source_target_pairs={{0,8},{8,16},{16,24},{24,32},{32,40},{40,48},{48,56},{56,64},{64,7... | collective-permute-start | bytes 792584 | tf_op jit(solution)/shard_map/ppermute | solution.py:17
  85.1 8.3 %collective-permute-start.5 = (f32[66048]{0:T(1024)S(1)}, f32[66048]{0:T(1024)S(1)}, u32[]{:S(2)}, u32[]{:S(2)}) collective-permute-start(f32[66048]{0:T(1024)S(1)} %add.175), channel_id=1, source_target_pairs={{0,64},{8,72},{16,80},{24,88},{32,96},{40,104},{48,112},{56,120},{... | collective-permute-start | bytes 792584 | tf_op jit(solution)/shard_map/ppermute | solution.py:17
  87.6 8.0 %copy-start.18 = (f32[8]{0:T(128)S(1)}, f32[8]{0:T(128)}, u32[]{:S(2)}) copy-start(f32[8]{0:T(128)} %get-tuple-element.17) | copy-start | bytes 100
  87.6 8.0 %copy-start.19 = (f32[8]{0:T(128)S(1)}, f32[8]{0:T(128)}, u32[]{:S(2)}) copy-start(f32[8]{0:T(128)} %get-tuple-element.18) | copy-start | bytes 100
  87.6 8.0 %copy-start.22 = (f32[128,8,512]{2,0,1:T(8,128)S(1)}, f32[128,8,512]{2,0,1:T(8,128)}, u32[]{:S(2)}) copy-start(f32[128,8,512]{2,0,1:T(8,128)} %fusion.10) | copy-start | bytes 6291460
  89.3 14.6 %collective-permute-start.10 = (f32[66048]{0:T(1024)S(1)}, f32[66048]{0:T(1024)S(1)}, u32[]{:S(2)}, u32[]{:S(2)}) collective-permute-start(f32[66048]{0:T(1024)S(1)} %add.183), channel_id=1, source_target_pairs={{0,16},{8,24},{16,32},{24,40},{32,48},{40,56},{48,64},{56,72},{64,... | collective-permute-start | bytes 792584 | tf_op jit(solution)/shard_map/ppermute | solution.py:17
  93.5 14.0 %collective-permute-start.6 = (f32[66048]{0:T(1024)S(1)}, f32[66048]{0:T(1024)S(1)}, u32[]{:S(2)}, u32[]{:S(2)}) collective-permute-start(f32[66048]{0:T(1024)S(1)} %add.177), channel_id=1, source_target_pairs={{0,128},{8,136},{16,144},{24,152},{32,160},{40,168},{48,176},{56,1... | collective-permute-start | bytes 792584 | tf_op jit(solution)/shard_map/ppermute | solution.py:17
  95.7 11.8 %copy-start.10 = (f32[66048]{0:T(1024)S(1)}, f32[66048]{0:T(1024)}, u32[]{:S(2)}) copy-start(f32[66048]{0:T(1024)} %copy-done.9) | copy-start | bytes 792580
  103.9 20.6 %collective-permute-start.11 = (f32[66048]{0:T(1024)S(1)}, f32[66048]{0:T(1024)S(1)}, u32[]{:S(2)}, u32[]{:S(2)}) collective-permute-start(f32[66048]{0:T(1024)S(1)} %add.185), channel_id=1, source_target_pairs={{0,32},{8,40},{16,48},{24,56},{32,64},{40,72},{48,80},{56,88},{64,... | collective-permute-start | bytes 792584 | tf_op jit(solution)/shard_map/ppermute | solution.py:17
  126.4 1.6 %copy-start.23 = (f32[512,1,8,128]{0,3,2,1:T(8,128)S(1)}, f32[512,1,8,128]{0,3,2,1:T(8,128)}, u32[]{:S(2)}) copy-start(f32[512,1,8,128]{0,3,2,1:T(8,128)} %fusion.17) | copy-start | bytes 6291460

commit v18 on v17

--- a/solution.py
+++ b/solution.py
@@ -171,7 +171,7 @@
         shifts.append(steps)
         steps *= 2
     half = len(shifts) // 2 + 1
-    orders = (shifts, shifts[half:] + shifts[:half])
+    orders = (shifts, shifts[half:] + shifts[:half][::-1])
     middle = packed.size // 2
     pieces = []
     for order, piece in zip(orders, (packed[:middle], packed[middle:])):

time: 152 us -> 149 us (0.980)
  waiting for transfers between devices: 46.6 us -> 33.7 us
  starting transfers between devices: 35.1 us -> 45.2 us
    ppermute x12, waiting for transfers between devices: 46.6 us -> 33.7 us  [passed_along(): lax.ppermute(value, axis, [(source, source + steps) for source in range(f...]
    ppermute x12, starting transfers between devices: 35.1 us -> 45.2 us  [passed_along(): lax.ppermute(value, axis, [(source, source + steps) for source in range(f...]
where the time goes in v18:
time: 149 us; the launch traced here: 148 us
  starting transfers between devices  45.2 us (30%)
  waiting for transfers between devices  33.7 us (23%)
  blocking collectives  20.3 us (14%)
  other arithmetic  20.1 us (13%)
  matrix products  13.9 us (9%)
  local copies, waits for them, and re-layouts  9.95 us (7%)
  Pallas kernels  4.59 us (3%)
    ppermute x12, starting transfers between devices, passed_along(): lax.ppermute(value, axis, [(source, source + steps) for source in range(f...  45.2 us
    ppermute x12, waiting for transfers between devices, passed_along(): lax.ppermute(value, axis, [(source, source + steps) for source in range(f...  33.7 us
    all_to_all x1, blocking collectives, body(): lax.all_to_all(result, 'head', split_axis=0, concat_axis=1, tiled=True)  20.3 us
    unnamed x50, local copies, waits for them, and re-layouts  5.58 us
    another operation x5, other arithmetic  4.76 us
    pallas_call x1, Pallas kernels, key_features(): pl.pallas_call(kernel, grid=(1,), in_specs=[pl.BlockSpec((rows, dim), lam...  4.59 us
    dot_general x1, matrix products, body(): jnp.einsum('gkij,jgd->igkd', weights.astype(jnp.bfloat16), ext_values, pr...  3.48 us
    add x8, other arithmetic, body(): inclusive = inclusive + received  3.27 us
  transfers between devices with their start and end apart: 12, of which 7 were waited for; matrix products, arithmetic and copies ran while one was open for 20% of the time, Pallas kernels for 0%

profile of v18, /device:TPU:2, one launch (start us, length us, event | category | flops | bytes accessed | tf_op | source)
XLA Modules:
  0.0 148.2 jit_solution(14125643114884667533)
XLA Ops:
  0.0 0.7 and_select_fusion.1
  0.7 0.1 fusion.52
  0.8 0.8 fusion.35
  1.6 0.9 bitcast_convert_fusion
  2.5 0.8 multiply_cosine_fusion.1
  3.3 0.8 fusion.43
  4.2 0.2 subtract_convert_fusion.3
  4.3 0.5 copy-done.2
  4.8 0.1 pad_maximum_fusion.15
  4.9 3.8 %collective-permute-start.1 = (bf16[64,1,128]{2,0,1:T(8,128)(2,1)S(1)}, bf16[64,1,128]{2,0,1:T(8,128)(2,1)S(1)}, u32[]{:S(2)}, u32[]{:S(2)}) collective-permute-start(bf16[64,1,128]{2,0,1:T(8,128)(2,1)S(1)} %pad_maximum_fusion.15), channel_id=1, source_target_pairs={{0,8},{8,16},{16,24},{24,32},{32,40},{40,48},{48,56},{56,64},{64,7... | collective-permute-start | bytes 49160 | tf_op jit(solution)/shard_map/ppermute | solution.py:17
  8.8 3.8 %collective-permute-start = (bf16[64,1,128]{2,0,1:T(8,128)(2,1)S(1)}, bf16[64,1,128]{2,0,1:T(8,128)(2,1)S(1)}, u32[]{:S(2)}, u32[]{:S(2)}) collective-permute-start(bf16[64,1,128]{2,0,1:T(8,128)(2,1)S(1)} %slice_bitcast_fusion), channel_id=1, source_target_pairs={{0,8},{8,16},{16,24},{24,32},{32,40},{40,48},{48,56},{56,64},{64,7... | collective-permute-start | bytes 49160 | tf_op jit(solution)/shard_map/ppermute | solution.py:17
  12.6 0.6 or_convert_fusion.mask_ref
  13.2 0.6 broadcast_subtract_fusion
  13.8 0.6 collective-permute-done.1
  14.4 0.8 fusion.67.k_ref
  15.1 1.4 collective-permute-done
  16.5 0.7 fusion.33.v_ref
  17.2 4.6 %shard_map.100 = (bf16[8,128,576]{2,1,0:T(8,128)(2,1)}, f32[8,128,128]{2,1,0:T(8,128)}, f32[8,128,1]{2,1,0:T(8,128)}) custom-call(bf16[576,128]{1,0:T(8,128)(2,1)} %fusion.67.k_ref, bf16[8,64,128]{2,1,0:T(8,128)(2,1)} %bitcast.151, bf16[576,128]{1,0:T(8,128)(2,1)} %fusion.33.v_ref, f32[1,576]{1,0:T(1,128)} %or_convert_fusion.mask_ref), custom_call_target="tpu_custom_call" | custom-call | tf_op jit(solution)/shard_map/pallas_call | solution.py:104
  21.8 1.0 slice.59
  22.8 1.9 %collective-permute-start.2 = (f32[66048]{0:T(1024)S(1)}, f32[66048]{0:T(1024)S(1)}, u32[]{:S(2)}, u32[]{:S(2)}) collective-permute-start(f32[66048]{0:T(1024)S(1)} %slice.59), channel_id=1, source_target_pairs={{0,8},{8,16},{16,24},{24,32},{32,40},{40,48},{48,56},{56,64},{64,7... | collective-permute-start | bytes 792584 | tf_op jit(solution)/shard_map/ppermute | solution.py:17
  24.8 1.2 fusion.22
  25.9 1.2 reduce.4
  27.2 6.7 %collective-permute-done.2 = f32[66048]{0:T(1024)S(1)} collective-permute-done((f32[66048]{0:T(1024)S(1)}, f32[66048]{0:T(1024)S(1)}, u32[]{:S(2)}, u32[]{:S(2)}) %collective-permute-start.2) | collective-permute-done | bytes 264224 | tf_op jit(solution)/shard_map/ppermute | solution.py:17
  33.9 0.9 slice_add_fusion
  34.8 3.4 %collective-permute-start.7 = (f32[66048]{0:T(1024)}, f32[66048]{0:T(1024)}, u32[]{:S(2)}, u32[]{:S(2)}) collective-permute-start(f32[66048]{0:T(1024)} %get-tuple-element.26), channel_id=1, source_target_pairs={{0,64},{8,72},{16,80},{24,88},{32,96},{40,104},{48,112},{56,120},{... | collective-permute-start | bytes 792584 | tf_op jit(solution)/shard_map/ppermute | solution.py:17
  38.2 0.5 copy.26
  38.8 0.3 fusion.69
  39.0 1.9 %copy.45 = f32[512,8,64]{2,0,1:T(8,128)} copy(f32[512,8,64]{0,2,1:T(8,128)S(1)} %get-tuple-element.22) | data formatting | bytes 2097152
  41.0 1.9 %copy.46 = f32[512,8,64]{2,0,1:T(8,128)} copy(f32[512,8,64]{0,2,1:T(8,128)S(1)} %get-tuple-element.21) | data formatting | bytes 2097152
  42.9 3.0 %collective-permute-start.3 = (f32[66048]{0:T(1024)}, f32[66048]{0:T(1024)}, u32[]{:S(2)}, u32[]{:S(2)}) collective-permute-start(f32[66048]{0:T(1024)} %get-tuple-element.25), channel_id=1, source_target_pairs={{0,16},{8,24},{16,32},{24,40},{32,48},{40,56},{48,64},{56,72},{64,... | collective-permute-start | bytes 792584 | tf_op jit(solution)/shard_map/ppermute | solution.py:17
  46.0 2.9 %subtract_convert_fusion = (bf16[512,8,64]{2,0,1:T(8,128)(2,1)S(1)}, bf16[512,8,64]{2,0,1:T(8,128)(2,1)S(1)}) fusion(f32[512,8,64]{2,0,1:T(8,128)} %copy.46, f32[512,8,64]{2,0,1:T(8,128)} %copy.45, f32[512,64]{1,0:T(8,128)S(1)} %bitcast.144, f32[512,64]{1,0:T(8,128)S(1)} %bitcast.142), kind=kLoop, calls=%fused_computation.26 | loop fusion | flops 2097152 | bytes 3407872 | tf_op jit(solution)/shard_map/convert.4
  48.9 2.3 %fusion.2 = (f32[8,512]{1,0:T(8,128)S(1)}, f32[576,512,8]{1,0,2:T(8,128)S(1)}) fusion(pred[512,576]{0,1:T(8,128)(4,1)S(1)} %copy-done.1, bf16[512,8,64]{2,0,1:T(8,128)(2,1)S(1)} %get-tuple-element.20, bf16[512,8,64]{2,0,1:T(8,128)(2,1)S(1)} %get-tuple-element.19, bf16[512,1,64]{2,0,1:T(8,128)(2,1)S(1)} %copy-done.8, bf16[512,1,64]{2,0,1:T(8,128)(2,1)S(1)} %copy-done.6, ...), kind=kOutput, calls=%fused_computation.4 | convolution fusion | flops 613593088 | bytes 10944512 | tf_op jit(solution)/shard_map/igkd,jgd->gkij/dot_general | solution.py:206
  51.2 1.9 %fusion.5 = f32[8,512]{1,0:T(8,128)S(1)} fusion(f32[576,512,8]{1,0,2:T(8,128)S(1)} %get-tuple-element.40, f32[8,512]{1,0:T(8,128)S(1)} %get-tuple-element.39, pred[512,576]{0,1:T(8,128)(4,1)S(1)} %copy-done.1), kind=kLoop, calls=%fused_computation.9 | loop fusion | flops 9433088 | bytes 9764864 | tf_op jit(solution)/shard_map/reduce_sum | solution.py:212
  53.2 3.5 %fusion.10 = f32[128,8,512]{2,0,1:T(8,128)} fusion(f32[576,512,8]{1,0,2:T(8,128)S(1)} %get-tuple-element.40, f32[8,512]{1,0:T(8,128)S(1)} %get-tuple-element.39, pred[512,576]{0,1:T(8,128)(4,1)S(1)} %copy-done.1, bf16[512,1,128]{2,0,1:T(8,128)(2,1)S(1)} %bitcast.149, bf16[64,1,128]{2,0,1:T(8,128)(2,1)S(1)} %copy-done.17), kind=kOutput, calls=%fused_computation.14 | convolution fusion | flops 613711872 | bytes 11993088 | tf_op jit(solution)/shard_map/gkij,jgd->igkd/dot_general | solution.py:216
  56.7 0.9 fusion.71
  57.5 1.9 %fusion.70 = (f32[512,8]{0,1:T(8,128)S(1)}, f32[512,8,64]{0,2,1:T(8,128)}) fusion(bf16[8,128,64]{1,2,0:T(8,128)(2,1)S(1)} %copy-done, bf16[512,8,64]{2,0,1:T(8,128)(2,1)S(1)} %get-tuple-element.20, bf16[512,8,64]{2,0,1:T(8,128)(2,1)S(1)} %get-tuple-element.19), kind=kOutput, calls=%fused_computation.128 | convolution fusion | flops 69992512 | bytes 2244608 | tf_op jit(solution)/shard_map/sub | solution.py:71
  59.4 1.1 add.179
  60.6 1.9 %collective-permute-start.8 = (f32[66048]{0:T(1024)S(1)}, f32[66048]{0:T(1024)S(1)}, u32[]{:S(2)}, u32[]{:S(2)}) collective-permute-start(f32[66048]{0:T(1024)S(1)} %add.179), channel_id=1, source_target_pairs={{0,128},{8,136},{16,144},{24,152},{32,160},{40,168},{48,176},{56,1... | collective-permute-start | bytes 792584 | tf_op jit(solution)/shard_map/ppermute | solution.py:17
  62.5 1.1 add.173
  63.6 5.1 %collective-permute-start.4 = (f32[66048]{0:T(1024)S(1)}, f32[66048]{0:T(1024)S(1)}, u32[]{:S(2)}, u32[]{:S(2)}) collective-permute-start(f32[66048]{0:T(1024)S(1)} %add.173), channel_id=1, source_target_pairs={{0,32},{8,40},{16,48},{24,56},{32,64},{40,72},{48,80},{56,88},{64,... | collective-permute-start | bytes 792584 | tf_op jit(solution)/shard_map/ppermute | solution.py:17
  68.7 0.3 divide_convert_fusion
  69.1 4.8 %collective-permute-start.9 = (f32[66048]{0:T(1024)S(1)}, f32[66048]{0:T(1024)S(1)}, u32[]{:S(2)}, u32[]{:S(2)}) collective-permute-start(f32[66048]{0:T(1024)S(1)} %add.181), channel_id=1, source_target_pairs={{0,32},{8,40},{16,48},{24,56},{32,64},{40,72},{48,80},{56,88},{64,... | collective-permute-start | bytes 792584 | tf_op jit(solution)/shard_map/ppermute | solution.py:17
  73.8 6.6 %collective-permute-done.4 = f32[66048]{0:T(1024)S(1)} collective-permute-done((f32[66048]{0:T(1024)S(1)}, f32[66048]{0:T(1024)S(1)}, u32[]{:S(2)}, u32[]{:S(2)}) %collective-permute-start.4) | collective-permute-done | bytes 264224 | tf_op jit(solution)/shard_map/ppermute | solution.py:17
  80.5 1.9 %collective-permute-start.5 = (f32[66048]{0:T(1024)S(1)}, f32[66048]{0:T(1024)S(1)}, u32[]{:S(2)}, u32[]{:S(2)}) collective-permute-start(f32[66048]{0:T(1024)S(1)} %add.175), channel_id=1, source_target_pairs={{0,64},{8,72},{16,80},{24,88},{32,96},{40,104},{48,112},{56,120},{... | collective-permute-start | bytes 792584 | tf_op jit(solution)/shard_map/ppermute | solution.py:17
  82.4 1.6 %select_reduce_fusion = (f32[8,512]{1,0:T(8,128)S(1)}, bf16[8,512,576]{1,2,0:T(8,128)(2,1)S(1)}) fusion(pred[512,576]{0,1:T(8,128)(4,1)S(1)} %copy-done.13, bf16[8,128,576]{2,1,0:T(8,128)(2,1)S(1)} %copy-done.20, bf16[512,8,64]{0,2,1:T(8,128)(2,1)S(1)} %get-tuple-element.47, bf16[512,8,64]{0,2,1:T(8,128)(2,1)S(1)} %get-tuple-element.48), kind=kOutput, calls=%fused_computation.7 | convolution fusion | flops 613150720 | bytes 7258112 | tf_op jit(solution)/shard_map/igkf,gkfj->gkij/dot_general | solution.py:213
  84.0 2.1 %collective-permute-done.9 = f32[66048]{0:T(1024)S(1)} collective-permute-done((f32[66048]{0:T(1024)S(1)}, f32[66048]{0:T(1024)S(1)}, u32[]{:S(2)}, u32[]{:S(2)}) %collective-permute-start.9) | collective-permute-done | bytes 264224 | tf_op jit(solution)/shard_map/ppermute | solution.py:17
  86.1 11.8 %collective-permute-start.10 = (f32[66048]{0:T(1024)S(1)}, f32[66048]{0:T(1024)S(1)}, u32[]{:S(2)}, u32[]{:S(2)}) collective-permute-start(f32[66048]{0:T(1024)S(1)} %add.183), channel_id=1, source_target_pairs={{0,16},{8,24},{16,32},{24,40},{32,48},{40,56},{48,64},{56,72},{64,... | collective-permute-start | bytes 792584 | tf_op jit(solution)/shard_map/ppermute | solution.py:17
  98.0 1.8 %collective-permute-start.6 = (f32[66048]{0:T(1024)S(1)}, f32[66048]{0:T(1024)S(1)}, u32[]{:S(2)}, u32[]{:S(2)}) collective-permute-start(f32[66048]{0:T(1024)S(1)} %add.177), channel_id=1, source_target_pairs={{0,128},{8,136},{16,144},{24,152},{32,160},{40,168},{48,176},{56,1... | collective-permute-start | bytes 792584 | tf_op jit(solution)/shard_map/ppermute | solution.py:17
  99.8 2.4 %fusion.17 = f32[512,1,8,128]{0,3,2,1:T(8,128)} fusion(f32[128,8,512]{2,0,1:T(8,128)S(1)} %copy-done.22, bf16[8,512,576]{1,2,0:T(8,128)(2,1)S(1)} %get-tuple-element.46, pred[512,576]{0,1:T(8,128)(4,1)S(1)} %copy-done.13, f32[8]{0:T(128)S(1)} %copy-done.18, f32[8]{0:T(128)S(1)} %copy-done.19, bf16[512,1,128]{2,0,1:T(8,128)(2,1)S(1)} %bitcast.150, ...), kind=kOutput, calls=%fused_computation.23 | convolution fusion | flops 608206848 | bytes 9355328 | tf_op jit(solution)/shard_map/gkij,jgd->igkd/dot_general | solution.py:222
  102.3 7.1 %collective-permute-done.10 = f32[66048]{0:T(1024)S(1)} collective-permute-done((f32[66048]{0:T(1024)S(1)}, f32[66048]{0:T(1024)S(1)}, u32[]{:S(2)}, u32[]{:S(2)}) %collective-permute-start.10) | collective-permute-done | bytes 264224 | tf_op jit(solution)/shard_map/ppermute | solution.py:17
  109.5 1.9 %collective-permute-start.11 = (f32[66048]{0:T(1024)S(1)}, f32[66048]{0:T(1024)S(1)}, u32[]{:S(2)}, u32[]{:S(2)}) collective-permute-start(f32[66048]{0:T(1024)S(1)} %add.185), channel_id=1, source_target_pairs={{0,8},{8,16},{16,24},{24,32},{32,40},{40,48},{48,56},{56,64},{64,7... | collective-permute-start | bytes 792584 | tf_op jit(solution)/shard_map/ppermute | solution.py:17
  111.4 1.0 add_add_fusion.1
  112.5 9.2 %collective-permute-done.11 = f32[66048]{0:T(1024)S(1)} collective-permute-done((f32[66048]{0:T(1024)S(1)}, f32[66048]{0:T(1024)S(1)}, u32[]{:S(2)}, u32[]{:S(2)}) %collective-permute-start.11) | collective-permute-done | bytes 264224 | tf_op jit(solution)/shard_map/ppermute | solution.py:17
  121.7 1.1 add_add_fusion
  122.8 0.2 fusion.47
  123.0 0.2 fusion.45
  123.3 0.2 copy.31
  123.5 0.4 fusion.31
  124.0 1.1 copy-done.23
  125.1 0.5 fusion.15
  125.6 0.8 copy.35
  126.4 0.5 all_to_all.14
  126.9 20.3 %all_to_all.19 = bf16[8,64,1024]{2,1,0:T(8,128)(2,1)S(1)} all-to-all(bf16[8,64,1024]{2,1,0:T(8,128)(2,1)S(1)} %all_to_all.14), channel_id=1, replica_groups=mesh['seq'=32,'head'=8] {'head'}, dimensions={0} | all-to-all | bytes 2097152 | tf_op jit(solution)/shard_map/all_to_all | solution.py:252
  147.2 1.1 copy.47
  (65 shorter events, 0.6 us)
Async XLA Ops:
  0.0 56.7 %copy-start = (bf16[8,128,64]{1,2,0:T(8,128)(2,1)S(1)}, bf16[8,128,64]{1,2,0:T(8,128)(2,1)}, u32[]{:S(2)}) copy-start(bf16[8,128,64]{1,2,0:T(8,128)(2,1)} %param.14) | copy-start | bytes 393220
  0.0 8.8 %copy-start.14 = (bf16[512,128]{1,0:T(8,128)(2,1)S(1)}, bf16[512,128]{1,0:T(8,128)(2,1)}, u32[]{:S(2)}) copy-start(bf16[512,128]{1,0:T(8,128)(2,1)} %param.12) | copy-start | bytes 393220
  0.0 13.2 %copy-start.21 = (f32[8]{0:T(128)S(1)}, f32[8]{0:T(128)}, u32[]{:S(2)}) copy-start(f32[8]{0:T(128)} %param.16) | copy-start | bytes 100
  4.1 0.7 copy-start.2
  4.8 12.4 %copy-start.5 = (bf16[512,1,64]{2,0,1:T(8,128)(2,1)}, bf16[512,1,64]{2,0,1:T(8,128)(2,1)S(1)}, u32[]{:S(2)}) copy-start(bf16[512,1,64]{2,0,1:T(8,128)(2,1)S(1)} %get-tuple-element.23) | copy-start | bytes 196612
  4.8 12.4 %copy-start.7 = (bf16[512,1,64]{2,0,1:T(8,128)(2,1)}, bf16[512,1,64]{2,0,1:T(8,128)(2,1)S(1)}, u32[]{:S(2)}) copy-start(bf16[512,1,64]{2,0,1:T(8,128)(2,1)S(1)} %get-tuple-element.24) | copy-start | bytes 196612
  4.9 9.4 %collective-permute-start.1 = (bf16[64,1,128]{2,0,1:T(8,128)(2,1)S(1)}, bf16[64,1,128]{2,0,1:T(8,128)(2,1)S(1)}, u32[]{:S(2)}, u32[]{:S(2)}) collective-permute-start(bf16[64,1,128]{2,0,1:T(8,128)(2,1)S(1)} %pad_maximum_fusion.15), channel_id=1, source_target_pairs={{0,8},{8,16},{16,24},{24,32},{32,40},{40,48},{48,56},{56,64},{64,7... | collective-permute-start | bytes 49160 | tf_op jit(solution)/shard_map/ppermute | solution.py:17
  8.8 7.7 %collective-permute-start = (bf16[64,1,128]{2,0,1:T(8,128)(2,1)S(1)}, bf16[64,1,128]{2,0,1:T(8,128)(2,1)S(1)}, u32[]{:S(2)}, u32[]{:S(2)}) collective-permute-start(bf16[64,1,128]{2,0,1:T(8,128)(2,1)S(1)} %slice_bitcast_fusion), channel_id=1, source_target_pairs={{0,8},{8,16},{16,24},{24,32},{32,40},{40,48},{48,56},{56,64},{64,7... | collective-permute-start | bytes 49160 | tf_op jit(solution)/shard_map/ppermute | solution.py:17
  15.1 23.1 %copy-start.12 = (bf16[512,1024]{1,0:T(8,128)(2,1)S(1)}, bf16[512,1024]{1,0:T(8,128)(2,1)}, u32[]{:S(2)}) copy-start(bf16[512,1024]{1,0:T(8,128)(2,1)} %param.10) | copy-start | bytes 3145732
  16.5 0.7 copy-start.16
  21.8 12.1 %copy-start.4 = (f32[8,128,128]{2,1,0:T(8,128)S(1)}, f32[8,128,128]{2,1,0:T(8,128)}, u32[]{:S(2)}) copy-start(f32[8,128,128]{2,1,0:T(8,128)} %get-tuple-element.11) | copy-start | bytes 1572868
  22.8 11.1 %collective-permute-start.2 = (f32[66048]{0:T(1024)S(1)}, f32[66048]{0:T(1024)S(1)}, u32[]{:S(2)}, u32[]{:S(2)}) collective-permute-start(f32[66048]{0:T(1024)S(1)} %slice.59), channel_id=1, source_target_pairs={{0,8},{8,16},{16,24},{24,32},{32,40},{40,48},{48,56},{56,64},{64,7... | collective-permute-start | bytes 792584 | tf_op jit(solution)/shard_map/ppermute | solution.py:17
  33.9 0.9 copy-start.9
  34.8 24.6 %collective-permute-start.7 = (f32[66048]{0:T(1024)}, f32[66048]{0:T(1024)}, u32[]{:S(2)}, u32[]{:S(2)}) collective-permute-start(f32[66048]{0:T(1024)} %get-tuple-element.26), channel_id=1, source_target_pairs={{0,64},{8,72},{16,80},{24,88},{32,96},{40,104},{48,112},{56,120},{... | collective-permute-start | bytes 792584 | tf_op jit(solution)/shard_map/ppermute | solution.py:17
  41.0 5.0 %copy-start.3 = (f32[2,4,64,64]{3,2,1,0:T(8,128)S(1)}, f32[2,4,64,64]{3,2,1,0:T(8,128)}, u32[]{:S(2)}) copy-start(f32[2,4,64,64]{3,2,1,0:T(8,128)} %copy-done.2) | copy-start | bytes 393220
  42.9 19.6 %collective-permute-start.3 = (f32[66048]{0:T(1024)}, f32[66048]{0:T(1024)}, u32[]{:S(2)}, u32[]{:S(2)}) collective-permute-start(f32[66048]{0:T(1024)} %get-tuple-element.25), channel_id=1, source_target_pairs={{0,16},{8,24},{16,32},{24,40},{32,48},{40,56},{48,64},{56,72},{64,... | collective-permute-start | bytes 792584 | tf_op jit(solution)/shard_map/ppermute | solution.py:17
  46.0 2.9 %copy-start.1 = (pred[512,576]{0,1:T(8,128)(4,1)S(1)}, pred[512,576]{0,1:T(8,128)(4,1)}, u32[]{:S(2)}) copy-start(pred[512,576]{0,1:T(8,128)(4,1)} %get-tuple-element.32) | copy-start | bytes 884740
  46.0 2.9 %copy-start.6 = (bf16[512,1,64]{2,0,1:T(8,128)(2,1)S(1)}, bf16[512,1,64]{2,0,1:T(8,128)(2,1)}, u32[]{:S(2)}) copy-start(bf16[512,1,64]{2,0,1:T(8,128)(2,1)} %copy-done.5) | copy-start | bytes 196612
  46.0 2.9 %copy-start.8 = (bf16[512,1,64]{2,0,1:T(8,128)(2,1)S(1)}, bf16[512,1,64]{2,0,1:T(8,128)(2,1)}, u32[]{:S(2)}) copy-start(bf16[512,1,64]{2,0,1:T(8,128)(2,1)} %copy-done.7) | copy-start | bytes 196612
  51.2 2.0 %copy-start.15 = (bf16[512,128]{1,0:T(8,128)(2,1)S(1)}, bf16[512,128]{1,0:T(8,128)(2,1)}, u32[]{:S(2)}) copy-start(bf16[512,128]{1,0:T(8,128)(2,1)} %param.12) | copy-start | bytes 393220
  51.2 2.0 %copy-start.17 = (bf16[64,1,128]{2,0,1:T(8,128)(2,1)S(1)}, bf16[64,1,128]{2,0,1:T(8,128)(2,1)}, u32[]{:S(2)}) copy-start(bf16[64,1,128]{2,0,1:T(8,128)(2,1)} %copy-done.16) | copy-start | bytes 49156
  59.4 9.3 %copy-start.11 = (f32[512,8,64]{0,2,1:T(8,128)S(1)}, f32[512,8,64]{0,2,1:T(8,128)}, u32[]{:S(2)}) copy-start(f32[512,8,64]{0,2,1:T(8,128)} %get-tuple-element.42) | copy-start | bytes 3145732
  60.6 8.5 %collective-permute-start.8 = (f32[66048]{0:T(1024)S(1)}, f32[66048]{0:T(1024)S(1)}, u32[]{:S(2)}, u32[]{:S(2)}) collective-permute-start(f32[66048]{0:T(1024)S(1)} %add.179), channel_id=1, source_target_pairs={{0,128},{8,136},{16,144},{24,152},{32,160},{40,168},{48,176},{56,1... | collective-permute-start | bytes 792584 | tf_op jit(solution)/shard_map/ppermute | solution.py:17
  63.6 16.8 %collective-permute-start.4 = (f32[66048]{0:T(1024)S(1)}, f32[66048]{0:T(1024)S(1)}, u32[]{:S(2)}, u32[]{:S(2)}) collective-permute-start(f32[66048]{0:T(1024)S(1)} %add.173), channel_id=1, source_target_pairs={{0,32},{8,40},{16,48},{24,56},{32,64},{40,72},{48,80},{56,88},{64,... | collective-permute-start | bytes 792584 | tf_op jit(solution)/shard_map/ppermute | solution.py:17
  68.7 13.7 %copy-start.13 = (pred[512,576]{0,1:T(8,128)(4,1)S(1)}, pred[512,576]{0,1:T(8,128)(4,1)}, u32[]{:S(2)}) copy-start(pred[512,576]{0,1:T(8,128)(4,1)} %get-tuple-element.31) | copy-start | bytes 884740
  68.7 13.7 %copy-start.20 = (bf16[8,128,576]{2,1,0:T(8,128)(2,1)S(1)}, bf16[8,128,576]{2,1,0:T(8,128)(2,1)}, u32[]{:S(2)}) copy-start(bf16[8,128,576]{2,1,0:T(8,128)(2,1)} %get-tuple-element.13) | copy-start | bytes 3538948
  69.1 17.0 %collective-permute-start.9 = (f32[66048]{0:T(1024)S(1)}, f32[66048]{0:T(1024)S(1)}, u32[]{:S(2)}, u32[]{:S(2)}) collective-permute-start(f32[66048]{0:T(1024)S(1)} %add.181), channel_id=1, source_target_pairs={{0,32},{8,40},{16,48},{24,56},{32,64},{40,72},{48,80},{56,88},{64,... | collective-permute-start | bytes 792584 | tf_op jit(solution)/shard_map/ppermute | solution.py:17
  80.5 17.5 %collective-permute-start.5 = (f32[66048]{0:T(1024)S(1)}, f32[66048]{0:T(1024)S(1)}, u32[]{:S(2)}, u32[]{:S(2)}) collective-permute-start(f32[66048]{0:T(1024)S(1)} %add.175), channel_id=1, source_target_pairs={{0,64},{8,72},{16,80},{24,88},{32,96},{40,104},{48,112},{56,120},{... | collective-permute-start | bytes 792584 | tf_op jit(solution)/shard_map/ppermute | solution.py:17
  82.4 17.4 %copy-start.18 = (f32[8]{0:T(128)S(1)}, f32[8]{0:T(128)}, u32[]{:S(2)}) copy-start(f32[8]{0:T(128)} %get-tuple-element.17) | copy-start | bytes 100
  82.4 17.4 %copy-start.19 = (f32[8]{0:T(128)S(1)}, f32[8]{0:T(128)}, u32[]{:S(2)}) copy-start(f32[8]{0:T(128)} %get-tuple-element.18) | copy-start | bytes 100
  82.4 17.4 %copy-start.22 = (f32[128,8,512]{2,0,1:T(8,128)S(1)}, f32[128,8,512]{2,0,1:T(8,128)}, u32[]{:S(2)}) copy-start(f32[128,8,512]{2,0,1:T(8,128)} %fusion.10) | copy-start | bytes 6291460
  86.1 23.3 %collective-permute-start.10 = (f32[66048]{0:T(1024)S(1)}, f32[66048]{0:T(1024)S(1)}, u32[]{:S(2)}, u32[]{:S(2)}) collective-permute-start(f32[66048]{0:T(1024)S(1)} %add.183), channel_id=1, source_target_pairs={{0,16},{8,24},{16,32},{24,40},{32,48},{40,56},{48,64},{56,72},{64,... | collective-permute-start | bytes 792584 | tf_op jit(solution)/shard_map/ppermute | solution.py:17
  98.0 13.4 %collective-permute-start.6 = (f32[66048]{0:T(1024)S(1)}, f32[66048]{0:T(1024)S(1)}, u32[]{:S(2)}, u32[]{:S(2)}) collective-permute-start(f32[66048]{0:T(1024)S(1)} %add.177), channel_id=1, source_target_pairs={{0,128},{8,136},{16,144},{24,152},{32,160},{40,168},{48,176},{56,1... | collective-permute-start | bytes 792584 | tf_op jit(solution)/shard_map/ppermute | solution.py:17
  99.8 11.6 %copy-start.10 = (f32[66048]{0:T(1024)S(1)}, f32[66048]{0:T(1024)}, u32[]{:S(2)}) copy-start(f32[66048]{0:T(1024)} %copy-done.9) | copy-start | bytes 792580
  109.5 12.2 %collective-permute-start.11 = (f32[66048]{0:T(1024)S(1)}, f32[66048]{0:T(1024)S(1)}, u32[]{:S(2)}, u32[]{:S(2)}) collective-permute-start(f32[66048]{0:T(1024)S(1)} %add.185), channel_id=1, source_target_pairs={{0,8},{8,16},{16,24},{24,32},{32,40},{40,48},{48,56},{56,64},{64,7... | collective-permute-start | bytes 792584 | tf_op jit(solution)/shard_map/ppermute | solution.py:17
  123.5 1.6 %copy-start.23 = (f32[512,1,8,128]{0,3,2,1:T(8,128)S(1)}, f32[512,1,8,128]{0,3,2,1:T(8,128)}, u32[]{:S(2)}) copy-start(f32[512,1,8,128]{0,3,2,1:T(8,128)} %fusion.17) | copy-start | bytes 6291460

commit v19 on v18

--- a/solution.py
+++ b/solution.py
@@ -171,7 +171,7 @@
         shifts.append(steps)
         steps *= 2
     half = len(shifts) // 2 + 1
-    orders = (shifts, shifts[half:] + shifts[:half][::-1])
+    orders = (shifts[:half] + shifts[half:][::-1], shifts[half:] + shifts[:half][::-1])
     middle = packed.size // 2
     pieces = []
     for order, piece in zip(orders, (packed[:middle], packed[middle:])):

time: 149 us -> 149 us (level)
  transfers between devices with their start and end apart: 12 -> 12, of which waited for: 7 -> 8; matrix products, arithmetic and copies ran while one was open for 20% -> 20% of each run, Pallas kernels for 0% -> 0%
where the time goes in v19:
time: 149 us
  starting transfers between devices  45.6 us (31%)
  waiting for transfers between devices  33.8 us (23%)
  blocking collectives  20.3 us (14%)
  other arithmetic  20.1 us (13%)
  matrix products  13.9 us (9%)
  local copies, waits for them, and re-layouts  9.95 us (7%)
  Pallas kernels  4.59 us (3%)
    ppermute x12, starting transfers between devices, passed_along(): lax.ppermute(value, axis, [(source, source + steps) for source in range(f...  45.6 us
    ppermute x12, waiting for transfers between devices, passed_along(): lax.ppermute(value, axis, [(source, source + steps) for source in range(f...  33.8 us
    all_to_all x1, blocking collectives, body(): lax.all_to_all(result, 'head', split_axis=0, concat_axis=1, tiled=True)  20.3 us
    unnamed x50, local copies, waits for them, and re-layouts  5.58 us
    another operation x5, other arithmetic  4.76 us
    pallas_call x1, Pallas kernels, key_features(): pl.pallas_call(kernel, grid=(1,), in_specs=[pl.BlockSpec((rows, dim), lam...  4.59 us
    dot_general x1, matrix products, body(): jnp.einsum('gkij,jgd->igkd', weights.astype(jnp.bfloat16), ext_values, pr...  3.48 us
    add x8, other arithmetic, body(): inclusive = inclusive + received  3.27 us
  transfers between devices with their start and end apart: 12, of which 8 were waited for; matrix products, arithmetic and copies ran while one was open for 20% of the time, Pallas kernels for 0%

profile of v19, /device:TPU:2, one launch (start us, length us, event | category | flops | bytes accessed | tf_op | source)
XLA Modules:
  0.0 148.7 jit_solution(9522561130268595934)
XLA Ops:
  0.0 0.7 and_select_fusion.1
  0.8 0.8 fusion.35
  1.6 0.9 bitcast_convert_fusion
  2.5 0.8 multiply_cosine_fusion.1
  3.3 0.8 fusion.43
  4.2 0.2 subtract_convert_fusion.3
  4.3 0.5 copy-done.2
  4.8 0.1 pad_maximum_fusion.15
  4.9 3.8 %collective-permute-start.1 = (bf16[64,1,128]{2,0,1:T(8,128)(2,1)S(1)}, bf16[64,1,128]{2,0,1:T(8,128)(2,1)S(1)}, u32[]{:S(2)}, u32[]{:S(2)}) collective-permute-start(bf16[64,1,128]{2,0,1:T(8,128)(2,1)S(1)} %pad_maximum_fusion.15), channel_id=1, source_target_pairs={{0,8},{8,16},{16,24},{24,32},{32,40},{40,48},{48,56},{56,64},{64,7... | collective-permute-start | bytes 49160 | tf_op jit(solution)/shard_map/ppermute | solution.py:17
  8.8 3.8 %collective-permute-start = (bf16[64,1,128]{2,0,1:T(8,128)(2,1)S(1)}, bf16[64,1,128]{2,0,1:T(8,128)(2,1)S(1)}, u32[]{:S(2)}, u32[]{:S(2)}) collective-permute-start(bf16[64,1,128]{2,0,1:T(8,128)(2,1)S(1)} %slice_bitcast_fusion), channel_id=1, source_target_pairs={{0,8},{8,16},{16,24},{24,32},{32,40},{40,48},{48,56},{56,64},{64,7... | collective-permute-start | bytes 49160 | tf_op jit(solution)/shard_map/ppermute | solution.py:17
  12.6 0.6 or_convert_fusion.mask_ref
  13.2 0.6 broadcast_subtract_fusion
  13.8 0.6 collective-permute-done.1
  14.4 0.8 fusion.67.k_ref
  15.1 1.4 collective-permute-done
  16.5 0.7 fusion.33.v_ref
  17.2 4.6 %shard_map.100 = (bf16[8,128,576]{2,1,0:T(8,128)(2,1)}, f32[8,128,128]{2,1,0:T(8,128)}, f32[8,128,1]{2,1,0:T(8,128)}) custom-call(bf16[576,128]{1,0:T(8,128)(2,1)} %fusion.67.k_ref, bf16[8,64,128]{2,1,0:T(8,128)(2,1)} %bitcast.151, bf16[576,128]{1,0:T(8,128)(2,1)} %fusion.33.v_ref, f32[1,576]{1,0:T(1,128)} %or_convert_fusion.mask_ref), custom_call_target="tpu_custom_call" | custom-call | tf_op jit(solution)/shard_map/pallas_call | solution.py:104
  21.8 1.0 slice.59
  22.8 1.9 %collective-permute-start.2 = (f32[66048]{0:T(1024)S(1)}, f32[66048]{0:T(1024)S(1)}, u32[]{:S(2)}, u32[]{:S(2)}) collective-permute-start(f32[66048]{0:T(1024)S(1)} %slice.59), channel_id=1, source_target_pairs={{0,8},{8,16},{16,24},{24,32},{32,40},{40,48},{48,56},{56,64},{64,7... | collective-permute-start | bytes 792584 | tf_op jit(solution)/shard_map/ppermute | solution.py:17
  24.8 1.2 fusion.22
  25.9 1.2 reduce.4
  27.2 6.7 %collective-permute-done.2 = f32[66048]{0:T(1024)S(1)} collective-permute-done((f32[66048]{0:T(1024)S(1)}, f32[66048]{0:T(1024)S(1)}, u32[]{:S(2)}, u32[]{:S(2)}) %collective-permute-start.2) | collective-permute-done | bytes 264224 | tf_op jit(solution)/shard_map/ppermute | solution.py:17
  33.9 0.9 slice_add_fusion
  34.8 3.4 %collective-permute-start.7 = (f32[66048]{0:T(1024)}, f32[66048]{0:T(1024)}, u32[]{:S(2)}, u32[]{:S(2)}) collective-permute-start(f32[66048]{0:T(1024)} %get-tuple-element.26), channel_id=1, source_target_pairs={{0,64},{8,72},{16,80},{24,88},{32,96},{40,104},{48,112},{56,120},{... | collective-permute-start | bytes 792584 | tf_op jit(solution)/shard_map/ppermute | solution.py:17
  38.2 0.5 copy.26
  38.8 0.3 fusion.69
  39.0 1.9 %copy.45 = f32[512,8,64]{2,0,1:T(8,128)} copy(f32[512,8,64]{0,2,1:T(8,128)S(1)} %get-tuple-element.22) | data formatting | bytes 2097152
  41.0 1.9 %copy.46 = f32[512,8,64]{2,0,1:T(8,128)} copy(f32[512,8,64]{0,2,1:T(8,128)S(1)} %get-tuple-element.21) | data formatting | bytes 2097152
  42.9 3.0 %collective-permute-start.3 = (f32[66048]{0:T(1024)}, f32[66048]{0:T(1024)}, u32[]{:S(2)}, u32[]{:S(2)}) collective-permute-start(f32[66048]{0:T(1024)} %get-tuple-element.25), channel_id=1, source_target_pairs={{0,16},{8,24},{16,32},{24,40},{32,48},{40,56},{48,64},{56,72},{64,... | collective-permute-start | bytes 792584 | tf_op jit(solution)/shard_map/ppermute | solution.py:17
  46.0 2.9 %subtract_convert_fusion = (bf16[512,8,64]{2,0,1:T(8,128)(2,1)S(1)}, bf16[512,8,64]{2,0,1:T(8,128)(2,1)S(1)}) fusion(f32[512,8,64]{2,0,1:T(8,128)} %copy.46, f32[512,8,64]{2,0,1:T(8,128)} %copy.45, f32[512,64]{1,0:T(8,128)S(1)} %bitcast.144, f32[512,64]{1,0:T(8,128)S(1)} %bitcast.142), kind=kLoop, calls=%fused_computation.26 | loop fusion | flops 2097152 | bytes 3407872 | tf_op jit(solution)/shard_map/convert.4
  48.9 2.3 %fusion.2 = (f32[8,512]{1,0:T(8,128)S(1)}, f32[576,512,8]{1,0,2:T(8,128)S(1)}) fusion(pred[512,576]{0,1:T(8,128)(4,1)S(1)} %copy-done.1, bf16[512,8,64]{2,0,1:T(8,128)(2,1)S(1)} %get-tuple-element.20, bf16[512,8,64]{2,0,1:T(8,128)(2,1)S(1)} %get-tuple-element.19, bf16[512,1,64]{2,0,1:T(8,128)(2,1)S(1)} %copy-done.8, bf16[512,1,64]{2,0,1:T(8,128)(2,1)S(1)} %copy-done.6, ...), kind=kOutput, calls=%fused_computation.4 | convolution fusion | flops 613593088 | bytes 10944512 | tf_op jit(solution)/shard_map/igkd,jgd->gkij/dot_general | solution.py:206
  51.2 1.9 %fusion.5 = f32[8,512]{1,0:T(8,128)S(1)} fusion(f32[576,512,8]{1,0,2:T(8,128)S(1)} %get-tuple-element.40, f32[8,512]{1,0:T(8,128)S(1)} %get-tuple-element.39, pred[512,576]{0,1:T(8,128)(4,1)S(1)} %copy-done.1), kind=kLoop, calls=%fused_computation.9 | loop fusion | flops 9433088 | bytes 9764864 | tf_op jit(solution)/shard_map/reduce_sum | solution.py:212
  53.2 3.5 %fusion.10 = f32[128,8,512]{2,0,1:T(8,128)} fusion(f32[576,512,8]{1,0,2:T(8,128)S(1)} %get-tuple-element.40, f32[8,512]{1,0:T(8,128)S(1)} %get-tuple-element.39, pred[512,576]{0,1:T(8,128)(4,1)S(1)} %copy-done.1, bf16[512,1,128]{2,0,1:T(8,128)(2,1)S(1)} %bitcast.149, bf16[64,1,128]{2,0,1:T(8,128)(2,1)S(1)} %copy-done.17), kind=kOutput, calls=%fused_computation.14 | convolution fusion | flops 613711872 | bytes 11993088 | tf_op jit(solution)/shard_map/gkij,jgd->igkd/dot_general | solution.py:216
  56.7 0.9 fusion.71
  57.5 1.9 %fusion.70 = (f32[512,8]{0,1:T(8,128)S(1)}, f32[512,8,64]{0,2,1:T(8,128)}) fusion(bf16[8,128,64]{1,2,0:T(8,128)(2,1)S(1)} %copy-done, bf16[512,8,64]{2,0,1:T(8,128)(2,1)S(1)} %get-tuple-element.20, bf16[512,8,64]{2,0,1:T(8,128)(2,1)S(1)} %get-tuple-element.19), kind=kOutput, calls=%fused_computation.128 | convolution fusion | flops 69992512 | bytes 2244608 | tf_op jit(solution)/shard_map/sub | solution.py:71
  59.4 1.1 add.179
  60.6 1.9 %collective-permute-start.8 = (f32[66048]{0:T(1024)S(1)}, f32[66048]{0:T(1024)S(1)}, u32[]{:S(2)}, u32[]{:S(2)}) collective-permute-start(f32[66048]{0:T(1024)S(1)} %add.179), channel_id=1, source_target_pairs={{0,128},{8,136},{16,144},{24,152},{32,160},{40,168},{48,176},{56,1... | collective-permute-start | bytes 792584 | tf_op jit(solution)/shard_map/ppermute | solution.py:17
  62.5 1.1 add.173
  63.6 5.1 %collective-permute-start.4 = (f32[66048]{0:T(1024)S(1)}, f32[66048]{0:T(1024)S(1)}, u32[]{:S(2)}, u32[]{:S(2)}) collective-permute-start(f32[66048]{0:T(1024)S(1)} %add.173), channel_id=1, source_target_pairs={{0,32},{8,40},{16,48},{24,56},{32,64},{40,72},{48,80},{56,88},{64,... | collective-permute-start | bytes 792584 | tf_op jit(solution)/shard_map/ppermute | solution.py:17
  68.7 0.3 divide_convert_fusion
  69.1 4.8 %collective-permute-start.9 = (f32[66048]{0:T(1024)S(1)}, f32[66048]{0:T(1024)S(1)}, u32[]{:S(2)}, u32[]{:S(2)}) collective-permute-start(f32[66048]{0:T(1024)S(1)} %add.181), channel_id=1, source_target_pairs={{0,32},{8,40},{16,48},{24,56},{32,64},{40,72},{48,80},{56,88},{64,... | collective-permute-start | bytes 792584 | tf_op jit(solution)/shard_map/ppermute | solution.py:17
  73.8 6.6 %collective-permute-done.4 = f32[66048]{0:T(1024)S(1)} collective-permute-done((f32[66048]{0:T(1024)S(1)}, f32[66048]{0:T(1024)S(1)}, u32[]{:S(2)}, u32[]{:S(2)}) %collective-permute-start.4) | collective-permute-done | bytes 264224 | tf_op jit(solution)/shard_map/ppermute | solution.py:17
  80.5 1.3 collective-permute-start.5
  81.8 1.6 %select_reduce_fusion = (f32[8,512]{1,0:T(8,128)S(1)}, bf16[8,512,576]{1,2,0:T(8,128)(2,1)S(1)}) fusion(pred[512,576]{0,1:T(8,128)(4,1)S(1)} %copy-done.13, bf16[8,128,576]{2,1,0:T(8,128)(2,1)S(1)} %copy-done.20, bf16[512,8,64]{0,2,1:T(8,128)(2,1)S(1)} %get-tuple-element.47, bf16[512,8,64]{0,2,1:T(8,128)(2,1)S(1)} %get-tuple-element.48), kind=kOutput, calls=%fused_computation.7 | convolution fusion | flops 613150720 | bytes 7258112 | tf_op jit(solution)/shard_map/igkf,gkfj->gkij/dot_general | solution.py:213
  83.4 2.7 %collective-permute-done.9 = f32[66048]{0:T(1024)S(1)} collective-permute-done((f32[66048]{0:T(1024)S(1)}, f32[66048]{0:T(1024)S(1)}, u32[]{:S(2)}, u32[]{:S(2)}) %collective-permute-start.9) | collective-permute-done | bytes 264224 | tf_op jit(solution)/shard_map/ppermute | solution.py:17
  86.1 11.8 %collective-permute-start.10 = (f32[66048]{0:T(1024)S(1)}, f32[66048]{0:T(1024)S(1)}, u32[]{:S(2)}, u32[]{:S(2)}) collective-permute-start(f32[66048]{0:T(1024)S(1)} %add.183), channel_id=1, source_target_pairs={{0,16},{8,24},{16,32},{24,40},{32,48},{40,56},{48,64},{56,72},{64,... | collective-permute-start | bytes 792584 | tf_op jit(solution)/shard_map/ppermute | solution.py:17
  98.0 2.7 %collective-permute-start.6 = (f32[66048]{0:T(1024)S(1)}, f32[66048]{0:T(1024)S(1)}, u32[]{:S(2)}, u32[]{:S(2)}) collective-permute-start(f32[66048]{0:T(1024)S(1)} %add.177), channel_id=1, source_target_pairs={{0,64},{8,72},{16,80},{24,88},{32,96},{40,104},{48,112},{56,120},{... | collective-permute-start | bytes 792584 | tf_op jit(solution)/shard_map/ppermute | solution.py:17
  100.8 2.4 %fusion.17 = f32[512,1,8,128]{0,3,2,1:T(8,128)} fusion(f32[128,8,512]{2,0,1:T(8,128)S(1)} %copy-done.22, bf16[8,512,576]{1,2,0:T(8,128)(2,1)S(1)} %get-tuple-element.46, pred[512,576]{0,1:T(8,128)(4,1)S(1)} %copy-done.13, f32[8]{0:T(128)S(1)} %copy-done.18, f32[8]{0:T(128)S(1)} %copy-done.19, bf16[512,1,128]{2,0,1:T(8,128)(2,1)S(1)} %bitcast.150, ...), kind=kOutput, calls=%fused_computation.23 | convolution fusion | flops 608206848 | bytes 9355328 | tf_op jit(solution)/shard_map/gkij,jgd->igkd/dot_general | solution.py:222
  103.3 6.6 %collective-permute-done.10 = f32[66048]{0:T(1024)S(1)} collective-permute-done((f32[66048]{0:T(1024)S(1)}, f32[66048]{0:T(1024)S(1)}, u32[]{:S(2)}, u32[]{:S(2)}) %collective-permute-start.10) | collective-permute-done | bytes 264224 | tf_op jit(solution)/shard_map/ppermute | solution.py:17
  109.9 1.9 %collective-permute-start.11 = (f32[66048]{0:T(1024)S(1)}, f32[66048]{0:T(1024)S(1)}, u32[]{:S(2)}, u32[]{:S(2)}) collective-permute-start(f32[66048]{0:T(1024)S(1)} %add.185), channel_id=1, source_target_pairs={{0,8},{8,16},{16,24},{24,32},{32,40},{40,48},{48,56},{56,64},{64,7... | collective-permute-start | bytes 792584 | tf_op jit(solution)/shard_map/ppermute | solution.py:17
  111.8 1.1 collective-permute-done.6
  112.8 1.0 add_add_fusion.1
  113.9 8.3 %collective-permute-done.11 = f32[66048]{0:T(1024)S(1)} collective-permute-done((f32[66048]{0:T(1024)S(1)}, f32[66048]{0:T(1024)S(1)}, u32[]{:S(2)}, u32[]{:S(2)}) %collective-permute-start.11) | collective-permute-done | bytes 264224 | tf_op jit(solution)/shard_map/ppermute | solution.py:17
  122.2 1.1 add_add_fusion
  123.3 0.2 fusion.47
  123.5 0.2 fusion.45
  123.8 0.2 copy.31
  124.0 0.4 fusion.31
  124.5 1.1 copy-done.23
  125.6 0.5 fusion.15
  126.1 0.8 copy.35
  126.9 0.5 all_to_all.14
  127.4 20.3 %all_to_all.19 = bf16[8,64,1024]{2,1,0:T(8,128)(2,1)S(1)} all-to-all(bf16[8,64,1024]{2,1,0:T(8,128)(2,1)S(1)} %all_to_all.14), channel_id=1, replica_groups=mesh['seq'=32,'head'=8] {'head'}, dimensions={0} | all-to-all | bytes 2097152 | tf_op jit(solution)/shard_map/all_to_all | solution.py:252
  147.6 1.1 copy.47
  (65 shorter events, 0.6 us)
Async XLA Ops:
  0.0 56.7 %copy-start = (bf16[8,128,64]{1,2,0:T(8,128)(2,1)S(1)}, bf16[8,128,64]{1,2,0:T(8,128)(2,1)}, u32[]{:S(2)}) copy-start(bf16[8,128,64]{1,2,0:T(8,128)(2,1)} %param.14) | copy-start | bytes 393220
  0.0 8.8 %copy-start.14 = (bf16[512,128]{1,0:T(8,128)(2,1)S(1)}, bf16[512,128]{1,0:T(8,128)(2,1)}, u32[]{:S(2)}) copy-start(bf16[512,128]{1,0:T(8,128)(2,1)} %param.12) | copy-start | bytes 393220
  0.0 13.2 %copy-start.21 = (f32[8]{0:T(128)S(1)}, f32[8]{0:T(128)}, u32[]{:S(2)}) copy-start(f32[8]{0:T(128)} %param.16) | copy-start | bytes 100
  4.1 0.7 copy-start.2
  4.8 12.4 %copy-start.5 = (bf16[512,1,64]{2,0,1:T(8,128)(2,1)}, bf16[512,1,64]{2,0,1:T(8,128)(2,1)S(1)}, u32[]{:S(2)}) copy-start(bf16[512,1,64]{2,0,1:T(8,128)(2,1)S(1)} %get-tuple-element.23) | copy-start | bytes 196612
  4.8 12.4 %copy-start.7 = (bf16[512,1,64]{2,0,1:T(8,128)(2,1)}, bf16[512,1,64]{2,0,1:T(8,128)(2,1)S(1)}, u32[]{:S(2)}) copy-start(bf16[512,1,64]{2,0,1:T(8,128)(2,1)S(1)} %get-tuple-element.24) | copy-start | bytes 196612
  4.9 9.4 %collective-permute-start.1 = (bf16[64,1,128]{2,0,1:T(8,128)(2,1)S(1)}, bf16[64,1,128]{2,0,1:T(8,128)(2,1)S(1)}, u32[]{:S(2)}, u32[]{:S(2)}) collective-permute-start(bf16[64,1,128]{2,0,1:T(8,128)(2,1)S(1)} %pad_maximum_fusion.15), channel_id=1, source_target_pairs={{0,8},{8,16},{16,24},{24,32},{32,40},{40,48},{48,56},{56,64},{64,7... | collective-permute-start | bytes 49160 | tf_op jit(solution)/shard_map/ppermute | solution.py:17
  8.8 7.7 %collective-permute-start = (bf16[64,1,128]{2,0,1:T(8,128)(2,1)S(1)}, bf16[64,1,128]{2,0,1:T(8,128)(2,1)S(1)}, u32[]{:S(2)}, u32[]{:S(2)}) collective-permute-start(bf16[64,1,128]{2,0,1:T(8,128)(2,1)S(1)} %slice_bitcast_fusion), channel_id=1, source_target_pairs={{0,8},{8,16},{16,24},{24,32},{32,40},{40,48},{48,56},{56,64},{64,7... | collective-permute-start | bytes 49160 | tf_op jit(solution)/shard_map/ppermute | solution.py:17
  15.1 23.1 %copy-start.12 = (bf16[512,1024]{1,0:T(8,128)(2,1)S(1)}, bf16[512,1024]{1,0:T(8,128)(2,1)}, u32[]{:S(2)}) copy-start(bf16[512,1024]{1,0:T(8,128)(2,1)} %param.10) | copy-start | bytes 3145732
  16.5 0.7 copy-start.16
  21.8 12.1 %copy-start.4 = (f32[8,128,128]{2,1,0:T(8,128)S(1)}, f32[8,128,128]{2,1,0:T(8,128)}, u32[]{:S(2)}) copy-start(f32[8,128,128]{2,1,0:T(8,128)} %get-tuple-element.11) | copy-start | bytes 1572868
  22.8 11.1 %collective-permute-start.2 = (f32[66048]{0:T(1024)S(1)}, f32[66048]{0:T(1024)S(1)}, u32[]{:S(2)}, u32[]{:S(2)}) collective-permute-start(f32[66048]{0:T(1024)S(1)} %slice.59), channel_id=1, source_target_pairs={{0,8},{8,16},{16,24},{24,32},{32,40},{40,48},{48,56},{56,64},{64,7... | collective-permute-start | bytes 792584 | tf_op jit(solution)/shard_map/ppermute | solution.py:17
  33.9 0.9 copy-start.9
  34.8 24.6 %collective-permute-start.7 = (f32[66048]{0:T(1024)}, f32[66048]{0:T(1024)}, u32[]{:S(2)}, u32[]{:S(2)}) collective-permute-start(f32[66048]{0:T(1024)} %get-tuple-element.26), channel_id=1, source_target_pairs={{0,64},{8,72},{16,80},{24,88},{32,96},{40,104},{48,112},{56,120},{... | collective-permute-start | bytes 792584 | tf_op jit(solution)/shard_map/ppermute | solution.py:17
  41.0 5.0 %copy-start.3 = (f32[2,4,64,64]{3,2,1,0:T(8,128)S(1)}, f32[2,4,64,64]{3,2,1,0:T(8,128)}, u32[]{:S(2)}) copy-start(f32[2,4,64,64]{3,2,1,0:T(8,128)} %copy-done.2) | copy-start | bytes 393220
  42.9 19.6 %collective-permute-start.3 = (f32[66048]{0:T(1024)}, f32[66048]{0:T(1024)}, u32[]{:S(2)}, u32[]{:S(2)}) collective-permute-start(f32[66048]{0:T(1024)} %get-tuple-element.25), channel_id=1, source_target_pairs={{0,16},{8,24},{16,32},{24,40},{32,48},{40,56},{48,64},{56,72},{64,... | collective-permute-start | bytes 792584 | tf_op jit(solution)/shard_map/ppermute | solution.py:17
  46.0 2.9 %copy-start.1 = (pred[512,576]{0,1:T(8,128)(4,1)S(1)}, pred[512,576]{0,1:T(8,128)(4,1)}, u32[]{:S(2)}) copy-start(pred[512,576]{0,1:T(8,128)(4,1)} %get-tuple-element.32) | copy-start | bytes 884740
  46.0 2.9 %copy-start.6 = (bf16[512,1,64]{2,0,1:T(8,128)(2,1)S(1)}, bf16[512,1,64]{2,0,1:T(8,128)(2,1)}, u32[]{:S(2)}) copy-start(bf16[512,1,64]{2,0,1:T(8,128)(2,1)} %copy-done.5) | copy-start | bytes 196612
  46.0 2.9 %copy-start.8 = (bf16[512,1,64]{2,0,1:T(8,128)(2,1)S(1)}, bf16[512,1,64]{2,0,1:T(8,128)(2,1)}, u32[]{:S(2)}) copy-start(bf16[512,1,64]{2,0,1:T(8,128)(2,1)} %copy-done.7) | copy-start | bytes 196612
  51.2 2.0 %copy-start.15 = (bf16[512,128]{1,0:T(8,128)(2,1)S(1)}, bf16[512,128]{1,0:T(8,128)(2,1)}, u32[]{:S(2)}) copy-start(bf16[512,128]{1,0:T(8,128)(2,1)} %param.12) | copy-start | bytes 393220
  51.2 2.0 %copy-start.17 = (bf16[64,1,128]{2,0,1:T(8,128)(2,1)S(1)}, bf16[64,1,128]{2,0,1:T(8,128)(2,1)}, u32[]{:S(2)}) copy-start(bf16[64,1,128]{2,0,1:T(8,128)(2,1)} %copy-done.16) | copy-start | bytes 49156
  59.4 9.3 %copy-start.11 = (f32[512,8,64]{0,2,1:T(8,128)S(1)}, f32[512,8,64]{0,2,1:T(8,128)}, u32[]{:S(2)}) copy-start(f32[512,8,64]{0,2,1:T(8,128)} %get-tuple-element.42) | copy-start | bytes 3145732
  60.6 8.5 %collective-permute-start.8 = (f32[66048]{0:T(1024)S(1)}, f32[66048]{0:T(1024)S(1)}, u32[]{:S(2)}, u32[]{:S(2)}) collective-permute-start(f32[66048]{0:T(1024)S(1)} %add.179), channel_id=1, source_target_pairs={{0,128},{8,136},{16,144},{24,152},{32,160},{40,168},{48,176},{56,1... | collective-permute-start | bytes 792584 | tf_op jit(solution)/shard_map/ppermute | solution.py:17
  63.6 16.8 %collective-permute-start.4 = (f32[66048]{0:T(1024)S(1)}, f32[66048]{0:T(1024)S(1)}, u32[]{:S(2)}, u32[]{:S(2)}) collective-permute-start(f32[66048]{0:T(1024)S(1)} %add.173), channel_id=1, source_target_pairs={{0,32},{8,40},{16,48},{24,56},{32,64},{40,72},{48,80},{56,88},{64,... | collective-permute-start | bytes 792584 | tf_op jit(solution)/shard_map/ppermute | solution.py:17
  68.7 13.1 %copy-start.13 = (pred[512,576]{0,1:T(8,128)(4,1)S(1)}, pred[512,576]{0,1:T(8,128)(4,1)}, u32[]{:S(2)}) copy-start(pred[512,576]{0,1:T(8,128)(4,1)} %get-tuple-element.31) | copy-start | bytes 884740
  68.7 13.1 %copy-start.20 = (bf16[8,128,576]{2,1,0:T(8,128)(2,1)S(1)}, bf16[8,128,576]{2,1,0:T(8,128)(2,1)}, u32[]{:S(2)}) copy-start(bf16[8,128,576]{2,1,0:T(8,128)(2,1)} %get-tuple-element.13) | copy-start | bytes 3538948
  69.1 17.0 %collective-permute-start.9 = (f32[66048]{0:T(1024)S(1)}, f32[66048]{0:T(1024)S(1)}, u32[]{:S(2)}, u32[]{:S(2)}) collective-permute-start(f32[66048]{0:T(1024)S(1)} %add.181), channel_id=1, source_target_pairs={{0,32},{8,40},{16,48},{24,56},{32,64},{40,72},{48,80},{56,88},{64,... | collective-permute-start | bytes 792584 | tf_op jit(solution)/shard_map/ppermute | solution.py:17
  80.5 17.5 %collective-permute-start.5 = (f32[66048]{0:T(1024)S(1)}, f32[66048]{0:T(1024)S(1)}, u32[]{:S(2)}, u32[]{:S(2)}) collective-permute-start(f32[66048]{0:T(1024)S(1)} %add.175), channel_id=1, source_target_pairs={{0,128},{8,136},{16,144},{24,152},{32,160},{40,168},{48,176},{56,1... | collective-permute-start | bytes 792584 | tf_op jit(solution)/shard_map/ppermute | solution.py:17
  81.8 18.9 %copy-start.18 = (f32[8]{0:T(128)S(1)}, f32[8]{0:T(128)}, u32[]{:S(2)}) copy-start(f32[8]{0:T(128)} %get-tuple-element.17) | copy-start | bytes 100
  81.8 18.9 %copy-start.19 = (f32[8]{0:T(128)S(1)}, f32[8]{0:T(128)}, u32[]{:S(2)}) copy-start(f32[8]{0:T(128)} %get-tuple-element.18) | copy-start | bytes 100
  81.8 18.9 %copy-start.22 = (f32[128,8,512]{2,0,1:T(8,128)S(1)}, f32[128,8,512]{2,0,1:T(8,128)}, u32[]{:S(2)}) copy-start(f32[128,8,512]{2,0,1:T(8,128)} %fusion.10) | copy-start | bytes 6291460
  86.1 23.7 %collective-permute-start.10 = (f32[66048]{0:T(1024)S(1)}, f32[66048]{0:T(1024)S(1)}, u32[]{:S(2)}, u32[]{:S(2)}) collective-permute-start(f32[66048]{0:T(1024)S(1)} %add.183), channel_id=1, source_target_pairs={{0,16},{8,24},{16,32},{24,40},{32,48},{40,56},{48,64},{56,72},{64,... | collective-permute-start | bytes 792584 | tf_op jit(solution)/shard_map/ppermute | solution.py:17
  98.0 14.8 %collective-permute-start.6 = (f32[66048]{0:T(1024)S(1)}, f32[66048]{0:T(1024)S(1)}, u32[]{:S(2)}, u32[]{:S(2)}) collective-permute-start(f32[66048]{0:T(1024)S(1)} %add.177), channel_id=1, source_target_pairs={{0,64},{8,72},{16,80},{24,88},{32,96},{40,104},{48,112},{56,120},{... | collective-permute-start | bytes 792584 | tf_op jit(solution)/shard_map/ppermute | solution.py:17
  100.8 12.1 %copy-start.10 = (f32[66048]{0:T(1024)S(1)}, f32[66048]{0:T(1024)}, u32[]{:S(2)}) copy-start(f32[66048]{0:T(1024)} %copy-done.9) | copy-start | bytes 792580
  109.9 12.3 %collective-permute-start.11 = (f32[66048]{0:T(1024)S(1)}, f32[66048]{0:T(1024)S(1)}, u32[]{:S(2)}, u32[]{:S(2)}) collective-permute-start(f32[66048]{0:T(1024)S(1)} %add.185), channel_id=1, source_target_pairs={{0,8},{8,16},{16,24},{24,32},{32,40},{40,48},{48,56},{56,64},{64,7... | collective-permute-start | bytes 792584 | tf_op jit(solution)/shard_map/ppermute | solution.py:17
  124.0 1.6 %copy-start.23 = (f32[512,1,8,128]{0,3,2,1:T(8,128)S(1)}, f32[512,1,8,128]{0,3,2,1:T(8,128)}, u32[]{:S(2)}) copy-start(f32[512,1,8,128]{0,3,2,1:T(8,128)} %fusion.17) | copy-start | bytes 6291460

commit v20 on v19

--- a/solution.py
+++ b/solution.py
@@ -171,7 +171,7 @@
         shifts.append(steps)
         steps *= 2
     half = len(shifts) // 2 + 1
-    orders = (shifts[:half] + shifts[half:][::-1], shifts[half:] + shifts[:half][::-1])
+    orders = (shifts, shifts[::-1])
     middle = packed.size // 2
     pieces = []
     for order, piece in zip(orders, (packed[:middle], packed[middle:])):

time: 149 us -> 147 us (0.987)
  waiting for transfers between devices: 33.8 us -> 29.7 us
  starting transfers between devices: 45.6 us -> 47.5 us
    ppermute x12, waiting for transfers between devices: 33.8 us -> 29.7 us  [passed_along(): lax.ppermute(value, axis, [(source, source + steps) for source in range(f...]
    ppermute x12, starting transfers between devices: 45.6 us -> 47.5 us  [passed_along(): lax.ppermute(value, axis, [(source, source + steps) for source in range(f...]
  transfers between devices with their start and end apart: 12 -> 12, of which waited for: 8 -> 7; matrix products, arithmetic and copies ran while one was open for 20% -> 21% of each run, Pallas kernels for 0% -> 0%
where the time goes in v20:
time: 147 us; the launch traced here: 146 us
  starting transfers between devices  47.5 us (32%)
  waiting for transfers between devices  29.7 us (20%)
  blocking collectives  20.2 us (14%)
  other arithmetic  20.1 us (14%)
  matrix products  13.9 us (9%)
  local copies, waits for them, and re-layouts  9.94 us (7%)
  Pallas kernels  4.59 us (3%)
    ppermute x12, starting transfers between devices, passed_along(): lax.ppermute(value, axis, [(source, source + steps) for source in range(f...  47.5 us
    ppermute x12, waiting for transfers between devices, passed_along(): lax.ppermute(value, axis, [(source, source + steps) for source in range(f...  29.7 us
    all_to_all x1, blocking collectives, body(): lax.all_to_all(result, 'head', split_axis=0, concat_axis=1, tiled=True)  20.2 us
    unnamed x50, local copies, waits for them, and re-layouts  5.57 us
    another operation x5, other arithmetic  4.76 us
    pallas_call x1, Pallas kernels, key_features(): pl.pallas_call(kernel, grid=(1,), in_specs=[pl.BlockSpec((rows, dim), lam...  4.59 us
    dot_general x1, matrix products, body(): jnp.einsum('gkij,jgd->igkd', weights.astype(jnp.bfloat16), ext_values, pr...  3.48 us
    add x8, other arithmetic, body(): inclusive = inclusive + received  3.27 us
  transfers between devices with their start and end apart: 12, of which 7 were waited for; matrix products, arithmetic and copies ran while one was open for 21% of the time, Pallas kernels for 0%

profile of v20, /device:TPU:2, one launch (start us, length us, event | category | flops | bytes accessed | tf_op | source)
XLA Modules:
  0.0 146.4 jit_solution(1257279430665040633)
XLA Ops:
  0.0 0.7 and_select_fusion.1
  0.7 0.1 fusion.52
  0.8 0.8 fusion.35
  1.6 0.9 bitcast_convert_fusion
  2.5 0.8 multiply_cosine_fusion.1
  3.3 0.8 fusion.43
  4.2 0.2 subtract_convert_fusion.3
  4.3 0.5 copy-done.2
  4.8 0.1 pad_maximum_fusion.15
  4.9 3.8 %collective-permute-start.1 = (bf16[64,1,128]{2,0,1:T(8,128)(2,1)S(1)}, bf16[64,1,128]{2,0,1:T(8,128)(2,1)S(1)}, u32[]{:S(2)}, u32[]{:S(2)}) collective-permute-start(bf16[64,1,128]{2,0,1:T(8,128)(2,1)S(1)} %pad_maximum_fusion.15), channel_id=1, source_target_pairs={{0,8},{8,16},{16,24},{24,32},{32,40},{40,48},{48,56},{56,64},{64,7... | collective-permute-start | bytes 49160 | tf_op jit(solution)/shard_map/ppermute | solution.py:17
  8.8 3.8 %collective-permute-start = (bf16[64,1,128]{2,0,1:T(8,128)(2,1)S(1)}, bf16[64,1,128]{2,0,1:T(8,128)(2,1)S(1)}, u32[]{:S(2)}, u32[]{:S(2)}) collective-permute-start(bf16[64,1,128]{2,0,1:T(8,128)(2,1)S(1)} %slice_bitcast_fusion), channel_id=1, source_target_pairs={{0,8},{8,16},{16,24},{24,32},{32,40},{40,48},{48,56},{56,64},{64,7... | collective-permute-start | bytes 49160 | tf_op jit(solution)/shard_map/ppermute | solution.py:17
  12.6 0.6 or_convert_fusion.mask_ref
  13.2 0.6 broadcast_subtract_fusion
  13.8 0.6 collective-permute-done.1
  14.4 0.8 fusion.67.k_ref
  15.1 1.4 collective-permute-done
  16.5 0.7 fusion.33.v_ref
  17.2 4.6 %shard_map.100 = (bf16[8,128,576]{2,1,0:T(8,128)(2,1)}, f32[8,128,128]{2,1,0:T(8,128)}, f32[8,128,1]{2,1,0:T(8,128)}) custom-call(bf16[576,128]{1,0:T(8,128)(2,1)} %fusion.67.k_ref, bf16[8,64,128]{2,1,0:T(8,128)(2,1)} %bitcast.151, bf16[576,128]{1,0:T(8,128)(2,1)} %fusion.33.v_ref, f32[1,576]{1,0:T(1,128)} %or_convert_fusion.mask_ref), custom_call_target="tpu_custom_call" | custom-call | tf_op jit(solution)/shard_map/pallas_call | solution.py:104
  21.8 1.0 slice.59
  22.8 1.9 %collective-permute-start.2 = (f32[66048]{0:T(1024)S(1)}, f32[66048]{0:T(1024)S(1)}, u32[]{:S(2)}, u32[]{:S(2)}) collective-permute-start(f32[66048]{0:T(1024)S(1)} %slice.59), channel_id=1, source_target_pairs={{0,8},{8,16},{16,24},{24,32},{32,40},{40,48},{48,56},{56,64},{64,7... | collective-permute-start | bytes 792584 | tf_op jit(solution)/shard_map/ppermute | solution.py:17
  24.8 1.2 fusion.22
  25.9 1.2 reduce.4
  27.2 6.7 %collective-permute-done.2 = f32[66048]{0:T(1024)S(1)} collective-permute-done((f32[66048]{0:T(1024)S(1)}, f32[66048]{0:T(1024)S(1)}, u32[]{:S(2)}, u32[]{:S(2)}) %collective-permute-start.2) | collective-permute-done | bytes 264224 | tf_op jit(solution)/shard_map/ppermute | solution.py:17
  33.9 0.9 slice_add_fusion
  34.8 5.0 %collective-permute-start.7 = (f32[66048]{0:T(1024)}, f32[66048]{0:T(1024)}, u32[]{:S(2)}, u32[]{:S(2)}) collective-permute-start(f32[66048]{0:T(1024)} %get-tuple-element.26), channel_id=1, source_target_pairs={{0,128},{8,136},{16,144},{24,152},{32,160},{40,168},{48,176},{56,1... | collective-permute-start | bytes 792584 | tf_op jit(solution)/shard_map/ppermute | solution.py:17
  39.8 0.5 copy.26
  40.4 0.3 fusion.69
  40.7 1.9 %copy.45 = f32[512,8,64]{2,0,1:T(8,128)} copy(f32[512,8,64]{0,2,1:T(8,128)S(1)} %get-tuple-element.22) | data formatting | bytes 2097152
  42.6 1.9 %copy.46 = f32[512,8,64]{2,0,1:T(8,128)} copy(f32[512,8,64]{0,2,1:T(8,128)S(1)} %get-tuple-element.21) | data formatting | bytes 2097152
  44.5 2.7 %collective-permute-start.3 = (f32[66048]{0:T(1024)}, f32[66048]{0:T(1024)}, u32[]{:S(2)}, u32[]{:S(2)}) collective-permute-start(f32[66048]{0:T(1024)} %get-tuple-element.25), channel_id=1, source_target_pairs={{0,16},{8,24},{16,32},{24,40},{32,48},{40,56},{48,64},{56,72},{64,... | collective-permute-start | bytes 792584 | tf_op jit(solution)/shard_map/ppermute | solution.py:17
  47.3 2.9 %subtract_convert_fusion = (bf16[512,8,64]{2,0,1:T(8,128)(2,1)S(1)}, bf16[512,8,64]{2,0,1:T(8,128)(2,1)S(1)}) fusion(f32[512,8,64]{2,0,1:T(8,128)} %copy.46, f32[512,8,64]{2,0,1:T(8,128)} %copy.45, f32[512,64]{1,0:T(8,128)S(1)} %bitcast.144, f32[512,64]{1,0:T(8,128)S(1)} %bitcast.142), kind=kLoop, calls=%fused_computation.26 | loop fusion | flops 2097152 | bytes 3407872 | tf_op jit(solution)/shard_map/convert.4
  50.2 2.3 %fusion.2 = (f32[8,512]{1,0:T(8,128)S(1)}, f32[576,512,8]{1,0,2:T(8,128)S(1)}) fusion(pred[512,576]{0,1:T(8,128)(4,1)S(1)} %copy-done.1, bf16[512,8,64]{2,0,1:T(8,128)(2,1)S(1)} %get-tuple-element.20, bf16[512,8,64]{2,0,1:T(8,128)(2,1)S(1)} %get-tuple-element.19, bf16[512,1,64]{2,0,1:T(8,128)(2,1)S(1)} %copy-done.8, bf16[512,1,64]{2,0,1:T(8,128)(2,1)S(1)} %copy-done.6, ...), kind=kOutput, calls=%fused_computation.4 | convolution fusion | flops 613593088 | bytes 10944512 | tf_op jit(solution)/shard_map/igkd,jgd->gkij/dot_general | solution.py:206
  52.6 1.9 %fusion.5 = f32[8,512]{1,0:T(8,128)S(1)} fusion(f32[576,512,8]{1,0,2:T(8,128)S(1)} %get-tuple-element.40, f32[8,512]{1,0:T(8,128)S(1)} %get-tuple-element.39, pred[512,576]{0,1:T(8,128)(4,1)S(1)} %copy-done.1), kind=kLoop, calls=%fused_computation.9 | loop fusion | flops 9433088 | bytes 9764864 | tf_op jit(solution)/shard_map/reduce_sum | solution.py:212
  54.5 3.5 %fusion.10 = f32[128,8,512]{2,0,1:T(8,128)} fusion(f32[576,512,8]{1,0,2:T(8,128)S(1)} %get-tuple-element.40, f32[8,512]{1,0:T(8,128)S(1)} %get-tuple-element.39, pred[512,576]{0,1:T(8,128)(4,1)S(1)} %copy-done.1, bf16[512,1,128]{2,0,1:T(8,128)(2,1)S(1)} %bitcast.149, bf16[64,1,128]{2,0,1:T(8,128)(2,1)S(1)} %copy-done.17), kind=kOutput, calls=%fused_computation.14 | convolution fusion | flops 613711872 | bytes 11993088 | tf_op jit(solution)/shard_map/gkij,jgd->igkd/dot_general | solution.py:216
  58.0 0.9 fusion.71
  58.9 1.9 %fusion.70 = (f32[512,8]{0,1:T(8,128)S(1)}, f32[512,8,64]{0,2,1:T(8,128)}) fusion(bf16[8,128,64]{1,2,0:T(8,128)(2,1)S(1)} %copy-done, bf16[512,8,64]{2,0,1:T(8,128)(2,1)S(1)} %get-tuple-element.20, bf16[512,8,64]{2,0,1:T(8,128)(2,1)S(1)} %get-tuple-element.19), kind=kOutput, calls=%fused_computation.128 | convolution fusion | flops 69992512 | bytes 2244608 | tf_op jit(solution)/shard_map/sub | solution.py:71
  60.7 1.1 add.179
  61.9 1.9 %collective-permute-start.8 = (f32[66048]{0:T(1024)S(1)}, f32[66048]{0:T(1024)S(1)}, u32[]{:S(2)}, u32[]{:S(2)}) collective-permute-start(f32[66048]{0:T(1024)S(1)} %add.179), channel_id=1, source_target_pairs={{0,64},{8,72},{16,80},{24,88},{32,96},{40,104},{48,112},{56,120},{... | collective-permute-start | bytes 792584 | tf_op jit(solution)/shard_map/ppermute | solution.py:17
  63.8 1.1 add.173
  64.9 5.1 %collective-permute-start.4 = (f32[66048]{0:T(1024)S(1)}, f32[66048]{0:T(1024)S(1)}, u32[]{:S(2)}, u32[]{:S(2)}) collective-permute-start(f32[66048]{0:T(1024)S(1)} %add.173), channel_id=1, source_target_pairs={{0,32},{8,40},{16,48},{24,56},{32,64},{40,72},{48,80},{56,88},{64,... | collective-permute-start | bytes 792584 | tf_op jit(solution)/shard_map/ppermute | solution.py:17
  70.0 0.3 divide_convert_fusion
  70.4 4.9 %collective-permute-start.9 = (f32[66048]{0:T(1024)S(1)}, f32[66048]{0:T(1024)S(1)}, u32[]{:S(2)}, u32[]{:S(2)}) collective-permute-start(f32[66048]{0:T(1024)S(1)} %add.181), channel_id=1, source_target_pairs={{0,32},{8,40},{16,48},{24,56},{32,64},{40,72},{48,80},{56,88},{64,... | collective-permute-start | bytes 792584 | tf_op jit(solution)/shard_map/ppermute | solution.py:17
  75.3 5.7 %collective-permute-done.4 = f32[66048]{0:T(1024)S(1)} collective-permute-done((f32[66048]{0:T(1024)S(1)}, f32[66048]{0:T(1024)S(1)}, u32[]{:S(2)}, u32[]{:S(2)}) %collective-permute-start.4) | collective-permute-done | bytes 264224 | tf_op jit(solution)/shard_map/ppermute | solution.py:17
  81.0 1.9 %collective-permute-start.5 = (f32[66048]{0:T(1024)S(1)}, f32[66048]{0:T(1024)S(1)}, u32[]{:S(2)}, u32[]{:S(2)}) collective-permute-start(f32[66048]{0:T(1024)S(1)} %add.175), channel_id=1, source_target_pairs={{0,64},{8,72},{16,80},{24,88},{32,96},{40,104},{48,112},{56,120},{... | collective-permute-start | bytes 792584 | tf_op jit(solution)/shard_map/ppermute | solution.py:17
  83.0 1.6 %select_reduce_fusion = (f32[8,512]{1,0:T(8,128)S(1)}, bf16[8,512,576]{1,2,0:T(8,128)(2,1)S(1)}) fusion(pred[512,576]{0,1:T(8,128)(4,1)S(1)} %copy-done.13, bf16[8,128,576]{2,1,0:T(8,128)(2,1)S(1)} %copy-done.20, bf16[512,8,64]{0,2,1:T(8,128)(2,1)S(1)} %get-tuple-element.47, bf16[512,8,64]{0,2,1:T(8,128)(2,1)S(1)} %get-tuple-element.48), kind=kOutput, calls=%fused_computation.7 | convolution fusion | flops 613150720 | bytes 7258112 | tf_op jit(solution)/shard_map/igkf,gkfj->gkij/dot_general | solution.py:213
  84.6 2.0 %collective-permute-done.9 = f32[66048]{0:T(1024)S(1)} collective-permute-done((f32[66048]{0:T(1024)S(1)}, f32[66048]{0:T(1024)S(1)}, u32[]{:S(2)}, u32[]{:S(2)}) %collective-permute-start.9) | collective-permute-done | bytes 264224 | tf_op jit(solution)/shard_map/ppermute | solution.py:17
  86.6 12.7 %collective-permute-start.10 = (f32[66048]{0:T(1024)S(1)}, f32[66048]{0:T(1024)S(1)}, u32[]{:S(2)}, u32[]{:S(2)}) collective-permute-start(f32[66048]{0:T(1024)S(1)} %add.183), channel_id=1, source_target_pairs={{0,16},{8,24},{16,32},{24,40},{32,48},{40,56},{48,64},{56,72},{64,... | collective-permute-start | bytes 792584 | tf_op jit(solution)/shard_map/ppermute | solution.py:17
  99.4 1.5 %collective-permute-start.6 = (f32[66048]{0:T(1024)S(1)}, f32[66048]{0:T(1024)S(1)}, u32[]{:S(2)}, u32[]{:S(2)}) collective-permute-start(f32[66048]{0:T(1024)S(1)} %add.177), channel_id=1, source_target_pairs={{0,128},{8,136},{16,144},{24,152},{32,160},{40,168},{48,176},{56,1... | collective-permute-start | bytes 792584 | tf_op jit(solution)/shard_map/ppermute | solution.py:17
  101.0 2.4 %fusion.17 = f32[512,1,8,128]{0,3,2,1:T(8,128)} fusion(f32[128,8,512]{2,0,1:T(8,128)S(1)} %copy-done.22, bf16[8,512,576]{1,2,0:T(8,128)(2,1)S(1)} %get-tuple-element.46, pred[512,576]{0,1:T(8,128)(4,1)S(1)} %copy-done.13, f32[8]{0:T(128)S(1)} %copy-done.18, f32[8]{0:T(128)S(1)} %copy-done.19, bf16[512,1,128]{2,0,1:T(8,128)(2,1)S(1)} %bitcast.150, ...), kind=kOutput, calls=%fused_computation.23 | convolution fusion | flops 608206848 | bytes 9355328 | tf_op jit(solution)/shard_map/gkij,jgd->igkd/dot_general | solution.py:222
  103.5 5.1 %collective-permute-done.10 = f32[66048]{0:T(1024)S(1)} collective-permute-done((f32[66048]{0:T(1024)S(1)}, f32[66048]{0:T(1024)S(1)}, u32[]{:S(2)}, u32[]{:S(2)}) %collective-permute-start.10) | collective-permute-done | bytes 264224 | tf_op jit(solution)/shard_map/ppermute | solution.py:17
  108.6 2.0 %collective-permute-start.11 = (f32[66048]{0:T(1024)S(1)}, f32[66048]{0:T(1024)S(1)}, u32[]{:S(2)}, u32[]{:S(2)}) collective-permute-start(f32[66048]{0:T(1024)S(1)} %add.185), channel_id=1, source_target_pairs={{0,8},{8,16},{16,24},{24,32},{32,40},{40,48},{48,56},{56,64},{64,7... | collective-permute-start | bytes 792584 | tf_op jit(solution)/shard_map/ppermute | solution.py:17
  110.6 1.0 add_add_fusion.1
  111.7 8.3 %collective-permute-done.11 = f32[66048]{0:T(1024)S(1)} collective-permute-done((f32[66048]{0:T(1024)S(1)}, f32[66048]{0:T(1024)S(1)}, u32[]{:S(2)}, u32[]{:S(2)}) %collective-permute-start.11) | collective-permute-done | bytes 264224 | tf_op jit(solution)/shard_map/ppermute | solution.py:17
  120.0 1.1 add_add_fusion
  121.1 0.2 fusion.47
  121.3 0.2 fusion.45
  121.6 0.2 copy.31
  121.8 0.4 fusion.31
  122.3 1.1 copy-done.23
  123.4 0.5 fusion.15
  123.9 0.8 copy.35
  124.7 0.5 all_to_all.14
  125.2 20.2 %all_to_all.19 = bf16[8,64,1024]{2,1,0:T(8,128)(2,1)S(1)} all-to-all(bf16[8,64,1024]{2,1,0:T(8,128)(2,1)S(1)} %all_to_all.14), channel_id=1, replica_groups=mesh['seq'=32,'head'=8] {'head'}, dimensions={0} | all-to-all | bytes 2097152 | tf_op jit(solution)/shard_map/all_to_all | solution.py:252
  145.4 1.1 copy.47
  (65 shorter events, 0.6 us)
Async XLA Ops:
  0.0 58.0 %copy-start = (bf16[8,128,64]{1,2,0:T(8,128)(2,1)S(1)}, bf16[8,128,64]{1,2,0:T(8,128)(2,1)}, u32[]{:S(2)}) copy-start(bf16[8,128,64]{1,2,0:T(8,128)(2,1)} %param.14) | copy-start | bytes 393220
  0.0 8.8 %copy-start.14 = (bf16[512,128]{1,0:T(8,128)(2,1)S(1)}, bf16[512,128]{1,0:T(8,128)(2,1)}, u32[]{:S(2)}) copy-start(bf16[512,128]{1,0:T(8,128)(2,1)} %param.12) | copy-start | bytes 393220
  0.0 13.2 %copy-start.21 = (f32[8]{0:T(128)S(1)}, f32[8]{0:T(128)}, u32[]{:S(2)}) copy-start(f32[8]{0:T(128)} %param.16) | copy-start | bytes 100
  4.1 0.7 copy-start.2
  4.8 12.4 %copy-start.5 = (bf16[512,1,64]{2,0,1:T(8,128)(2,1)}, bf16[512,1,64]{2,0,1:T(8,128)(2,1)S(1)}, u32[]{:S(2)}) copy-start(bf16[512,1,64]{2,0,1:T(8,128)(2,1)S(1)} %get-tuple-element.23) | copy-start | bytes 196612
  4.8 12.4 %copy-start.7 = (bf16[512,1,64]{2,0,1:T(8,128)(2,1)}, bf16[512,1,64]{2,0,1:T(8,128)(2,1)S(1)}, u32[]{:S(2)}) copy-start(bf16[512,1,64]{2,0,1:T(8,128)(2,1)S(1)} %get-tuple-element.24) | copy-start | bytes 196612
  4.9 9.4 %collective-permute-start.1 = (bf16[64,1,128]{2,0,1:T(8,128)(2,1)S(1)}, bf16[64,1,128]{2,0,1:T(8,128)(2,1)S(1)}, u32[]{:S(2)}, u32[]{:S(2)}) collective-permute-start(bf16[64,1,128]{2,0,1:T(8,128)(2,1)S(1)} %pad_maximum_fusion.15), channel_id=1, source_target_pairs={{0,8},{8,16},{16,24},{24,32},{32,40},{40,48},{48,56},{56,64},{64,7... | collective-permute-start | bytes 49160 | tf_op jit(solution)/shard_map/ppermute | solution.py:17
  8.8 7.7 %collective-permute-start = (bf16[64,1,128]{2,0,1:T(8,128)(2,1)S(1)}, bf16[64,1,128]{2,0,1:T(8,128)(2,1)S(1)}, u32[]{:S(2)}, u32[]{:S(2)}) collective-permute-start(bf16[64,1,128]{2,0,1:T(8,128)(2,1)S(1)} %slice_bitcast_fusion), channel_id=1, source_target_pairs={{0,8},{8,16},{16,24},{24,32},{32,40},{40,48},{48,56},{56,64},{64,7... | collective-permute-start | bytes 49160 | tf_op jit(solution)/shard_map/ppermute | solution.py:17
  15.1 24.7 %copy-start.12 = (bf16[512,1024]{1,0:T(8,128)(2,1)S(1)}, bf16[512,1024]{1,0:T(8,128)(2,1)}, u32[]{:S(2)}) copy-start(bf16[512,1024]{1,0:T(8,128)(2,1)} %param.10) | copy-start | bytes 3145732
  16.5 0.7 copy-start.16
  21.8 12.1 %copy-start.4 = (f32[8,128,128]{2,1,0:T(8,128)S(1)}, f32[8,128,128]{2,1,0:T(8,128)}, u32[]{:S(2)}) copy-start(f32[8,128,128]{2,1,0:T(8,128)} %get-tuple-element.11) | copy-start | bytes 1572868
  22.8 11.1 %collective-permute-start.2 = (f32[66048]{0:T(1024)S(1)}, f32[66048]{0:T(1024)S(1)}, u32[]{:S(2)}, u32[]{:S(2)}) collective-permute-start(f32[66048]{0:T(1024)S(1)} %slice.59), channel_id=1, source_target_pairs={{0,8},{8,16},{16,24},{24,32},{32,40},{40,48},{48,56},{56,64},{64,7... | collective-permute-start | bytes 792584 | tf_op jit(solution)/shard_map/ppermute | solution.py:17
  33.9 0.9 copy-start.9
  34.8 25.9 %collective-permute-start.7 = (f32[66048]{0:T(1024)}, f32[66048]{0:T(1024)}, u32[]{:S(2)}, u32[]{:S(2)}) collective-permute-start(f32[66048]{0:T(1024)} %get-tuple-element.26), channel_id=1, source_target_pairs={{0,128},{8,136},{16,144},{24,152},{32,160},{40,168},{48,176},{56,1... | collective-permute-start | bytes 792584 | tf_op jit(solution)/shard_map/ppermute | solution.py:17
  42.6 4.7 %copy-start.3 = (f32[2,4,64,64]{3,2,1,0:T(8,128)S(1)}, f32[2,4,64,64]{3,2,1,0:T(8,128)}, u32[]{:S(2)}) copy-start(f32[2,4,64,64]{3,2,1,0:T(8,128)} %copy-done.2) | copy-start | bytes 393220
  44.5 19.3 %collective-permute-start.3 = (f32[66048]{0:T(1024)}, f32[66048]{0:T(1024)}, u32[]{:S(2)}, u32[]{:S(2)}) collective-permute-start(f32[66048]{0:T(1024)} %get-tuple-element.25), channel_id=1, source_target_pairs={{0,16},{8,24},{16,32},{24,40},{32,48},{40,56},{48,64},{56,72},{64,... | collective-permute-start | bytes 792584 | tf_op jit(solution)/shard_map/ppermute | solution.py:17
  47.3 2.9 %copy-start.1 = (pred[512,576]{0,1:T(8,128)(4,1)S(1)}, pred[512,576]{0,1:T(8,128)(4,1)}, u32[]{:S(2)}) copy-start(pred[512,576]{0,1:T(8,128)(4,1)} %get-tuple-element.32) | copy-start | bytes 884740
  47.3 2.9 %copy-start.6 = (bf16[512,1,64]{2,0,1:T(8,128)(2,1)S(1)}, bf16[512,1,64]{2,0,1:T(8,128)(2,1)}, u32[]{:S(2)}) copy-start(bf16[512,1,64]{2,0,1:T(8,128)(2,1)} %copy-done.5) | copy-start | bytes 196612
  47.3 2.9 %copy-start.8 = (bf16[512,1,64]{2,0,1:T(8,128)(2,1)S(1)}, bf16[512,1,64]{2,0,1:T(8,128)(2,1)}, u32[]{:S(2)}) copy-start(bf16[512,1,64]{2,0,1:T(8,128)(2,1)} %copy-done.7) | copy-start | bytes 196612
  52.5 2.0 %copy-start.15 = (bf16[512,128]{1,0:T(8,128)(2,1)S(1)}, bf16[512,128]{1,0:T(8,128)(2,1)}, u32[]{:S(2)}) copy-start(bf16[512,128]{1,0:T(8,128)(2,1)} %param.12) | copy-start | bytes 393220
  52.6 2.0 %copy-start.17 = (bf16[64,1,128]{2,0,1:T(8,128)(2,1)S(1)}, bf16[64,1,128]{2,0,1:T(8,128)(2,1)}, u32[]{:S(2)}) copy-start(bf16[64,1,128]{2,0,1:T(8,128)(2,1)} %copy-done.16) | copy-start | bytes 49156
  60.7 9.3 %copy-start.11 = (f32[512,8,64]{0,2,1:T(8,128)S(1)}, f32[512,8,64]{0,2,1:T(8,128)}, u32[]{:S(2)}) copy-start(f32[512,8,64]{0,2,1:T(8,128)} %get-tuple-element.42) | copy-start | bytes 3145732
  61.9 8.4 %collective-permute-start.8 = (f32[66048]{0:T(1024)S(1)}, f32[66048]{0:T(1024)S(1)}, u32[]{:S(2)}, u32[]{:S(2)}) collective-permute-start(f32[66048]{0:T(1024)S(1)} %add.179), channel_id=1, source_target_pairs={{0,64},{8,72},{16,80},{24,88},{32,96},{40,104},{48,112},{56,120},{... | collective-permute-start | bytes 792584 | tf_op jit(solution)/shard_map/ppermute | solution.py:17
  64.9 16.1 %collective-permute-start.4 = (f32[66048]{0:T(1024)S(1)}, f32[66048]{0:T(1024)S(1)}, u32[]{:S(2)}, u32[]{:S(2)}) collective-permute-start(f32[66048]{0:T(1024)S(1)} %add.173), channel_id=1, source_target_pairs={{0,32},{8,40},{16,48},{24,56},{32,64},{40,72},{48,80},{56,88},{64,... | collective-permute-start | bytes 792584 | tf_op jit(solution)/shard_map/ppermute | solution.py:17
  70.0 13.0 %copy-start.13 = (pred[512,576]{0,1:T(8,128)(4,1)S(1)}, pred[512,576]{0,1:T(8,128)(4,1)}, u32[]{:S(2)}) copy-start(pred[512,576]{0,1:T(8,128)(4,1)} %get-tuple-element.31) | copy-start | bytes 884740
  70.0 13.0 %copy-start.20 = (bf16[8,128,576]{2,1,0:T(8,128)(2,1)S(1)}, bf16[8,128,576]{2,1,0:T(8,128)(2,1)}, u32[]{:S(2)}) copy-start(bf16[8,128,576]{2,1,0:T(8,128)(2,1)} %get-tuple-element.13) | copy-start | bytes 3538948
  70.4 16.2 %collective-permute-start.9 = (f32[66048]{0:T(1024)S(1)}, f32[66048]{0:T(1024)S(1)}, u32[]{:S(2)}, u32[]{:S(2)}) collective-permute-start(f32[66048]{0:T(1024)S(1)} %add.181), channel_id=1, source_target_pairs={{0,32},{8,40},{16,48},{24,56},{32,64},{40,72},{48,80},{56,88},{64,... | collective-permute-start | bytes 792584 | tf_op jit(solution)/shard_map/ppermute | solution.py:17
  81.0 18.3 %collective-permute-start.5 = (f32[66048]{0:T(1024)S(1)}, f32[66048]{0:T(1024)S(1)}, u32[]{:S(2)}, u32[]{:S(2)}) collective-permute-start(f32[66048]{0:T(1024)S(1)} %add.175), channel_id=1, source_target_pairs={{0,64},{8,72},{16,80},{24,88},{32,96},{40,104},{48,112},{56,120},{... | collective-permute-start | bytes 792584 | tf_op jit(solution)/shard_map/ppermute | solution.py:17
  83.0 18.0 %copy-start.18 = (f32[8]{0:T(128)S(1)}, f32[8]{0:T(128)}, u32[]{:S(2)}) copy-start(f32[8]{0:T(128)} %get-tuple-element.17) | copy-start | bytes 100
  83.0 18.0 %copy-start.19 = (f32[8]{0:T(128)S(1)}, f32[8]{0:T(128)}, u32[]{:S(2)}) copy-start(f32[8]{0:T(128)} %get-tuple-element.18) | copy-start | bytes 100
  83.0 18.0 %copy-start.22 = (f32[128,8,512]{2,0,1:T(8,128)S(1)}, f32[128,8,512]{2,0,1:T(8,128)}, u32[]{:S(2)}) copy-start(f32[128,8,512]{2,0,1:T(8,128)} %fusion.10) | copy-start | bytes 6291460
  86.6 21.9 %collective-permute-start.10 = (f32[66048]{0:T(1024)S(1)}, f32[66048]{0:T(1024)S(1)}, u32[]{:S(2)}, u32[]{:S(2)}) collective-permute-start(f32[66048]{0:T(1024)S(1)} %add.183), channel_id=1, source_target_pairs={{0,16},{8,24},{16,32},{24,40},{32,48},{40,56},{48,64},{56,72},{64,... | collective-permute-start | bytes 792584 | tf_op jit(solution)/shard_map/ppermute | solution.py:17
  99.4 11.2 %collective-permute-start.6 = (f32[66048]{0:T(1024)S(1)}, f32[66048]{0:T(1024)S(1)}, u32[]{:S(2)}, u32[]{:S(2)}) collective-permute-start(f32[66048]{0:T(1024)S(1)} %add.177), channel_id=1, source_target_pairs={{0,128},{8,136},{16,144},{24,152},{32,160},{40,168},{48,176},{56,1... | collective-permute-start | bytes 792584 | tf_op jit(solution)/shard_map/ppermute | solution.py:17
  101.0 9.7 %copy-start.10 = (f32[66048]{0:T(1024)S(1)}, f32[66048]{0:T(1024)}, u32[]{:S(2)}) copy-start(f32[66048]{0:T(1024)} %copy-done.9) | copy-start | bytes 792580
  108.6 11.4 %collective-permute-start.11 = (f32[66048]{0:T(1024)S(1)}, f32[66048]{0:T(1024)S(1)}, u32[]{:S(2)}, u32[]{:S(2)}) collective-permute-start(f32[66048]{0:T(1024)S(1)} %add.185), channel_id=1, source_target_pairs={{0,8},{8,16},{16,24},{24,32},{32,40},{40,48},{48,56},{56,64},{64,7... | collective-permute-start | bytes 792584 | tf_op jit(solution)/shard_map/ppermute | solution.py:17
  121.8 1.6 %copy-start.23 = (f32[512,1,8,128]{0,3,2,1:T(8,128)S(1)}, f32[512,1,8,128]{0,3,2,1:T(8,128)}, u32[]{:S(2)}) copy-start(f32[512,1,8,128]{0,3,2,1:T(8,128)} %fusion.17) | copy-start | bytes 6291460
